TPU v7x, 128 devices: a whole 4x4x4 slice. The times are simulated.
128 devices in a mesh: role: 2 (over core), slab: 64 (over x, y, z).
Axes of the slice: x: 4, y: 4, z: 4, core: 2. Of those that a mesh axis runs over, the one named last changes fastest.
Arguments:
- velocity: float32 [4, 128, 128, 256], P(None, 'slab', 'role'), may hold values from -18 to 18
- basis: bfloat16 [256, 128, 128, 256], P(None, 'slab', 'role'), may hold values from -1 to 1, as said below
- mean_flow: float32 [128], replicated, may hold values from 0.2 to 2
- shear: float32 [128], replicated, may hold values from -1 to 1
Outputs:
- advanced: float32 [4, 128, 128, 256], P(None, 'slab', 'role')
- coeffs: float32 [256, 8], replicated
- rfactor: float32 [8, 8], replicated
- directions: float32 [8, 128, 128, 256], P(None, 'slab', 'role')
Inputs may be any that keep to these rules, and one draw needn't show every extreme that they name: Every column of the basis has length within a few percent of one, and distinct columns are nearly orthogonal.
All inputs are finite; a program needn't handle non-finite values.
Results may differ from a plain program's by a relative error of at most 0.00035.
The roundings to bfloat16 on the way count: a program that leaves them out, or rounds other values in their place, can miss the bound.
Values sent between devices are 32-bit elements; how exact they have to be, the bound alone decides.
No kernel may reach another device: no remote copies, remote signals or barrier semaphores. Data moves between devices by JAX's collectives and lax.ppermute only.
A program may use at most 128 MiB of HBM per device.

v0:
```python
import jax
import jax.numpy as jnp
from jax import lax
from jax.sharding import PartitionSpec as P

viscosity = 0.1
time_step = 0.4


def extended(cells, sides, width, closed):
    for axis, dim in sides:
        count = lax.axis_size(axis)
        ends = count if closed else count - 1
        head = lax.slice_in_dim(cells, 0, width, axis=dim)
        tail = lax.slice_in_dim(cells, cells.shape[dim] - width, cells.shape[dim], axis=dim)
        cells = jnp.concatenate(
            [
                lax.ppermute(tail, axis, [(i, (i + 1) % count) for i in range(ends)]),
                cells,
                lax.ppermute(head, axis, [((i + 1) % count, i) for i in range(ends)]),
            ],
            axis=dim,
        )
    return cells


def offset_slice(padded, offset, dimension, length):
    return lax.slice_in_dim(padded, 2 + offset, 2 + offset + length, axis=dimension)


def second_diff(padded, center, dimension, length):
    return (
        -offset_slice(padded, 2, dimension, length)
        + 16.0 * offset_slice(padded, 1, dimension, length)
        - 30.0 * center
        + 16.0 * offset_slice(padded, -1, dimension, length)
        - offset_slice(padded, -2, dimension, length)
    ) / 12.0


def stencil(center, xpadded, ypadded, flow_rows, shear_rows):
    nx_loc = center.shape[1]
    ny_loc = center.shape[2]
    nz_loc = center.shape[3]
    zpadded = jnp.concatenate([center[..., -2:], center, center[..., :2]], axis=3)
    first_x = (
        -offset_slice(xpadded, 2, 1, nx_loc)
        + 8.0 * offset_slice(xpadded, 1, 1, nx_loc)
        - 8.0 * offset_slice(xpadded, -1, 1, nx_loc)
        + offset_slice(xpadded, -2, 1, nx_loc)
    ) / 12.0
    laplace = (
        second_diff(xpadded, center, 1, nx_loc)
        + second_diff(ypadded, center, 2, ny_loc)
        + second_diff(zpadded, center, 3, nz_loc)
    )
    profile = flow_rows[None, None, :, None]
    result = -profile * first_x + viscosity * laplace
    shear_term = shear_rows[None, None, :, None] * center[1:2]
    return jnp.concatenate([result[:1] - shear_term, result[1:]], axis=0)


def segmented_tendency(center, flow_rows, shear_rows):
    xpadded = extended(center, (("slab", 1),), 2, True)
    ypadded = extended(center, (("role", 2),), 2, False)
    return stencil(center, xpadded, ypadded, flow_rows, shear_rows)


def on_device(velocity, basis, mean_flow, shear):
    ny_loc = velocity.shape[2]
    role_index = lax.axis_index("role")
    flow_rows = lax.dynamic_slice_in_dim(mean_flow, role_index * ny_loc, ny_loc)
    shear_rows = lax.dynamic_slice_in_dim(shear, role_index * ny_loc, ny_loc)
    tend_zero = segmented_tendency(velocity, flow_rows, shear_rows)
    segment_one = velocity + time_step * (8.0 / 15.0) * tend_zero
    tend_one = segmented_tendency(segment_one, flow_rows, shear_rows)
    advanced = segment_one + time_step * (5.0 / 12.0 * tend_one - 17.0 / 60.0 * tend_zero)
    snapshots = jnp.concatenate([segment_one, advanced], axis=0)
    flat_snaps = snapshots.reshape(snapshots.shape[0], -1)
    snaps_bf = flat_snaps.astype(jnp.bfloat16)
    basis_rows = basis.reshape(basis.shape[0], -1)
    partial_proj = jnp.einsum("km,sm->ks", basis_rows, snaps_bf, preferred_element_type=jnp.float32)
    coeffs = lax.psum(partial_proj, ("role", "slab"))
    coeffs_bf = coeffs.astype(jnp.bfloat16)
    residual = flat_snaps - jnp.einsum(
        "ks,km->sm", coeffs_bf, basis_rows, preferred_element_type=jnp.float32
    )
    local_gram = jnp.dot(residual, residual.T, precision=lax.Precision.HIGHEST)
    total_gram = lax.psum(local_gram, ("role", "slab"))
    lower_factor = jnp.linalg.cholesky(total_gram)
    directions = jax.scipy.linalg.solve_triangular(lower_factor, residual, lower=True)
    return (advanced, coeffs, lower_factor.T, directions.reshape(snapshots.shape))


def solution(mesh):
    return jax.shard_map(
        on_device,
        mesh=mesh,
        in_specs=(P(None, "slab", "role", None), P(None, "slab", "role", None), P(), P()),
        out_specs=(P(None, "slab", "role", None), P(), P(), P(None, "slab", "role", None)),
        check_vma=False,
    )
```

profile of v0, /device:TPU:0, one launch (start us, length us, event | category | flops | bytes accessed | tf_op | source)
XLA Modules:
  0.0 225.5 jit_solution(16287235402208856212)
XLA Ops:
  0.6 1.4 copy.23
  2.0 2.1 collective-permute-start.1
  4.1 6.8 %collective-permute-start = (f32[4,2,64,256]{3,0,2,1:T(4,128)S(1)}, f32[4,2,64,256]{3,0,2,1:T(4,128)S(1)}, u32[]{:S(2)}, u32[]{:S(2)}) collective-permute-start(f32[4,2,64,256]{3,0,2,1:T(4,128)S(1)} %copy.23), channel_id=1, source_target_pairs={{1,0},{2,1},{3,2},{4,3},{5,4},{6,5},{7,6},{8,7},{9,8},{10,9},{11,1... | collective-permute-start | bytes 1572872 | tf_op jit(solution)/shard_map/ppermute | solution.py:20
  10.9 1.3 collective-permute-start.2
  12.2 3.0 %collective-permute-start.3 = (f32[4,2,2,256]{3,0,2,1:T(4,128)S(1)}, f32[4,2,2,256]{3,0,2,1:T(4,128)S(1)}, u32[]{:S(2)}, u32[]{:S(2)}) collective-permute-start(f32[4,2,2,256]{3,0,2,1:T(4,128)S(1)} %get-tuple-element.13), channel_id=1, source_target_pairs={{0,64},{1,65},{2,66},{3,67},{4,68},{5,69},{6,70},{7,71},{8,72},{9,... | collective-permute-start | bytes 49160 | tf_op jit(solution)/shard_map/ppermute | solution.py:18
  15.3 0.2 fusion.58
  15.5 0.7 dynamic_slice.7
  16.2 1.0 slice_multiply_fusion.3
  17.2 0.7 negate_multiply_fusion
  17.9 0.0 collective-permute-done.3
  17.9 1.5 constant_dynamic-update-slice_fusion.1
  19.4 0.0 collective-permute-done.2
  19.4 3.3 %collective-permute-done.1 = f32[4,2,64,256]{3,0,2,1:T(4,128)S(1)} collective-permute-done((f32[4,2,64,256]{3,0,2,1:T(4,128)S(1)}, f32[4,2,64,256]{3,0,2,1:T(4,128)S(1)}, u32[]{:S(2)}, u32[]{:S(2)}) %collective-permute-start.1) | collective-permute-done | bytes 524320 | tf_op jit(solution)/shard_map/ppermute | solution.py:18
  22.8 0.0 collective-permute-done
  22.8 1.9 fusion.31
  24.7 0.1 slice.185
  24.9 0.2 slice_subtract_fusion.1
  25.1 1.6 multiply_add_fusion
  26.7 0.1 collective-permute-start.5
  26.8 7.4 %collective-permute-start.4 = (f32[4,2,64,256]{3,0,2,1:T(4,128)S(1)}, f32[4,2,64,256]{3,0,2,1:T(4,128)S(1)}, u32[]{:S(2)}, u32[]{:S(2)}) collective-permute-start(f32[4,2,64,256]{3,0,2,1:T(4,128)S(1)} %multiply_add_fusion), channel_id=1, source_target_pairs={{1,0},{2,1},{3,2},{4,3},{5,4},{6,5},{7,6},{8,7},{9,8},{10,9},{11,1... | collective-permute-start | bytes 1572872 | tf_op jit(solution)/shard_map/ppermute | solution.py:20
  34.2 0.0 copy-start
  34.2 17.9 %copy.34 = bf16[32,8,128,256]{3,1,2,0:T(8,128)(2,1)} copy(bf16[32,8,128,256]{3,2,1,0:T(8,128)(2,1)} %bitcast.33) | data formatting | bytes 33554432
  52.1 1.3 collective-permute-start.6
  53.4 3.2 %collective-permute-start.7 = (f32[4,2,2,256]{3,0,2,1:T(4,128)S(1)}, f32[4,2,2,256]{3,0,2,1:T(4,128)S(1)}, u32[]{:S(2)}, u32[]{:S(2)}) collective-permute-start(f32[4,2,2,256]{3,0,2,1:T(4,128)S(1)} %get-tuple-element.11), channel_id=1, source_target_pairs={{0,64},{1,65},{2,66},{3,67},{4,68},{5,69},{6,70},{7,71},{8,72},{9,... | collective-permute-start | bytes 49160 | tf_op jit(solution)/shard_map/ppermute | solution.py:18
  56.6 0.2 fusion.55
  56.8 0.0 collective-permute-done.6
  56.8 0.4 collective-permute-done.7
  57.3 0.0 collective-permute-done.5
  57.3 0.0 collective-permute-done.4
  57.3 2.6 %fusion.12 = f32[4,2,64,256]{3,0,2,1:T(4,128)S(1)} fusion(f32[4,2,2,256]{3,0,2,1:T(4,128)S(1)} %collective-permute-done.7, f32[4,2,64,256]{3,0,2,1:T(4,128)S(1)} %multiply_add_fusion, f32[4,2,2,256]{3,0,2,1:T(4,128)S(1)} %collective-permute-done.6, f32[4,2,64,2]{3,0,2,1:T(4,128)S(1)} %get-tuple-element.9, f32[4,2,64,2]{3,0,2,1:T(4,128)S(1)} %get-tuple-element.8, ...), kind=kLoop, calls=%fused_computation.24 | loop fusion | flops 5505024 | bytes 2138368 | tf_op jit(solution)/shard_map/add | solution.py:58
  59.8 0.2 fusion.49
  60.1 0.1 slice.200
  60.2 0.0 copy-done
  60.2 0.9 fusion.47
  61.1 20.8 %fusion.2 = f32[256,8]{0,1:T(8,128)S(1)} fusion(bf16[256,2,64,256]{3,2,1,0:T(8,128)(2,1)} %param.5, f32[4,2,64,256]{3,0,2,1:T(4,128)S(1)} %fusion.47, f32[4,2,64,256]{3,0,2,1:T(4,128)S(1)} %multiply_add_fusion), kind=kOutput, calls=%fused_computation.3 | convolution fusion | flops 135266304 | bytes 17833984 | tf_op jit(solution)/shard_map/km,sm->ks/dot_general | solution.py:82
  81.9 0.2 pad_maximum_fusion
  82.1 0.9 copy.28
  83.0 62.2 %psum.14 = f32[256,8]{0,1:T(8,128)S(1)} all-reduce(f32[256,8]{0,1:T(8,128)S(1)} %fusion.2), channel_id=1, replica_groups=mesh['role'=2,'slab'=64] {'role','slab'}, use_global_device_ids=true, to_apply=%region_0.0 | all-reduce | flops 2048 | bytes 16384 | tf_op jit(solution)/shard_map/psum | solution.py:83
  145.3 0.0 copy-start.1
  145.3 8.0 %convolution_subtract_fusion = f32[8,32768]{1,0:T(8,128)S(1)} fusion(f32[8,32768]{1,0:T(8,128)S(1)} %bitcast.36, bf16[256,32768]{1,0:T(8,128)(2,1)} %bitcast.34, f32[256,8]{0,1:T(8,128)S(1)} %psum.14), kind=kOutput, calls=%fused_computation | convolution fusion | flops 134481920 | bytes 18882560 | tf_op jit(solution)/shard_map/ks,km->sm/dot_general | solution.py:85
  153.3 2.3 %fusion.59 = f32[8,8]{0,1:T(8,128)S(1)} fusion(f32[8,32768]{1,0:T(8,128)S(1)} %convolution_subtract_fusion), kind=kOutput, calls=%fused_computation.104 | convolution fusion | flops 25165824 | bytes 1048832 | tf_op jit(solution)/shard_map/dot_general | solution.py:88
  155.7 64.0 %psum.15 = f32[8,8]{0,1:T(8,128)S(1)} all-reduce(f32[8,8]{0,1:T(8,128)S(1)} %fusion.59), channel_id=1, replica_groups=mesh['role'=2,'slab'=64] {'role','slab'}, use_global_device_ids=true, to_apply=%region_1.0 | all-reduce | flops 64 | bytes 512 | tf_op jit(solution)/shard_map/psum | solution.py:89
  219.7 0.1 copy.26
  219.8 0.7 cholesky.18
  220.5 0.1 select_reduce_fusion
  220.5 0.6 compare_reduce_fusion
  221.2 0.6 select_bitcast_fusion
  221.8 0.6 custom-call.7
  222.4 1.0 fusion.50
  223.5 1.3 copy.30
  224.8 0.7 copy.29
  225.5 0.0 copy-done.1
  (5 shorter events, 0.0 us)
Async XLA Ops:
  2.0 20.8 %collective-permute-start.1 = (f32[4,2,64,256]{3,0,2,1:T(4,128)S(1)}, f32[4,2,64,256]{3,0,2,1:T(4,128)S(1)}, u32[]{:S(2)}, u32[]{:S(2)}) collective-permute-start(f32[4,2,64,256]{3,0,2,1:T(4,128)S(1)} %copy.23), channel_id=1, source_target_pairs={{0,1},{1,2},{2,3},{3,4},{4,5},{5,6},{6,7},{7,8},{8,9},{9,10},{10,1... | collective-permute-start | bytes 1572872 | tf_op jit(solution)/shard_map/ppermute | solution.py:18
  4.1 18.7 %collective-permute-start = (f32[4,2,64,256]{3,0,2,1:T(4,128)S(1)}, f32[4,2,64,256]{3,0,2,1:T(4,128)S(1)}, u32[]{:S(2)}, u32[]{:S(2)}) collective-permute-start(f32[4,2,64,256]{3,0,2,1:T(4,128)S(1)} %copy.23), channel_id=1, source_target_pairs={{1,0},{2,1},{3,2},{4,3},{5,4},{6,5},{7,6},{8,7},{9,8},{10,9},{11,1... | collective-permute-start | bytes 1572872 | tf_op jit(solution)/shard_map/ppermute | solution.py:20
  10.9 8.5 %collective-permute-start.2 = (f32[4,2,2,256]{3,0,2,1:T(4,128)S(1)}, f32[4,2,2,256]{3,0,2,1:T(4,128)S(1)}, u32[]{:S(2)}, u32[]{:S(2)}) collective-permute-start(f32[4,2,2,256]{3,0,2,1:T(4,128)S(1)} %get-tuple-element.12), channel_id=1, source_target_pairs={{64,0},{65,1},{66,2},{67,3},{68,4},{69,5},{70,6},{71,7},{72,8},{73... | collective-permute-start | bytes 49160 | tf_op jit(solution)/shard_map/ppermute | solution.py:20
  12.2 5.7 %collective-permute-start.3 = (f32[4,2,2,256]{3,0,2,1:T(4,128)S(1)}, f32[4,2,2,256]{3,0,2,1:T(4,128)S(1)}, u32[]{:S(2)}, u32[]{:S(2)}) collective-permute-start(f32[4,2,2,256]{3,0,2,1:T(4,128)S(1)} %get-tuple-element.13), channel_id=1, source_target_pairs={{0,64},{1,65},{2,66},{3,67},{4,68},{5,69},{6,70},{7,71},{8,72},{9,... | collective-permute-start | bytes 49160 | tf_op jit(solution)/shard_map/ppermute | solution.py:18
  26.7 30.6 %collective-permute-start.5 = (f32[4,2,64,256]{3,0,2,1:T(4,128)S(1)}, f32[4,2,64,256]{3,0,2,1:T(4,128)S(1)}, u32[]{:S(2)}, u32[]{:S(2)}) collective-permute-start(f32[4,2,64,256]{3,0,2,1:T(4,128)S(1)} %multiply_add_fusion), channel_id=1, source_target_pairs={{0,1},{1,2},{2,3},{3,4},{4,5},{5,6},{6,7},{7,8},{8,9},{9,10},{10,1... | collective-permute-start | bytes 1572872 | tf_op jit(solution)/shard_map/ppermute | solution.py:18
  26.8 30.5 %collective-permute-start.4 = (f32[4,2,64,256]{3,0,2,1:T(4,128)S(1)}, f32[4,2,64,256]{3,0,2,1:T(4,128)S(1)}, u32[]{:S(2)}, u32[]{:S(2)}) collective-permute-start(f32[4,2,64,256]{3,0,2,1:T(4,128)S(1)} %multiply_add_fusion), channel_id=1, source_target_pairs={{1,0},{2,1},{3,2},{4,3},{5,4},{6,5},{7,6},{8,7},{9,8},{10,9},{11,1... | collective-permute-start | bytes 1572872 | tf_op jit(solution)/shard_map/ppermute | solution.py:20
  34.2 26.0 %copy-start = (f32[4,2,64,256]{3,2,1,0:T(8,128)S(1)}, f32[4,2,64,256]{3,2,1,0:T(8,128)}, u32[]{:S(2)}) copy-start(f32[4,2,64,256]{3,2,1,0:T(8,128)} %param.4) | copy-start | bytes 1572868
  52.1 4.7 %collective-permute-start.6 = (f32[4,2,2,256]{3,0,2,1:T(4,128)S(1)}, f32[4,2,2,256]{3,0,2,1:T(4,128)S(1)}, u32[]{:S(2)}, u32[]{:S(2)}) collective-permute-start(f32[4,2,2,256]{3,0,2,1:T(4,128)S(1)} %get-tuple-element.10), channel_id=1, source_target_pairs={{64,0},{65,1},{66,2},{67,3},{68,4},{69,5},{70,6},{71,7},{72,8},{73... | collective-permute-start | bytes 49160 | tf_op jit(solution)/shard_map/ppermute | solution.py:20
  53.4 3.9 %collective-permute-start.7 = (f32[4,2,2,256]{3,0,2,1:T(4,128)S(1)}, f32[4,2,2,256]{3,0,2,1:T(4,128)S(1)}, u32[]{:S(2)}, u32[]{:S(2)}) collective-permute-start(f32[4,2,2,256]{3,0,2,1:T(4,128)S(1)} %get-tuple-element.11), channel_id=1, source_target_pairs={{0,64},{1,65},{2,66},{3,67},{4,68},{5,69},{6,70},{7,71},{8,72},{9,... | collective-permute-start | bytes 49160 | tf_op jit(solution)/shard_map/ppermute | solution.py:18
  145.3 80.2 %copy-start.1 = (f32[256,8]{0,1:T(8,128)}, f32[256,8]{0,1:T(8,128)S(1)}, u32[]{:S(2)}) copy-start(f32[256,8]{0,1:T(8,128)S(1)} %psum.14) | copy-start | bytes 24580
where the time goes:
time: 227 us; the launch traced here: 225 us
  blocking collectives  126 us (56%)
  matrix products  32.2 us (14%)
  starting transfers between devices  25.2 us (11%)
  local copies, waits for them, and re-layouts  25.1 us (11%)
  other arithmetic  12 us (5%)
  waiting for transfers between devices  3.79 us (2%)
    psum x1, blocking collectives, on_device(): total_gram = lax.psum(local_gram, ('role', 'slab'))  64 us
    psum x1, blocking collectives, on_device(): coeffs = lax.psum(partial_proj, ('role', 'slab'))  62.2 us
    unnamed x11, local copies, waits for them, and re-layouts  23.6 us
    dot_general x1, matrix products, on_device(): jnp.einsum('km,sm->ks', basis_rows, snaps_bf, preferred_element_type=jnp....  20.8 us
    ppermute x4, starting transfers between devices, extended(): lax.ppermute(head, axis, [((i + 1) % count, i) for i in range(ends)])  16.8 us
    ppermute x4, starting transfers between devices, extended(): lax.ppermute(tail, axis, [(i, (i + 1) % count) for i in range(ends)])  8.38 us
    dot_general x1, matrix products, on_device(): jnp.einsum('ks,km->sm', coeffs_bf, basis_rows, preferred_element_type=jnp...  8.05 us
  transfers between devices with their start and end apart: 8, of which 2 were waited for; matrix products, arithmetic and copies ran while one was open for 10% of the time, Pallas kernels for 0%

commit v1 on v0

--- a/solution.py
+++ b/solution.py
@@ -22,6 +22,40 @@
             axis=dim,
         )
     return cells
+
+
+def ring_pairs(size, stride, count, second):
+    pairs = []
+    for i in range(count):
+        digit = (i // stride) % size
+        if size == 2 or not second:
+            partner = digit ^ 1
+        else:
+            partner = (digit + 1) % size if digit % 2 else (digit - 1) % size
+        pairs.append((i, i + (partner - digit) * stride))
+    return pairs
+
+
+def exchange_rounds(axis, count):
+    rounds = []
+    stride = 1
+    while stride < count:
+        size = 4 if count % (stride * 4) == 0 else 2
+        rounds.append(ring_pairs(size, stride, count, False))
+        if size == 4:
+            rounds.append(ring_pairs(size, stride, count, True))
+        stride *= size
+    return [(axis, pairs) for pairs in rounds]
+
+
+def allreduce(value, axes):
+    sizes = [lax.axis_size(axis) for axis in axes]
+    if any(size & (size - 1) for size in sizes):
+        return lax.psum(value, axes)
+    for axis, size in zip(axes, sizes):
+        for name, pairs in exchange_rounds(axis, size):
+            value = value + lax.ppermute(value, name, pairs)
+    return value
 
 
 def offset_slice(padded, offset, dimension, length):
@@ -80,13 +114,13 @@
     snaps_bf = flat_snaps.astype(jnp.bfloat16)
     basis_rows = basis.reshape(basis.shape[0], -1)
     partial_proj = jnp.einsum("km,sm->ks", basis_rows, snaps_bf, preferred_element_type=jnp.float32)
-    coeffs = lax.psum(partial_proj, ("role", "slab"))
+    coeffs = allreduce(partial_proj, ("role", "slab"))
     coeffs_bf = coeffs.astype(jnp.bfloat16)
     residual = flat_snaps - jnp.einsum(
         "ks,km->sm", coeffs_bf, basis_rows, preferred_element_type=jnp.float32
     )
     local_gram = jnp.dot(residual, residual.T, precision=lax.Precision.HIGHEST)
-    total_gram = lax.psum(local_gram, ("role", "slab"))
+    total_gram = allreduce(local_gram, ("role", "slab"))
     lower_factor = jnp.linalg.cholesky(total_gram)
     directions = jax.scipy.linalg.solve_triangular(lower_factor, residual, lower=True)
     return (advanced, coeffs, lower_factor.T, directions.reshape(snapshots.shape))

time: 227 us -> 146 us (0.64)
  blocking collectives: 126 us -> 0 us
  waiting for transfers between devices: 3.79 us -> 50 us
  starting transfers between devices: 25.2 us -> 33.7 us
  matrix products: 32.2 us -> 26.3 us
    psum x2 -> x0, blocking collectives: 126 us -> none  [the longest x1 64 us: on_device(): total_gram = lax.psum(local_gram, ('role', 'slab'))]
    ppermute x0 -> x14, waiting for transfers between devices: none -> 40.2 us  [allreduce(): value = value + lax.ppermute(value, name, pairs)]
    ppermute x0 -> x14, starting transfers between devices: none -> 8.47 us  [allreduce(): value = value + lax.ppermute(value, name, pairs)]
    ppermute x4, waiting for transfers between devices: 3.78 us -> 9.71 us  [extended(): lax.ppermute(tail, axis, [(i, (i + 1) % count) for i in range(ends)])]
    dot_general x1, matrix products: 8.05 us -> 2.3 us  [on_device(): jnp.einsum('ks,km->sm', coeffs_bf, basis_rows, preferred_element_type=jnp...]
  transfers between devices with their start and end apart: 8 -> 22, of which waited for: 2 -> 16; matrix products, arithmetic and copies ran while one was open for 10% -> 15% of each run, Pallas kernels for 0% -> 0%
where the time goes in v1:
time: 146 us
  waiting for transfers between devices  50 us (34%)
  starting transfers between devices  33.7 us (23%)
  matrix products  26.3 us (18%)
  local copies, waits for them, and re-layouts  23.1 us (16%)
  other arithmetic  12.1 us (8%)
    ppermute x14, waiting for transfers between devices, allreduce(): value = value + lax.ppermute(value, name, pairs)  40.2 us
    unnamed x11, local copies, waits for them, and re-layouts  21.6 us
    dot_general x1, matrix products, on_device(): jnp.einsum('km,sm->ks', basis_rows, snaps_bf, preferred_element_type=jnp....  20.7 us
    ppermute x4, starting transfers between devices, extended(): lax.ppermute(head, axis, [((i + 1) % count, i) for i in range(ends)])  16.8 us
    ppermute x4, waiting for transfers between devices, extended(): lax.ppermute(tail, axis, [(i, (i + 1) % count) for i in range(ends)])  9.71 us
    ppermute x14, starting transfers between devices, allreduce(): value = value + lax.ppermute(value, name, pairs)  8.47 us
    ppermute x4, starting transfers between devices, extended(): lax.ppermute(tail, axis, [(i, (i + 1) % count) for i in range(ends)])  8.38 us
    add x2, other arithmetic, stencil(): result = -profile * first_x + viscosity * laplace  4.52 us
  transfers between devices with their start and end apart: 22, of which 16 were waited for; matrix products, arithmetic and copies ran while one was open for 15% of the time, Pallas kernels for 0%

profile of v1, /device:TPU:0, one launch (start us, length us, event | category | flops | bytes accessed | tf_op | source)
XLA Modules:
  0.0 146.0 jit_solution(16724926785958282069)
XLA Ops:
  0.6 0.0 copy-start
  0.6 1.4 copy.23
  2.1 2.1 %collective-permute-start.1 = (f32[4,2,64,256]{3,0,2,1:T(4,128)S(1)}, f32[4,2,64,256]{3,0,2,1:T(4,128)S(1)}, u32[]{:S(2)}, u32[]{:S(2)}) collective-permute-start(f32[4,2,64,256]{3,0,2,1:T(4,128)S(1)} %copy.23), channel_id=1, source_target_pairs={{0,1},{1,2},{2,3},{3,4},{4,5},{5,6},{6,7},{7,8},{8,9},{9,10},{10,1... | collective-permute-start | bytes 1572872 | tf_op jit(solution)/shard_map/ppermute | solution.py:18
  4.2 6.8 %collective-permute-start = (f32[4,2,64,256]{3,0,2,1:T(4,128)S(1)}, f32[4,2,64,256]{3,0,2,1:T(4,128)S(1)}, u32[]{:S(2)}, u32[]{:S(2)}) collective-permute-start(f32[4,2,64,256]{3,0,2,1:T(4,128)S(1)} %copy.23), channel_id=1, source_target_pairs={{1,0},{2,1},{3,2},{4,3},{5,4},{6,5},{7,6},{8,7},{9,8},{10,9},{11,1... | collective-permute-start | bytes 1572872 | tf_op jit(solution)/shard_map/ppermute | solution.py:20
  11.0 1.3 collective-permute-start.2
  12.3 3.0 %collective-permute-start.3 = (f32[4,2,2,256]{3,0,2,1:T(4,128)S(1)}, f32[4,2,2,256]{3,0,2,1:T(4,128)S(1)}, u32[]{:S(2)}, u32[]{:S(2)}) collective-permute-start(f32[4,2,2,256]{3,0,2,1:T(4,128)S(1)} %get-tuple-element.13), channel_id=1, source_target_pairs={{0,64},{1,65},{2,66},{3,67},{4,68},{5,69},{6,70},{7,71},{8,72},{9,... | collective-permute-start | bytes 49160 | tf_op jit(solution)/shard_map/ppermute | solution.py:18
  15.3 0.2 fusion.58
  15.5 0.7 dynamic_slice.7
  16.3 1.0 slice_multiply_fusion.3
  17.3 0.7 negate_multiply_fusion
  18.0 1.5 %constant_dynamic-update-slice_fusion.1 = (f32[4,2,66,256]{3,0,2,1:T(4,128)S(1)}, f32[4,2,66,256]{3,0,2,1:T(4,128)S(1)}) fusion(f32[4,2,64,256]{3,2,1,0:T(8,128)} %param.4, f32[4,2,66,256]{3,0,2,1:T(4,128)S(1)} %constant_dynamic-update-slice_fusion.3), kind=kLoop, calls=%fused_computation.84 | loop fusion | bytes 1572864
  19.5 0.0 collective-permute-done.2
  19.5 3.3 %collective-permute-done.1 = f32[4,2,64,256]{3,0,2,1:T(4,128)S(1)} collective-permute-done((f32[4,2,64,256]{3,0,2,1:T(4,128)S(1)}, f32[4,2,64,256]{3,0,2,1:T(4,128)S(1)}, u32[]{:S(2)}, u32[]{:S(2)}) %collective-permute-start.1) | collective-permute-done | bytes 524320 | tf_op jit(solution)/shard_map/ppermute | solution.py:18
  22.8 0.0 collective-permute-done
  22.9 1.9 %fusion.31 = f32[4,2,64,256]{3,0,2,1:T(4,128)S(1)} fusion(f32[4,2,64,2]{3,0,2,1:T(4,128)S(1)} %get-tuple-element.17, f32[4,2,64,256]{3,0,2,1:T(4,128)S(1)} %copy.23, f32[4,2,64,2]{3,0,2,1:T(4,128)S(1)} %get-tuple-element.16, f32[4,2,66,256]{3,0,2,1:T(4,128)S(1)} %get-tuple-element.15, f32[4,2,66,256]{3,0,2,1:T(4,128)S(1)} %constant_dynamic-update-slice_fusion, ...), kind=kLoop, calls=%fused_computation.43 | loop fusion | flops 4980736 | bytes 4202752 | tf_op jit(solution)/shard_map/add | solution.py:92
  24.8 0.1 slice.185
  25.0 0.2 slice_subtract_fusion.1
  25.1 1.6 %multiply_add_fusion = f32[4,2,64,256]{3,0,2,1:T(4,128)S(1)} fusion(f32[3,2,64,256]{3,0,2,1:T(4,128)S(1)} %slice.185, f32[1,2,64,256]{3,0,2,1:T(1,128)S(1)} %slice_subtract_fusion.1, f32[4,2,64,256]{3,2,1,0:T(8,128)} %param.4), kind=kLoop, calls=%fused_computation.78 | loop fusion | flops 393216 | bytes 1572864 | tf_op jit(solution)/shard_map/add | solution.py:109
  26.8 0.1 collective-permute-start.5
  26.8 7.4 %collective-permute-start.4 = (f32[4,2,64,256]{3,0,2,1:T(4,128)S(1)}, f32[4,2,64,256]{3,0,2,1:T(4,128)S(1)}, u32[]{:S(2)}, u32[]{:S(2)}) collective-permute-start(f32[4,2,64,256]{3,0,2,1:T(4,128)S(1)} %multiply_add_fusion), channel_id=1, source_target_pairs={{1,0},{2,1},{3,2},{4,3},{5,4},{6,5},{7,6},{8,7},{9,8},{10,9},{11,1... | collective-permute-start | bytes 1572872 | tf_op jit(solution)/shard_map/ppermute | solution.py:20
  34.3 1.3 collective-permute-start.6
  35.6 3.2 %collective-permute-start.7 = (f32[4,2,2,256]{3,0,2,1:T(4,128)S(1)}, f32[4,2,2,256]{3,0,2,1:T(4,128)S(1)}, u32[]{:S(2)}, u32[]{:S(2)}) collective-permute-start(f32[4,2,2,256]{3,0,2,1:T(4,128)S(1)} %get-tuple-element.11), channel_id=1, source_target_pairs={{0,64},{1,65},{2,66},{3,67},{4,68},{5,69},{6,70},{7,71},{8,72},{9,... | collective-permute-start | bytes 49160 | tf_op jit(solution)/shard_map/ppermute | solution.py:18
  38.8 0.2 fusion.55
  39.0 0.0 collective-permute-done.6
  39.0 0.4 collective-permute-done.7
  39.4 5.9 %collective-permute-done.5 = f32[4,2,64,256]{3,0,2,1:T(4,128)S(1)} collective-permute-done((f32[4,2,64,256]{3,0,2,1:T(4,128)S(1)}, f32[4,2,64,256]{3,0,2,1:T(4,128)S(1)}, u32[]{:S(2)}, u32[]{:S(2)}) %collective-permute-start.5) | collective-permute-done | bytes 524320 | tf_op jit(solution)/shard_map/ppermute | solution.py:18
  45.4 2.6 %fusion.12 = f32[4,2,64,256]{3,0,2,1:T(4,128)S(1)} fusion(f32[4,2,2,256]{3,0,2,1:T(4,128)S(1)} %collective-permute-done.7, f32[4,2,64,256]{3,0,2,1:T(4,128)S(1)} %multiply_add_fusion, f32[4,2,2,256]{3,0,2,1:T(4,128)S(1)} %collective-permute-done.6, f32[4,2,64,2]{3,0,2,1:T(4,128)S(1)} %get-tuple-element.9, f32[4,2,64,2]{3,0,2,1:T(4,128)S(1)} %get-tuple-element.8, ...), kind=kLoop, calls=%fused_computation.24 | loop fusion | flops 5505024 | bytes 2138368 | tf_op jit(solution)/shard_map/add | solution.py:92
  48.0 0.2 fusion.49
  48.2 0.1 slice.200
  48.3 0.9 fusion.47
  49.3 20.7 %fusion.2 = f32[256,8]{0,1:T(8,128)S(1)} fusion(bf16[256,2,64,256]{3,2,1,0:T(8,128)(2,1)} %param.5, f32[4,2,64,256]{3,0,2,1:T(4,128)S(1)} %fusion.47, f32[4,2,64,256]{3,0,2,1:T(4,128)S(1)} %multiply_add_fusion), kind=kOutput, calls=%fused_computation.3 | convolution fusion | flops 135266304 | bytes 17833984 | tf_op jit(solution)/shard_map/km,sm->ks/dot_general | solution.py:116
  69.9 0.2 collective-permute-start.8
  70.1 1.2 collective-permute-done.8
  71.3 0.0 collective-permute-start.9
  71.3 3.6 %collective-permute-done.9 = f32[256,8]{0,1:T(8,128)S(1)} collective-permute-done((f32[256,8]{0,1:T(8,128)S(1)}, f32[256,8]{0,1:T(8,128)S(1)}, u32[]{:S(2)}, u32[]{:S(2)}) %collective-permute-start.9) | collective-permute-done | bytes 8224 | tf_op jit(solution)/shard_map/ppermute | solution.py:57
  75.0 4.9 %collective-permute-done.10 = f32[256,8]{0,1:T(8,128)S(1)} collective-permute-done((f32[256,8]{0,1:T(8,128)S(1)}, f32[256,8]{0,1:T(8,128)S(1)}, u32[]{:S(2)}, u32[]{:S(2)}) %collective-permute-start.10) | collective-permute-done | bytes 8224 | tf_op jit(solution)/shard_map/ppermute | solution.py:57
  79.8 3.6 %collective-permute-done.11 = f32[256,8]{0,1:T(8,128)S(1)} collective-permute-done((f32[256,8]{0,1:T(8,128)S(1)}, f32[256,8]{0,1:T(8,128)S(1)}, u32[]{:S(2)}, u32[]{:S(2)}) %collective-permute-start.11) | collective-permute-done | bytes 8224 | tf_op jit(solution)/shard_map/ppermute | solution.py:57
  83.5 4.9 %collective-permute-done.12 = f32[256,8]{0,1:T(8,128)S(1)} collective-permute-done((f32[256,8]{0,1:T(8,128)S(1)}, f32[256,8]{0,1:T(8,128)S(1)}, u32[]{:S(2)}, u32[]{:S(2)}) %collective-permute-start.12) | collective-permute-done | bytes 8224 | tf_op jit(solution)/shard_map/ppermute | solution.py:57
  88.3 15.8 %copy.35 = bf16[32,8,128,256]{3,1,2,0:T(8,128)(2,1)S(1)} copy(bf16[32,8,128,256]{3,2,1,0:T(8,128)(2,1)} %bitcast.33) | data formatting | bytes 33554432
  104.2 1.9 %collective-permute-start.14 = (f32[256,8]{0,1:T(8,128)S(1)}, f32[256,8]{0,1:T(8,128)S(1)}, u32[]{:S(2)}, u32[]{:S(2)}) collective-permute-start(f32[256,8]{0,1:T(8,128)S(1)} %add.160), channel_id=1, source_target_pairs={{0,48},{1,49},{2,50},{3,51},{4,52},{5,53},{6,54},{7,55},{8,56},{9,... | collective-permute-start | bytes 24584 | tf_op jit(solution)/shard_map/ppermute | solution.py:57
  106.1 0.2 pad_maximum_fusion
  106.3 2.8 %collective-permute-done.14 = f32[256,8]{0,1:T(8,128)S(1)} collective-permute-done((f32[256,8]{0,1:T(8,128)S(1)}, f32[256,8]{0,1:T(8,128)S(1)}, u32[]{:S(2)}, u32[]{:S(2)}) %collective-permute-start.14) | collective-permute-done | bytes 8224 | tf_op jit(solution)/shard_map/ppermute | solution.py:57
  109.1 2.3 %convolution_subtract_fusion = f32[8,32768]{1,0:T(8,128)S(1)} fusion(f32[8,32768]{1,0:T(8,128)S(1)} %bitcast.36, bf16[256,32768]{1,0:T(8,128)(2,1)S(1)} %bitcast.34, f32[256,8]{0,1:T(8,128)S(1)} %add.161), kind=kOutput, calls=%fused_computation | convolution fusion | flops 134481920 | bytes 18882560 | tf_op jit(solution)/shard_map/ks,km->sm/dot_general | solution.py:119
  111.4 2.3 %fusion.59 = f32[8,8]{0,1:T(8,128)S(1)} fusion(f32[8,32768]{1,0:T(8,128)S(1)} %convolution_subtract_fusion), kind=kOutput, calls=%fused_computation.104 | convolution fusion | flops 25165824 | bytes 1048832 | tf_op jit(solution)/shard_map/dot_general | solution.py:122
  113.8 1.2 collective-permute-done.15
  115.0 3.6 %collective-permute-done.16 = f32[8,8]{0,1:T(8,128)S(1)} collective-permute-done((f32[8,8]{0,1:T(8,128)S(1)}, f32[8,8]{0,1:T(8,128)S(1)}, u32[]{:S(2)}, u32[]{:S(2)}) %collective-permute-start.16) | collective-permute-done | bytes 288 | tf_op jit(solution)/shard_map/ppermute | solution.py:57
  118.6 1.8 %collective-permute-start.17 = (f32[8,8]{0,1:T(8,128)S(1)}, f32[8,8]{0,1:T(8,128)S(1)}, u32[]{:S(2)}, u32[]{:S(2)}) collective-permute-start(f32[8,8]{0,1:T(8,128)S(1)} %add.163), channel_id=1, source_target_pairs={{0,3},{1,2},{2,1},{3,0},{4,7},{5,6},{6,5},{7,4},{8,11},{9,10},{10,... | collective-permute-start | bytes 776 | tf_op jit(solution)/shard_map/ppermute | solution.py:57
  120.4 3.0 %collective-permute-done.17 = f32[8,8]{0,1:T(8,128)S(1)} collective-permute-done((f32[8,8]{0,1:T(8,128)S(1)}, f32[8,8]{0,1:T(8,128)S(1)}, u32[]{:S(2)}, u32[]{:S(2)}) %collective-permute-start.17) | collective-permute-done | bytes 288 | tf_op jit(solution)/shard_map/ppermute | solution.py:57
  123.4 3.6 %collective-permute-done.18 = f32[8,8]{0,1:T(8,128)S(1)} collective-permute-done((f32[8,8]{0,1:T(8,128)S(1)}, f32[8,8]{0,1:T(8,128)S(1)}, u32[]{:S(2)}, u32[]{:S(2)}) %collective-permute-start.18) | collective-permute-done | bytes 288 | tf_op jit(solution)/shard_map/ppermute | solution.py:57
  127.0 1.8 %collective-permute-start.19 = (f32[8,8]{0,1:T(8,128)S(1)}, f32[8,8]{0,1:T(8,128)S(1)}, u32[]{:S(2)}, u32[]{:S(2)}) collective-permute-start(f32[8,8]{0,1:T(8,128)S(1)} %add.165), channel_id=1, source_target_pairs={{0,12},{1,13},{2,14},{3,15},{4,8},{5,9},{6,10},{7,11},{8,4},{9,5},... | collective-permute-start | bytes 776 | tf_op jit(solution)/shard_map/ppermute | solution.py:57
  128.8 3.0 %collective-permute-done.19 = f32[8,8]{0,1:T(8,128)S(1)} collective-permute-done((f32[8,8]{0,1:T(8,128)S(1)}, f32[8,8]{0,1:T(8,128)S(1)}, u32[]{:S(2)}, u32[]{:S(2)}) %collective-permute-start.19) | collective-permute-done | bytes 288 | tf_op jit(solution)/shard_map/ppermute | solution.py:57
  131.8 0.8 collective-permute-start.20
  132.6 2.8 %collective-permute-done.20 = f32[8,8]{0,1:T(8,128)S(1)} collective-permute-done((f32[8,8]{0,1:T(8,128)S(1)}, f32[8,8]{0,1:T(8,128)S(1)}, u32[]{:S(2)}, u32[]{:S(2)}) %collective-permute-start.20) | collective-permute-done | bytes 288 | tf_op jit(solution)/shard_map/ppermute | solution.py:57
  135.4 1.8 %collective-permute-start.21 = (f32[8,8]{0,1:T(8,128)S(1)}, f32[8,8]{0,1:T(8,128)S(1)}, u32[]{:S(2)}, u32[]{:S(2)}) collective-permute-start(f32[8,8]{0,1:T(8,128)S(1)} %add.167), channel_id=1, source_target_pairs={{0,48},{1,49},{2,50},{3,51},{4,52},{5,53},{6,54},{7,55},{8,56},{9,... | collective-permute-start | bytes 776 | tf_op jit(solution)/shard_map/ppermute | solution.py:57
  137.3 0.9 copy.29
  138.2 2.1 %collective-permute-done.21 = f32[8,8]{0,1:T(8,128)S(1)} collective-permute-done((f32[8,8]{0,1:T(8,128)S(1)}, f32[8,8]{0,1:T(8,128)S(1)}, u32[]{:S(2)}, u32[]{:S(2)}) %collective-permute-start.21) | collective-permute-done | bytes 288 | tf_op jit(solution)/shard_map/ppermute | solution.py:57
  140.3 0.1 copy.27
  140.3 0.7 cholesky.18
  141.1 0.6 compare_reduce_fusion
  141.7 0.6 select_bitcast_fusion
  142.4 0.6 custom-call.7
  143.0 1.0 fusion.50
  144.1 1.3 copy.31
  145.4 0.7 copy.30
  (33 shorter events, 0.2 us)
Async XLA Ops:
  0.6 47.7 %copy-start = (f32[4,2,64,256]{3,2,1,0:T(8,128)S(1)}, f32[4,2,64,256]{3,2,1,0:T(8,128)}, u32[]{:S(2)}) copy-start(f32[4,2,64,256]{3,2,1,0:T(8,128)} %param.4) | copy-start | bytes 1572868
  2.1 20.8 %collective-permute-start.1 = (f32[4,2,64,256]{3,0,2,1:T(4,128)S(1)}, f32[4,2,64,256]{3,0,2,1:T(4,128)S(1)}, u32[]{:S(2)}, u32[]{:S(2)}) collective-permute-start(f32[4,2,64,256]{3,0,2,1:T(4,128)S(1)} %copy.23), channel_id=1, source_target_pairs={{0,1},{1,2},{2,3},{3,4},{4,5},{5,6},{6,7},{7,8},{8,9},{9,10},{10,1... | collective-permute-start | bytes 1572872 | tf_op jit(solution)/shard_map/ppermute | solution.py:18
  4.2 18.7 %collective-permute-start = (f32[4,2,64,256]{3,0,2,1:T(4,128)S(1)}, f32[4,2,64,256]{3,0,2,1:T(4,128)S(1)}, u32[]{:S(2)}, u32[]{:S(2)}) collective-permute-start(f32[4,2,64,256]{3,0,2,1:T(4,128)S(1)} %copy.23), channel_id=1, source_target_pairs={{1,0},{2,1},{3,2},{4,3},{5,4},{6,5},{7,6},{8,7},{9,8},{10,9},{11,1... | collective-permute-start | bytes 1572872 | tf_op jit(solution)/shard_map/ppermute | solution.py:20
  11.0 8.5 %collective-permute-start.2 = (f32[4,2,2,256]{3,0,2,1:T(4,128)S(1)}, f32[4,2,2,256]{3,0,2,1:T(4,128)S(1)}, u32[]{:S(2)}, u32[]{:S(2)}) collective-permute-start(f32[4,2,2,256]{3,0,2,1:T(4,128)S(1)} %get-tuple-element.12), channel_id=1, source_target_pairs={{64,0},{65,1},{66,2},{67,3},{68,4},{69,5},{70,6},{71,7},{72,8},{73... | collective-permute-start | bytes 49160 | tf_op jit(solution)/shard_map/ppermute | solution.py:20
  12.3 5.7 %collective-permute-start.3 = (f32[4,2,2,256]{3,0,2,1:T(4,128)S(1)}, f32[4,2,2,256]{3,0,2,1:T(4,128)S(1)}, u32[]{:S(2)}, u32[]{:S(2)}) collective-permute-start(f32[4,2,2,256]{3,0,2,1:T(4,128)S(1)} %get-tuple-element.13), channel_id=1, source_target_pairs={{0,64},{1,65},{2,66},{3,67},{4,68},{5,69},{6,70},{7,71},{8,72},{9,... | collective-permute-start | bytes 49160 | tf_op jit(solution)/shard_map/ppermute | solution.py:18
  26.8 18.6 %collective-permute-start.5 = (f32[4,2,64,256]{3,0,2,1:T(4,128)S(1)}, f32[4,2,64,256]{3,0,2,1:T(4,128)S(1)}, u32[]{:S(2)}, u32[]{:S(2)}) collective-permute-start(f32[4,2,64,256]{3,0,2,1:T(4,128)S(1)} %multiply_add_fusion), channel_id=1, source_target_pairs={{0,1},{1,2},{2,3},{3,4},{4,5},{5,6},{6,7},{7,8},{8,9},{9,10},{10,1... | collective-permute-start | bytes 1572872 | tf_op jit(solution)/shard_map/ppermute | solution.py:18
  26.8 18.5 %collective-permute-start.4 = (f32[4,2,64,256]{3,0,2,1:T(4,128)S(1)}, f32[4,2,64,256]{3,0,2,1:T(4,128)S(1)}, u32[]{:S(2)}, u32[]{:S(2)}) collective-permute-start(f32[4,2,64,256]{3,0,2,1:T(4,128)S(1)} %multiply_add_fusion), channel_id=1, source_target_pairs={{1,0},{2,1},{3,2},{4,3},{5,4},{6,5},{7,6},{8,7},{9,8},{10,9},{11,1... | collective-permute-start | bytes 1572872 | tf_op jit(solution)/shard_map/ppermute | solution.py:20
  34.3 4.7 %collective-permute-start.6 = (f32[4,2,2,256]{3,0,2,1:T(4,128)S(1)}, f32[4,2,2,256]{3,0,2,1:T(4,128)S(1)}, u32[]{:S(2)}, u32[]{:S(2)}) collective-permute-start(f32[4,2,2,256]{3,0,2,1:T(4,128)S(1)} %get-tuple-element.10), channel_id=1, source_target_pairs={{64,0},{65,1},{66,2},{67,3},{68,4},{69,5},{70,6},{71,7},{72,8},{73... | collective-permute-start | bytes 49160 | tf_op jit(solution)/shard_map/ppermute | solution.py:20
  35.6 3.9 %collective-permute-start.7 = (f32[4,2,2,256]{3,0,2,1:T(4,128)S(1)}, f32[4,2,2,256]{3,0,2,1:T(4,128)S(1)}, u32[]{:S(2)}, u32[]{:S(2)}) collective-permute-start(f32[4,2,2,256]{3,0,2,1:T(4,128)S(1)} %get-tuple-element.11), channel_id=1, source_target_pairs={{0,64},{1,65},{2,66},{3,67},{4,68},{5,69},{6,70},{7,71},{8,72},{9,... | collective-permute-start | bytes 49160 | tf_op jit(solution)/shard_map/ppermute | solution.py:18
  69.9 1.4 collective-permute-start.8
  71.3 3.7 %collective-permute-start.9 = (f32[256,8]{0,1:T(8,128)S(1)}, f32[256,8]{0,1:T(8,128)S(1)}, u32[]{:S(2)}, u32[]{:S(2)}) collective-permute-start(f32[256,8]{0,1:T(8,128)S(1)} %add.155), channel_id=1, source_target_pairs={{0,1},{1,0},{2,3},{3,2},{4,5},{5,4},{6,7},{7,6},{8,9},{9,8},{10,11... | collective-permute-start | bytes 24584 | tf_op jit(solution)/shard_map/ppermute | solution.py:57
  75.0 4.9 %collective-permute-start.10 = (f32[256,8]{0,1:T(8,128)S(1)}, f32[256,8]{0,1:T(8,128)S(1)}, u32[]{:S(2)}, u32[]{:S(2)}) collective-permute-start(f32[256,8]{0,1:T(8,128)S(1)} %add.156), channel_id=1, source_target_pairs={{0,3},{1,2},{2,1},{3,0},{4,7},{5,6},{6,5},{7,4},{8,11},{9,10},{10,... | collective-permute-start | bytes 24584 | tf_op jit(solution)/shard_map/ppermute | solution.py:57
  79.8 3.7 %collective-permute-start.11 = (f32[256,8]{0,1:T(8,128)S(1)}, f32[256,8]{0,1:T(8,128)S(1)}, u32[]{:S(2)}, u32[]{:S(2)}) collective-permute-start(f32[256,8]{0,1:T(8,128)S(1)} %add.157), channel_id=1, source_target_pairs={{0,4},{1,5},{2,6},{3,7},{4,0},{5,1},{6,2},{7,3},{8,12},{9,13},{10,... | collective-permute-start | bytes 24584 | tf_op jit(solution)/shard_map/ppermute | solution.py:57
  83.5 4.9 %collective-permute-start.12 = (f32[256,8]{0,1:T(8,128)S(1)}, f32[256,8]{0,1:T(8,128)S(1)}, u32[]{:S(2)}, u32[]{:S(2)}) collective-permute-start(f32[256,8]{0,1:T(8,128)S(1)} %add.158), channel_id=1, source_target_pairs={{0,12},{1,13},{2,14},{3,15},{4,8},{5,9},{6,10},{7,11},{8,4},{9,5},... | collective-permute-start | bytes 24584 | tf_op jit(solution)/shard_map/ppermute | solution.py:57
  88.3 15.8 %collective-permute-start.13 = (f32[256,8]{0,1:T(8,128)S(1)}, f32[256,8]{0,1:T(8,128)S(1)}, u32[]{:S(2)}, u32[]{:S(2)}) collective-permute-start(f32[256,8]{0,1:T(8,128)S(1)} %add.159), channel_id=1, source_target_pairs={{0,16},{1,17},{2,18},{3,19},{4,20},{5,21},{6,22},{7,23},{8,24},{9,... | collective-permute-start | bytes 24584 | tf_op jit(solution)/shard_map/ppermute | solution.py:57
  104.2 4.9 %collective-permute-start.14 = (f32[256,8]{0,1:T(8,128)S(1)}, f32[256,8]{0,1:T(8,128)S(1)}, u32[]{:S(2)}, u32[]{:S(2)}) collective-permute-start(f32[256,8]{0,1:T(8,128)S(1)} %add.160), channel_id=1, source_target_pairs={{0,48},{1,49},{2,50},{3,51},{4,52},{5,53},{6,54},{7,55},{8,56},{9,... | collective-permute-start | bytes 24584 | tf_op jit(solution)/shard_map/ppermute | solution.py:57
  109.1 36.9 %copy-start.1 = (f32[256,8]{0,1:T(8,128)}, f32[256,8]{0,1:T(8,128)S(1)}, u32[]{:S(2)}) copy-start(f32[256,8]{0,1:T(8,128)S(1)} %add.161) | copy-start | bytes 24580
  113.8 1.2 collective-permute-start.15
  114.9 3.6 %collective-permute-start.16 = (f32[8,8]{0,1:T(8,128)S(1)}, f32[8,8]{0,1:T(8,128)S(1)}, u32[]{:S(2)}, u32[]{:S(2)}) collective-permute-start(f32[8,8]{0,1:T(8,128)S(1)} %add.162), channel_id=1, source_target_pairs={{0,1},{1,0},{2,3},{3,2},{4,5},{5,4},{6,7},{7,6},{8,9},{9,8},{10,11... | collective-permute-start | bytes 776 | tf_op jit(solution)/shard_map/ppermute | solution.py:57
  118.6 4.8 %collective-permute-start.17 = (f32[8,8]{0,1:T(8,128)S(1)}, f32[8,8]{0,1:T(8,128)S(1)}, u32[]{:S(2)}, u32[]{:S(2)}) collective-permute-start(f32[8,8]{0,1:T(8,128)S(1)} %add.163), channel_id=1, source_target_pairs={{0,3},{1,2},{2,1},{3,0},{4,7},{5,6},{6,5},{7,4},{8,11},{9,10},{10,... | collective-permute-start | bytes 776 | tf_op jit(solution)/shard_map/ppermute | solution.py:57
  123.4 3.6 %collective-permute-start.18 = (f32[8,8]{0,1:T(8,128)S(1)}, f32[8,8]{0,1:T(8,128)S(1)}, u32[]{:S(2)}, u32[]{:S(2)}) collective-permute-start(f32[8,8]{0,1:T(8,128)S(1)} %add.164), channel_id=1, source_target_pairs={{0,4},{1,5},{2,6},{3,7},{4,0},{5,1},{6,2},{7,3},{8,12},{9,13},{10,... | collective-permute-start | bytes 776 | tf_op jit(solution)/shard_map/ppermute | solution.py:57
  127.0 4.8 %collective-permute-start.19 = (f32[8,8]{0,1:T(8,128)S(1)}, f32[8,8]{0,1:T(8,128)S(1)}, u32[]{:S(2)}, u32[]{:S(2)}) collective-permute-start(f32[8,8]{0,1:T(8,128)S(1)} %add.165), channel_id=1, source_target_pairs={{0,12},{1,13},{2,14},{3,15},{4,8},{5,9},{6,10},{7,11},{8,4},{9,5},... | collective-permute-start | bytes 776 | tf_op jit(solution)/shard_map/ppermute | solution.py:57
  131.8 3.6 %collective-permute-start.20 = (f32[8,8]{0,1:T(8,128)S(1)}, f32[8,8]{0,1:T(8,128)S(1)}, u32[]{:S(2)}, u32[]{:S(2)}) collective-permute-start(f32[8,8]{0,1:T(8,128)S(1)} %add.166), channel_id=1, source_target_pairs={{0,16},{1,17},{2,18},{3,19},{4,20},{5,21},{6,22},{7,23},{8,24},{9,... | collective-permute-start | bytes 776 | tf_op jit(solution)/shard_map/ppermute | solution.py:57
  135.4 4.8 %collective-permute-start.21 = (f32[8,8]{0,1:T(8,128)S(1)}, f32[8,8]{0,1:T(8,128)S(1)}, u32[]{:S(2)}, u32[]{:S(2)}) collective-permute-start(f32[8,8]{0,1:T(8,128)S(1)} %add.167), channel_id=1, source_target_pairs={{0,48},{1,49},{2,50},{3,51},{4,52},{5,53},{6,54},{7,55},{8,56},{9,... | collective-permute-start | bytes 776 | tf_op jit(solution)/shard_map/ppermute | solution.py:57

commit v2 on v1

--- a/solution.py
+++ b/solution.py
@@ -1,9 +1,11 @@
 import jax
 import jax.numpy as jnp
 from jax import lax
+from jax.experimental import pallas as pl
 from jax.sharding import PartitionSpec as P
 
 viscosity = 0.1
+ROWS = 16
 time_step = 0.4
 
 
@@ -58,6 +60,62 @@
     return value
 
 
+def project_kernel(b_ref, s_ref, o_ref):
+    tk, nr, nz = b_ref.shape
+    ns = s_ref.shape[0]
+    acc = jnp.zeros((tk * ROWS, ns * ROWS), jnp.float32)
+    for j in range(nr // ROWS):
+        rows = pl.ds(j * ROWS, ROWS)
+        lhs = b_ref[:, rows, :].reshape(tk * ROWS, nz)
+        rhs = s_ref[:, rows, :].reshape(ns * ROWS, nz)
+        acc = acc + lax.dot_general(lhs, rhs, (((1,), (1,)), ((), ())), preferred_element_type=jnp.float32)
+    row_t = lax.broadcasted_iota(jnp.int32, acc.shape, 0) % ROWS
+    col_t = lax.broadcasted_iota(jnp.int32, acc.shape, 1) % ROWS
+    acc = jnp.where(row_t == col_t, acc, 0.0)
+    o_ref[...] = jnp.sum(acc.reshape(tk, ROWS, ns * ROWS), axis=1)
+
+
+def project(basis3, snaps3, tk=32):
+    nk, nr, nz = basis3.shape
+    ns = snaps3.shape[0]
+    out = pl.pallas_call(
+        project_kernel,
+        grid=(nk // tk,),
+        in_specs=[pl.BlockSpec((tk, nr, nz), lambda i: (i, 0, 0)),
+                  pl.BlockSpec((ns, nr, nz), lambda i: (0, 0, 0))],
+        out_specs=pl.BlockSpec((tk, ns * ROWS), lambda i: (i, 0)),
+        out_shape=jax.ShapeDtypeStruct((nk, ns * ROWS), jnp.float32),
+        cost_estimate=pl.CostEstimate(flops=2 * nk * nr * nz * ns * ROWS, transcendentals=0,
+                                      bytes_accessed=nk * nr * nz * 2 + ns * nr * nz * 2 + nk * ns * ROWS * 4),
+    )(basis3, snaps3)
+    return jnp.sum(out.reshape(nk, ns, ROWS), axis=2)
+
+
+def residual_kernel(l_ref, b_ref, s_ref, o_ref):
+    nk, rows, nz = b_ref.shape
+    ns = s_ref.shape[0]
+    prod = jnp.dot(l_ref[...], b_ref[...].reshape(nk * rows, nz), preferred_element_type=jnp.float32)
+    o_ref[...] = s_ref[...] - prod.reshape(ns, rows, nz)
+
+
+def residual(coeffs_bf, basis3, snaps3):
+    nk, nr, nz = basis3.shape
+    ns = snaps3.shape[0]
+    eye = jnp.eye(ROWS, dtype=jnp.bfloat16)
+    spread = (coeffs_bf.T[:, None, :, None] * eye[None, :, None, :]).reshape(ns * ROWS, nk * ROWS)
+    return pl.pallas_call(
+        residual_kernel,
+        grid=(nr // ROWS,),
+        in_specs=[pl.BlockSpec((ns * ROWS, nk * ROWS), lambda j: (0, 0)),
+                  pl.BlockSpec((nk, ROWS, nz), lambda j: (0, j, 0)),
+                  pl.BlockSpec((ns, ROWS, nz), lambda j: (0, j, 0))],
+        out_specs=pl.BlockSpec((ns, ROWS, nz), lambda j: (0, j, 0)),
+        out_shape=jax.ShapeDtypeStruct((ns, nr, nz), jnp.float32),
+        cost_estimate=pl.CostEstimate(flops=2 * ns * ROWS * nk * ROWS * nz * (nr // ROWS), transcendentals=0,
+                                      bytes_accessed=nk * nr * nz * 2 + 2 * ns * nr * nz * 4),
+    )(spread, basis3, snaps3)
+
+
 def offset_slice(padded, offset, dimension, length):
     return lax.slice_in_dim(padded, 2 + offset, 2 + offset + length, axis=dimension)
 
@@ -110,19 +168,17 @@
     tend_one = segmented_tendency(segment_one, flow_rows, shear_rows)
     advanced = segment_one + time_step * (5.0 / 12.0 * tend_one - 17.0 / 60.0 * tend_zero)
     snapshots = jnp.concatenate([segment_one, advanced], axis=0)
-    flat_snaps = snapshots.reshape(snapshots.shape[0], -1)
-    snaps_bf = flat_snaps.astype(jnp.bfloat16)
-    basis_rows = basis.reshape(basis.shape[0], -1)
-    partial_proj = jnp.einsum("km,sm->ks", basis_rows, snaps_bf, preferred_element_type=jnp.float32)
+    ns = snapshots.shape[0]
+    snaps3 = snapshots.reshape(ns, -1, snapshots.shape[3])
+    basis3 = basis.reshape(basis.shape[0], -1, basis.shape[3])
+    partial_proj = project(basis3, snaps3.astype(jnp.bfloat16))
     coeffs = allreduce(partial_proj, ("role", "slab"))
     coeffs_bf = coeffs.astype(jnp.bfloat16)
-    residual = flat_snaps - jnp.einsum(
-        "ks,km->sm", coeffs_bf, basis_rows, preferred_element_type=jnp.float32
-    )
-    local_gram = jnp.dot(residual, residual.T, precision=lax.Precision.HIGHEST)
+    residual3 = residual(coeffs_bf, basis3, snaps3)
+    local_gram = jnp.einsum("srz,trz->st", residual3, residual3, precision=lax.Precision.HIGHEST)
     total_gram = allreduce(local_gram, ("role", "slab"))
     lower_factor = jnp.linalg.cholesky(total_gram)
-    directions = jax.scipy.linalg.solve_triangular(lower_factor, residual, lower=True)
+    directions = jax.scipy.linalg.solve_triangular(lower_factor, residual3.reshape(ns, -1), lower=True)
     return (advanced, coeffs, lower_factor.T, directions.reshape(snapshots.shape))
 
 

time: 146 us -> 156 us (1.068)
  Pallas kernels: 0 us -> 21.8 us
  matrix products: 26.3 us -> 5.55 us
  other arithmetic: 12.1 us -> 16.5 us
  waiting for transfers between devices: 50 us -> 53.6 us
  local copies, waits for them, and re-layouts: 23.1 us -> 24.7 us
    pallas_call x0 -> x2, Pallas kernels: none -> 21.8 us  [the longest x1 11.1 us: project(): pl.pallas_call(project_kernel, grid=(nk // tk,), in_specs=[pl.BlockSpec((...]
    dot_general x3 -> x1, matrix products: 25.3 us -> 4.52 us  [on_device(): jnp.einsum('srz,trz->st', residual3, residual3, precision=lax.Precision.H...]
    unnamed x11 -> x10, local copies, waits for them, and re-layouts: 21.6 us -> 4.89 us
    mul x0 -> x1, local copies, waits for them, and re-layouts: none -> 15.8 us  [residual(): coeffs_bf.T[:, None, :, None] * eye[None, :, None, :]]
    ppermute x14, waiting for transfers between devices: 40.2 us -> 44 us  [allreduce(): value = value + lax.ppermute(value, name, pairs)]
    mul x1, other arithmetic: 0.98 us -> 3.9 us  [residual(): coeffs_bf.T[:, None, :, None] * eye[None, :, None, :]]
  transfers between devices with their start and end apart: 22 -> 22, of which waited for: 16 -> 17; matrix products, arithmetic and copies ran while one was open for 15% -> 4% of each run, Pallas kernels for 0% -> 0%
where the time goes in v2:
time: 156 us
  waiting for transfers between devices  53.6 us (34%)
  starting transfers between devices  32.5 us (21%)
  local copies, waits for them, and re-layouts  24.7 us (16%)
  Pallas kernels  21.8 us (14%)
  other arithmetic  16.5 us (11%)
  matrix products  5.55 us (4%)
    ppermute x14, waiting for transfers between devices, allreduce(): value = value + lax.ppermute(value, name, pairs)  44 us
    ppermute x4, starting transfers between devices, extended(): lax.ppermute(head, axis, [((i + 1) % count, i) for i in range(ends)])  16.9 us
    mul x1, local copies, waits for them, and re-layouts, residual(): coeffs_bf.T[:, None, :, None] * eye[None, :, None, :]  15.8 us
    pallas_call x1, Pallas kernels, project(): pl.pallas_call(project_kernel, grid=(nk // tk,), in_specs=[pl.BlockSpec((...  11.1 us
    pallas_call x1, Pallas kernels, residual(): pl.pallas_call(residual_kernel, grid=(nr // ROWS,), in_specs=[pl.BlockSpe...  10.7 us
    ppermute x4, waiting for transfers between devices, extended(): lax.ppermute(tail, axis, [(i, (i + 1) % count) for i in range(ends)])  9.67 us
    ppermute x4, starting transfers between devices, extended(): lax.ppermute(tail, axis, [(i, (i + 1) % count) for i in range(ends)])  8.2 us
    ppermute x14, starting transfers between devices, allreduce(): value = value + lax.ppermute(value, name, pairs)  7.43 us
  transfers between devices with their start and end apart: 22, of which 17 were waited for; matrix products, arithmetic and copies ran while one was open for 4% of the time, Pallas kernels for 0%

profile of v2, /device:TPU:0, one launch (start us, length us, event | category | flops | bytes accessed | tf_op | source)
XLA Modules:
  0.0 155.5 jit_solution(6412998927429339903)
XLA Ops:
  0.6 0.0 copy-start
  0.6 2.1 %collective-permute-start.1 = (f32[4,2,64,256]{3,2,1,0:T(8,128)}, f32[4,2,64,256]{3,2,1,0:T(8,128)S(1)}, u32[]{:S(2)}, u32[]{:S(2)}) collective-permute-start(f32[4,2,64,256]{3,2,1,0:T(8,128)} %param.4), channel_id=1, source_target_pairs={{0,1},{1,2},{2,3},{3,4},{4,5},{5,6},{6,7},{7,8},{8,9},{9,10},{10,1... | collective-permute-start | bytes 1572872 | tf_op jit(solution)/shard_map/ppermute | solution.py:20
  2.7 6.8 %collective-permute-start = (f32[4,2,64,256]{3,2,1,0:T(8,128)}, f32[4,2,64,256]{3,2,1,0:T(8,128)S(1)}, u32[]{:S(2)}, u32[]{:S(2)}) collective-permute-start(f32[4,2,64,256]{3,2,1,0:T(8,128)} %param.4), channel_id=1, source_target_pairs={{1,0},{2,1},{3,2},{4,3},{5,4},{6,5},{7,6},{8,7},{9,8},{10,9},{11,1... | collective-permute-start | bytes 1572872 | tf_op jit(solution)/shard_map/ppermute | solution.py:22
  9.6 0.9 fusion.55
  10.5 1.3 collective-permute-start.2
  11.8 3.0 %collective-permute-start.3 = (f32[4,2,2,256]{3,2,1,0:T(2,128)S(1)}, f32[4,2,2,256]{3,2,1,0:T(2,128)S(1)}, u32[]{:S(2)}, u32[]{:S(2)}) collective-permute-start(f32[4,2,2,256]{3,2,1,0:T(2,128)S(1)} %get-tuple-element.19), channel_id=1, source_target_pairs={{0,64},{1,65},{2,66},{3,67},{4,68},{5,69},{6,70},{7,71},{8,72},{9,... | collective-permute-start | bytes 49160 | tf_op jit(solution)/shard_map/ppermute | solution.py:20
  14.8 1.1 constant_dynamic-update-slice_fusion.1
  15.9 1.2 fusion.56
  17.0 0.7 negate_multiply_fusion
  17.8 0.7 dynamic_slice.7
  18.5 0.0 collective-permute-done.3
  18.5 3.1 %collective-permute-done.1 = f32[4,2,64,256]{3,2,1,0:T(8,128)S(1)} collective-permute-done((f32[4,2,64,256]{3,2,1,0:T(8,128)}, f32[4,2,64,256]{3,2,1,0:T(8,128)S(1)}, u32[]{:S(2)}, u32[]{:S(2)}) %collective-permute-start.1) | collective-permute-done | bytes 524320 | tf_op jit(solution)/shard_map/ppermute | solution.py:20
  21.6 0.0 collective-permute-done
  21.6 4.2 %fusion.20 = f32[4,2,64,256]{3,2,1,0:T(8,128)S(1)} fusion(f32[4,2,2,256]{3,2,1,0:T(2,128)S(1)} %collective-permute-done.3, f32[4,2,64,256]{3,2,1,0:T(8,128)} %param.4, f32[4,2,64,2]{3,2,1,0:T(8,128)S(1)} %get-tuple-element.21, f32[4,2,64,2]{3,2,1,0:T(8,128)S(1)} %get-tuple-element.20, f32[4,2,66,256]{3,2,1,0:T(8,128)S(1)} %constant_dynamic-update-slice_fusion, ...), kind=kLoop, calls=%fused_computation.37 | loop fusion | flops 5242880 | bytes 3170560 | tf_op jit(solution)/shard_map/add | solution.py:150
  25.8 1.0 slice_subtract_fusion
  26.8 1.1 multiply_add_fusion
  27.9 0.1 collective-permute-start.5
  28.0 7.4 %collective-permute-start.4 = (f32[4,2,64,256]{3,2,1,0:T(8,128)S(1)}, f32[4,2,64,256]{3,2,1,0:T(8,128)S(1)}, u32[]{:S(2)}, u32[]{:S(2)}) collective-permute-start(f32[4,2,64,256]{3,2,1,0:T(8,128)S(1)} %multiply_add_fusion), channel_id=1, source_target_pairs={{1,0},{2,1},{3,2},{4,3},{5,4},{6,5},{7,6},{8,7},{9,8},{10,9},{11,1... | collective-permute-start | bytes 1572872 | tf_op jit(solution)/shard_map/ppermute | solution.py:22
  35.5 1.3 collective-permute-start.6
  36.8 3.0 %collective-permute-start.7 = (f32[4,2,2,256]{3,2,1,0:T(2,128)S(1)}, f32[4,2,2,256]{3,2,1,0:T(2,128)S(1)}, u32[]{:S(2)}, u32[]{:S(2)}) collective-permute-start(f32[4,2,2,256]{3,2,1,0:T(2,128)S(1)} %get-tuple-element.17), channel_id=1, source_target_pairs={{0,64},{1,65},{2,66},{3,67},{4,68},{5,69},{6,70},{7,71},{8,72},{9,... | collective-permute-start | bytes 49160 | tf_op jit(solution)/shard_map/ppermute | solution.py:20
  39.8 0.1 fusion.53
  40.0 0.7 collective-permute-done.7
  40.6 5.9 %collective-permute-done.5 = f32[4,2,64,256]{3,2,1,0:T(8,128)S(1)} collective-permute-done((f32[4,2,64,256]{3,2,1,0:T(8,128)S(1)}, f32[4,2,64,256]{3,2,1,0:T(8,128)S(1)}, u32[]{:S(2)}, u32[]{:S(2)}) %collective-permute-start.5) | collective-permute-done | bytes 524320 | tf_op jit(solution)/shard_map/ppermute | solution.py:20
  46.6 0.9 fusion.8
  47.5 0.1 fusion.47
  47.6 0.1 fusion.46
  47.7 0.0 copy-start.2
  47.8 0.1 pad_maximum_fusion
  47.9 1.0 bitcast_convert_fusion.s_ref
  48.8 11.1 %shard_map.75 = f32[256,128]{1,0:T(8,128)} custom-call(bf16[256,128,256]{2,1,0:T(8,128)(2,1)} %bitcast.36, bf16[8,128,256]{2,1,0:T(8,128)(2,1)} %bitcast_convert_fusion.s_ref), custom_call_target="tpu_custom_call" | custom-call | flops 2147483648 | bytes 17432576 | tf_op jit(solution)/shard_map/pallas_call | solution.py:81
  60.0 1.0 copy.16
  61.0 0.1 collective-permute-start.8
  61.1 1.2 collective-permute-done.8
  62.2 3.6 %collective-permute-done.9 = f32[256,8]{0,1:T(8,128)S(1)} collective-permute-done((f32[256,8]{0,1:T(8,128)S(1)}, f32[256,8]{0,1:T(8,128)S(1)}, u32[]{:S(2)}, u32[]{:S(2)}) %collective-permute-start.9) | collective-permute-done | bytes 8224 | tf_op jit(solution)/shard_map/ppermute | solution.py:59
  65.9 4.9 %collective-permute-done.10 = f32[256,8]{0,1:T(8,128)S(1)} collective-permute-done((f32[256,8]{0,1:T(8,128)S(1)}, f32[256,8]{0,1:T(8,128)S(1)}, u32[]{:S(2)}, u32[]{:S(2)}) %collective-permute-start.10) | collective-permute-done | bytes 8224 | tf_op jit(solution)/shard_map/ppermute | solution.py:59
  70.8 3.6 %collective-permute-done.11 = f32[256,8]{0,1:T(8,128)S(1)} collective-permute-done((f32[256,8]{0,1:T(8,128)S(1)}, f32[256,8]{0,1:T(8,128)S(1)}, u32[]{:S(2)}, u32[]{:S(2)}) %collective-permute-start.11) | collective-permute-done | bytes 8224 | tf_op jit(solution)/shard_map/ppermute | solution.py:59
  74.4 4.9 %collective-permute-done.12 = f32[256,8]{0,1:T(8,128)S(1)} collective-permute-done((f32[256,8]{0,1:T(8,128)S(1)}, f32[256,8]{0,1:T(8,128)S(1)}, u32[]{:S(2)}, u32[]{:S(2)}) %collective-permute-start.12) | collective-permute-done | bytes 8224 | tf_op jit(solution)/shard_map/ppermute | solution.py:59
  79.3 3.6 %collective-permute-done.13 = f32[256,8]{0,1:T(8,128)S(1)} collective-permute-done((f32[256,8]{0,1:T(8,128)S(1)}, f32[256,8]{0,1:T(8,128)S(1)}, u32[]{:S(2)}, u32[]{:S(2)}) %collective-permute-start.13) | collective-permute-done | bytes 8224 | tf_op jit(solution)/shard_map/ppermute | solution.py:59
  82.9 1.8 %collective-permute-start.14 = (f32[256,8]{0,1:T(8,128)S(1)}, f32[256,8]{0,1:T(8,128)S(1)}, u32[]{:S(2)}, u32[]{:S(2)}) collective-permute-start(f32[256,8]{0,1:T(8,128)S(1)} %add.160), channel_id=1, source_target_pairs={{0,48},{1,49},{2,50},{3,51},{4,52},{5,53},{6,54},{7,55},{8,56},{9,... | collective-permute-start | bytes 24584 | tf_op jit(solution)/shard_map/ppermute | solution.py:59
  84.8 3.0 %collective-permute-done.14 = f32[256,8]{0,1:T(8,128)S(1)} collective-permute-done((f32[256,8]{0,1:T(8,128)S(1)}, f32[256,8]{0,1:T(8,128)S(1)}, u32[]{:S(2)}, u32[]{:S(2)}) %collective-permute-start.14) | collective-permute-done | bytes 8224 | tf_op jit(solution)/shard_map/ppermute | solution.py:59
  87.8 0.6 convert_bitcast_fusion
  88.4 3.9 %broadcast_multiply_fusion = bf16[8,16,256,16]{3,2,1,0:T(8,128)(2,1)} fusion(bf16[16,16]{1,0:T(8,128)(2,1)S(1)} %fusion.48, bf16[8,256]{1,0:T(8,128)(2,1)S(1)} %get-tuple-element.12), kind=kLoop, calls=%fused_computation | loop fusion | flops 524288 | bytes 1053184 | tf_op jit(solution)/shard_map/mul | solution.py:105
  92.3 15.8 %mul.181.l_ref = bf16[128,4096]{1,0:T(8,128)(2,1)} reshape(bf16[8,16,256,16]{3,2,1,0:T(8,128)(2,1)} %broadcast_multiply_fusion) | data formatting | bytes 2097152 | tf_op jit(solution)/shard_map/mul | solution.py:105
  108.1 10.7 %shard_map.76 = f32[8,128,256]{2,1,0:T(8,128)} custom-call(bf16[128,4096]{1,0:T(8,128)(2,1)} %mul.181.l_ref, bf16[256,128,256]{2,1,0:T(8,128)(2,1)} %bitcast.37, f32[8,128,256]{2,1,0:T(8,128)} %bitcast.38), custom_call_target="tpu_custom_call" | custom-call | flops 2147483648 | bytes 18874368 | tf_op jit(solution)/shard_map/pallas_call | solution.py:106
  118.8 4.5 %convolution_bitcast_fusion = f32[8,8]{0,1:T(8,128)S(1)} fusion(f32[8,128,256]{2,1,0:T(8,128)} %shard_map.76), kind=kOutput, calls=%fused_computation.1 | convolution fusion | flops 25165824 | bytes 1048832 | tf_op jit(solution)/shard_map/srz,trz->st/dot_general | solution.py:178
  123.3 1.2 collective-permute-done.15
  124.5 3.6 %collective-permute-done.16 = f32[8,8]{0,1:T(8,128)S(1)} collective-permute-done((f32[8,8]{0,1:T(8,128)S(1)}, f32[8,8]{0,1:T(8,128)S(1)}, u32[]{:S(2)}, u32[]{:S(2)}) %collective-permute-start.16) | collective-permute-done | bytes 288 | tf_op jit(solution)/shard_map/ppermute | solution.py:59
  128.1 1.8 %collective-permute-start.17 = (f32[8,8]{0,1:T(8,128)S(1)}, f32[8,8]{0,1:T(8,128)S(1)}, u32[]{:S(2)}, u32[]{:S(2)}) collective-permute-start(f32[8,8]{0,1:T(8,128)S(1)} %add.163), channel_id=1, source_target_pairs={{0,3},{1,2},{2,1},{3,0},{4,7},{5,6},{6,5},{7,4},{8,11},{9,10},{10,... | collective-permute-start | bytes 776 | tf_op jit(solution)/shard_map/ppermute | solution.py:59
  129.9 3.0 %collective-permute-done.17 = f32[8,8]{0,1:T(8,128)S(1)} collective-permute-done((f32[8,8]{0,1:T(8,128)S(1)}, f32[8,8]{0,1:T(8,128)S(1)}, u32[]{:S(2)}, u32[]{:S(2)}) %collective-permute-start.17) | collective-permute-done | bytes 288 | tf_op jit(solution)/shard_map/ppermute | solution.py:59
  132.9 3.6 %collective-permute-done.18 = f32[8,8]{0,1:T(8,128)S(1)} collective-permute-done((f32[8,8]{0,1:T(8,128)S(1)}, f32[8,8]{0,1:T(8,128)S(1)}, u32[]{:S(2)}, u32[]{:S(2)}) %collective-permute-start.18) | collective-permute-done | bytes 288 | tf_op jit(solution)/shard_map/ppermute | solution.py:59
  136.5 1.8 %collective-permute-start.19 = (f32[8,8]{0,1:T(8,128)S(1)}, f32[8,8]{0,1:T(8,128)S(1)}, u32[]{:S(2)}, u32[]{:S(2)}) collective-permute-start(f32[8,8]{0,1:T(8,128)S(1)} %add.165), channel_id=1, source_target_pairs={{0,12},{1,13},{2,14},{3,15},{4,8},{5,9},{6,10},{7,11},{8,4},{9,5},... | collective-permute-start | bytes 776 | tf_op jit(solution)/shard_map/ppermute | solution.py:59
  138.4 3.0 %collective-permute-done.19 = f32[8,8]{0,1:T(8,128)S(1)} collective-permute-done((f32[8,8]{0,1:T(8,128)S(1)}, f32[8,8]{0,1:T(8,128)S(1)}, u32[]{:S(2)}, u32[]{:S(2)}) %collective-permute-start.19) | collective-permute-done | bytes 288 | tf_op jit(solution)/shard_map/ppermute | solution.py:59
  141.3 3.6 %collective-permute-done.20 = f32[8,8]{0,1:T(8,128)S(1)} collective-permute-done((f32[8,8]{0,1:T(8,128)S(1)}, f32[8,8]{0,1:T(8,128)S(1)}, u32[]{:S(2)}, u32[]{:S(2)}) %collective-permute-start.20) | collective-permute-done | bytes 288 | tf_op jit(solution)/shard_map/ppermute | solution.py:59
  145.0 1.8 %collective-permute-start.21 = (f32[8,8]{0,1:T(8,128)S(1)}, f32[8,8]{0,1:T(8,128)S(1)}, u32[]{:S(2)}, u32[]{:S(2)}) collective-permute-start(f32[8,8]{0,1:T(8,128)S(1)} %add.167), channel_id=1, source_target_pairs={{0,48},{1,49},{2,50},{3,51},{4,52},{5,53},{6,54},{7,55},{8,56},{9,... | collective-permute-start | bytes 776 | tf_op jit(solution)/shard_map/ppermute | solution.py:59
  146.8 1.8 %copy.29 = f32[1,8,128,256]{3,1,2,0:T(8,128)S(1)} copy(f32[1,8,128,256]{3,2,1,0:T(8,128)} %bitcast.39) | data formatting | bytes 2097152
  148.6 1.2 collective-permute-done.21
  149.8 0.1 copy.21
  149.9 0.7 cholesky.18
  150.6 0.6 compare_reduce_fusion
  151.3 0.6 select_bitcast_fusion
  151.9 0.6 custom-call.7
  152.5 0.7 copy.23
  153.2 1.0 fusion.49
  154.2 1.3 copy.24
  (37 shorter events, 0.3 us)
Async XLA Ops:
  0.6 47.0 %copy-start = (f32[4,2,64,256]{3,2,1,0:T(8,128)S(1)}, f32[4,2,64,256]{3,2,1,0:T(8,128)}, u32[]{:S(2)}) copy-start(f32[4,2,64,256]{3,2,1,0:T(8,128)} %param.4) | copy-start | bytes 1572868
  0.6 21.0 %collective-permute-start.1 = (f32[4,2,64,256]{3,2,1,0:T(8,128)}, f32[4,2,64,256]{3,2,1,0:T(8,128)S(1)}, u32[]{:S(2)}, u32[]{:S(2)}) collective-permute-start(f32[4,2,64,256]{3,2,1,0:T(8,128)} %param.4), channel_id=1, source_target_pairs={{0,1},{1,2},{2,3},{3,4},{4,5},{5,6},{6,7},{7,8},{8,9},{9,10},{10,1... | collective-permute-start | bytes 1572872 | tf_op jit(solution)/shard_map/ppermute | solution.py:20
  2.7 18.9 %collective-permute-start = (f32[4,2,64,256]{3,2,1,0:T(8,128)}, f32[4,2,64,256]{3,2,1,0:T(8,128)S(1)}, u32[]{:S(2)}, u32[]{:S(2)}) collective-permute-start(f32[4,2,64,256]{3,2,1,0:T(8,128)} %param.4), channel_id=1, source_target_pairs={{1,0},{2,1},{3,2},{4,3},{5,4},{6,5},{7,6},{8,7},{9,8},{10,9},{11,1... | collective-permute-start | bytes 1572872 | tf_op jit(solution)/shard_map/ppermute | solution.py:22
  10.5 8.1 %collective-permute-start.2 = (f32[4,2,2,256]{3,2,1,0:T(2,128)S(1)}, f32[4,2,2,256]{3,2,1,0:T(2,128)S(1)}, u32[]{:S(2)}, u32[]{:S(2)}) collective-permute-start(f32[4,2,2,256]{3,2,1,0:T(2,128)S(1)} %get-tuple-element.18), channel_id=1, source_target_pairs={{64,0},{65,1},{66,2},{67,3},{68,4},{69,5},{70,6},{71,7},{72,8},{73... | collective-permute-start | bytes 49160 | tf_op jit(solution)/shard_map/ppermute | solution.py:22
  11.8 6.8 %collective-permute-start.3 = (f32[4,2,2,256]{3,2,1,0:T(2,128)S(1)}, f32[4,2,2,256]{3,2,1,0:T(2,128)S(1)}, u32[]{:S(2)}, u32[]{:S(2)}) collective-permute-start(f32[4,2,2,256]{3,2,1,0:T(2,128)S(1)} %get-tuple-element.19), channel_id=1, source_target_pairs={{0,64},{1,65},{2,66},{3,67},{4,68},{5,69},{6,70},{7,71},{8,72},{9,... | collective-permute-start | bytes 49160 | tf_op jit(solution)/shard_map/ppermute | solution.py:20
  27.9 18.6 %collective-permute-start.5 = (f32[4,2,64,256]{3,2,1,0:T(8,128)S(1)}, f32[4,2,64,256]{3,2,1,0:T(8,128)S(1)}, u32[]{:S(2)}, u32[]{:S(2)}) collective-permute-start(f32[4,2,64,256]{3,2,1,0:T(8,128)S(1)} %multiply_add_fusion), channel_id=1, source_target_pairs={{0,1},{1,2},{2,3},{3,4},{4,5},{5,6},{6,7},{7,8},{8,9},{9,10},{10,1... | collective-permute-start | bytes 1572872 | tf_op jit(solution)/shard_map/ppermute | solution.py:20
  28.0 18.5 %collective-permute-start.4 = (f32[4,2,64,256]{3,2,1,0:T(8,128)S(1)}, f32[4,2,64,256]{3,2,1,0:T(8,128)S(1)}, u32[]{:S(2)}, u32[]{:S(2)}) collective-permute-start(f32[4,2,64,256]{3,2,1,0:T(8,128)S(1)} %multiply_add_fusion), channel_id=1, source_target_pairs={{1,0},{2,1},{3,2},{4,3},{5,4},{6,5},{7,6},{8,7},{9,8},{10,9},{11,1... | collective-permute-start | bytes 1572872 | tf_op jit(solution)/shard_map/ppermute | solution.py:22
  35.5 4.5 %collective-permute-start.6 = (f32[4,2,2,256]{3,2,1,0:T(2,128)S(1)}, f32[4,2,2,256]{3,2,1,0:T(2,128)S(1)}, u32[]{:S(2)}, u32[]{:S(2)}) collective-permute-start(f32[4,2,2,256]{3,2,1,0:T(2,128)S(1)} %get-tuple-element.16), channel_id=1, source_target_pairs={{64,0},{65,1},{66,2},{67,3},{68,4},{69,5},{70,6},{71,7},{72,8},{73... | collective-permute-start | bytes 49160 | tf_op jit(solution)/shard_map/ppermute | solution.py:22
  36.8 3.9 %collective-permute-start.7 = (f32[4,2,2,256]{3,2,1,0:T(2,128)S(1)}, f32[4,2,2,256]{3,2,1,0:T(2,128)S(1)}, u32[]{:S(2)}, u32[]{:S(2)}) collective-permute-start(f32[4,2,2,256]{3,2,1,0:T(2,128)S(1)} %get-tuple-element.17), channel_id=1, source_target_pairs={{0,64},{1,65},{2,66},{3,67},{4,68},{5,69},{6,70},{7,71},{8,72},{9,... | collective-permute-start | bytes 49160 | tf_op jit(solution)/shard_map/ppermute | solution.py:20
  47.7 12.2 %copy-start.2 = (f32[4,2,64,256]{3,2,1,0:T(8,128)}, f32[4,2,64,256]{3,2,1,0:T(8,128)S(1)}, u32[]{:S(2)}) copy-start(f32[4,2,64,256]{3,2,1,0:T(8,128)S(1)} %fusion.46) | copy-start | bytes 1572868
  47.8 12.1 %copy-start.1 = (f32[8,2,64,256]{3,2,1,0:T(8,128)}, f32[8,2,64,256]{3,2,1,0:T(8,128)S(1)}, u32[]{:S(2)}) copy-start(f32[8,2,64,256]{3,2,1,0:T(8,128)S(1)} %pad_maximum_fusion) | copy-start | bytes 3145732
  61.0 1.3 collective-permute-start.8
  62.2 3.7 %collective-permute-start.9 = (f32[256,8]{0,1:T(8,128)S(1)}, f32[256,8]{0,1:T(8,128)S(1)}, u32[]{:S(2)}, u32[]{:S(2)}) collective-permute-start(f32[256,8]{0,1:T(8,128)S(1)} %add.155), channel_id=1, source_target_pairs={{0,1},{1,0},{2,3},{3,2},{4,5},{5,4},{6,7},{7,6},{8,9},{9,8},{10,11... | collective-permute-start | bytes 24584 | tf_op jit(solution)/shard_map/ppermute | solution.py:59
  65.9 4.9 %collective-permute-start.10 = (f32[256,8]{0,1:T(8,128)S(1)}, f32[256,8]{0,1:T(8,128)S(1)}, u32[]{:S(2)}, u32[]{:S(2)}) collective-permute-start(f32[256,8]{0,1:T(8,128)S(1)} %add.156), channel_id=1, source_target_pairs={{0,3},{1,2},{2,1},{3,0},{4,7},{5,6},{6,5},{7,4},{8,11},{9,10},{10,... | collective-permute-start | bytes 24584 | tf_op jit(solution)/shard_map/ppermute | solution.py:59
  70.8 3.7 %collective-permute-start.11 = (f32[256,8]{0,1:T(8,128)S(1)}, f32[256,8]{0,1:T(8,128)S(1)}, u32[]{:S(2)}, u32[]{:S(2)}) collective-permute-start(f32[256,8]{0,1:T(8,128)S(1)} %add.157), channel_id=1, source_target_pairs={{0,4},{1,5},{2,6},{3,7},{4,0},{5,1},{6,2},{7,3},{8,12},{9,13},{10,... | collective-permute-start | bytes 24584 | tf_op jit(solution)/shard_map/ppermute | solution.py:59
  74.4 4.9 %collective-permute-start.12 = (f32[256,8]{0,1:T(8,128)S(1)}, f32[256,8]{0,1:T(8,128)S(1)}, u32[]{:S(2)}, u32[]{:S(2)}) collective-permute-start(f32[256,8]{0,1:T(8,128)S(1)} %add.158), channel_id=1, source_target_pairs={{0,12},{1,13},{2,14},{3,15},{4,8},{5,9},{6,10},{7,11},{8,4},{9,5},... | collective-permute-start | bytes 24584 | tf_op jit(solution)/shard_map/ppermute | solution.py:59
  79.3 3.7 %collective-permute-start.13 = (f32[256,8]{0,1:T(8,128)S(1)}, f32[256,8]{0,1:T(8,128)S(1)}, u32[]{:S(2)}, u32[]{:S(2)}) collective-permute-start(f32[256,8]{0,1:T(8,128)S(1)} %add.159), channel_id=1, source_target_pairs={{0,16},{1,17},{2,18},{3,19},{4,20},{5,21},{6,22},{7,23},{8,24},{9,... | collective-permute-start | bytes 24584 | tf_op jit(solution)/shard_map/ppermute | solution.py:59
  82.9 4.9 %collective-permute-start.14 = (f32[256,8]{0,1:T(8,128)S(1)}, f32[256,8]{0,1:T(8,128)S(1)}, u32[]{:S(2)}, u32[]{:S(2)}) collective-permute-start(f32[256,8]{0,1:T(8,128)S(1)} %add.160), channel_id=1, source_target_pairs={{0,48},{1,49},{2,50},{3,51},{4,52},{5,53},{6,54},{7,55},{8,56},{9,... | collective-permute-start | bytes 24584 | tf_op jit(solution)/shard_map/ppermute | solution.py:59
  123.3 1.2 collective-permute-start.15
  124.5 3.6 %collective-permute-start.16 = (f32[8,8]{0,1:T(8,128)S(1)}, f32[8,8]{0,1:T(8,128)S(1)}, u32[]{:S(2)}, u32[]{:S(2)}) collective-permute-start(f32[8,8]{0,1:T(8,128)S(1)} %add.162), channel_id=1, source_target_pairs={{0,1},{1,0},{2,3},{3,2},{4,5},{5,4},{6,7},{7,6},{8,9},{9,8},{10,11... | collective-permute-start | bytes 776 | tf_op jit(solution)/shard_map/ppermute | solution.py:59
  128.1 4.8 %collective-permute-start.17 = (f32[8,8]{0,1:T(8,128)S(1)}, f32[8,8]{0,1:T(8,128)S(1)}, u32[]{:S(2)}, u32[]{:S(2)}) collective-permute-start(f32[8,8]{0,1:T(8,128)S(1)} %add.163), channel_id=1, source_target_pairs={{0,3},{1,2},{2,1},{3,0},{4,7},{5,6},{6,5},{7,4},{8,11},{9,10},{10,... | collective-permute-start | bytes 776 | tf_op jit(solution)/shard_map/ppermute | solution.py:59
  132.9 3.6 %collective-permute-start.18 = (f32[8,8]{0,1:T(8,128)S(1)}, f32[8,8]{0,1:T(8,128)S(1)}, u32[]{:S(2)}, u32[]{:S(2)}) collective-permute-start(f32[8,8]{0,1:T(8,128)S(1)} %add.164), channel_id=1, source_target_pairs={{0,4},{1,5},{2,6},{3,7},{4,0},{5,1},{6,2},{7,3},{8,12},{9,13},{10,... | collective-permute-start | bytes 776 | tf_op jit(solution)/shard_map/ppermute | solution.py:59
  136.5 4.8 %collective-permute-start.19 = (f32[8,8]{0,1:T(8,128)S(1)}, f32[8,8]{0,1:T(8,128)S(1)}, u32[]{:S(2)}, u32[]{:S(2)}) collective-permute-start(f32[8,8]{0,1:T(8,128)S(1)} %add.165), channel_id=1, source_target_pairs={{0,12},{1,13},{2,14},{3,15},{4,8},{5,9},{6,10},{7,11},{8,4},{9,5},... | collective-permute-start | bytes 776 | tf_op jit(solution)/shard_map/ppermute | solution.py:59
  141.3 3.6 %collective-permute-start.20 = (f32[8,8]{0,1:T(8,128)S(1)}, f32[8,8]{0,1:T(8,128)S(1)}, u32[]{:S(2)}, u32[]{:S(2)}) collective-permute-start(f32[8,8]{0,1:T(8,128)S(1)} %add.166), channel_id=1, source_target_pairs={{0,16},{1,17},{2,18},{3,19},{4,20},{5,21},{6,22},{7,23},{8,24},{9,... | collective-permute-start | bytes 776 | tf_op jit(solution)/shard_map/ppermute | solution.py:59
  145.0 4.8 %collective-permute-start.21 = (f32[8,8]{0,1:T(8,128)S(1)}, f32[8,8]{0,1:T(8,128)S(1)}, u32[]{:S(2)}, u32[]{:S(2)}) collective-permute-start(f32[8,8]{0,1:T(8,128)S(1)} %add.167), channel_id=1, source_target_pairs={{0,48},{1,49},{2,50},{3,51},{4,52},{5,53},{6,54},{7,55},{8,56},{9,... | collective-permute-start | bytes 776 | tf_op jit(solution)/shard_map/ppermute | solution.py:59

commit v3 on v2

--- a/solution.py
+++ b/solution.py
@@ -1,7 +1,9 @@
+import numpy as np
 import jax
 import jax.numpy as jnp
 from jax import lax
 from jax.experimental import pallas as pl
+from jax.experimental.pallas import tpu as pltpu
 from jax.sharding import PartitionSpec as P
 
 viscosity = 0.1
@@ -91,29 +93,66 @@
     return jnp.sum(out.reshape(nk, ns, ROWS), axis=2)
 
 
-def residual_kernel(l_ref, b_ref, s_ref, o_ref):
+def residual_kernel(c_ref, b_ref, s_ref, o_ref, g_ref, spread_ref, acc_ref):
     nk, rows, nz = b_ref.shape
     ns = s_ref.shape[0]
-    prod = jnp.dot(l_ref[...], b_ref[...].reshape(nk * rows, nz), preferred_element_type=jnp.float32)
-    o_ref[...] = s_ref[...] - prod.reshape(ns, rows, nz)
+    step = pl.program_id(0)
+
+    @pl.when(step == 0)
+    def _():
+        col = lax.broadcasted_iota(jnp.int32, (nk, nk * rows), 1)
+        row = lax.broadcasted_iota(jnp.int32, (nk, nk * rows), 0)
+        expand = jnp.where(col // rows == row, 1.0, 0.0).astype(jnp.bfloat16)
+        wide = jnp.dot(c_ref[...], expand, preferred_element_type=jnp.float32)
+        tall = jnp.broadcast_to(wide[:, None, :], (ns, rows, nk * rows)).reshape(ns * rows, nk * rows)
+        r_t = lax.broadcasted_iota(jnp.int32, tall.shape, 0) % rows
+        c_t = lax.broadcasted_iota(jnp.int32, tall.shape, 1) % rows
+        spread_ref[...] = jnp.where(r_t == c_t, tall, 0.0).astype(jnp.bfloat16)
+        acc_ref[...] = jnp.zeros_like(acc_ref)
+
+    prod = jnp.dot(spread_ref[...], b_ref[...].reshape(nk * rows, nz), preferred_element_type=jnp.float32)
+    w = s_ref[...] - prod.reshape(ns, rows, nz)
+    o_ref[...] = w
+    p = 0
+    for a in range(ns):
+        for b in range(a, ns):
+            term = w[a] * w[b]
+            acc_ref[p] += term[: rows // 2] + term[rows // 2:]
+            p += 1
+
+    @pl.when(step == pl.num_programs(0) - 1)
+    def _():
+        g_ref[...] = jnp.sum(acc_ref[...], axis=1)
 
 
 def residual(coeffs_bf, basis3, snaps3):
     nk, nr, nz = basis3.shape
     ns = snaps3.shape[0]
-    eye = jnp.eye(ROWS, dtype=jnp.bfloat16)
-    spread = (coeffs_bf.T[:, None, :, None] * eye[None, :, None, :]).reshape(ns * ROWS, nk * ROWS)
-    return pl.pallas_call(
+    pairs = ns * (ns + 1) // 2
+    w, g = pl.pallas_call(
         residual_kernel,
         grid=(nr // ROWS,),
-        in_specs=[pl.BlockSpec((ns * ROWS, nk * ROWS), lambda j: (0, 0)),
+        in_specs=[pl.BlockSpec((ns, nk), lambda j: (0, 0)),
                   pl.BlockSpec((nk, ROWS, nz), lambda j: (0, j, 0)),
                   pl.BlockSpec((ns, ROWS, nz), lambda j: (0, j, 0))],
-        out_specs=pl.BlockSpec((ns, ROWS, nz), lambda j: (0, j, 0)),
-        out_shape=jax.ShapeDtypeStruct((ns, nr, nz), jnp.float32),
+        out_specs=[pl.BlockSpec((ns, ROWS, nz), lambda j: (0, j, 0)),
+                   pl.BlockSpec((pairs, nz), lambda j: (0, 0))],
+        out_shape=[jax.ShapeDtypeStruct((ns, nr, nz), jnp.float32),
+                   jax.ShapeDtypeStruct((pairs, nz), jnp.float32)],
+        scratch_shapes=[pltpu.VMEM((ns * ROWS, nk * ROWS), jnp.bfloat16),
+                        pltpu.VMEM((pairs, ROWS // 2, nz), jnp.float32)],
+        compiler_params=pltpu.CompilerParams(dimension_semantics=("arbitrary",)),
         cost_estimate=pl.CostEstimate(flops=2 * ns * ROWS * nk * ROWS * nz * (nr // ROWS), transcendentals=0,
                                       bytes_accessed=nk * nr * nz * 2 + 2 * ns * nr * nz * 4),
-    )(spread, basis3, snaps3)
+    )(coeffs_bf.T, basis3, snaps3)
+    sums = jnp.sum(g, axis=1)
+    table = np.zeros((ns, ns), np.int32)
+    p = 0
+    for a in range(ns):
+        for b in range(a, ns):
+            table[a, b] = p; table[b, a] = p; p += 1
+    gram = sums[jnp.asarray(table)]
+    return w, gram
 
 
 def offset_slice(padded, offset, dimension, length):
@@ -174,8 +213,7 @@
     partial_proj = project(basis3, snaps3.astype(jnp.bfloat16))
     coeffs = allreduce(partial_proj, ("role", "slab"))
     coeffs_bf = coeffs.astype(jnp.bfloat16)
-    residual3 = residual(coeffs_bf, basis3, snaps3)
-    local_gram = jnp.einsum("srz,trz->st", residual3, residual3, precision=lax.Precision.HIGHEST)
+    residual3, local_gram = residual(coeffs_bf, basis3, snaps3)
     total_gram = allreduce(local_gram, ("role", "slab"))
     lower_factor = jnp.linalg.cholesky(total_gram)
     directions = jax.scipy.linalg.solve_triangular(lower_factor, residual3.reshape(ns, -1), lower=True)

time: 156 us -> 142 us (0.910)
  waiting for transfers between devices: 53.6 us -> 73 us
  local copies, waits for them, and re-layouts: 24.7 us -> 9.91 us
  starting transfers between devices: 32.5 us -> 19.7 us
  matrix products: 5.55 us -> 1.05 us
  other arithmetic: 16.5 us -> 14.5 us
    mul x1 -> x0, local copies, waits for them, and re-layouts: 15.8 us -> none  [residual(): coeffs_bf.T[:, None, :, None] * eye[None, :, None, :]]
    ppermute x4, waiting for transfers between devices: 0.01 us -> 7.77 us  [extended(): lax.ppermute(head, axis, [((i + 1) % count, i) for i in range(ends)])]
    ppermute x14, starting transfers between devices: 7.43 us -> 0.12 us  [allreduce(): value = value + lax.ppermute(value, name, pairs)]
    ppermute x14, waiting for transfers between devices: 44 us -> 51.3 us  [allreduce(): value = value + lax.ppermute(value, name, pairs)]
    ppermute x4, starting transfers between devices: 16.9 us -> 11.8 us  [extended(): lax.ppermute(head, axis, [((i + 1) % count, i) for i in range(ends)])]
    dot_general x1 -> x0, matrix products: 4.52 us -> none  [on_device(): jnp.einsum('srz,trz->st', residual3, residual3, precision=lax.Precision.H...]
    ppermute x4, waiting for transfers between devices: 9.67 us -> 14 us  [extended(): lax.ppermute(tail, axis, [(i, (i + 1) % count) for i in range(ends)])]
    mul x1 -> x0, other arithmetic: 3.9 us -> none  [residual(): coeffs_bf.T[:, None, :, None] * eye[None, :, None, :]]
  transfers between devices with their start and end apart: 22 -> 22, of which waited for: 17 -> 19; matrix products, arithmetic and copies ran while one was open for 4% -> 5% of each run, Pallas kernels for 0% -> 0%
where the time goes in v3:
time: 142 us; the launch traced here: 141 us
  waiting for transfers between devices  73 us (51%)
  Pallas kernels  22.2 us (16%)
  starting transfers between devices  19.7 us (14%)
  other arithmetic  14.5 us (10%)
  local copies, waits for them, and re-layouts  9.91 us (7%)
    ppermute x14, waiting for transfers between devices, allreduce(): value = value + lax.ppermute(value, name, pairs)  51.3 us
    ppermute x4, waiting for transfers between devices, extended(): lax.ppermute(tail, axis, [(i, (i + 1) % count) for i in range(ends)])  14 us
    ppermute x4, starting transfers between devices, extended(): lax.ppermute(head, axis, [((i + 1) % count, i) for i in range(ends)])  11.8 us
    pallas_call x1, Pallas kernels, project(): pl.pallas_call(project_kernel, grid=(nk // tk,), in_specs=[pl.BlockSpec((...  11.1 us
    pallas_call x1, Pallas kernels, residual(): pl.pallas_call(residual_kernel, grid=(nr // ROWS,), in_specs=[pl.BlockSpe...  11 us
    ppermute x4, starting transfers between devices, extended(): lax.ppermute(tail, axis, [(i, (i + 1) % count) for i in range(ends)])  7.8 us
    ppermute x4, waiting for transfers between devices, extended(): lax.ppermute(head, axis, [((i + 1) % count, i) for i in range(ends)])  7.77 us
    add x2, other arithmetic, stencil(): result = -profile * first_x + viscosity * laplace  5.08 us
  transfers between devices with their start and end apart: 22, of which 19 were waited for; matrix products, arithmetic and copies ran while one was open for 5% of the time, Pallas kernels for 0%

profile of v3, /device:TPU:0, one launch (start us, length us, event | category | flops | bytes accessed | tf_op | source)
XLA Modules:
  0.0 141.1 jit_solution(5475608213418800748)
XLA Ops:
  0.6 8.8 %collective-permute-start = (f32[4,2,64,256]{3,2,1,0:T(8,128)}, f32[4,2,64,256]{3,2,1,0:T(8,128)S(1)}, u32[]{:S(2)}, u32[]{:S(2)}) collective-permute-start(f32[4,2,64,256]{3,2,1,0:T(8,128)} %param.5), channel_id=1, source_target_pairs={{1,0},{2,1},{3,2},{4,3},{5,4},{6,5},{7,6},{8,7},{9,8},{10,9},{11,1... | collective-permute-start | bytes 1572872 | tf_op jit(solution)/shard_map/ppermute | solution.py:24
  9.5 0.0 collective-permute-start.1
  9.5 0.9 fusion.53
  10.4 1.3 collective-permute-start.2
  11.7 3.0 %collective-permute-start.3 = (f32[4,2,2,256]{3,2,1,0:T(2,128)S(1)}, f32[4,2,2,256]{3,2,1,0:T(2,128)S(1)}, u32[]{:S(2)}, u32[]{:S(2)}) collective-permute-start(f32[4,2,2,256]{3,2,1,0:T(2,128)S(1)} %get-tuple-element.23), channel_id=1, source_target_pairs={{0,64},{1,65},{2,66},{3,67},{4,68},{5,69},{6,70},{7,71},{8,72},{9,... | collective-permute-start | bytes 49160 | tf_op jit(solution)/shard_map/ppermute | solution.py:22
  14.7 1.1 constant_dynamic-update-slice_fusion.1
  15.8 1.2 fusion.54
  17.0 0.7 negate_multiply_fusion
  17.7 0.7 dynamic_slice.7
  18.5 0.0 collective-permute-done.3
  18.5 2.5 %collective-permute-done = f32[4,2,64,256]{3,2,1,0:T(8,128)S(1)} collective-permute-done((f32[4,2,64,256]{3,2,1,0:T(8,128)}, f32[4,2,64,256]{3,2,1,0:T(8,128)S(1)}, u32[]{:S(2)}, u32[]{:S(2)}) %collective-permute-start) | collective-permute-done | bytes 524320 | tf_op jit(solution)/shard_map/ppermute | solution.py:24
  21.0 7.5 %collective-permute-done.1 = f32[4,2,64,256]{3,2,1,0:T(8,128)S(1)} collective-permute-done((f32[4,2,64,256]{3,2,1,0:T(8,128)}, f32[4,2,64,256]{3,2,1,0:T(8,128)S(1)}, u32[]{:S(2)}, u32[]{:S(2)}) %collective-permute-start.1) | collective-permute-done | bytes 524320 | tf_op jit(solution)/shard_map/ppermute | solution.py:22
  28.5 4.2 %fusion.19 = f32[4,2,64,256]{3,2,1,0:T(8,128)S(1)} fusion(f32[4,2,2,256]{3,2,1,0:T(2,128)S(1)} %collective-permute-done.3, f32[4,2,64,256]{3,2,1,0:T(8,128)} %param.5, f32[4,2,64,2]{3,2,1,0:T(8,128)S(1)} %get-tuple-element.25, f32[4,2,64,2]{3,2,1,0:T(8,128)S(1)} %get-tuple-element.24, f32[4,2,66,256]{3,2,1,0:T(8,128)S(1)} %constant_dynamic-update-slice_fusion, ...), kind=kLoop, calls=%fused_computation.35 | loop fusion | flops 5242880 | bytes 3170560 | tf_op jit(solution)/shard_map/add | solution.py:189
  32.7 1.0 slice_subtract_fusion
  33.7 1.1 multiply_add_fusion
  34.8 0.4 collective-permute-start.4
  35.2 1.7 %collective-permute-start.5 = (f32[4,2,64,256]{3,2,1,0:T(8,128)S(1)}, f32[4,2,64,256]{3,2,1,0:T(8,128)S(1)}, u32[]{:S(2)}, u32[]{:S(2)}) collective-permute-start(f32[4,2,64,256]{3,2,1,0:T(8,128)S(1)} %multiply_add_fusion), channel_id=1, source_target_pairs={{0,1},{1,2},{2,3},{3,4},{4,5},{5,6},{6,7},{7,8},{8,9},{9,10},{10,1... | collective-permute-start | bytes 1572872 | tf_op jit(solution)/shard_map/ppermute | solution.py:22
  36.9 1.3 collective-permute-start.6
  38.2 3.0 %collective-permute-start.7 = (f32[4,2,2,256]{3,2,1,0:T(2,128)S(1)}, f32[4,2,2,256]{3,2,1,0:T(2,128)S(1)}, u32[]{:S(2)}, u32[]{:S(2)}) collective-permute-start(f32[4,2,2,256]{3,2,1,0:T(2,128)S(1)} %get-tuple-element.21), channel_id=1, source_target_pairs={{0,64},{1,65},{2,66},{3,67},{4,68},{5,69},{6,70},{7,71},{8,72},{9,... | collective-permute-start | bytes 49160 | tf_op jit(solution)/shard_map/ppermute | solution.py:22
  41.3 0.1 fusion.51
  41.4 0.0 collective-permute-done.6
  41.4 0.7 collective-permute-done.7
  42.1 5.3 %collective-permute-done.4 = f32[4,2,64,256]{3,2,1,0:T(8,128)S(1)} collective-permute-done((f32[4,2,64,256]{3,2,1,0:T(8,128)S(1)}, f32[4,2,64,256]{3,2,1,0:T(8,128)S(1)}, u32[]{:S(2)}, u32[]{:S(2)}) %collective-permute-start.4) | collective-permute-done | bytes 524320 | tf_op jit(solution)/shard_map/ppermute | solution.py:24
  47.4 5.8 %collective-permute-done.5 = f32[4,2,64,256]{3,2,1,0:T(8,128)S(1)} collective-permute-done((f32[4,2,64,256]{3,2,1,0:T(8,128)S(1)}, f32[4,2,64,256]{3,2,1,0:T(8,128)S(1)}, u32[]{:S(2)}, u32[]{:S(2)}) %collective-permute-start.5) | collective-permute-done | bytes 524320 | tf_op jit(solution)/shard_map/ppermute | solution.py:22
  53.1 0.9 fusion.7
  54.0 0.1 fusion.46
  54.1 1.2 fusion.45
  55.3 0.0 copy-start.1
  55.3 0.1 pad_maximum_fusion
  55.4 0.0 copy-start
  55.4 1.0 bitcast_convert_fusion.s_ref
  56.4 11.1 %shard_map.84 = f32[256,128]{1,0:T(8,128)} custom-call(bf16[256,128,256]{2,1,0:T(8,128)(2,1)} %bitcast.30, bf16[8,128,256]{2,1,0:T(8,128)(2,1)} %bitcast_convert_fusion.s_ref), custom_call_target="tpu_custom_call" | custom-call | flops 2147483648 | bytes 17432576 | tf_op jit(solution)/shard_map/pallas_call | solution.py:83
  67.5 1.0 copy.15
  68.6 0.1 collective-permute-start.8
  68.7 1.2 collective-permute-done.8
  69.8 3.6 %collective-permute-done.9 = f32[256,8]{0,1:T(8,128)S(1)} collective-permute-done((f32[256,8]{0,1:T(8,128)S(1)}, f32[256,8]{0,1:T(8,128)S(1)}, u32[]{:S(2)}, u32[]{:S(2)}) %collective-permute-start.9) | collective-permute-done | bytes 8224 | tf_op jit(solution)/shard_map/ppermute | solution.py:61
  73.5 0.0 collective-permute-start.10
  73.5 4.9 %collective-permute-done.10 = f32[256,8]{0,1:T(8,128)S(1)} collective-permute-done((f32[256,8]{0,1:T(8,128)S(1)}, f32[256,8]{0,1:T(8,128)S(1)}, u32[]{:S(2)}, u32[]{:S(2)}) %collective-permute-start.10) | collective-permute-done | bytes 8224 | tf_op jit(solution)/shard_map/ppermute | solution.py:61
  78.3 3.6 %collective-permute-done.11 = f32[256,8]{0,1:T(8,128)S(1)} collective-permute-done((f32[256,8]{0,1:T(8,128)S(1)}, f32[256,8]{0,1:T(8,128)S(1)}, u32[]{:S(2)}, u32[]{:S(2)}) %collective-permute-start.11) | collective-permute-done | bytes 8224 | tf_op jit(solution)/shard_map/ppermute | solution.py:61
  82.0 4.9 %collective-permute-done.12 = f32[256,8]{0,1:T(8,128)S(1)} collective-permute-done((f32[256,8]{0,1:T(8,128)S(1)}, f32[256,8]{0,1:T(8,128)S(1)}, u32[]{:S(2)}, u32[]{:S(2)}) %collective-permute-start.12) | collective-permute-done | bytes 8224 | tf_op jit(solution)/shard_map/ppermute | solution.py:61
  86.9 3.6 %collective-permute-done.13 = f32[256,8]{0,1:T(8,128)S(1)} collective-permute-done((f32[256,8]{0,1:T(8,128)S(1)}, f32[256,8]{0,1:T(8,128)S(1)}, u32[]{:S(2)}, u32[]{:S(2)}) %collective-permute-start.13) | collective-permute-done | bytes 8224 | tf_op jit(solution)/shard_map/ppermute | solution.py:61
  90.5 4.8 %collective-permute-done.14 = f32[256,8]{0,1:T(8,128)S(1)} collective-permute-done((f32[256,8]{0,1:T(8,128)S(1)}, f32[256,8]{0,1:T(8,128)S(1)}, u32[]{:S(2)}, u32[]{:S(2)}) %collective-permute-start.14) | collective-permute-done | bytes 8224 | tf_op jit(solution)/shard_map/ppermute | solution.py:61
  95.4 0.6 convert_bitcast_fusion
  96.0 11.0 %shard_map.85 = (f32[8,128,256]{2,1,0:T(8,128)}, f32[36,256]{1,0:T(8,128)}) custom-call(bf16[8,256]{1,0:T(8,128)(2,1)} %get-tuple-element.16.c_ref, bf16[256,128,256]{2,1,0:T(8,128)(2,1)} %bitcast.31, f32[8,128,256]{2,1,0:T(8,128)} %bitcast.32), custom_call_target="tpu_custom_call" | custom-call | flops 2147483648 | bytes 18874368 | tf_op jit(solution)/shard_map/pallas_call | solution.py:132
  107.0 0.9 reduce_sum.19
  107.9 0.8 gather_fusion
  108.7 0.1 reshape.42
  108.8 0.1 copy.17
  108.9 1.2 collective-permute-done.15
  110.0 3.6 %collective-permute-done.16 = f32[8,8]{0,1:T(8,128)S(1)} collective-permute-done((f32[8,8]{0,1:T(8,128)S(1)}, f32[8,8]{0,1:T(8,128)S(1)}, u32[]{:S(2)}, u32[]{:S(2)}) %collective-permute-start.16) | collective-permute-done | bytes 288 | tf_op jit(solution)/shard_map/ppermute | solution.py:61
  113.7 4.8 %collective-permute-done.17 = f32[8,8]{0,1:T(8,128)S(1)} collective-permute-done((f32[8,8]{0,1:T(8,128)S(1)}, f32[8,8]{0,1:T(8,128)S(1)}, u32[]{:S(2)}, u32[]{:S(2)}) %collective-permute-start.17) | collective-permute-done | bytes 288 | tf_op jit(solution)/shard_map/ppermute | solution.py:61
  118.5 3.6 %collective-permute-done.18 = f32[8,8]{0,1:T(8,128)S(1)} collective-permute-done((f32[8,8]{0,1:T(8,128)S(1)}, f32[8,8]{0,1:T(8,128)S(1)}, u32[]{:S(2)}, u32[]{:S(2)}) %collective-permute-start.18) | collective-permute-done | bytes 288 | tf_op jit(solution)/shard_map/ppermute | solution.py:61
  122.1 4.8 %collective-permute-done.19 = f32[8,8]{0,1:T(8,128)S(1)} collective-permute-done((f32[8,8]{0,1:T(8,128)S(1)}, f32[8,8]{0,1:T(8,128)S(1)}, u32[]{:S(2)}, u32[]{:S(2)}) %collective-permute-start.19) | collective-permute-done | bytes 288 | tf_op jit(solution)/shard_map/ppermute | solution.py:61
  126.9 3.6 %collective-permute-done.20 = f32[8,8]{0,1:T(8,128)S(1)} collective-permute-done((f32[8,8]{0,1:T(8,128)S(1)}, f32[8,8]{0,1:T(8,128)S(1)}, u32[]{:S(2)}, u32[]{:S(2)}) %collective-permute-start.20) | collective-permute-done | bytes 288 | tf_op jit(solution)/shard_map/ppermute | solution.py:61
  130.5 1.8 %copy.23 = f32[1,8,128,256]{3,1,2,0:T(8,128)S(1)} copy(f32[1,8,128,256]{3,2,1,0:T(8,128)} %bitcast.34) | data formatting | bytes 2097152
  132.4 3.0 %collective-permute-done.21 = f32[8,8]{0,1:T(8,128)S(1)} collective-permute-done((f32[8,8]{0,1:T(8,128)S(1)}, f32[8,8]{0,1:T(8,128)S(1)}, u32[]{:S(2)}, u32[]{:S(2)}) %collective-permute-start.21) | collective-permute-done | bytes 288 | tf_op jit(solution)/shard_map/ppermute | solution.py:61
  135.3 0.1 copy.18
  135.4 0.7 cholesky.18
  136.2 0.6 compare_reduce_fusion
  136.8 0.6 select_bitcast_fusion
  137.5 0.6 custom-call.7
  138.1 1.0 fusion.47
  139.2 1.3 copy.21
  140.4 0.7 copy.20
  (38 shorter events, 0.3 us)
Async XLA Ops:
  0.6 20.3 %collective-permute-start = (f32[4,2,64,256]{3,2,1,0:T(8,128)}, f32[4,2,64,256]{3,2,1,0:T(8,128)S(1)}, u32[]{:S(2)}, u32[]{:S(2)}) collective-permute-start(f32[4,2,64,256]{3,2,1,0:T(8,128)} %param.5), channel_id=1, source_target_pairs={{1,0},{2,1},{3,2},{4,3},{5,4},{6,5},{7,6},{8,7},{9,8},{10,9},{11,1... | collective-permute-start | bytes 1572872 | tf_op jit(solution)/shard_map/ppermute | solution.py:24
  9.5 19.0 %collective-permute-start.1 = (f32[4,2,64,256]{3,2,1,0:T(8,128)}, f32[4,2,64,256]{3,2,1,0:T(8,128)S(1)}, u32[]{:S(2)}, u32[]{:S(2)}) collective-permute-start(f32[4,2,64,256]{3,2,1,0:T(8,128)} %param.5), channel_id=1, source_target_pairs={{0,1},{1,2},{2,3},{3,4},{4,5},{5,6},{6,7},{7,8},{8,9},{9,10},{10,1... | collective-permute-start | bytes 1572872 | tf_op jit(solution)/shard_map/ppermute | solution.py:22
  10.4 8.1 %collective-permute-start.2 = (f32[4,2,2,256]{3,2,1,0:T(2,128)S(1)}, f32[4,2,2,256]{3,2,1,0:T(2,128)S(1)}, u32[]{:S(2)}, u32[]{:S(2)}) collective-permute-start(f32[4,2,2,256]{3,2,1,0:T(2,128)S(1)} %get-tuple-element.22), channel_id=1, source_target_pairs={{64,0},{65,1},{66,2},{67,3},{68,4},{69,5},{70,6},{71,7},{72,8},{73... | collective-permute-start | bytes 49160 | tf_op jit(solution)/shard_map/ppermute | solution.py:24
  11.7 6.8 %collective-permute-start.3 = (f32[4,2,2,256]{3,2,1,0:T(2,128)S(1)}, f32[4,2,2,256]{3,2,1,0:T(2,128)S(1)}, u32[]{:S(2)}, u32[]{:S(2)}) collective-permute-start(f32[4,2,2,256]{3,2,1,0:T(2,128)S(1)} %get-tuple-element.23), channel_id=1, source_target_pairs={{0,64},{1,65},{2,66},{3,67},{4,68},{5,69},{6,70},{7,71},{8,72},{9,... | collective-permute-start | bytes 49160 | tf_op jit(solution)/shard_map/ppermute | solution.py:22
  28.5 62.0 %copy-start.2 = (s32[64]{0:T(128)S(1)}, s32[64]{0:T(128)}, u32[]{:S(2)}) copy-start(s32[64]{0:T(128)} %constant.95) | copy-start | bytes 772
  34.8 12.5 %collective-permute-start.4 = (f32[4,2,64,256]{3,2,1,0:T(8,128)S(1)}, f32[4,2,64,256]{3,2,1,0:T(8,128)S(1)}, u32[]{:S(2)}, u32[]{:S(2)}) collective-permute-start(f32[4,2,64,256]{3,2,1,0:T(8,128)S(1)} %multiply_add_fusion), channel_id=1, source_target_pairs={{1,0},{2,1},{3,2},{4,3},{5,4},{6,5},{7,6},{8,7},{9,8},{10,9},{11,1... | collective-permute-start | bytes 1572872 | tf_op jit(solution)/shard_map/ppermute | solution.py:24
  35.2 17.9 %collective-permute-start.5 = (f32[4,2,64,256]{3,2,1,0:T(8,128)S(1)}, f32[4,2,64,256]{3,2,1,0:T(8,128)S(1)}, u32[]{:S(2)}, u32[]{:S(2)}) collective-permute-start(f32[4,2,64,256]{3,2,1,0:T(8,128)S(1)} %multiply_add_fusion), channel_id=1, source_target_pairs={{0,1},{1,2},{2,3},{3,4},{4,5},{5,6},{6,7},{7,8},{8,9},{9,10},{10,1... | collective-permute-start | bytes 1572872 | tf_op jit(solution)/shard_map/ppermute | solution.py:22
  36.9 4.5 %collective-permute-start.6 = (f32[4,2,2,256]{3,2,1,0:T(2,128)S(1)}, f32[4,2,2,256]{3,2,1,0:T(2,128)S(1)}, u32[]{:S(2)}, u32[]{:S(2)}) collective-permute-start(f32[4,2,2,256]{3,2,1,0:T(2,128)S(1)} %get-tuple-element.20), channel_id=1, source_target_pairs={{64,0},{65,1},{66,2},{67,3},{68,4},{69,5},{70,6},{71,7},{72,8},{73... | collective-permute-start | bytes 49160 | tf_op jit(solution)/shard_map/ppermute | solution.py:24
  38.2 3.9 %collective-permute-start.7 = (f32[4,2,2,256]{3,2,1,0:T(2,128)S(1)}, f32[4,2,2,256]{3,2,1,0:T(2,128)S(1)}, u32[]{:S(2)}, u32[]{:S(2)}) collective-permute-start(f32[4,2,2,256]{3,2,1,0:T(2,128)S(1)} %get-tuple-element.21), channel_id=1, source_target_pairs={{0,64},{1,65},{2,66},{3,67},{4,68},{5,69},{6,70},{7,71},{8,72},{9,... | collective-permute-start | bytes 49160 | tf_op jit(solution)/shard_map/ppermute | solution.py:22
  55.3 51.7 %copy-start.1 = (f32[4,2,64,256]{3,2,1,0:T(8,128)}, f32[4,2,64,256]{3,2,1,0:T(8,128)S(1)}, u32[]{:S(2)}) copy-start(f32[4,2,64,256]{3,2,1,0:T(8,128)S(1)} %fusion.45) | copy-start | bytes 1572868
  55.4 40.6 %copy-start = (f32[8,2,64,256]{3,2,1,0:T(8,128)}, f32[8,2,64,256]{3,2,1,0:T(8,128)S(1)}, u32[]{:S(2)}) copy-start(f32[8,2,64,256]{3,2,1,0:T(8,128)S(1)} %pad_maximum_fusion) | copy-start | bytes 3145732
  68.6 1.3 collective-permute-start.8
  69.8 3.7 %collective-permute-start.9 = (f32[256,8]{0,1:T(8,128)S(1)}, f32[256,8]{0,1:T(8,128)S(1)}, u32[]{:S(2)}, u32[]{:S(2)}) collective-permute-start(f32[256,8]{0,1:T(8,128)S(1)} %add.161), channel_id=1, source_target_pairs={{0,1},{1,0},{2,3},{3,2},{4,5},{5,4},{6,7},{7,6},{8,9},{9,8},{10,11... | collective-permute-start | bytes 24584 | tf_op jit(solution)/shard_map/ppermute | solution.py:61
  73.5 4.9 %collective-permute-start.10 = (f32[256,8]{0,1:T(8,128)S(1)}, f32[256,8]{0,1:T(8,128)S(1)}, u32[]{:S(2)}, u32[]{:S(2)}) collective-permute-start(f32[256,8]{0,1:T(8,128)S(1)} %add.162), channel_id=1, source_target_pairs={{0,3},{1,2},{2,1},{3,0},{4,7},{5,6},{6,5},{7,4},{8,11},{9,10},{10,... | collective-permute-start | bytes 24584 | tf_op jit(solution)/shard_map/ppermute | solution.py:61
  78.3 3.7 %collective-permute-start.11 = (f32[256,8]{0,1:T(8,128)S(1)}, f32[256,8]{0,1:T(8,128)S(1)}, u32[]{:S(2)}, u32[]{:S(2)}) collective-permute-start(f32[256,8]{0,1:T(8,128)S(1)} %add.163), channel_id=1, source_target_pairs={{0,4},{1,5},{2,6},{3,7},{4,0},{5,1},{6,2},{7,3},{8,12},{9,13},{10,... | collective-permute-start | bytes 24584 | tf_op jit(solution)/shard_map/ppermute | solution.py:61
  82.0 4.9 %collective-permute-start.12 = (f32[256,8]{0,1:T(8,128)S(1)}, f32[256,8]{0,1:T(8,128)S(1)}, u32[]{:S(2)}, u32[]{:S(2)}) collective-permute-start(f32[256,8]{0,1:T(8,128)S(1)} %add.164), channel_id=1, source_target_pairs={{0,12},{1,13},{2,14},{3,15},{4,8},{5,9},{6,10},{7,11},{8,4},{9,5},... | collective-permute-start | bytes 24584 | tf_op jit(solution)/shard_map/ppermute | solution.py:61
  86.9 3.7 %collective-permute-start.13 = (f32[256,8]{0,1:T(8,128)S(1)}, f32[256,8]{0,1:T(8,128)S(1)}, u32[]{:S(2)}, u32[]{:S(2)}) collective-permute-start(f32[256,8]{0,1:T(8,128)S(1)} %add.165), channel_id=1, source_target_pairs={{0,16},{1,17},{2,18},{3,19},{4,20},{5,21},{6,22},{7,23},{8,24},{9,... | collective-permute-start | bytes 24584 | tf_op jit(solution)/shard_map/ppermute | solution.py:61
  90.5 4.9 %collective-permute-start.14 = (f32[256,8]{0,1:T(8,128)S(1)}, f32[256,8]{0,1:T(8,128)S(1)}, u32[]{:S(2)}, u32[]{:S(2)}) collective-permute-start(f32[256,8]{0,1:T(8,128)S(1)} %add.166), channel_id=1, source_target_pairs={{0,48},{1,49},{2,50},{3,51},{4,52},{5,53},{6,54},{7,55},{8,56},{9,... | collective-permute-start | bytes 24584 | tf_op jit(solution)/shard_map/ppermute | solution.py:61
  108.9 1.2 collective-permute-start.15
  110.0 3.6 %collective-permute-start.16 = (f32[8,8]{0,1:T(8,128)S(1)}, f32[8,8]{0,1:T(8,128)S(1)}, u32[]{:S(2)}, u32[]{:S(2)}) collective-permute-start(f32[8,8]{0,1:T(8,128)S(1)} %add.170), channel_id=1, source_target_pairs={{0,1},{1,0},{2,3},{3,2},{4,5},{5,4},{6,7},{7,6},{8,9},{9,8},{10,11... | collective-permute-start | bytes 776 | tf_op jit(solution)/shard_map/ppermute | solution.py:61
  113.7 4.8 %collective-permute-start.17 = (f32[8,8]{0,1:T(8,128)S(1)}, f32[8,8]{0,1:T(8,128)S(1)}, u32[]{:S(2)}, u32[]{:S(2)}) collective-permute-start(f32[8,8]{0,1:T(8,128)S(1)} %add.171), channel_id=1, source_target_pairs={{0,3},{1,2},{2,1},{3,0},{4,7},{5,6},{6,5},{7,4},{8,11},{9,10},{10,... | collective-permute-start | bytes 776 | tf_op jit(solution)/shard_map/ppermute | solution.py:61
  118.5 3.6 %collective-permute-start.18 = (f32[8,8]{0,1:T(8,128)S(1)}, f32[8,8]{0,1:T(8,128)S(1)}, u32[]{:S(2)}, u32[]{:S(2)}) collective-permute-start(f32[8,8]{0,1:T(8,128)S(1)} %add.172), channel_id=1, source_target_pairs={{0,4},{1,5},{2,6},{3,7},{4,0},{5,1},{6,2},{7,3},{8,12},{9,13},{10,... | collective-permute-start | bytes 776 | tf_op jit(solution)/shard_map/ppermute | solution.py:61
  122.1 4.8 %collective-permute-start.19 = (f32[8,8]{0,1:T(8,128)S(1)}, f32[8,8]{0,1:T(8,128)S(1)}, u32[]{:S(2)}, u32[]{:S(2)}) collective-permute-start(f32[8,8]{0,1:T(8,128)S(1)} %add.173), channel_id=1, source_target_pairs={{0,12},{1,13},{2,14},{3,15},{4,8},{5,9},{6,10},{7,11},{8,4},{9,5},... | collective-permute-start | bytes 776 | tf_op jit(solution)/shard_map/ppermute | solution.py:61
  126.9 3.6 %collective-permute-start.20 = (f32[8,8]{0,1:T(8,128)S(1)}, f32[8,8]{0,1:T(8,128)S(1)}, u32[]{:S(2)}, u32[]{:S(2)}) collective-permute-start(f32[8,8]{0,1:T(8,128)S(1)} %add.174), channel_id=1, source_target_pairs={{0,16},{1,17},{2,18},{3,19},{4,20},{5,21},{6,22},{7,23},{8,24},{9,... | collective-permute-start | bytes 776 | tf_op jit(solution)/shard_map/ppermute | solution.py:61
  130.5 4.8 %collective-permute-start.21 = (f32[8,8]{0,1:T(8,128)S(1)}, f32[8,8]{0,1:T(8,128)S(1)}, u32[]{:S(2)}, u32[]{:S(2)}) collective-permute-start(f32[8,8]{0,1:T(8,128)S(1)} %add.175), channel_id=1, source_target_pairs={{0,48},{1,49},{2,50},{3,51},{4,52},{5,53},{6,54},{7,55},{8,56},{9,... | collective-permute-start | bytes 776 | tf_op jit(solution)/shard_map/ppermute | solution.py:61

commit v4 on v3

--- a/solution.py
+++ b/solution.py
@@ -77,7 +77,7 @@
     o_ref[...] = jnp.sum(acc.reshape(tk, ROWS, ns * ROWS), axis=1)
 
 
-def project(basis3, snaps3, tk=32):
+def project(basis3, snaps3, tk=64):
     nk, nr, nz = basis3.shape
     ns = snaps3.shape[0]
     out = pl.pallas_call(
@@ -94,8 +94,9 @@
 
 
 def residual_kernel(c_ref, b_ref, s_ref, o_ref, g_ref, spread_ref, acc_ref):
-    nk, rows, nz = b_ref.shape
+    nk, _, nz = b_ref.shape
     ns = s_ref.shape[0]
+    rows = ROWS
     step = pl.program_id(0)
 
     @pl.when(step == 0)
@@ -110,32 +111,35 @@
         spread_ref[...] = jnp.where(r_t == c_t, tall, 0.0).astype(jnp.bfloat16)
         acc_ref[...] = jnp.zeros_like(acc_ref)
 
-    prod = jnp.dot(spread_ref[...], b_ref[...].reshape(nk * rows, nz), preferred_element_type=jnp.float32)
-    w = s_ref[...] - prod.reshape(ns, rows, nz)
-    o_ref[...] = w
-    p = 0
-    for a in range(ns):
-        for b in range(a, ns):
-            term = w[a] * w[b]
-            acc_ref[p] += term[: rows // 2] + term[rows // 2:]
-            p += 1
+    for part in range(b_ref.shape[1] // ROWS):
+        window = pl.ds(part * ROWS, ROWS)
+        block = b_ref[:, window, :].reshape(nk * ROWS, nz)
+        prod = jnp.dot(spread_ref[...], block, preferred_element_type=jnp.float32)
+        w = s_ref[:, window, :] - prod.reshape(ns, ROWS, nz)
+        o_ref[:, window, :] = w
+        p = 0
+        for a in range(ns):
+            for b in range(a, ns):
+                term = w[a] * w[b]
+                acc_ref[p] += term[: ROWS // 2] + term[ROWS // 2:]
+                p += 1
 
     @pl.when(step == pl.num_programs(0) - 1)
     def _():
         g_ref[...] = jnp.sum(acc_ref[...], axis=1)
 
 
-def residual(coeffs_bf, basis3, snaps3):
+def residual(coeffs_bf, basis3, snaps3, block_rows=2 * ROWS):
     nk, nr, nz = basis3.shape
     ns = snaps3.shape[0]
     pairs = ns * (ns + 1) // 2
     w, g = pl.pallas_call(
         residual_kernel,
-        grid=(nr // ROWS,),
+        grid=(nr // block_rows,),
         in_specs=[pl.BlockSpec((ns, nk), lambda j: (0, 0)),
-                  pl.BlockSpec((nk, ROWS, nz), lambda j: (0, j, 0)),
-                  pl.BlockSpec((ns, ROWS, nz), lambda j: (0, j, 0))],
-        out_specs=[pl.BlockSpec((ns, ROWS, nz), lambda j: (0, j, 0)),
+                  pl.BlockSpec((nk, block_rows, nz), lambda j: (0, j, 0)),
+                  pl.BlockSpec((ns, block_rows, nz), lambda j: (0, j, 0))],
+        out_specs=[pl.BlockSpec((ns, block_rows, nz), lambda j: (0, j, 0)),
                    pl.BlockSpec((pairs, nz), lambda j: (0, 0))],
         out_shape=[jax.ShapeDtypeStruct((ns, nr, nz), jnp.float32),
                    jax.ShapeDtypeStruct((pairs, nz), jnp.float32)],

time: 142 us -> 138 us (0.972)
  Pallas kernels: 22.2 us -> 18.2 us
    pallas_call x1, Pallas kernels: 11 us -> 9.02 us  [residual(): pl.pallas_call(residual_kernel, grid=(nr // block_rows,), in_specs=[pl.Bl...]
    pallas_call x1, Pallas kernels: 11.1 us -> 9.16 us  [project(): pl.pallas_call(project_kernel, grid=(nk // tk,), in_specs=[pl.BlockSpec((...]
where the time goes in v4:
time: 138 us; the launch traced here: 137 us
  waiting for transfers between devices  73 us (53%)
  starting transfers between devices  19.7 us (14%)
  Pallas kernels  18.2 us (13%)
  other arithmetic  14.5 us (11%)
  local copies, waits for them, and re-layouts  9.9 us (7%)
    ppermute x14, waiting for transfers between devices, allreduce(): value = value + lax.ppermute(value, name, pairs)  51.2 us
    ppermute x4, waiting for transfers between devices, extended(): lax.ppermute(tail, axis, [(i, (i + 1) % count) for i in range(ends)])  14 us
    ppermute x4, starting transfers between devices, extended(): lax.ppermute(head, axis, [((i + 1) % count, i) for i in range(ends)])  11.8 us
    pallas_call x1, Pallas kernels, project(): pl.pallas_call(project_kernel, grid=(nk // tk,), in_specs=[pl.BlockSpec((...  9.16 us
    pallas_call x1, Pallas kernels, residual(): pl.pallas_call(residual_kernel, grid=(nr // block_rows,), in_specs=[pl.Bl...  9.02 us
    ppermute x4, starting transfers between devices, extended(): lax.ppermute(tail, axis, [(i, (i + 1) % count) for i in range(ends)])  7.8 us
    ppermute x4, waiting for transfers between devices, extended(): lax.ppermute(head, axis, [((i + 1) % count, i) for i in range(ends)])  7.77 us
    add x2, other arithmetic, stencil(): result = -profile * first_x + viscosity * laplace  5.08 us
  transfers between devices with their start and end apart: 22, of which 19 were waited for; matrix products, arithmetic and copies ran while one was open for 5% of the time, Pallas kernels for 0%

profile of v4, /device:TPU:0, one launch (start us, length us, event | category | flops | bytes accessed | tf_op | source)
XLA Modules:
  0.0 137.1 jit_solution(7286693882230480546)
XLA Ops:
  0.6 8.8 %collective-permute-start = (f32[4,2,64,256]{3,2,1,0:T(8,128)}, f32[4,2,64,256]{3,2,1,0:T(8,128)S(1)}, u32[]{:S(2)}, u32[]{:S(2)}) collective-permute-start(f32[4,2,64,256]{3,2,1,0:T(8,128)} %param.5), channel_id=1, source_target_pairs={{1,0},{2,1},{3,2},{4,3},{5,4},{6,5},{7,6},{8,7},{9,8},{10,9},{11,1... | collective-permute-start | bytes 1572872 | tf_op jit(solution)/shard_map/ppermute | solution.py:24
  9.5 0.0 collective-permute-start.1
  9.5 0.9 fusion.53
  10.4 1.3 collective-permute-start.2
  11.7 3.0 %collective-permute-start.3 = (f32[4,2,2,256]{3,2,1,0:T(2,128)S(1)}, f32[4,2,2,256]{3,2,1,0:T(2,128)S(1)}, u32[]{:S(2)}, u32[]{:S(2)}) collective-permute-start(f32[4,2,2,256]{3,2,1,0:T(2,128)S(1)} %get-tuple-element.23), channel_id=1, source_target_pairs={{0,64},{1,65},{2,66},{3,67},{4,68},{5,69},{6,70},{7,71},{8,72},{9,... | collective-permute-start | bytes 49160 | tf_op jit(solution)/shard_map/ppermute | solution.py:22
  14.7 1.1 constant_dynamic-update-slice_fusion.1
  15.8 1.2 fusion.54
  17.0 0.7 negate_multiply_fusion
  17.7 0.7 dynamic_slice.7
  18.5 0.0 collective-permute-done.3
  18.5 2.5 %collective-permute-done = f32[4,2,64,256]{3,2,1,0:T(8,128)S(1)} collective-permute-done((f32[4,2,64,256]{3,2,1,0:T(8,128)}, f32[4,2,64,256]{3,2,1,0:T(8,128)S(1)}, u32[]{:S(2)}, u32[]{:S(2)}) %collective-permute-start) | collective-permute-done | bytes 524320 | tf_op jit(solution)/shard_map/ppermute | solution.py:24
  21.0 7.5 %collective-permute-done.1 = f32[4,2,64,256]{3,2,1,0:T(8,128)S(1)} collective-permute-done((f32[4,2,64,256]{3,2,1,0:T(8,128)}, f32[4,2,64,256]{3,2,1,0:T(8,128)S(1)}, u32[]{:S(2)}, u32[]{:S(2)}) %collective-permute-start.1) | collective-permute-done | bytes 524320 | tf_op jit(solution)/shard_map/ppermute | solution.py:22
  28.5 4.2 %fusion.19 = f32[4,2,64,256]{3,2,1,0:T(8,128)S(1)} fusion(f32[4,2,2,256]{3,2,1,0:T(2,128)S(1)} %collective-permute-done.3, f32[4,2,64,256]{3,2,1,0:T(8,128)} %param.5, f32[4,2,64,2]{3,2,1,0:T(8,128)S(1)} %get-tuple-element.25, f32[4,2,64,2]{3,2,1,0:T(8,128)S(1)} %get-tuple-element.24, f32[4,2,66,256]{3,2,1,0:T(8,128)S(1)} %constant_dynamic-update-slice_fusion, ...), kind=kLoop, calls=%fused_computation.35 | loop fusion | flops 5242880 | bytes 3170560 | tf_op jit(solution)/shard_map/add | solution.py:193
  32.7 1.0 slice_subtract_fusion
  33.7 1.1 multiply_add_fusion
  34.8 0.4 collective-permute-start.4
  35.2 1.7 %collective-permute-start.5 = (f32[4,2,64,256]{3,2,1,0:T(8,128)S(1)}, f32[4,2,64,256]{3,2,1,0:T(8,128)S(1)}, u32[]{:S(2)}, u32[]{:S(2)}) collective-permute-start(f32[4,2,64,256]{3,2,1,0:T(8,128)S(1)} %multiply_add_fusion), channel_id=1, source_target_pairs={{0,1},{1,2},{2,3},{3,4},{4,5},{5,6},{6,7},{7,8},{8,9},{9,10},{10,1... | collective-permute-start | bytes 1572872 | tf_op jit(solution)/shard_map/ppermute | solution.py:22
  36.9 1.3 collective-permute-start.6
  38.2 3.0 %collective-permute-start.7 = (f32[4,2,2,256]{3,2,1,0:T(2,128)S(1)}, f32[4,2,2,256]{3,2,1,0:T(2,128)S(1)}, u32[]{:S(2)}, u32[]{:S(2)}) collective-permute-start(f32[4,2,2,256]{3,2,1,0:T(2,128)S(1)} %get-tuple-element.21), channel_id=1, source_target_pairs={{0,64},{1,65},{2,66},{3,67},{4,68},{5,69},{6,70},{7,71},{8,72},{9,... | collective-permute-start | bytes 49160 | tf_op jit(solution)/shard_map/ppermute | solution.py:22
  41.3 0.1 fusion.51
  41.4 0.0 collective-permute-done.6
  41.4 0.7 collective-permute-done.7
  42.1 5.3 %collective-permute-done.4 = f32[4,2,64,256]{3,2,1,0:T(8,128)S(1)} collective-permute-done((f32[4,2,64,256]{3,2,1,0:T(8,128)S(1)}, f32[4,2,64,256]{3,2,1,0:T(8,128)S(1)}, u32[]{:S(2)}, u32[]{:S(2)}) %collective-permute-start.4) | collective-permute-done | bytes 524320 | tf_op jit(solution)/shard_map/ppermute | solution.py:24
  47.4 5.8 %collective-permute-done.5 = f32[4,2,64,256]{3,2,1,0:T(8,128)S(1)} collective-permute-done((f32[4,2,64,256]{3,2,1,0:T(8,128)S(1)}, f32[4,2,64,256]{3,2,1,0:T(8,128)S(1)}, u32[]{:S(2)}, u32[]{:S(2)}) %collective-permute-start.5) | collective-permute-done | bytes 524320 | tf_op jit(solution)/shard_map/ppermute | solution.py:22
  53.1 0.9 fusion.7
  54.0 0.1 fusion.46
  54.1 1.2 fusion.45
  55.3 0.0 copy-start.1
  55.3 0.1 pad_maximum_fusion
  55.4 0.0 copy-start
  55.4 1.0 bitcast_convert_fusion.s_ref
  56.4 9.2 %shard_map.84 = f32[256,128]{1,0:T(8,128)} custom-call(bf16[256,128,256]{2,1,0:T(8,128)(2,1)} %bitcast.30, bf16[8,128,256]{2,1,0:T(8,128)(2,1)} %bitcast_convert_fusion.s_ref), custom_call_target="tpu_custom_call" | custom-call | flops 2147483648 | bytes 17432576 | tf_op jit(solution)/shard_map/pallas_call | solution.py:83
  65.6 1.0 copy.15
  66.6 0.1 collective-permute-start.8
  66.7 1.2 collective-permute-done.8
  67.9 3.6 %collective-permute-done.9 = f32[256,8]{0,1:T(8,128)S(1)} collective-permute-done((f32[256,8]{0,1:T(8,128)S(1)}, f32[256,8]{0,1:T(8,128)S(1)}, u32[]{:S(2)}, u32[]{:S(2)}) %collective-permute-start.9) | collective-permute-done | bytes 8224 | tf_op jit(solution)/shard_map/ppermute | solution.py:61
  71.5 4.9 %collective-permute-done.10 = f32[256,8]{0,1:T(8,128)S(1)} collective-permute-done((f32[256,8]{0,1:T(8,128)S(1)}, f32[256,8]{0,1:T(8,128)S(1)}, u32[]{:S(2)}, u32[]{:S(2)}) %collective-permute-start.10) | collective-permute-done | bytes 8224 | tf_op jit(solution)/shard_map/ppermute | solution.py:61
  76.4 3.6 %collective-permute-done.11 = f32[256,8]{0,1:T(8,128)S(1)} collective-permute-done((f32[256,8]{0,1:T(8,128)S(1)}, f32[256,8]{0,1:T(8,128)S(1)}, u32[]{:S(2)}, u32[]{:S(2)}) %collective-permute-start.11) | collective-permute-done | bytes 8224 | tf_op jit(solution)/shard_map/ppermute | solution.py:61
  80.1 4.9 %collective-permute-done.12 = f32[256,8]{0,1:T(8,128)S(1)} collective-permute-done((f32[256,8]{0,1:T(8,128)S(1)}, f32[256,8]{0,1:T(8,128)S(1)}, u32[]{:S(2)}, u32[]{:S(2)}) %collective-permute-start.12) | collective-permute-done | bytes 8224 | tf_op jit(solution)/shard_map/ppermute | solution.py:61
  84.9 3.6 %collective-permute-done.13 = f32[256,8]{0,1:T(8,128)S(1)} collective-permute-done((f32[256,8]{0,1:T(8,128)S(1)}, f32[256,8]{0,1:T(8,128)S(1)}, u32[]{:S(2)}, u32[]{:S(2)}) %collective-permute-start.13) | collective-permute-done | bytes 8224 | tf_op jit(solution)/shard_map/ppermute | solution.py:61
  88.6 4.8 %collective-permute-done.14 = f32[256,8]{0,1:T(8,128)S(1)} collective-permute-done((f32[256,8]{0,1:T(8,128)S(1)}, f32[256,8]{0,1:T(8,128)S(1)}, u32[]{:S(2)}, u32[]{:S(2)}) %collective-permute-start.14) | collective-permute-done | bytes 8224 | tf_op jit(solution)/shard_map/ppermute | solution.py:61
  93.4 0.6 convert_bitcast_fusion
  94.0 9.0 %shard_map.85 = (f32[8,128,256]{2,1,0:T(8,128)}, f32[36,256]{1,0:T(8,128)}) custom-call(bf16[8,256]{1,0:T(8,128)(2,1)} %get-tuple-element.16.c_ref, bf16[256,128,256]{2,1,0:T(8,128)(2,1)} %bitcast.31, f32[8,128,256]{2,1,0:T(8,128)} %bitcast.32), custom_call_target="tpu_custom_call" | custom-call | flops 2147483648 | bytes 18874368 | tf_op jit(solution)/shard_map/pallas_call | solution.py:136
  103.1 0.9 reduce_sum.19
  104.0 0.8 gather_fusion
  104.7 0.1 reshape.42
  104.8 0.1 copy.17
  104.9 1.2 collective-permute-done.15
  106.1 3.6 %collective-permute-done.16 = f32[8,8]{0,1:T(8,128)S(1)} collective-permute-done((f32[8,8]{0,1:T(8,128)S(1)}, f32[8,8]{0,1:T(8,128)S(1)}, u32[]{:S(2)}, u32[]{:S(2)}) %collective-permute-start.16) | collective-permute-done | bytes 288 | tf_op jit(solution)/shard_map/ppermute | solution.py:61
  109.7 4.8 %collective-permute-done.17 = f32[8,8]{0,1:T(8,128)S(1)} collective-permute-done((f32[8,8]{0,1:T(8,128)S(1)}, f32[8,8]{0,1:T(8,128)S(1)}, u32[]{:S(2)}, u32[]{:S(2)}) %collective-permute-start.17) | collective-permute-done | bytes 288 | tf_op jit(solution)/shard_map/ppermute | solution.py:61
  114.5 3.6 %collective-permute-done.18 = f32[8,8]{0,1:T(8,128)S(1)} collective-permute-done((f32[8,8]{0,1:T(8,128)S(1)}, f32[8,8]{0,1:T(8,128)S(1)}, u32[]{:S(2)}, u32[]{:S(2)}) %collective-permute-start.18) | collective-permute-done | bytes 288 | tf_op jit(solution)/shard_map/ppermute | solution.py:61
  118.1 4.8 %collective-permute-done.19 = f32[8,8]{0,1:T(8,128)S(1)} collective-permute-done((f32[8,8]{0,1:T(8,128)S(1)}, f32[8,8]{0,1:T(8,128)S(1)}, u32[]{:S(2)}, u32[]{:S(2)}) %collective-permute-start.19) | collective-permute-done | bytes 288 | tf_op jit(solution)/shard_map/ppermute | solution.py:61
  122.9 3.6 %collective-permute-done.20 = f32[8,8]{0,1:T(8,128)S(1)} collective-permute-done((f32[8,8]{0,1:T(8,128)S(1)}, f32[8,8]{0,1:T(8,128)S(1)}, u32[]{:S(2)}, u32[]{:S(2)}) %collective-permute-start.20) | collective-permute-done | bytes 288 | tf_op jit(solution)/shard_map/ppermute | solution.py:61
  126.5 0.0 collective-permute-start.21
  126.6 1.8 %copy.23 = f32[1,8,128,256]{3,1,2,0:T(8,128)S(1)} copy(f32[1,8,128,256]{3,2,1,0:T(8,128)} %bitcast.34) | data formatting | bytes 2097152
  128.4 3.0 %collective-permute-done.21 = f32[8,8]{0,1:T(8,128)S(1)} collective-permute-done((f32[8,8]{0,1:T(8,128)S(1)}, f32[8,8]{0,1:T(8,128)S(1)}, u32[]{:S(2)}, u32[]{:S(2)}) %collective-permute-start.21) | collective-permute-done | bytes 288 | tf_op jit(solution)/shard_map/ppermute | solution.py:61
  131.4 0.1 copy.18
  131.5 0.7 cholesky.18
  132.2 0.6 compare_reduce_fusion
  132.8 0.6 select_bitcast_fusion
  133.5 0.6 custom-call.7
  134.1 1.0 fusion.47
  135.2 1.3 copy.21
  136.5 0.7 copy.20
  (38 shorter events, 0.3 us)
Async XLA Ops:
  0.6 20.3 %collective-permute-start = (f32[4,2,64,256]{3,2,1,0:T(8,128)}, f32[4,2,64,256]{3,2,1,0:T(8,128)S(1)}, u32[]{:S(2)}, u32[]{:S(2)}) collective-permute-start(f32[4,2,64,256]{3,2,1,0:T(8,128)} %param.5), channel_id=1, source_target_pairs={{1,0},{2,1},{3,2},{4,3},{5,4},{6,5},{7,6},{8,7},{9,8},{10,9},{11,1... | collective-permute-start | bytes 1572872 | tf_op jit(solution)/shard_map/ppermute | solution.py:24
  9.5 19.0 %collective-permute-start.1 = (f32[4,2,64,256]{3,2,1,0:T(8,128)}, f32[4,2,64,256]{3,2,1,0:T(8,128)S(1)}, u32[]{:S(2)}, u32[]{:S(2)}) collective-permute-start(f32[4,2,64,256]{3,2,1,0:T(8,128)} %param.5), channel_id=1, source_target_pairs={{0,1},{1,2},{2,3},{3,4},{4,5},{5,6},{6,7},{7,8},{8,9},{9,10},{10,1... | collective-permute-start | bytes 1572872 | tf_op jit(solution)/shard_map/ppermute | solution.py:22
  10.4 8.1 %collective-permute-start.2 = (f32[4,2,2,256]{3,2,1,0:T(2,128)S(1)}, f32[4,2,2,256]{3,2,1,0:T(2,128)S(1)}, u32[]{:S(2)}, u32[]{:S(2)}) collective-permute-start(f32[4,2,2,256]{3,2,1,0:T(2,128)S(1)} %get-tuple-element.22), channel_id=1, source_target_pairs={{64,0},{65,1},{66,2},{67,3},{68,4},{69,5},{70,6},{71,7},{72,8},{73... | collective-permute-start | bytes 49160 | tf_op jit(solution)/shard_map/ppermute | solution.py:24
  11.7 6.8 %collective-permute-start.3 = (f32[4,2,2,256]{3,2,1,0:T(2,128)S(1)}, f32[4,2,2,256]{3,2,1,0:T(2,128)S(1)}, u32[]{:S(2)}, u32[]{:S(2)}) collective-permute-start(f32[4,2,2,256]{3,2,1,0:T(2,128)S(1)} %get-tuple-element.23), channel_id=1, source_target_pairs={{0,64},{1,65},{2,66},{3,67},{4,68},{5,69},{6,70},{7,71},{8,72},{9,... | collective-permute-start | bytes 49160 | tf_op jit(solution)/shard_map/ppermute | solution.py:22
  28.5 60.1 %copy-start.2 = (s32[64]{0:T(128)S(1)}, s32[64]{0:T(128)}, u32[]{:S(2)}) copy-start(s32[64]{0:T(128)} %constant.95) | copy-start | bytes 772
  34.8 12.5 %collective-permute-start.4 = (f32[4,2,64,256]{3,2,1,0:T(8,128)S(1)}, f32[4,2,64,256]{3,2,1,0:T(8,128)S(1)}, u32[]{:S(2)}, u32[]{:S(2)}) collective-permute-start(f32[4,2,64,256]{3,2,1,0:T(8,128)S(1)} %multiply_add_fusion), channel_id=1, source_target_pairs={{1,0},{2,1},{3,2},{4,3},{5,4},{6,5},{7,6},{8,7},{9,8},{10,9},{11,1... | collective-permute-start | bytes 1572872 | tf_op jit(solution)/shard_map/ppermute | solution.py:24
  35.2 17.9 %collective-permute-start.5 = (f32[4,2,64,256]{3,2,1,0:T(8,128)S(1)}, f32[4,2,64,256]{3,2,1,0:T(8,128)S(1)}, u32[]{:S(2)}, u32[]{:S(2)}) collective-permute-start(f32[4,2,64,256]{3,2,1,0:T(8,128)S(1)} %multiply_add_fusion), channel_id=1, source_target_pairs={{0,1},{1,2},{2,3},{3,4},{4,5},{5,6},{6,7},{7,8},{8,9},{9,10},{10,1... | collective-permute-start | bytes 1572872 | tf_op jit(solution)/shard_map/ppermute | solution.py:22
  36.9 4.5 %collective-permute-start.6 = (f32[4,2,2,256]{3,2,1,0:T(2,128)S(1)}, f32[4,2,2,256]{3,2,1,0:T(2,128)S(1)}, u32[]{:S(2)}, u32[]{:S(2)}) collective-permute-start(f32[4,2,2,256]{3,2,1,0:T(2,128)S(1)} %get-tuple-element.20), channel_id=1, source_target_pairs={{64,0},{65,1},{66,2},{67,3},{68,4},{69,5},{70,6},{71,7},{72,8},{73... | collective-permute-start | bytes 49160 | tf_op jit(solution)/shard_map/ppermute | solution.py:24
  38.2 3.9 %collective-permute-start.7 = (f32[4,2,2,256]{3,2,1,0:T(2,128)S(1)}, f32[4,2,2,256]{3,2,1,0:T(2,128)S(1)}, u32[]{:S(2)}, u32[]{:S(2)}) collective-permute-start(f32[4,2,2,256]{3,2,1,0:T(2,128)S(1)} %get-tuple-element.21), channel_id=1, source_target_pairs={{0,64},{1,65},{2,66},{3,67},{4,68},{5,69},{6,70},{7,71},{8,72},{9,... | collective-permute-start | bytes 49160 | tf_op jit(solution)/shard_map/ppermute | solution.py:22
  55.3 47.7 %copy-start.1 = (f32[4,2,64,256]{3,2,1,0:T(8,128)}, f32[4,2,64,256]{3,2,1,0:T(8,128)S(1)}, u32[]{:S(2)}) copy-start(f32[4,2,64,256]{3,2,1,0:T(8,128)S(1)} %fusion.45) | copy-start | bytes 1572868
  55.4 38.6 %copy-start = (f32[8,2,64,256]{3,2,1,0:T(8,128)}, f32[8,2,64,256]{3,2,1,0:T(8,128)S(1)}, u32[]{:S(2)}) copy-start(f32[8,2,64,256]{3,2,1,0:T(8,128)S(1)} %pad_maximum_fusion) | copy-start | bytes 3145732
  66.6 1.3 collective-permute-start.8
  67.9 3.7 %collective-permute-start.9 = (f32[256,8]{0,1:T(8,128)S(1)}, f32[256,8]{0,1:T(8,128)S(1)}, u32[]{:S(2)}, u32[]{:S(2)}) collective-permute-start(f32[256,8]{0,1:T(8,128)S(1)} %add.161), channel_id=1, source_target_pairs={{0,1},{1,0},{2,3},{3,2},{4,5},{5,4},{6,7},{7,6},{8,9},{9,8},{10,11... | collective-permute-start | bytes 24584 | tf_op jit(solution)/shard_map/ppermute | solution.py:61
  71.5 4.9 %collective-permute-start.10 = (f32[256,8]{0,1:T(8,128)S(1)}, f32[256,8]{0,1:T(8,128)S(1)}, u32[]{:S(2)}, u32[]{:S(2)}) collective-permute-start(f32[256,8]{0,1:T(8,128)S(1)} %add.162), channel_id=1, source_target_pairs={{0,3},{1,2},{2,1},{3,0},{4,7},{5,6},{6,5},{7,4},{8,11},{9,10},{10,... | collective-permute-start | bytes 24584 | tf_op jit(solution)/shard_map/ppermute | solution.py:61
  76.4 3.7 %collective-permute-start.11 = (f32[256,8]{0,1:T(8,128)S(1)}, f32[256,8]{0,1:T(8,128)S(1)}, u32[]{:S(2)}, u32[]{:S(2)}) collective-permute-start(f32[256,8]{0,1:T(8,128)S(1)} %add.163), channel_id=1, source_target_pairs={{0,4},{1,5},{2,6},{3,7},{4,0},{5,1},{6,2},{7,3},{8,12},{9,13},{10,... | collective-permute-start | bytes 24584 | tf_op jit(solution)/shard_map/ppermute | solution.py:61
  80.1 4.9 %collective-permute-start.12 = (f32[256,8]{0,1:T(8,128)S(1)}, f32[256,8]{0,1:T(8,128)S(1)}, u32[]{:S(2)}, u32[]{:S(2)}) collective-permute-start(f32[256,8]{0,1:T(8,128)S(1)} %add.164), channel_id=1, source_target_pairs={{0,12},{1,13},{2,14},{3,15},{4,8},{5,9},{6,10},{7,11},{8,4},{9,5},... | collective-permute-start | bytes 24584 | tf_op jit(solution)/shard_map/ppermute | solution.py:61
  84.9 3.7 %collective-permute-start.13 = (f32[256,8]{0,1:T(8,128)S(1)}, f32[256,8]{0,1:T(8,128)S(1)}, u32[]{:S(2)}, u32[]{:S(2)}) collective-permute-start(f32[256,8]{0,1:T(8,128)S(1)} %add.165), channel_id=1, source_target_pairs={{0,16},{1,17},{2,18},{3,19},{4,20},{5,21},{6,22},{7,23},{8,24},{9,... | collective-permute-start | bytes 24584 | tf_op jit(solution)/shard_map/ppermute | solution.py:61
  88.6 4.9 %collective-permute-start.14 = (f32[256,8]{0,1:T(8,128)S(1)}, f32[256,8]{0,1:T(8,128)S(1)}, u32[]{:S(2)}, u32[]{:S(2)}) collective-permute-start(f32[256,8]{0,1:T(8,128)S(1)} %add.166), channel_id=1, source_target_pairs={{0,48},{1,49},{2,50},{3,51},{4,52},{5,53},{6,54},{7,55},{8,56},{9,... | collective-permute-start | bytes 24584 | tf_op jit(solution)/shard_map/ppermute | solution.py:61
  104.9 1.2 collective-permute-start.15
  106.1 3.6 %collective-permute-start.16 = (f32[8,8]{0,1:T(8,128)S(1)}, f32[8,8]{0,1:T(8,128)S(1)}, u32[]{:S(2)}, u32[]{:S(2)}) collective-permute-start(f32[8,8]{0,1:T(8,128)S(1)} %add.170), channel_id=1, source_target_pairs={{0,1},{1,0},{2,3},{3,2},{4,5},{5,4},{6,7},{7,6},{8,9},{9,8},{10,11... | collective-permute-start | bytes 776 | tf_op jit(solution)/shard_map/ppermute | solution.py:61
  109.7 4.8 %collective-permute-start.17 = (f32[8,8]{0,1:T(8,128)S(1)}, f32[8,8]{0,1:T(8,128)S(1)}, u32[]{:S(2)}, u32[]{:S(2)}) collective-permute-start(f32[8,8]{0,1:T(8,128)S(1)} %add.171), channel_id=1, source_target_pairs={{0,3},{1,2},{2,1},{3,0},{4,7},{5,6},{6,5},{7,4},{8,11},{9,10},{10,... | collective-permute-start | bytes 776 | tf_op jit(solution)/shard_map/ppermute | solution.py:61
  114.5 3.6 %collective-permute-start.18 = (f32[8,8]{0,1:T(8,128)S(1)}, f32[8,8]{0,1:T(8,128)S(1)}, u32[]{:S(2)}, u32[]{:S(2)}) collective-permute-start(f32[8,8]{0,1:T(8,128)S(1)} %add.172), channel_id=1, source_target_pairs={{0,4},{1,5},{2,6},{3,7},{4,0},{5,1},{6,2},{7,3},{8,12},{9,13},{10,... | collective-permute-start | bytes 776 | tf_op jit(solution)/shard_map/ppermute | solution.py:61
  118.1 4.8 %collective-permute-start.19 = (f32[8,8]{0,1:T(8,128)S(1)}, f32[8,8]{0,1:T(8,128)S(1)}, u32[]{:S(2)}, u32[]{:S(2)}) collective-permute-start(f32[8,8]{0,1:T(8,128)S(1)} %add.173), channel_id=1, source_target_pairs={{0,12},{1,13},{2,14},{3,15},{4,8},{5,9},{6,10},{7,11},{8,4},{9,5},... | collective-permute-start | bytes 776 | tf_op jit(solution)/shard_map/ppermute | solution.py:61
  122.9 3.6 %collective-permute-start.20 = (f32[8,8]{0,1:T(8,128)S(1)}, f32[8,8]{0,1:T(8,128)S(1)}, u32[]{:S(2)}, u32[]{:S(2)}) collective-permute-start(f32[8,8]{0,1:T(8,128)S(1)} %add.174), channel_id=1, source_target_pairs={{0,16},{1,17},{2,18},{3,19},{4,20},{5,21},{6,22},{7,23},{8,24},{9,... | collective-permute-start | bytes 776 | tf_op jit(solution)/shard_map/ppermute | solution.py:61
  126.5 4.8 %collective-permute-start.21 = (f32[8,8]{0,1:T(8,128)S(1)}, f32[8,8]{0,1:T(8,128)S(1)}, u32[]{:S(2)}, u32[]{:S(2)}) collective-permute-start(f32[8,8]{0,1:T(8,128)S(1)} %add.175), channel_id=1, source_target_pairs={{0,48},{1,49},{2,50},{3,51},{4,52},{5,53},{6,54},{7,55},{8,56},{9,... | collective-permute-start | bytes 776 | tf_op jit(solution)/shard_map/ppermute | solution.py:61

commit v5 on v4

--- a/solution.py
+++ b/solution.py
@@ -17,6 +17,14 @@
         ends = count if closed else count - 1
         head = lax.slice_in_dim(cells, 0, width, axis=dim)
         tail = lax.slice_in_dim(cells, cells.shape[dim] - width, cells.shape[dim], axis=dim)
+        if count == 2 and not closed:
+            lower_side = lax.axis_index(axis) == 0
+            got = lax.ppermute(jnp.where(lower_side, tail, head), axis, [(0, 1), (1, 0)])
+            zeros = jnp.zeros_like(got)
+            cells = jnp.concatenate(
+                [jnp.where(lower_side, zeros, got), cells, jnp.where(lower_side, got, zeros)], axis=dim
+            )
+            continue
         cells = jnp.concatenate(
             [
                 lax.ppermute(tail, axis, [(i, (i + 1) % count) for i in range(ends)]),

time: 138 us -> 138 us (level)
  waiting for transfers between devices: 73 us -> 82.5 us
  starting transfers between devices: 19.7 us -> 11.2 us
  local copies, waits for them, and re-layouts: 9.9 us -> 7.88 us
  other arithmetic: 14.5 us -> 16.2 us
    ppermute x4 -> x2, waiting for transfers between devices: 7.77 us -> 17 us  [extended(): lax.ppermute(head, axis, [((i + 1) % count, i) for i in range(ends)])]
    ppermute x4 -> x2, starting transfers between devices: 7.8 us -> 1.75 us  [extended(): lax.ppermute(tail, axis, [(i, (i + 1) % count) for i in range(ends)])]
    ppermute x4 -> x2, starting transfers between devices: 11.8 us -> 9.19 us  [extended(): lax.ppermute(head, axis, [((i + 1) % count, i) for i in range(ends)])]
    unnamed x10 -> x9, local copies, waits for them, and re-layouts: 4.89 us -> 3.81 us
    ppermute x4 -> x2, waiting for transfers between devices: 14 us -> 13.3 us  [extended(): lax.ppermute(tail, axis, [(i, (i + 1) % count) for i in range(ends)])]
  transfers between devices with their start and end apart: 22 -> 20, of which waited for: 19 -> 19; matrix products, arithmetic and copies ran while one was open for 5% -> 4% of each run, Pallas kernels for 0% -> 0%
where the time goes in v5:
time: 138 us
  waiting for transfers between devices  82.5 us (60%)
  Pallas kernels  18.2 us (13%)
  other arithmetic  16.2 us (12%)
  starting transfers between devices  11.2 us (8%)
  local copies, waits for them, and re-layouts  7.88 us (6%)
    ppermute x14, waiting for transfers between devices, allreduce(): value = value + lax.ppermute(value, name, pairs)  51.2 us
    ppermute x2, waiting for transfers between devices, extended(): lax.ppermute(head, axis, [((i + 1) % count, i) for i in range(ends)])  17 us
    ppermute x2, waiting for transfers between devices, extended(): lax.ppermute(tail, axis, [(i, (i + 1) % count) for i in range(ends)])  13.3 us
    ppermute x2, starting transfers between devices, extended(): lax.ppermute(head, axis, [((i + 1) % count, i) for i in range(ends)])  9.19 us
    pallas_call x1, Pallas kernels, project(): pl.pallas_call(project_kernel, grid=(nk // tk,), in_specs=[pl.BlockSpec((...  9.18 us
    pallas_call x1, Pallas kernels, residual(): pl.pallas_call(residual_kernel, grid=(nr // block_rows,), in_specs=[pl.Bl...  8.99 us
    add x2, other arithmetic, stencil(): result = -profile * first_x + viscosity * laplace  5.77 us
    unnamed x9, local copies, waits for them, and re-layouts  3.81 us
  transfers between devices with their start and end apart: 20, of which 19 were waited for; matrix products, arithmetic and copies ran while one was open for 4% of the time, Pallas kernels for 0%

profile of v5, /device:TPU:0, one launch (start us, length us, event | category | flops | bytes accessed | tf_op | source)
XLA Modules:
  0.0 137.8 jit_solution(5232949512882015252)
XLA Ops:
  0.6 8.8 %collective-permute-start = (f32[4,2,64,256]{3,2,1,0:T(8,128)}, f32[4,2,64,256]{3,2,1,0:T(8,128)S(1)}, u32[]{:S(2)}, u32[]{:S(2)}) collective-permute-start(f32[4,2,64,256]{3,2,1,0:T(8,128)} %param.5), channel_id=1, source_target_pairs={{1,0},{2,1},{3,2},{4,3},{5,4},{6,5},{7,6},{8,7},{9,8},{10,9},{11,1... | collective-permute-start | bytes 1572872 | tf_op jit(solution)/shard_map/ppermute | solution.py:32
  9.5 0.0 collective-permute-start.1
  9.5 0.9 slice_select_fusion.1
  10.4 0.1 collective-permute-start.2
  10.5 1.2 fusion.53
  11.6 0.7 negate_multiply_fusion
  12.4 0.7 dynamic_slice.7
  13.1 0.0 collective-permute-done.2
  13.1 7.8 %collective-permute-done = f32[4,2,64,256]{3,2,1,0:T(8,128)S(1)} collective-permute-done((f32[4,2,64,256]{3,2,1,0:T(8,128)}, f32[4,2,64,256]{3,2,1,0:T(8,128)S(1)}, u32[]{:S(2)}, u32[]{:S(2)}) %collective-permute-start) | collective-permute-done | bytes 524320 | tf_op jit(solution)/shard_map/ppermute | solution.py:32
  21.0 7.5 %collective-permute-done.1 = f32[4,2,64,256]{3,2,1,0:T(8,128)S(1)} collective-permute-done((f32[4,2,64,256]{3,2,1,0:T(8,128)}, f32[4,2,64,256]{3,2,1,0:T(8,128)S(1)}, u32[]{:S(2)}, u32[]{:S(2)}) %collective-permute-start.1) | collective-permute-done | bytes 524320 | tf_op jit(solution)/shard_map/ppermute | solution.py:30
  28.5 4.9 %fusion.19 = f32[4,2,64,256]{3,2,1,0:T(8,128)S(1)} fusion(f32[4,2,2,256]{3,2,1,0:T(2,128)S(1)} %get-tuple-element.25, f32[4,2,64,256]{3,2,1,0:T(8,128)} %param.5, f32[4,2,2,256]{3,2,1,0:T(2,128)S(1)} %get-tuple-element.24, f32[4,2,64,2]{3,2,1,0:T(8,128)S(1)} %get-tuple-element.21, f32[4,2,64,2]{3,2,1,0:T(8,128)S(1)} %get-tuple-element.20, ...), kind=kLoop, calls=%fused_computation.37 | loop fusion | flops 5505024 | bytes 2138368 | tf_op jit(solution)/shard_map/add | solution.py:201
  33.4 1.0 slice_subtract_fusion
  34.4 1.1 multiply_add_fusion
  35.5 0.4 collective-permute-start.3
  35.9 1.7 %collective-permute-start.4 = (f32[4,2,64,256]{3,2,1,0:T(8,128)S(1)}, f32[4,2,64,256]{3,2,1,0:T(8,128)S(1)}, u32[]{:S(2)}, u32[]{:S(2)}) collective-permute-start(f32[4,2,64,256]{3,2,1,0:T(8,128)S(1)} %multiply_add_fusion), channel_id=1, source_target_pairs={{0,1},{1,2},{2,3},{3,4},{4,5},{5,6},{6,7},{7,8},{8,9},{9,10},{10,1... | collective-permute-start | bytes 1572872 | tf_op jit(solution)/shard_map/ppermute | solution.py:30
  37.6 0.1 collective-permute-start.5
  37.7 0.1 fusion.52
  37.8 1.0 collective-permute-done.5
  38.9 9.2 %collective-permute-done.3 = f32[4,2,64,256]{3,2,1,0:T(8,128)S(1)} collective-permute-done((f32[4,2,64,256]{3,2,1,0:T(8,128)S(1)}, f32[4,2,64,256]{3,2,1,0:T(8,128)S(1)}, u32[]{:S(2)}, u32[]{:S(2)}) %collective-permute-start.3) | collective-permute-done | bytes 524320 | tf_op jit(solution)/shard_map/ppermute | solution.py:32
  48.0 5.8 %collective-permute-done.4 = f32[4,2,64,256]{3,2,1,0:T(8,128)S(1)} collective-permute-done((f32[4,2,64,256]{3,2,1,0:T(8,128)S(1)}, f32[4,2,64,256]{3,2,1,0:T(8,128)S(1)}, u32[]{:S(2)}, u32[]{:S(2)}) %collective-permute-start.4) | collective-permute-done | bytes 524320 | tf_op jit(solution)/shard_map/ppermute | solution.py:30
  53.8 0.9 fusion.7
  54.7 0.1 fusion.47
  54.8 1.2 fusion.46
  56.0 0.0 copy-start.1
  56.0 0.1 pad_maximum_fusion
  56.1 0.0 copy-start
  56.1 1.0 bitcast_convert_fusion.s_ref
  57.1 9.2 %shard_map.84 = f32[256,128]{1,0:T(8,128)} custom-call(bf16[256,128,256]{2,1,0:T(8,128)(2,1)} %bitcast.30, bf16[8,128,256]{2,1,0:T(8,128)(2,1)} %bitcast_convert_fusion.s_ref), custom_call_target="tpu_custom_call" | custom-call | flops 2147483648 | bytes 17432576 | tf_op jit(solution)/shard_map/pallas_call | solution.py:91
  66.3 1.0 copy.15
  67.3 0.1 collective-permute-start.6
  67.4 1.2 collective-permute-done.6
  68.6 0.0 collective-permute-start.7
  68.6 3.6 %collective-permute-done.7 = f32[256,8]{0,1:T(8,128)S(1)} collective-permute-done((f32[256,8]{0,1:T(8,128)S(1)}, f32[256,8]{0,1:T(8,128)S(1)}, u32[]{:S(2)}, u32[]{:S(2)}) %collective-permute-start.7) | collective-permute-done | bytes 8224 | tf_op jit(solution)/shard_map/ppermute | solution.py:69
  72.3 4.9 %collective-permute-done.8 = f32[256,8]{0,1:T(8,128)S(1)} collective-permute-done((f32[256,8]{0,1:T(8,128)S(1)}, f32[256,8]{0,1:T(8,128)S(1)}, u32[]{:S(2)}, u32[]{:S(2)}) %collective-permute-start.8) | collective-permute-done | bytes 8224 | tf_op jit(solution)/shard_map/ppermute | solution.py:69
  77.1 0.0 collective-permute-start.9
  77.1 3.6 %collective-permute-done.9 = f32[256,8]{0,1:T(8,128)S(1)} collective-permute-done((f32[256,8]{0,1:T(8,128)S(1)}, f32[256,8]{0,1:T(8,128)S(1)}, u32[]{:S(2)}, u32[]{:S(2)}) %collective-permute-start.9) | collective-permute-done | bytes 8224 | tf_op jit(solution)/shard_map/ppermute | solution.py:69
  80.8 0.0 collective-permute-start.10
  80.8 4.9 %collective-permute-done.10 = f32[256,8]{0,1:T(8,128)S(1)} collective-permute-done((f32[256,8]{0,1:T(8,128)S(1)}, f32[256,8]{0,1:T(8,128)S(1)}, u32[]{:S(2)}, u32[]{:S(2)}) %collective-permute-start.10) | collective-permute-done | bytes 8224 | tf_op jit(solution)/shard_map/ppermute | solution.py:69
  85.7 3.6 %collective-permute-done.11 = f32[256,8]{0,1:T(8,128)S(1)} collective-permute-done((f32[256,8]{0,1:T(8,128)S(1)}, f32[256,8]{0,1:T(8,128)S(1)}, u32[]{:S(2)}, u32[]{:S(2)}) %collective-permute-start.11) | collective-permute-done | bytes 8224 | tf_op jit(solution)/shard_map/ppermute | solution.py:69
  89.3 4.8 %collective-permute-done.12 = f32[256,8]{0,1:T(8,128)S(1)} collective-permute-done((f32[256,8]{0,1:T(8,128)S(1)}, f32[256,8]{0,1:T(8,128)S(1)}, u32[]{:S(2)}, u32[]{:S(2)}) %collective-permute-start.12) | collective-permute-done | bytes 8224 | tf_op jit(solution)/shard_map/ppermute | solution.py:69
  94.2 0.6 convert_bitcast_fusion
  94.8 9.0 %shard_map.85 = (f32[8,128,256]{2,1,0:T(8,128)}, f32[36,256]{1,0:T(8,128)}) custom-call(bf16[8,256]{1,0:T(8,128)(2,1)} %get-tuple-element.16.c_ref, bf16[256,128,256]{2,1,0:T(8,128)(2,1)} %bitcast.31, f32[8,128,256]{2,1,0:T(8,128)} %bitcast.32), custom_call_target="tpu_custom_call" | custom-call | flops 2147483648 | bytes 18874368 | tf_op jit(solution)/shard_map/pallas_call | solution.py:144
  103.8 0.9 reduce_sum.19
  104.7 0.8 gather_fusion
  105.4 0.1 reshape.42
  105.5 0.1 copy.17
  105.6 1.2 collective-permute-done.13
  106.8 3.6 %collective-permute-done.14 = f32[8,8]{0,1:T(8,128)S(1)} collective-permute-done((f32[8,8]{0,1:T(8,128)S(1)}, f32[8,8]{0,1:T(8,128)S(1)}, u32[]{:S(2)}, u32[]{:S(2)}) %collective-permute-start.14) | collective-permute-done | bytes 288 | tf_op jit(solution)/shard_map/ppermute | solution.py:69
  110.4 4.8 %collective-permute-done.15 = f32[8,8]{0,1:T(8,128)S(1)} collective-permute-done((f32[8,8]{0,1:T(8,128)S(1)}, f32[8,8]{0,1:T(8,128)S(1)}, u32[]{:S(2)}, u32[]{:S(2)}) %collective-permute-start.15) | collective-permute-done | bytes 288 | tf_op jit(solution)/shard_map/ppermute | solution.py:69
  115.2 3.6 %collective-permute-done.16 = f32[8,8]{0,1:T(8,128)S(1)} collective-permute-done((f32[8,8]{0,1:T(8,128)S(1)}, f32[8,8]{0,1:T(8,128)S(1)}, u32[]{:S(2)}, u32[]{:S(2)}) %collective-permute-start.16) | collective-permute-done | bytes 288 | tf_op jit(solution)/shard_map/ppermute | solution.py:69
  118.8 4.8 %collective-permute-done.17 = f32[8,8]{0,1:T(8,128)S(1)} collective-permute-done((f32[8,8]{0,1:T(8,128)S(1)}, f32[8,8]{0,1:T(8,128)S(1)}, u32[]{:S(2)}, u32[]{:S(2)}) %collective-permute-start.17) | collective-permute-done | bytes 288 | tf_op jit(solution)/shard_map/ppermute | solution.py:69
  123.6 0.0 collective-permute-start.18
  123.6 3.6 %collective-permute-done.18 = f32[8,8]{0,1:T(8,128)S(1)} collective-permute-done((f32[8,8]{0,1:T(8,128)S(1)}, f32[8,8]{0,1:T(8,128)S(1)}, u32[]{:S(2)}, u32[]{:S(2)}) %collective-permute-start.18) | collective-permute-done | bytes 288 | tf_op jit(solution)/shard_map/ppermute | solution.py:69
  127.2 0.0 collective-permute-start.19
  127.3 1.8 %copy.23 = f32[1,8,128,256]{3,1,2,0:T(8,128)S(1)} copy(f32[1,8,128,256]{3,2,1,0:T(8,128)} %bitcast.34) | data formatting | bytes 2097152
  129.1 3.0 %collective-permute-done.19 = f32[8,8]{0,1:T(8,128)S(1)} collective-permute-done((f32[8,8]{0,1:T(8,128)S(1)}, f32[8,8]{0,1:T(8,128)S(1)}, u32[]{:S(2)}, u32[]{:S(2)}) %collective-permute-start.19) | collective-permute-done | bytes 288 | tf_op jit(solution)/shard_map/ppermute | solution.py:69
  132.1 0.1 copy.18
  132.2 0.7 cholesky.18
  132.9 0.6 compare_reduce_fusion
  133.5 0.6 select_bitcast_fusion
  134.2 0.6 custom-call.7
  134.8 1.0 fusion.48
  135.9 1.3 copy.21
  137.2 0.7 copy.20
  (34 shorter events, 0.3 us)
Async XLA Ops:
  0.6 20.3 %collective-permute-start = (f32[4,2,64,256]{3,2,1,0:T(8,128)}, f32[4,2,64,256]{3,2,1,0:T(8,128)S(1)}, u32[]{:S(2)}, u32[]{:S(2)}) collective-permute-start(f32[4,2,64,256]{3,2,1,0:T(8,128)} %param.5), channel_id=1, source_target_pairs={{1,0},{2,1},{3,2},{4,3},{5,4},{6,5},{7,6},{8,7},{9,8},{10,9},{11,1... | collective-permute-start | bytes 1572872 | tf_op jit(solution)/shard_map/ppermute | solution.py:32
  9.5 19.0 %collective-permute-start.1 = (f32[4,2,64,256]{3,2,1,0:T(8,128)}, f32[4,2,64,256]{3,2,1,0:T(8,128)S(1)}, u32[]{:S(2)}, u32[]{:S(2)}) collective-permute-start(f32[4,2,64,256]{3,2,1,0:T(8,128)} %param.5), channel_id=1, source_target_pairs={{0,1},{1,2},{2,3},{3,4},{4,5},{5,6},{6,7},{7,8},{8,9},{9,10},{10,1... | collective-permute-start | bytes 1572872 | tf_op jit(solution)/shard_map/ppermute | solution.py:30
  10.4 2.7 %collective-permute-start.2 = (f32[4,2,2,256]{3,2,1,0:T(2,128)S(1)}, f32[4,2,2,256]{3,2,1,0:T(2,128)S(1)}, u32[]{:S(2)}, u32[]{:S(2)}) collective-permute-start(f32[4,2,2,256]{3,2,1,0:T(2,128)S(1)} %slice_select_fusion.1), channel_id=1, source_target_pairs={{0,64},{64,0},{1,65},{65,1},{2,66},{66,2},{3,67},{67,3},{4,68},{68... | collective-permute-start | bytes 49160 | tf_op jit(solution)/shard_map/ppermute | solution.py:22
  28.5 60.8 %copy-start.2 = (s32[64]{0:T(128)S(1)}, s32[64]{0:T(128)}, u32[]{:S(2)}) copy-start(s32[64]{0:T(128)} %constant.96) | copy-start | bytes 772
  35.5 12.5 %collective-permute-start.3 = (f32[4,2,64,256]{3,2,1,0:T(8,128)S(1)}, f32[4,2,64,256]{3,2,1,0:T(8,128)S(1)}, u32[]{:S(2)}, u32[]{:S(2)}) collective-permute-start(f32[4,2,64,256]{3,2,1,0:T(8,128)S(1)} %multiply_add_fusion), channel_id=1, source_target_pairs={{1,0},{2,1},{3,2},{4,3},{5,4},{6,5},{7,6},{8,7},{9,8},{10,9},{11,1... | collective-permute-start | bytes 1572872 | tf_op jit(solution)/shard_map/ppermute | solution.py:32
  35.9 17.9 %collective-permute-start.4 = (f32[4,2,64,256]{3,2,1,0:T(8,128)S(1)}, f32[4,2,64,256]{3,2,1,0:T(8,128)S(1)}, u32[]{:S(2)}, u32[]{:S(2)}) collective-permute-start(f32[4,2,64,256]{3,2,1,0:T(8,128)S(1)} %multiply_add_fusion), channel_id=1, source_target_pairs={{0,1},{1,2},{2,3},{3,4},{4,5},{5,6},{6,7},{7,8},{8,9},{9,10},{10,1... | collective-permute-start | bytes 1572872 | tf_op jit(solution)/shard_map/ppermute | solution.py:30
  37.6 1.3 collective-permute-start.5
  56.0 47.7 %copy-start.1 = (f32[4,2,64,256]{3,2,1,0:T(8,128)}, f32[4,2,64,256]{3,2,1,0:T(8,128)S(1)}, u32[]{:S(2)}) copy-start(f32[4,2,64,256]{3,2,1,0:T(8,128)S(1)} %fusion.46) | copy-start | bytes 1572868
  56.1 38.7 %copy-start = (f32[8,2,64,256]{3,2,1,0:T(8,128)}, f32[8,2,64,256]{3,2,1,0:T(8,128)S(1)}, u32[]{:S(2)}) copy-start(f32[8,2,64,256]{3,2,1,0:T(8,128)S(1)} %pad_maximum_fusion) | copy-start | bytes 3145732
  67.3 1.3 collective-permute-start.6
  68.6 3.7 %collective-permute-start.7 = (f32[256,8]{0,1:T(8,128)S(1)}, f32[256,8]{0,1:T(8,128)S(1)}, u32[]{:S(2)}, u32[]{:S(2)}) collective-permute-start(f32[256,8]{0,1:T(8,128)S(1)} %add.161), channel_id=1, source_target_pairs={{0,1},{1,0},{2,3},{3,2},{4,5},{5,4},{6,7},{7,6},{8,9},{9,8},{10,11... | collective-permute-start | bytes 24584 | tf_op jit(solution)/shard_map/ppermute | solution.py:69
  72.3 4.9 %collective-permute-start.8 = (f32[256,8]{0,1:T(8,128)S(1)}, f32[256,8]{0,1:T(8,128)S(1)}, u32[]{:S(2)}, u32[]{:S(2)}) collective-permute-start(f32[256,8]{0,1:T(8,128)S(1)} %add.162), channel_id=1, source_target_pairs={{0,3},{1,2},{2,1},{3,0},{4,7},{5,6},{6,5},{7,4},{8,11},{9,10},{10,... | collective-permute-start | bytes 24584 | tf_op jit(solution)/shard_map/ppermute | solution.py:69
  77.1 3.7 %collective-permute-start.9 = (f32[256,8]{0,1:T(8,128)S(1)}, f32[256,8]{0,1:T(8,128)S(1)}, u32[]{:S(2)}, u32[]{:S(2)}) collective-permute-start(f32[256,8]{0,1:T(8,128)S(1)} %add.163), channel_id=1, source_target_pairs={{0,4},{1,5},{2,6},{3,7},{4,0},{5,1},{6,2},{7,3},{8,12},{9,13},{10,... | collective-permute-start | bytes 24584 | tf_op jit(solution)/shard_map/ppermute | solution.py:69
  80.8 4.9 %collective-permute-start.10 = (f32[256,8]{0,1:T(8,128)S(1)}, f32[256,8]{0,1:T(8,128)S(1)}, u32[]{:S(2)}, u32[]{:S(2)}) collective-permute-start(f32[256,8]{0,1:T(8,128)S(1)} %add.164), channel_id=1, source_target_pairs={{0,12},{1,13},{2,14},{3,15},{4,8},{5,9},{6,10},{7,11},{8,4},{9,5},... | collective-permute-start | bytes 24584 | tf_op jit(solution)/shard_map/ppermute | solution.py:69
  85.6 3.7 %collective-permute-start.11 = (f32[256,8]{0,1:T(8,128)S(1)}, f32[256,8]{0,1:T(8,128)S(1)}, u32[]{:S(2)}, u32[]{:S(2)}) collective-permute-start(f32[256,8]{0,1:T(8,128)S(1)} %add.165), channel_id=1, source_target_pairs={{0,16},{1,17},{2,18},{3,19},{4,20},{5,21},{6,22},{7,23},{8,24},{9,... | collective-permute-start | bytes 24584 | tf_op jit(solution)/shard_map/ppermute | solution.py:69
  89.3 4.9 %collective-permute-start.12 = (f32[256,8]{0,1:T(8,128)S(1)}, f32[256,8]{0,1:T(8,128)S(1)}, u32[]{:S(2)}, u32[]{:S(2)}) collective-permute-start(f32[256,8]{0,1:T(8,128)S(1)} %add.166), channel_id=1, source_target_pairs={{0,48},{1,49},{2,50},{3,51},{4,52},{5,53},{6,54},{7,55},{8,56},{9,... | collective-permute-start | bytes 24584 | tf_op jit(solution)/shard_map/ppermute | solution.py:69
  105.6 1.2 collective-permute-start.13
  106.8 3.6 %collective-permute-start.14 = (f32[8,8]{0,1:T(8,128)S(1)}, f32[8,8]{0,1:T(8,128)S(1)}, u32[]{:S(2)}, u32[]{:S(2)}) collective-permute-start(f32[8,8]{0,1:T(8,128)S(1)} %add.170), channel_id=1, source_target_pairs={{0,1},{1,0},{2,3},{3,2},{4,5},{5,4},{6,7},{7,6},{8,9},{9,8},{10,11... | collective-permute-start | bytes 776 | tf_op jit(solution)/shard_map/ppermute | solution.py:69
  110.4 4.8 %collective-permute-start.15 = (f32[8,8]{0,1:T(8,128)S(1)}, f32[8,8]{0,1:T(8,128)S(1)}, u32[]{:S(2)}, u32[]{:S(2)}) collective-permute-start(f32[8,8]{0,1:T(8,128)S(1)} %add.171), channel_id=1, source_target_pairs={{0,3},{1,2},{2,1},{3,0},{4,7},{5,6},{6,5},{7,4},{8,11},{9,10},{10,... | collective-permute-start | bytes 776 | tf_op jit(solution)/shard_map/ppermute | solution.py:69
  115.2 3.6 %collective-permute-start.16 = (f32[8,8]{0,1:T(8,128)S(1)}, f32[8,8]{0,1:T(8,128)S(1)}, u32[]{:S(2)}, u32[]{:S(2)}) collective-permute-start(f32[8,8]{0,1:T(8,128)S(1)} %add.172), channel_id=1, source_target_pairs={{0,4},{1,5},{2,6},{3,7},{4,0},{5,1},{6,2},{7,3},{8,12},{9,13},{10,... | collective-permute-start | bytes 776 | tf_op jit(solution)/shard_map/ppermute | solution.py:69
  118.8 4.8 %collective-permute-start.17 = (f32[8,8]{0,1:T(8,128)S(1)}, f32[8,8]{0,1:T(8,128)S(1)}, u32[]{:S(2)}, u32[]{:S(2)}) collective-permute-start(f32[8,8]{0,1:T(8,128)S(1)} %add.173), channel_id=1, source_target_pairs={{0,12},{1,13},{2,14},{3,15},{4,8},{5,9},{6,10},{7,11},{8,4},{9,5},... | collective-permute-start | bytes 776 | tf_op jit(solution)/shard_map/ppermute | solution.py:69
  123.6 3.6 %collective-permute-start.18 = (f32[8,8]{0,1:T(8,128)S(1)}, f32[8,8]{0,1:T(8,128)S(1)}, u32[]{:S(2)}, u32[]{:S(2)}) collective-permute-start(f32[8,8]{0,1:T(8,128)S(1)} %add.174), channel_id=1, source_target_pairs={{0,16},{1,17},{2,18},{3,19},{4,20},{5,21},{6,22},{7,23},{8,24},{9,... | collective-permute-start | bytes 776 | tf_op jit(solution)/shard_map/ppermute | solution.py:69
  127.2 4.8 %collective-permute-start.19 = (f32[8,8]{0,1:T(8,128)S(1)}, f32[8,8]{0,1:T(8,128)S(1)}, u32[]{:S(2)}, u32[]{:S(2)}) collective-permute-start(f32[8,8]{0,1:T(8,128)S(1)} %add.175), channel_id=1, source_target_pairs={{0,48},{1,49},{2,50},{3,51},{4,52},{5,53},{6,54},{7,55},{8,56},{9,... | collective-permute-start | bytes 776 | tf_op jit(solution)/shard_map/ppermute | solution.py:69

commit v6 on v5

--- a/solution.py
+++ b/solution.py
@@ -228,7 +228,8 @@
     residual3, local_gram = residual(coeffs_bf, basis3, snaps3)
     total_gram = allreduce(local_gram, ("role", "slab"))
     lower_factor = jnp.linalg.cholesky(total_gram)
-    directions = jax.scipy.linalg.solve_triangular(lower_factor, residual3.reshape(ns, -1), lower=True)
+    inverse_factor = jax.scipy.linalg.solve_triangular(lower_factor, jnp.eye(ns, dtype=jnp.float32), lower=True)
+    directions = jnp.sum(inverse_factor[:, :, None, None] * residual3[None], axis=1)
     return (advanced, coeffs, lower_factor.T, directions.reshape(snapshots.shape))
 
 

time: 138 us -> 138 us (level)
  local copies, waits for them, and re-layouts: 7.88 us -> 4.78 us
  waiting for transfers between devices: 82.5 us -> 84.4 us
  other arithmetic: 16.2 us -> 18.1 us
    unnamed x9, local copies, waits for them, and re-layouts: 3.81 us -> 0.7 us
    reduce_sum x0 -> x1, other arithmetic: none -> 2.96 us  [on_device(): jnp.sum(inverse_factor[:, :, None, None] * residual3[None], axis=1)]
    ppermute x14, waiting for transfers between devices: 51.2 us -> 53.1 us  [allreduce(): value = value + lax.ppermute(value, name, pairs)]
  transfers between devices with their start and end apart: 20 -> 20, of which waited for: 19 -> 19; matrix products, arithmetic and copies ran while one was open for 4% -> 3% of each run, Pallas kernels for 0% -> 0%
where the time goes in v6:
time: 138 us
  waiting for transfers between devices  84.4 us (61%)
  Pallas kernels  18.2 us (13%)
  other arithmetic  18.1 us (13%)
  starting transfers between devices  11.2 us (8%)
  local copies, waits for them, and re-layouts  4.78 us (3%)
    ppermute x14, waiting for transfers between devices, allreduce(): value = value + lax.ppermute(value, name, pairs)  53.1 us
    ppermute x2, waiting for transfers between devices, extended(): lax.ppermute(head, axis, [((i + 1) % count, i) for i in range(ends)])  17 us
    ppermute x2, waiting for transfers between devices, extended(): lax.ppermute(tail, axis, [(i, (i + 1) % count) for i in range(ends)])  13.3 us
    ppermute x2, starting transfers between devices, extended(): lax.ppermute(head, axis, [((i + 1) % count, i) for i in range(ends)])  9.19 us
    pallas_call x1, Pallas kernels, project(): pl.pallas_call(project_kernel, grid=(nk // tk,), in_specs=[pl.BlockSpec((...  9.18 us
    pallas_call x1, Pallas kernels, residual(): pl.pallas_call(residual_kernel, grid=(nr // block_rows,), in_specs=[pl.Bl...  8.98 us
    add x2, other arithmetic, stencil(): result = -profile * first_x + viscosity * laplace  5.77 us
    reduce_sum x1, other arithmetic, on_device(): jnp.sum(inverse_factor[:, :, None, None] * residual3[None], axis=1)  2.96 us
  transfers between devices with their start and end apart: 20, of which 19 were waited for; matrix products, arithmetic and copies ran while one was open for 3% of the time, Pallas kernels for 0%

profile of v6, /device:TPU:0, one launch (start us, length us, event | category | flops | bytes accessed | tf_op | source)
XLA Modules:
  0.0 137.6 jit_solution(6727990470600670244)
XLA Ops:
  0.6 0.0 copy-start
  0.6 8.8 %collective-permute-start = (f32[4,2,64,256]{3,2,1,0:T(8,128)}, f32[4,2,64,256]{3,2,1,0:T(8,128)S(1)}, u32[]{:S(2)}, u32[]{:S(2)}) collective-permute-start(f32[4,2,64,256]{3,2,1,0:T(8,128)} %param.5), channel_id=1, source_target_pairs={{1,0},{2,1},{3,2},{4,3},{5,4},{6,5},{7,6},{8,7},{9,8},{10,9},{11,1... | collective-permute-start | bytes 1572872 | tf_op jit(solution)/shard_map/ppermute | solution.py:32
  9.5 0.9 slice_select_fusion.1
  10.4 0.1 collective-permute-start.2
  10.5 1.2 fusion.53
  11.7 0.7 negate_multiply_fusion
  12.4 0.7 dynamic_slice.7
  13.1 7.8 %collective-permute-done = f32[4,2,64,256]{3,2,1,0:T(8,128)S(1)} collective-permute-done((f32[4,2,64,256]{3,2,1,0:T(8,128)}, f32[4,2,64,256]{3,2,1,0:T(8,128)S(1)}, u32[]{:S(2)}, u32[]{:S(2)}) %collective-permute-start) | collective-permute-done | bytes 524320 | tf_op jit(solution)/shard_map/ppermute | solution.py:32
  21.0 7.5 %collective-permute-done.1 = f32[4,2,64,256]{3,2,1,0:T(8,128)S(1)} collective-permute-done((f32[4,2,64,256]{3,2,1,0:T(8,128)}, f32[4,2,64,256]{3,2,1,0:T(8,128)S(1)}, u32[]{:S(2)}, u32[]{:S(2)}) %collective-permute-start.1) | collective-permute-done | bytes 524320 | tf_op jit(solution)/shard_map/ppermute | solution.py:30
  28.5 4.9 %fusion.19 = f32[4,2,64,256]{3,2,1,0:T(8,128)S(1)} fusion(f32[4,2,2,256]{3,2,1,0:T(2,128)S(1)} %get-tuple-element.29, f32[4,2,64,256]{3,2,1,0:T(8,128)} %param.5, f32[4,2,2,256]{3,2,1,0:T(2,128)S(1)} %get-tuple-element.28, f32[4,2,64,2]{3,2,1,0:T(8,128)S(1)} %get-tuple-element.25, f32[4,2,64,2]{3,2,1,0:T(8,128)S(1)} %get-tuple-element.24, ...), kind=kLoop, calls=%fused_computation.38 | loop fusion | flops 5505024 | bytes 2138368 | tf_op jit(solution)/shard_map/add | solution.py:201
  33.4 1.0 slice_subtract_fusion
  34.4 1.1 multiply_add_fusion
  35.5 0.4 collective-permute-start.3
  35.9 1.7 %collective-permute-start.4 = (f32[4,2,64,256]{3,2,1,0:T(8,128)S(1)}, f32[4,2,64,256]{3,2,1,0:T(8,128)S(1)}, u32[]{:S(2)}, u32[]{:S(2)}) collective-permute-start(f32[4,2,64,256]{3,2,1,0:T(8,128)S(1)} %multiply_add_fusion), channel_id=1, source_target_pairs={{0,1},{1,2},{2,3},{3,4},{4,5},{5,6},{6,7},{7,8},{8,9},{9,10},{10,1... | collective-permute-start | bytes 1572872 | tf_op jit(solution)/shard_map/ppermute | solution.py:30
  37.6 0.1 collective-permute-start.5
  37.7 0.1 fusion.52
  37.9 1.0 collective-permute-done.5
  38.9 9.2 %collective-permute-done.3 = f32[4,2,64,256]{3,2,1,0:T(8,128)S(1)} collective-permute-done((f32[4,2,64,256]{3,2,1,0:T(8,128)S(1)}, f32[4,2,64,256]{3,2,1,0:T(8,128)S(1)}, u32[]{:S(2)}, u32[]{:S(2)}) %collective-permute-start.3) | collective-permute-done | bytes 524320 | tf_op jit(solution)/shard_map/ppermute | solution.py:32
  48.1 5.8 %collective-permute-done.4 = f32[4,2,64,256]{3,2,1,0:T(8,128)S(1)} collective-permute-done((f32[4,2,64,256]{3,2,1,0:T(8,128)S(1)}, f32[4,2,64,256]{3,2,1,0:T(8,128)S(1)}, u32[]{:S(2)}, u32[]{:S(2)}) %collective-permute-start.4) | collective-permute-done | bytes 524320 | tf_op jit(solution)/shard_map/ppermute | solution.py:30
  53.8 0.9 fusion.7
  54.7 0.1 fusion.47
  54.8 0.1 fusion.46
  55.0 0.0 copy-start.2
  55.0 0.1 pad_maximum_fusion
  55.1 0.0 copy-start.1
  55.1 1.0 bitcast_convert_fusion.s_ref
  56.1 9.2 %shard_map.84 = f32[256,128]{1,0:T(8,128)} custom-call(bf16[256,128,256]{2,1,0:T(8,128)(2,1)} %bitcast.20, bf16[8,128,256]{2,1,0:T(8,128)(2,1)} %bitcast_convert_fusion.s_ref), custom_call_target="tpu_custom_call" | custom-call | flops 2147483648 | bytes 17432576 | tf_op jit(solution)/shard_map/pallas_call | solution.py:91
  65.3 1.0 copy.20
  66.3 0.1 collective-permute-start.6
  66.4 1.2 collective-permute-done.6
  67.6 3.6 %collective-permute-done.7 = f32[256,8]{0,1:T(8,128)S(1)} collective-permute-done((f32[256,8]{0,1:T(8,128)S(1)}, f32[256,8]{0,1:T(8,128)S(1)}, u32[]{:S(2)}, u32[]{:S(2)}) %collective-permute-start.7) | collective-permute-done | bytes 8224 | tf_op jit(solution)/shard_map/ppermute | solution.py:69
  71.2 0.0 collective-permute-start.8
  71.2 4.9 %collective-permute-done.8 = f32[256,8]{0,1:T(8,128)S(1)} collective-permute-done((f32[256,8]{0,1:T(8,128)S(1)}, f32[256,8]{0,1:T(8,128)S(1)}, u32[]{:S(2)}, u32[]{:S(2)}) %collective-permute-start.8) | collective-permute-done | bytes 8224 | tf_op jit(solution)/shard_map/ppermute | solution.py:69
  76.1 0.0 collective-permute-start.9
  76.1 3.6 %collective-permute-done.9 = f32[256,8]{0,1:T(8,128)S(1)} collective-permute-done((f32[256,8]{0,1:T(8,128)S(1)}, f32[256,8]{0,1:T(8,128)S(1)}, u32[]{:S(2)}, u32[]{:S(2)}) %collective-permute-start.9) | collective-permute-done | bytes 8224 | tf_op jit(solution)/shard_map/ppermute | solution.py:69
  79.8 4.9 %collective-permute-done.10 = f32[256,8]{0,1:T(8,128)S(1)} collective-permute-done((f32[256,8]{0,1:T(8,128)S(1)}, f32[256,8]{0,1:T(8,128)S(1)}, u32[]{:S(2)}, u32[]{:S(2)}) %collective-permute-start.10) | collective-permute-done | bytes 8224 | tf_op jit(solution)/shard_map/ppermute | solution.py:69
  84.6 0.0 collective-permute-start.11
  84.6 3.6 %collective-permute-done.11 = f32[256,8]{0,1:T(8,128)S(1)} collective-permute-done((f32[256,8]{0,1:T(8,128)S(1)}, f32[256,8]{0,1:T(8,128)S(1)}, u32[]{:S(2)}, u32[]{:S(2)}) %collective-permute-start.11) | collective-permute-done | bytes 8224 | tf_op jit(solution)/shard_map/ppermute | solution.py:69
  88.3 0.0 collective-permute-start.12
  88.3 4.8 %collective-permute-done.12 = f32[256,8]{0,1:T(8,128)S(1)} collective-permute-done((f32[256,8]{0,1:T(8,128)S(1)}, f32[256,8]{0,1:T(8,128)S(1)}, u32[]{:S(2)}, u32[]{:S(2)}) %collective-permute-start.12) | collective-permute-done | bytes 8224 | tf_op jit(solution)/shard_map/ppermute | solution.py:69
  93.1 0.6 convert_bitcast_fusion
  93.7 9.0 %shard_map.85 = (f32[8,128,256]{2,1,0:T(8,128)}, f32[36,256]{1,0:T(8,128)}) custom-call(bf16[8,256]{1,0:T(8,128)(2,1)} %get-tuple-element.20.c_ref, bf16[256,128,256]{2,1,0:T(8,128)(2,1)} %bitcast.21, f32[8,128,256]{2,1,0:T(8,128)} %bitcast.22), custom_call_target="tpu_custom_call" | custom-call | flops 2147483648 | bytes 18874368 | tf_op jit(solution)/shard_map/pallas_call | solution.py:144
  102.7 0.9 reduce_sum.28
  103.6 0.8 gather_fusion
  104.4 0.1 reshape.42
  104.5 0.1 copy.22
  104.6 1.2 collective-permute-done.13
  105.7 3.6 %collective-permute-done.14 = f32[8,8]{0,1:T(8,128)S(1)} collective-permute-done((f32[8,8]{0,1:T(8,128)S(1)}, f32[8,8]{0,1:T(8,128)S(1)}, u32[]{:S(2)}, u32[]{:S(2)}) %collective-permute-start.14) | collective-permute-done | bytes 288 | tf_op jit(solution)/shard_map/ppermute | solution.py:69
  109.3 0.0 collective-permute-start.15
  109.4 4.8 %collective-permute-done.15 = f32[8,8]{0,1:T(8,128)S(1)} collective-permute-done((f32[8,8]{0,1:T(8,128)S(1)}, f32[8,8]{0,1:T(8,128)S(1)}, u32[]{:S(2)}, u32[]{:S(2)}) %collective-permute-start.15) | collective-permute-done | bytes 288 | tf_op jit(solution)/shard_map/ppermute | solution.py:69
  114.2 3.6 %collective-permute-done.16 = f32[8,8]{0,1:T(8,128)S(1)} collective-permute-done((f32[8,8]{0,1:T(8,128)S(1)}, f32[8,8]{0,1:T(8,128)S(1)}, u32[]{:S(2)}, u32[]{:S(2)}) %collective-permute-start.16) | collective-permute-done | bytes 288 | tf_op jit(solution)/shard_map/ppermute | solution.py:69
  117.8 0.0 collective-permute-start.17
  117.8 4.8 %collective-permute-done.17 = f32[8,8]{0,1:T(8,128)S(1)} collective-permute-done((f32[8,8]{0,1:T(8,128)S(1)}, f32[8,8]{0,1:T(8,128)S(1)}, u32[]{:S(2)}, u32[]{:S(2)}) %collective-permute-start.17) | collective-permute-done | bytes 288 | tf_op jit(solution)/shard_map/ppermute | solution.py:69
  122.6 3.6 %collective-permute-done.18 = f32[8,8]{0,1:T(8,128)S(1)} collective-permute-done((f32[8,8]{0,1:T(8,128)S(1)}, f32[8,8]{0,1:T(8,128)S(1)}, u32[]{:S(2)}, u32[]{:S(2)}) %collective-permute-start.18) | collective-permute-done | bytes 288 | tf_op jit(solution)/shard_map/ppermute | solution.py:69
  126.2 0.0 collective-permute-start.19
  126.2 4.8 %collective-permute-done.19 = f32[8,8]{0,1:T(8,128)S(1)} collective-permute-done((f32[8,8]{0,1:T(8,128)S(1)}, f32[8,8]{0,1:T(8,128)S(1)}, u32[]{:S(2)}, u32[]{:S(2)}) %collective-permute-start.19) | collective-permute-done | bytes 288 | tf_op jit(solution)/shard_map/ppermute | solution.py:69
  131.0 0.1 copy.23
  131.1 0.7 cholesky.20
  131.9 0.6 compare_reduce_fusion
  132.5 0.6 select_bitcast_fusion
  133.2 0.6 custom-call.7
  133.8 0.2 fusion.48
  134.0 0.7 copy.25
  134.7 3.0 %multiply_reduce_fusion = f32[8,128,256]{2,1,0:T(8,128)} fusion(f32[8,128,256]{2,1,0:T(8,128)} %get-tuple-element.7, f32[8,8]{1,0:T(8,128)S(1)} %fusion.48), kind=kLoop, calls=%fused_computation.1 | loop fusion | flops 3932160 | bytes 2097408 | tf_op jit(solution)/shard_map/reduce_sum | solution.py:232
  (35 shorter events, 0.3 us)
Async XLA Ops:
  0.6 54.2 %copy-start = (f32[4,2,64,256]{3,2,1,0:T(8,128)S(1)}, f32[4,2,64,256]{3,2,1,0:T(8,128)}, u32[]{:S(2)}) copy-start(f32[4,2,64,256]{3,2,1,0:T(8,128)} %param.5) | copy-start | bytes 1572868
  0.6 20.3 %collective-permute-start = (f32[4,2,64,256]{3,2,1,0:T(8,128)}, f32[4,2,64,256]{3,2,1,0:T(8,128)S(1)}, u32[]{:S(2)}, u32[]{:S(2)}) collective-permute-start(f32[4,2,64,256]{3,2,1,0:T(8,128)} %param.5), channel_id=1, source_target_pairs={{1,0},{2,1},{3,2},{4,3},{5,4},{6,5},{7,6},{8,7},{9,8},{10,9},{11,1... | collective-permute-start | bytes 1572872 | tf_op jit(solution)/shard_map/ppermute | solution.py:32
  9.5 19.0 %collective-permute-start.1 = (f32[4,2,64,256]{3,2,1,0:T(8,128)}, f32[4,2,64,256]{3,2,1,0:T(8,128)S(1)}, u32[]{:S(2)}, u32[]{:S(2)}) collective-permute-start(f32[4,2,64,256]{3,2,1,0:T(8,128)} %param.5), channel_id=1, source_target_pairs={{0,1},{1,2},{2,3},{3,4},{4,5},{5,6},{6,7},{7,8},{8,9},{9,10},{10,1... | collective-permute-start | bytes 1572872 | tf_op jit(solution)/shard_map/ppermute | solution.py:30
  10.4 2.7 %collective-permute-start.2 = (f32[4,2,2,256]{3,2,1,0:T(2,128)S(1)}, f32[4,2,2,256]{3,2,1,0:T(2,128)S(1)}, u32[]{:S(2)}, u32[]{:S(2)}) collective-permute-start(f32[4,2,2,256]{3,2,1,0:T(2,128)S(1)} %slice_select_fusion.1), channel_id=1, source_target_pairs={{0,64},{64,0},{1,65},{65,1},{2,66},{66,2},{3,67},{67,3},{4,68},{68... | collective-permute-start | bytes 49160 | tf_op jit(solution)/shard_map/ppermute | solution.py:22
  35.5 12.5 %collective-permute-start.3 = (f32[4,2,64,256]{3,2,1,0:T(8,128)S(1)}, f32[4,2,64,256]{3,2,1,0:T(8,128)S(1)}, u32[]{:S(2)}, u32[]{:S(2)}) collective-permute-start(f32[4,2,64,256]{3,2,1,0:T(8,128)S(1)} %multiply_add_fusion), channel_id=1, source_target_pairs={{1,0},{2,1},{3,2},{4,3},{5,4},{6,5},{7,6},{8,7},{9,8},{10,9},{11,1... | collective-permute-start | bytes 1572872 | tf_op jit(solution)/shard_map/ppermute | solution.py:32
  35.9 17.9 %collective-permute-start.4 = (f32[4,2,64,256]{3,2,1,0:T(8,128)S(1)}, f32[4,2,64,256]{3,2,1,0:T(8,128)S(1)}, u32[]{:S(2)}, u32[]{:S(2)}) collective-permute-start(f32[4,2,64,256]{3,2,1,0:T(8,128)S(1)} %multiply_add_fusion), channel_id=1, source_target_pairs={{0,1},{1,2},{2,3},{3,4},{4,5},{5,6},{6,7},{7,8},{8,9},{9,10},{10,1... | collective-permute-start | bytes 1572872 | tf_op jit(solution)/shard_map/ppermute | solution.py:30
  37.6 1.3 collective-permute-start.5
  55.0 10.3 %copy-start.2 = (f32[4,2,64,256]{3,2,1,0:T(8,128)}, f32[4,2,64,256]{3,2,1,0:T(8,128)S(1)}, u32[]{:S(2)}) copy-start(f32[4,2,64,256]{3,2,1,0:T(8,128)S(1)} %fusion.46) | copy-start | bytes 1572868
  55.1 10.2 %copy-start.1 = (f32[8,2,64,256]{3,2,1,0:T(8,128)}, f32[8,2,64,256]{3,2,1,0:T(8,128)S(1)}, u32[]{:S(2)}) copy-start(f32[8,2,64,256]{3,2,1,0:T(8,128)S(1)} %pad_maximum_fusion) | copy-start | bytes 3145732
  56.1 32.2 %copy-start.3 = (s32[64]{0:T(128)S(1)}, s32[64]{0:T(128)}, u32[]{:S(2)}) copy-start(s32[64]{0:T(128)} %constant.96) | copy-start | bytes 772
  66.3 1.3 collective-permute-start.6
  67.6 3.7 %collective-permute-start.7 = (f32[256,8]{0,1:T(8,128)S(1)}, f32[256,8]{0,1:T(8,128)S(1)}, u32[]{:S(2)}, u32[]{:S(2)}) collective-permute-start(f32[256,8]{0,1:T(8,128)S(1)} %add.161), channel_id=1, source_target_pairs={{0,1},{1,0},{2,3},{3,2},{4,5},{5,4},{6,7},{7,6},{8,9},{9,8},{10,11... | collective-permute-start | bytes 24584 | tf_op jit(solution)/shard_map/ppermute | solution.py:69
  71.2 4.9 %collective-permute-start.8 = (f32[256,8]{0,1:T(8,128)S(1)}, f32[256,8]{0,1:T(8,128)S(1)}, u32[]{:S(2)}, u32[]{:S(2)}) collective-permute-start(f32[256,8]{0,1:T(8,128)S(1)} %add.162), channel_id=1, source_target_pairs={{0,3},{1,2},{2,1},{3,0},{4,7},{5,6},{6,5},{7,4},{8,11},{9,10},{10,... | collective-permute-start | bytes 24584 | tf_op jit(solution)/shard_map/ppermute | solution.py:69
  76.1 3.7 %collective-permute-start.9 = (f32[256,8]{0,1:T(8,128)S(1)}, f32[256,8]{0,1:T(8,128)S(1)}, u32[]{:S(2)}, u32[]{:S(2)}) collective-permute-start(f32[256,8]{0,1:T(8,128)S(1)} %add.163), channel_id=1, source_target_pairs={{0,4},{1,5},{2,6},{3,7},{4,0},{5,1},{6,2},{7,3},{8,12},{9,13},{10,... | collective-permute-start | bytes 24584 | tf_op jit(solution)/shard_map/ppermute | solution.py:69
  79.8 4.9 %collective-permute-start.10 = (f32[256,8]{0,1:T(8,128)S(1)}, f32[256,8]{0,1:T(8,128)S(1)}, u32[]{:S(2)}, u32[]{:S(2)}) collective-permute-start(f32[256,8]{0,1:T(8,128)S(1)} %add.164), channel_id=1, source_target_pairs={{0,12},{1,13},{2,14},{3,15},{4,8},{5,9},{6,10},{7,11},{8,4},{9,5},... | collective-permute-start | bytes 24584 | tf_op jit(solution)/shard_map/ppermute | solution.py:69
  84.6 3.7 %collective-permute-start.11 = (f32[256,8]{0,1:T(8,128)S(1)}, f32[256,8]{0,1:T(8,128)S(1)}, u32[]{:S(2)}, u32[]{:S(2)}) collective-permute-start(f32[256,8]{0,1:T(8,128)S(1)} %add.165), channel_id=1, source_target_pairs={{0,16},{1,17},{2,18},{3,19},{4,20},{5,21},{6,22},{7,23},{8,24},{9,... | collective-permute-start | bytes 24584 | tf_op jit(solution)/shard_map/ppermute | solution.py:69
  88.3 4.9 %collective-permute-start.12 = (f32[256,8]{0,1:T(8,128)S(1)}, f32[256,8]{0,1:T(8,128)S(1)}, u32[]{:S(2)}, u32[]{:S(2)}) collective-permute-start(f32[256,8]{0,1:T(8,128)S(1)} %add.166), channel_id=1, source_target_pairs={{0,48},{1,49},{2,50},{3,51},{4,52},{5,53},{6,54},{7,55},{8,56},{9,... | collective-permute-start | bytes 24584 | tf_op jit(solution)/shard_map/ppermute | solution.py:69
  104.6 1.2 collective-permute-start.13
  105.7 3.6 %collective-permute-start.14 = (f32[8,8]{0,1:T(8,128)S(1)}, f32[8,8]{0,1:T(8,128)S(1)}, u32[]{:S(2)}, u32[]{:S(2)}) collective-permute-start(f32[8,8]{0,1:T(8,128)S(1)} %add.170), channel_id=1, source_target_pairs={{0,1},{1,0},{2,3},{3,2},{4,5},{5,4},{6,7},{7,6},{8,9},{9,8},{10,11... | collective-permute-start | bytes 776 | tf_op jit(solution)/shard_map/ppermute | solution.py:69
  109.3 4.8 %collective-permute-start.15 = (f32[8,8]{0,1:T(8,128)S(1)}, f32[8,8]{0,1:T(8,128)S(1)}, u32[]{:S(2)}, u32[]{:S(2)}) collective-permute-start(f32[8,8]{0,1:T(8,128)S(1)} %add.171), channel_id=1, source_target_pairs={{0,3},{1,2},{2,1},{3,0},{4,7},{5,6},{6,5},{7,4},{8,11},{9,10},{10,... | collective-permute-start | bytes 776 | tf_op jit(solution)/shard_map/ppermute | solution.py:69
  114.2 3.6 %collective-permute-start.16 = (f32[8,8]{0,1:T(8,128)S(1)}, f32[8,8]{0,1:T(8,128)S(1)}, u32[]{:S(2)}, u32[]{:S(2)}) collective-permute-start(f32[8,8]{0,1:T(8,128)S(1)} %add.172), channel_id=1, source_target_pairs={{0,4},{1,5},{2,6},{3,7},{4,0},{5,1},{6,2},{7,3},{8,12},{9,13},{10,... | collective-permute-start | bytes 776 | tf_op jit(solution)/shard_map/ppermute | solution.py:69
  117.8 4.8 %collective-permute-start.17 = (f32[8,8]{0,1:T(8,128)S(1)}, f32[8,8]{0,1:T(8,128)S(1)}, u32[]{:S(2)}, u32[]{:S(2)}) collective-permute-start(f32[8,8]{0,1:T(8,128)S(1)} %add.173), channel_id=1, source_target_pairs={{0,12},{1,13},{2,14},{3,15},{4,8},{5,9},{6,10},{7,11},{8,4},{9,5},... | collective-permute-start | bytes 776 | tf_op jit(solution)/shard_map/ppermute | solution.py:69
  122.6 3.6 %collective-permute-start.18 = (f32[8,8]{0,1:T(8,128)S(1)}, f32[8,8]{0,1:T(8,128)S(1)}, u32[]{:S(2)}, u32[]{:S(2)}) collective-permute-start(f32[8,8]{0,1:T(8,128)S(1)} %add.174), channel_id=1, source_target_pairs={{0,16},{1,17},{2,18},{3,19},{4,20},{5,21},{6,22},{7,23},{8,24},{9,... | collective-permute-start | bytes 776 | tf_op jit(solution)/shard_map/ppermute | solution.py:69
  126.2 4.8 %collective-permute-start.19 = (f32[8,8]{0,1:T(8,128)S(1)}, f32[8,8]{0,1:T(8,128)S(1)}, u32[]{:S(2)}, u32[]{:S(2)}) collective-permute-start(f32[8,8]{0,1:T(8,128)S(1)} %add.175), channel_id=1, source_target_pairs={{0,48},{1,49},{2,50},{3,51},{4,52},{5,53},{6,54},{7,55},{8,56},{9,... | collective-permute-start | bytes 776 | tf_op jit(solution)/shard_map/ppermute | solution.py:69

commit v7 on v6

--- a/solution.py
+++ b/solution.py
@@ -181,32 +181,32 @@
     ) / 12.0
 
 
-def stencil(center, xpadded, ypadded, flow_rows, shear_rows):
-    nx_loc = center.shape[1]
+def local_terms(center, ypadded, flow_rows, shear_rows):
     ny_loc = center.shape[2]
     nz_loc = center.shape[3]
     zpadded = jnp.concatenate([center[..., -2:], center, center[..., :2]], axis=3)
+    local = viscosity * (second_diff(ypadded, center, 2, ny_loc) + second_diff(zpadded, center, 3, nz_loc))
+    shear_term = shear_rows[None, None, :, None] * center[1:2]
+    return jnp.concatenate([local[:1] - shear_term, local[1:]], axis=0)
+
+
+def streamwise_terms(center, xpadded, flow_rows):
+    nx_loc = center.shape[1]
     first_x = (
         -offset_slice(xpadded, 2, 1, nx_loc)
         + 8.0 * offset_slice(xpadded, 1, 1, nx_loc)
         - 8.0 * offset_slice(xpadded, -1, 1, nx_loc)
         + offset_slice(xpadded, -2, 1, nx_loc)
     ) / 12.0
-    laplace = (
-        second_diff(xpadded, center, 1, nx_loc)
-        + second_diff(ypadded, center, 2, ny_loc)
-        + second_diff(zpadded, center, 3, nz_loc)
-    )
     profile = flow_rows[None, None, :, None]
-    result = -profile * first_x + viscosity * laplace
-    shear_term = shear_rows[None, None, :, None] * center[1:2]
-    return jnp.concatenate([result[:1] - shear_term, result[1:]], axis=0)
+    return -profile * first_x + viscosity * second_diff(xpadded, center, 1, nx_loc)
 
 
 def segmented_tendency(center, flow_rows, shear_rows):
     xpadded = extended(center, (("slab", 1),), 2, True)
     ypadded = extended(center, (("role", 2),), 2, False)
-    return stencil(center, xpadded, ypadded, flow_rows, shear_rows)
+    local = local_terms(center, ypadded, flow_rows, shear_rows)
+    return streamwise_terms(center, xpadded, flow_rows) + local
 
 
 def on_device(velocity, basis, mean_flow, shear):

time: 138 us -> 134 us (0.971)
  waiting for transfers between devices: 84.4 us -> 79.9 us
    add x2 -> x0, other arithmetic: 5.77 us -> none  [stencil(): result = -profile * first_x + viscosity * laplace]
    mul x1 -> x3, other arithmetic: 0.74 us -> 5.96 us  [the longest x2 5.22 us: local_terms(): viscosity * (second_diff(ypadded, center, 2, ny_loc) + second_diff(zpadde...]
    ppermute x2, waiting for transfers between devices: 17 us -> 13.7 us  [extended(): lax.ppermute(head, axis, [((i + 1) % count, i) for i in range(ends)])]
  transfers between devices with their start and end apart: 20 -> 20, of which waited for: 19 -> 18; matrix products, arithmetic and copies ran while one was open for 3% -> 8% of each run, Pallas kernels for 0% -> 0%
where the time goes in v7:
time: 134 us; the launch traced here: 133 us
  waiting for transfers between devices  79.9 us (60%)
  other arithmetic  18.3 us (14%)
  Pallas kernels  18.2 us (14%)
  starting transfers between devices  11.2 us (8%)
  local copies, waits for them, and re-layouts  4.77 us (4%)
    ppermute x14, waiting for transfers between devices, allreduce(): value = value + lax.ppermute(value, name, pairs)  53.1 us
    ppermute x2, waiting for transfers between devices, extended(): lax.ppermute(head, axis, [((i + 1) % count, i) for i in range(ends)])  13.7 us
    ppermute x2, waiting for transfers between devices, extended(): lax.ppermute(tail, axis, [(i, (i + 1) % count) for i in range(ends)])  13 us
    ppermute x2, starting transfers between devices, extended(): lax.ppermute(head, axis, [((i + 1) % count, i) for i in range(ends)])  9.19 us
    pallas_call x1, Pallas kernels, project(): pl.pallas_call(project_kernel, grid=(nk // tk,), in_specs=[pl.BlockSpec((...  9.17 us
    pallas_call x1, Pallas kernels, residual(): pl.pallas_call(residual_kernel, grid=(nr // block_rows,), in_specs=[pl.Bl...  8.99 us
    mul x2, other arithmetic, local_terms(): viscosity * (second_diff(ypadded, center, 2, ny_loc) + second_diff(zpadde...  5.22 us
    reduce_sum x1, other arithmetic, on_device(): jnp.sum(inverse_factor[:, :, None, None] * residual3[None], axis=1)  2.96 us
  transfers between devices with their start and end apart: 20, of which 18 were waited for; matrix products, arithmetic and copies ran while one was open for 8% of the time, Pallas kernels for 0%

profile of v7, /device:TPU:0, one launch (start us, length us, event | category | flops | bytes accessed | tf_op | source)
XLA Modules:
  0.0 133.3 jit_solution(6070235415273290822)
XLA Ops:
  0.6 8.8 %collective-permute-start = (f32[4,2,64,256]{3,2,1,0:T(8,128)}, f32[4,2,64,256]{3,2,1,0:T(8,128)S(1)}, u32[]{:S(2)}, u32[]{:S(2)}) collective-permute-start(f32[4,2,64,256]{3,2,1,0:T(8,128)} %param.5), channel_id=1, source_target_pairs={{1,0},{2,1},{3,2},{4,3},{5,4},{6,5},{7,6},{8,7},{9,8},{10,9},{11,1... | collective-permute-start | bytes 1572872 | tf_op jit(solution)/shard_map/ppermute | solution.py:32
  9.5 0.0 collective-permute-start.1
  9.5 0.9 slice_select_fusion.1
  10.4 0.1 collective-permute-start.2
  10.5 1.2 fusion.50
  11.6 0.7 negate_multiply_fusion
  12.4 0.7 dynamic_slice.7
  13.1 0.0 collective-permute-done.2
  13.1 4.4 %fusion.15 = f32[4,2,64,256]{3,2,1,0:T(8,128)S(1)} fusion(f32[4,2,2,256]{3,2,1,0:T(2,128)S(1)} %get-tuple-element.31, f32[4,2,64,256]{3,2,1,0:T(8,128)} %param.5, f32[4,2,2,256]{3,2,1,0:T(2,128)S(1)} %get-tuple-element.30, f32[4,2,64,2]{3,2,1,0:T(8,128)S(1)} %get-tuple-element.27, f32[4,2,64,2]{3,2,1,0:T(8,128)S(1)} %get-tuple-element.26), kind=kLoop, calls=%fused_computation.34 | loop fusion | flops 3276800 | bytes 1089536 | tf_op jit(solution)/shard_map/mul | solution.py:188
  17.6 1.0 slice_subtract_fusion
  18.6 2.4 %collective-permute-done = f32[4,2,64,256]{3,2,1,0:T(8,128)S(1)} collective-permute-done((f32[4,2,64,256]{3,2,1,0:T(8,128)}, f32[4,2,64,256]{3,2,1,0:T(8,128)S(1)}, u32[]{:S(2)}, u32[]{:S(2)}) %collective-permute-start) | collective-permute-done | bytes 524320 | tf_op jit(solution)/shard_map/ppermute | solution.py:32
  21.0 7.5 %collective-permute-done.1 = f32[4,2,64,256]{3,2,1,0:T(8,128)S(1)} collective-permute-done((f32[4,2,64,256]{3,2,1,0:T(8,128)}, f32[4,2,64,256]{3,2,1,0:T(8,128)S(1)}, u32[]{:S(2)}, u32[]{:S(2)}) %collective-permute-start.1) | collective-permute-done | bytes 524320 | tf_op jit(solution)/shard_map/ppermute | solution.py:30
  28.5 1.6 %multiply_add_fusion = (f32[4,2,64,256]{3,2,1,0:T(8,128)S(1)}, f32[4,2,64,256]{3,2,1,0:T(8,128)S(1)}) fusion(f32[4,2,64,256]{3,2,1,0:T(8,128)} %param.5, f32[3,2,64,256]{3,2,1,0:T(8,128)S(1)} %slice.183, f32[1,2,64,256]{3,2,1,0:T(8,128)S(1)} %slice_subtract_fusion, f32[4,2,64,256]{3,2,1,0:T(8,128)S(1)} %collective-permute-done.1, ...), kind=kLoop, calls=%fused_computation.77 | loop fusion | flops 2883584 | bytes 3145984 | tf_op jit(solution)/shard_map/add | solution.py:218
  30.1 0.1 collective-permute-start.5
  30.2 0.1 fusion.49
  30.3 0.4 collective-permute-start.3
  30.7 1.7 %collective-permute-start.4 = (f32[4,2,64,256]{3,2,1,0:T(8,128)S(1)}, f32[4,2,64,256]{3,2,1,0:T(8,128)S(1)}, u32[]{:S(2)}, u32[]{:S(2)}) collective-permute-start(f32[4,2,64,256]{3,2,1,0:T(8,128)S(1)} %get-tuple-element.22), channel_id=1, source_target_pairs={{0,1},{1,2},{2,3},{3,4},{4,5},{5,6},{6,7},{7,8},{8,9},{9,10},{10,1... | collective-permute-start | bytes 1572872 | tf_op jit(solution)/shard_map/ppermute | solution.py:30
  32.5 0.8 fusion.5
  33.3 0.1 fusion.44
  33.4 11.3 %collective-permute-done.3 = f32[4,2,64,256]{3,2,1,0:T(8,128)S(1)} collective-permute-done((f32[4,2,64,256]{3,2,1,0:T(8,128)S(1)}, f32[4,2,64,256]{3,2,1,0:T(8,128)S(1)}, u32[]{:S(2)}, u32[]{:S(2)}) %collective-permute-start.3) | collective-permute-done | bytes 524320 | tf_op jit(solution)/shard_map/ppermute | solution.py:32
  44.7 5.5 %collective-permute-done.4 = f32[4,2,64,256]{3,2,1,0:T(8,128)S(1)} collective-permute-done((f32[4,2,64,256]{3,2,1,0:T(8,128)S(1)}, f32[4,2,64,256]{3,2,1,0:T(8,128)S(1)}, u32[]{:S(2)}, u32[]{:S(2)}) %collective-permute-start.4) | collective-permute-done | bytes 524320 | tf_op jit(solution)/shard_map/ppermute | solution.py:30
  50.3 0.4 fusion.43
  50.7 0.0 copy-start.1
  50.7 0.1 pad_maximum_fusion
  50.8 0.0 copy-start
  50.8 1.0 bitcast_convert_fusion.s_ref
  51.8 9.2 %shard_map.84 = f32[256,128]{1,0:T(8,128)} custom-call(bf16[256,128,256]{2,1,0:T(8,128)(2,1)} %bitcast.20, bf16[8,128,256]{2,1,0:T(8,128)(2,1)} %bitcast_convert_fusion.s_ref), custom_call_target="tpu_custom_call" | custom-call | flops 2147483648 | bytes 17432576 | tf_op jit(solution)/shard_map/pallas_call | solution.py:91
  60.9 1.0 copy.20
  62.0 0.1 collective-permute-start.6
  62.1 1.2 collective-permute-done.6
  63.2 3.6 %collective-permute-done.7 = f32[256,8]{0,1:T(8,128)S(1)} collective-permute-done((f32[256,8]{0,1:T(8,128)S(1)}, f32[256,8]{0,1:T(8,128)S(1)}, u32[]{:S(2)}, u32[]{:S(2)}) %collective-permute-start.7) | collective-permute-done | bytes 8224 | tf_op jit(solution)/shard_map/ppermute | solution.py:69
  66.9 0.0 collective-permute-start.8
  66.9 4.9 %collective-permute-done.8 = f32[256,8]{0,1:T(8,128)S(1)} collective-permute-done((f32[256,8]{0,1:T(8,128)S(1)}, f32[256,8]{0,1:T(8,128)S(1)}, u32[]{:S(2)}, u32[]{:S(2)}) %collective-permute-start.8) | collective-permute-done | bytes 8224 | tf_op jit(solution)/shard_map/ppermute | solution.py:69
  71.7 0.0 collective-permute-start.9
  71.7 3.6 %collective-permute-done.9 = f32[256,8]{0,1:T(8,128)S(1)} collective-permute-done((f32[256,8]{0,1:T(8,128)S(1)}, f32[256,8]{0,1:T(8,128)S(1)}, u32[]{:S(2)}, u32[]{:S(2)}) %collective-permute-start.9) | collective-permute-done | bytes 8224 | tf_op jit(solution)/shard_map/ppermute | solution.py:69
  75.4 4.9 %collective-permute-done.10 = f32[256,8]{0,1:T(8,128)S(1)} collective-permute-done((f32[256,8]{0,1:T(8,128)S(1)}, f32[256,8]{0,1:T(8,128)S(1)}, u32[]{:S(2)}, u32[]{:S(2)}) %collective-permute-start.10) | collective-permute-done | bytes 8224 | tf_op jit(solution)/shard_map/ppermute | solution.py:69
  80.3 0.0 collective-permute-start.11
  80.3 3.6 %collective-permute-done.11 = f32[256,8]{0,1:T(8,128)S(1)} collective-permute-done((f32[256,8]{0,1:T(8,128)S(1)}, f32[256,8]{0,1:T(8,128)S(1)}, u32[]{:S(2)}, u32[]{:S(2)}) %collective-permute-start.11) | collective-permute-done | bytes 8224 | tf_op jit(solution)/shard_map/ppermute | solution.py:69
  83.9 0.0 collective-permute-start.12
  83.9 4.8 %collective-permute-done.12 = f32[256,8]{0,1:T(8,128)S(1)} collective-permute-done((f32[256,8]{0,1:T(8,128)S(1)}, f32[256,8]{0,1:T(8,128)S(1)}, u32[]{:S(2)}, u32[]{:S(2)}) %collective-permute-start.12) | collective-permute-done | bytes 8224 | tf_op jit(solution)/shard_map/ppermute | solution.py:69
  88.8 0.6 convert_bitcast_fusion
  89.4 9.0 %shard_map.85 = (f32[8,128,256]{2,1,0:T(8,128)}, f32[36,256]{1,0:T(8,128)}) custom-call(bf16[8,256]{1,0:T(8,128)(2,1)} %get-tuple-element.20.c_ref, bf16[256,128,256]{2,1,0:T(8,128)(2,1)} %bitcast.21, f32[8,128,256]{2,1,0:T(8,128)} %bitcast.22), custom_call_target="tpu_custom_call" | custom-call | flops 2147483648 | bytes 18874368 | tf_op jit(solution)/shard_map/pallas_call | solution.py:144
  98.4 0.9 reduce_sum.28
  99.3 0.8 gather_fusion
  100.0 0.1 reshape.42
  100.1 0.1 copy.22
  100.2 0.0 collective-permute-start.13
  100.2 1.2 collective-permute-done.13
  101.4 0.0 collective-permute-start.14
  101.4 3.6 %collective-permute-done.14 = f32[8,8]{0,1:T(8,128)S(1)} collective-permute-done((f32[8,8]{0,1:T(8,128)S(1)}, f32[8,8]{0,1:T(8,128)S(1)}, u32[]{:S(2)}, u32[]{:S(2)}) %collective-permute-start.14) | collective-permute-done | bytes 288 | tf_op jit(solution)/shard_map/ppermute | solution.py:69
  105.0 4.8 %collective-permute-done.15 = f32[8,8]{0,1:T(8,128)S(1)} collective-permute-done((f32[8,8]{0,1:T(8,128)S(1)}, f32[8,8]{0,1:T(8,128)S(1)}, u32[]{:S(2)}, u32[]{:S(2)}) %collective-permute-start.15) | collective-permute-done | bytes 288 | tf_op jit(solution)/shard_map/ppermute | solution.py:69
  109.8 0.0 collective-permute-start.16
  109.8 3.6 %collective-permute-done.16 = f32[8,8]{0,1:T(8,128)S(1)} collective-permute-done((f32[8,8]{0,1:T(8,128)S(1)}, f32[8,8]{0,1:T(8,128)S(1)}, u32[]{:S(2)}, u32[]{:S(2)}) %collective-permute-start.16) | collective-permute-done | bytes 288 | tf_op jit(solution)/shard_map/ppermute | solution.py:69
  113.4 4.8 %collective-permute-done.17 = f32[8,8]{0,1:T(8,128)S(1)} collective-permute-done((f32[8,8]{0,1:T(8,128)S(1)}, f32[8,8]{0,1:T(8,128)S(1)}, u32[]{:S(2)}, u32[]{:S(2)}) %collective-permute-start.17) | collective-permute-done | bytes 288 | tf_op jit(solution)/shard_map/ppermute | solution.py:69
  118.2 3.6 %collective-permute-done.18 = f32[8,8]{0,1:T(8,128)S(1)} collective-permute-done((f32[8,8]{0,1:T(8,128)S(1)}, f32[8,8]{0,1:T(8,128)S(1)}, u32[]{:S(2)}, u32[]{:S(2)}) %collective-permute-start.18) | collective-permute-done | bytes 288 | tf_op jit(solution)/shard_map/ppermute | solution.py:69
  121.9 4.8 %collective-permute-done.19 = f32[8,8]{0,1:T(8,128)S(1)} collective-permute-done((f32[8,8]{0,1:T(8,128)S(1)}, f32[8,8]{0,1:T(8,128)S(1)}, u32[]{:S(2)}, u32[]{:S(2)}) %collective-permute-start.19) | collective-permute-done | bytes 288 | tf_op jit(solution)/shard_map/ppermute | solution.py:69
  126.7 0.1 copy.23
  126.8 0.7 cholesky.20
  127.5 0.6 compare_reduce_fusion
  128.2 0.6 select_bitcast_fusion
  128.8 0.6 custom-call.7
  129.4 0.2 fusion.45
  129.6 0.7 copy.25
  130.3 3.0 %multiply_reduce_fusion = f32[8,128,256]{2,1,0:T(8,128)} fusion(f32[8,128,256]{2,1,0:T(8,128)} %get-tuple-element.7, f32[8,8]{1,0:T(8,128)S(1)} %fusion.45), kind=kLoop, calls=%fused_computation.1 | loop fusion | flops 3932160 | bytes 2097408 | tf_op jit(solution)/shard_map/reduce_sum | solution.py:232
  (33 shorter events, 0.2 us)
Async XLA Ops:
  0.6 20.3 %collective-permute-start = (f32[4,2,64,256]{3,2,1,0:T(8,128)}, f32[4,2,64,256]{3,2,1,0:T(8,128)S(1)}, u32[]{:S(2)}, u32[]{:S(2)}) collective-permute-start(f32[4,2,64,256]{3,2,1,0:T(8,128)} %param.5), channel_id=1, source_target_pairs={{1,0},{2,1},{3,2},{4,3},{5,4},{6,5},{7,6},{8,7},{9,8},{10,9},{11,1... | collective-permute-start | bytes 1572872 | tf_op jit(solution)/shard_map/ppermute | solution.py:32
  9.5 19.0 %collective-permute-start.1 = (f32[4,2,64,256]{3,2,1,0:T(8,128)}, f32[4,2,64,256]{3,2,1,0:T(8,128)S(1)}, u32[]{:S(2)}, u32[]{:S(2)}) collective-permute-start(f32[4,2,64,256]{3,2,1,0:T(8,128)} %param.5), channel_id=1, source_target_pairs={{0,1},{1,2},{2,3},{3,4},{4,5},{5,6},{6,7},{7,8},{8,9},{9,10},{10,1... | collective-permute-start | bytes 1572872 | tf_op jit(solution)/shard_map/ppermute | solution.py:30
  10.4 2.7 %collective-permute-start.2 = (f32[4,2,2,256]{3,2,1,0:T(2,128)S(1)}, f32[4,2,2,256]{3,2,1,0:T(2,128)S(1)}, u32[]{:S(2)}, u32[]{:S(2)}) collective-permute-start(f32[4,2,2,256]{3,2,1,0:T(2,128)S(1)} %slice_select_fusion.1), channel_id=1, source_target_pairs={{0,64},{64,0},{1,65},{65,1},{2,66},{66,2},{3,67},{67,3},{4,68},{68... | collective-permute-start | bytes 49160 | tf_op jit(solution)/shard_map/ppermute | solution.py:22
  30.1 2.3 %collective-permute-start.5 = (f32[4,2,2,256]{3,2,1,0:T(2,128)S(1)}, f32[4,2,2,256]{3,2,1,0:T(2,128)S(1)}, u32[]{:S(2)}, u32[]{:S(2)}) collective-permute-start(f32[4,2,2,256]{3,2,1,0:T(2,128)S(1)} %slice_select_fusion), channel_id=1, source_target_pairs={{0,64},{64,0},{1,65},{65,1},{2,66},{66,2},{3,67},{67,3},{4,68},{68... | collective-permute-start | bytes 49160 | tf_op jit(solution)/shard_map/ppermute | solution.py:22
  30.3 14.4 %collective-permute-start.3 = (f32[4,2,64,256]{3,2,1,0:T(8,128)S(1)}, f32[4,2,64,256]{3,2,1,0:T(8,128)S(1)}, u32[]{:S(2)}, u32[]{:S(2)}) collective-permute-start(f32[4,2,64,256]{3,2,1,0:T(8,128)S(1)} %get-tuple-element.22), channel_id=1, source_target_pairs={{1,0},{2,1},{3,2},{4,3},{5,4},{6,5},{7,6},{8,7},{9,8},{10,9},{11,1... | collective-permute-start | bytes 1572872 | tf_op jit(solution)/shard_map/ppermute | solution.py:32
  30.7 19.6 %collective-permute-start.4 = (f32[4,2,64,256]{3,2,1,0:T(8,128)S(1)}, f32[4,2,64,256]{3,2,1,0:T(8,128)S(1)}, u32[]{:S(2)}, u32[]{:S(2)}) collective-permute-start(f32[4,2,64,256]{3,2,1,0:T(8,128)S(1)} %get-tuple-element.22), channel_id=1, source_target_pairs={{0,1},{1,2},{2,3},{3,4},{4,5},{5,6},{6,7},{7,8},{8,9},{9,10},{10,1... | collective-permute-start | bytes 1572872 | tf_op jit(solution)/shard_map/ppermute | solution.py:30
  50.7 10.3 %copy-start.1 = (f32[4,2,64,256]{3,2,1,0:T(8,128)}, f32[4,2,64,256]{3,2,1,0:T(8,128)S(1)}, u32[]{:S(2)}) copy-start(f32[4,2,64,256]{3,2,1,0:T(8,128)S(1)} %fusion.43) | copy-start | bytes 1572868
  50.8 10.2 %copy-start = (f32[8,2,64,256]{3,2,1,0:T(8,128)}, f32[8,2,64,256]{3,2,1,0:T(8,128)S(1)}, u32[]{:S(2)}) copy-start(f32[8,2,64,256]{3,2,1,0:T(8,128)S(1)} %pad_maximum_fusion) | copy-start | bytes 3145732
  51.8 32.2 %copy-start.2 = (s32[64]{0:T(128)S(1)}, s32[64]{0:T(128)}, u32[]{:S(2)}) copy-start(s32[64]{0:T(128)} %constant.99) | copy-start | bytes 772
  62.0 1.3 collective-permute-start.6
  63.2 3.7 %collective-permute-start.7 = (f32[256,8]{0,1:T(8,128)S(1)}, f32[256,8]{0,1:T(8,128)S(1)}, u32[]{:S(2)}, u32[]{:S(2)}) collective-permute-start(f32[256,8]{0,1:T(8,128)S(1)} %add.161), channel_id=1, source_target_pairs={{0,1},{1,0},{2,3},{3,2},{4,5},{5,4},{6,7},{7,6},{8,9},{9,8},{10,11... | collective-permute-start | bytes 24584 | tf_op jit(solution)/shard_map/ppermute | solution.py:69
  66.9 4.9 %collective-permute-start.8 = (f32[256,8]{0,1:T(8,128)S(1)}, f32[256,8]{0,1:T(8,128)S(1)}, u32[]{:S(2)}, u32[]{:S(2)}) collective-permute-start(f32[256,8]{0,1:T(8,128)S(1)} %add.162), channel_id=1, source_target_pairs={{0,3},{1,2},{2,1},{3,0},{4,7},{5,6},{6,5},{7,4},{8,11},{9,10},{10,... | collective-permute-start | bytes 24584 | tf_op jit(solution)/shard_map/ppermute | solution.py:69
  71.7 3.7 %collective-permute-start.9 = (f32[256,8]{0,1:T(8,128)S(1)}, f32[256,8]{0,1:T(8,128)S(1)}, u32[]{:S(2)}, u32[]{:S(2)}) collective-permute-start(f32[256,8]{0,1:T(8,128)S(1)} %add.163), channel_id=1, source_target_pairs={{0,4},{1,5},{2,6},{3,7},{4,0},{5,1},{6,2},{7,3},{8,12},{9,13},{10,... | collective-permute-start | bytes 24584 | tf_op jit(solution)/shard_map/ppermute | solution.py:69
  75.4 4.9 %collective-permute-start.10 = (f32[256,8]{0,1:T(8,128)S(1)}, f32[256,8]{0,1:T(8,128)S(1)}, u32[]{:S(2)}, u32[]{:S(2)}) collective-permute-start(f32[256,8]{0,1:T(8,128)S(1)} %add.164), channel_id=1, source_target_pairs={{0,12},{1,13},{2,14},{3,15},{4,8},{5,9},{6,10},{7,11},{8,4},{9,5},... | collective-permute-start | bytes 24584 | tf_op jit(solution)/shard_map/ppermute | solution.py:69
  80.3 3.7 %collective-permute-start.11 = (f32[256,8]{0,1:T(8,128)S(1)}, f32[256,8]{0,1:T(8,128)S(1)}, u32[]{:S(2)}, u32[]{:S(2)}) collective-permute-start(f32[256,8]{0,1:T(8,128)S(1)} %add.165), channel_id=1, source_target_pairs={{0,16},{1,17},{2,18},{3,19},{4,20},{5,21},{6,22},{7,23},{8,24},{9,... | collective-permute-start | bytes 24584 | tf_op jit(solution)/shard_map/ppermute | solution.py:69
  83.9 4.9 %collective-permute-start.12 = (f32[256,8]{0,1:T(8,128)S(1)}, f32[256,8]{0,1:T(8,128)S(1)}, u32[]{:S(2)}, u32[]{:S(2)}) collective-permute-start(f32[256,8]{0,1:T(8,128)S(1)} %add.166), channel_id=1, source_target_pairs={{0,48},{1,49},{2,50},{3,51},{4,52},{5,53},{6,54},{7,55},{8,56},{9,... | collective-permute-start | bytes 24584 | tf_op jit(solution)/shard_map/ppermute | solution.py:69
  100.2 1.2 collective-permute-start.13
  101.4 3.6 %collective-permute-start.14 = (f32[8,8]{0,1:T(8,128)S(1)}, f32[8,8]{0,1:T(8,128)S(1)}, u32[]{:S(2)}, u32[]{:S(2)}) collective-permute-start(f32[8,8]{0,1:T(8,128)S(1)} %add.170), channel_id=1, source_target_pairs={{0,1},{1,0},{2,3},{3,2},{4,5},{5,4},{6,7},{7,6},{8,9},{9,8},{10,11... | collective-permute-start | bytes 776 | tf_op jit(solution)/shard_map/ppermute | solution.py:69
  105.0 4.8 %collective-permute-start.15 = (f32[8,8]{0,1:T(8,128)S(1)}, f32[8,8]{0,1:T(8,128)S(1)}, u32[]{:S(2)}, u32[]{:S(2)}) collective-permute-start(f32[8,8]{0,1:T(8,128)S(1)} %add.171), channel_id=1, source_target_pairs={{0,3},{1,2},{2,1},{3,0},{4,7},{5,6},{6,5},{7,4},{8,11},{9,10},{10,... | collective-permute-start | bytes 776 | tf_op jit(solution)/shard_map/ppermute | solution.py:69
  109.8 3.6 %collective-permute-start.16 = (f32[8,8]{0,1:T(8,128)S(1)}, f32[8,8]{0,1:T(8,128)S(1)}, u32[]{:S(2)}, u32[]{:S(2)}) collective-permute-start(f32[8,8]{0,1:T(8,128)S(1)} %add.172), channel_id=1, source_target_pairs={{0,4},{1,5},{2,6},{3,7},{4,0},{5,1},{6,2},{7,3},{8,12},{9,13},{10,... | collective-permute-start | bytes 776 | tf_op jit(solution)/shard_map/ppermute | solution.py:69
  113.4 4.8 %collective-permute-start.17 = (f32[8,8]{0,1:T(8,128)S(1)}, f32[8,8]{0,1:T(8,128)S(1)}, u32[]{:S(2)}, u32[]{:S(2)}) collective-permute-start(f32[8,8]{0,1:T(8,128)S(1)} %add.173), channel_id=1, source_target_pairs={{0,12},{1,13},{2,14},{3,15},{4,8},{5,9},{6,10},{7,11},{8,4},{9,5},... | collective-permute-start | bytes 776 | tf_op jit(solution)/shard_map/ppermute | solution.py:69
  118.2 3.6 %collective-permute-start.18 = (f32[8,8]{0,1:T(8,128)S(1)}, f32[8,8]{0,1:T(8,128)S(1)}, u32[]{:S(2)}, u32[]{:S(2)}) collective-permute-start(f32[8,8]{0,1:T(8,128)S(1)} %add.174), channel_id=1, source_target_pairs={{0,16},{1,17},{2,18},{3,19},{4,20},{5,21},{6,22},{7,23},{8,24},{9,... | collective-permute-start | bytes 776 | tf_op jit(solution)/shard_map/ppermute | solution.py:69
  121.9 4.8 %collective-permute-start.19 = (f32[8,8]{0,1:T(8,128)S(1)}, f32[8,8]{0,1:T(8,128)S(1)}, u32[]{:S(2)}, u32[]{:S(2)}) collective-permute-start(f32[8,8]{0,1:T(8,128)S(1)} %add.175), channel_id=1, source_target_pairs={{0,48},{1,49},{2,50},{3,51},{4,52},{5,53},{6,54},{7,55},{8,56},{9,... | collective-permute-start | bytes 776 | tf_op jit(solution)/shard_map/ppermute | solution.py:69

commit v8 on v7

--- a/solution.py
+++ b/solution.py
@@ -70,35 +70,62 @@
     return value
 
 
-def project_kernel(b_ref, s_ref, o_ref):
+def project_kernel(b_ref, first_ref, second_ref, o_ref):
     tk, nr, nz = b_ref.shape
-    ns = s_ref.shape[0]
+    ns = first_ref.shape[0] + second_ref.shape[0]
     acc = jnp.zeros((tk * ROWS, ns * ROWS), jnp.float32)
     for j in range(nr // ROWS):
         rows = pl.ds(j * ROWS, ROWS)
         lhs = b_ref[:, rows, :].reshape(tk * ROWS, nz)
-        rhs = s_ref[:, rows, :].reshape(ns * ROWS, nz)
+        both = jnp.concatenate([first_ref[:, rows, :], second_ref[:, rows, :]], axis=0)
+        rhs = both.astype(jnp.bfloat16).reshape(ns * ROWS, nz)
         acc = acc + lax.dot_general(lhs, rhs, (((1,), (1,)), ((), ())), preferred_element_type=jnp.float32)
     row_t = lax.broadcasted_iota(jnp.int32, acc.shape, 0) % ROWS
     col_t = lax.broadcasted_iota(jnp.int32, acc.shape, 1) % ROWS
     acc = jnp.where(row_t == col_t, acc, 0.0)
-    o_ref[...] = jnp.sum(acc.reshape(tk, ROWS, ns * ROWS), axis=1)
-
-
-def project(basis3, snaps3, tk=64):
+    lanes = jnp.sum(acc.reshape(tk, ROWS, ns * ROWS), axis=1)
+    group = lax.broadcasted_iota(jnp.int32, (ns * ROWS, ns), 0) // ROWS
+    column = lax.broadcasted_iota(jnp.int32, (ns * ROWS, ns), 1)
+    gather = jnp.where(group == column, 1.0, 0.0)
+    o_ref[...] = jnp.dot(lanes, gather, precision=lax.Precision.HIGHEST, preferred_element_type=jnp.float32)
+
+
+def project(basis3, first3, second3, tk=64):
     nk, nr, nz = basis3.shape
-    ns = snaps3.shape[0]
-    out = pl.pallas_call(
+    ns = first3.shape[0] + second3.shape[0]
+    return pl.pallas_call(
         project_kernel,
         grid=(nk // tk,),
         in_specs=[pl.BlockSpec((tk, nr, nz), lambda i: (i, 0, 0)),
-                  pl.BlockSpec((ns, nr, nz), lambda i: (0, 0, 0))],
-        out_specs=pl.BlockSpec((tk, ns * ROWS), lambda i: (i, 0)),
-        out_shape=jax.ShapeDtypeStruct((nk, ns * ROWS), jnp.float32),
+                  pl.BlockSpec(first3.shape, lambda i: (0, 0, 0)),
+                  pl.BlockSpec(second3.shape, lambda i: (0, 0, 0))],
+        out_specs=pl.BlockSpec((tk, ns), lambda i: (i, 0)),
+        out_shape=jax.ShapeDtypeStruct((nk, ns), jnp.float32),
         cost_estimate=pl.CostEstimate(flops=2 * nk * nr * nz * ns * ROWS, transcendentals=0,
-                                      bytes_accessed=nk * nr * nz * 2 + ns * nr * nz * 2 + nk * ns * ROWS * 4),
-    )(basis3, snaps3)
-    return jnp.sum(out.reshape(nk, ns, ROWS), axis=2)
+                                      bytes_accessed=nk * nr * nz * 2 + ns * nr * nz * 4 + nk * ns * 4),
+    )(basis3, first3, second3)
+
+
+def directions_kernel(l_ref, w_ref, o_ref):
+    ns = w_ref.shape[0]
+    for s in range(ns):
+        acc = l_ref[s, 0] * w_ref[0]
+        for t in range(1, s + 1):
+            acc = acc + l_ref[s, t] * w_ref[t]
+        o_ref[s] = acc
+
+
+def apply_inverse(inverse_factor, residual3, block_rows=2 * ROWS):
+    ns, nr, nz = residual3.shape
+    return pl.pallas_call(
+        directions_kernel,
+        grid=(nr // block_rows,),
+        in_specs=[pl.BlockSpec(memory_space=pltpu.SMEM),
+                  pl.BlockSpec((ns, block_rows, nz), lambda j: (0, j, 0))],
+        out_specs=pl.BlockSpec((ns, block_rows, nz), lambda j: (0, j, 0)),
+        out_shape=jax.ShapeDtypeStruct(residual3.shape, jnp.float32),
+        cost_estimate=pl.CostEstimate(flops=ns * ns * nr * nz, transcendentals=0, bytes_accessed=2 * ns * nr * nz * 4),
+    )(inverse_factor, residual3)
 
 
 def residual_kernel(c_ref, b_ref, s_ref, o_ref, g_ref, spread_ref, acc_ref):
@@ -222,14 +249,16 @@
     ns = snapshots.shape[0]
     snaps3 = snapshots.reshape(ns, -1, snapshots.shape[3])
     basis3 = basis.reshape(basis.shape[0], -1, basis.shape[3])
-    partial_proj = project(basis3, snaps3.astype(jnp.bfloat16))
+    first3 = segment_one.reshape(segment_one.shape[0], -1, segment_one.shape[3])
+    second3 = advanced.reshape(advanced.shape[0], -1, advanced.shape[3])
+    partial_proj = project(basis3, first3, second3)
     coeffs = allreduce(partial_proj, ("role", "slab"))
     coeffs_bf = coeffs.astype(jnp.bfloat16)
     residual3, local_gram = residual(coeffs_bf, basis3, snaps3)
     total_gram = allreduce(local_gram, ("role", "slab"))
     lower_factor = jnp.linalg.cholesky(total_gram)
     inverse_factor = jax.scipy.linalg.solve_triangular(lower_factor, jnp.eye(ns, dtype=jnp.float32), lower=True)
-    directions = jnp.sum(inverse_factor[:, :, None, None] * residual3[None], axis=1)
+    directions = apply_inverse(inverse_factor, residual3)
     return (advanced, coeffs, lower_factor.T, directions.reshape(snapshots.shape))
 
 

time: 134 us -> 135 us (level)
  Pallas kernels: 18.2 us -> 22.5 us
  waiting for transfers between devices: 79.9 us -> 77.3 us
    pallas_call x0 -> x1, Pallas kernels: none -> 3.51 us  [apply_inverse(): pl.pallas_call(directions_kernel, grid=(nr // block_rows,), in_specs=[pl....]
    reduce_sum x2 -> x0, other arithmetic: 2.99 us -> none  [the longest x1 2.96 us: on_device(): jnp.sum(inverse_factor[:, :, None, None] * residual3[None], axis=1)]
    ppermute x14, waiting for transfers between devices: 53.1 us -> 50.5 us  [allreduce(): value = value + lax.ppermute(value, name, pairs)]
    concatenate x1, other arithmetic: 0.08 us -> 2.1 us  [on_device(): snapshots = jnp.concatenate([segment_one, advanced], axis=0)]
  transfers between devices with their start and end apart: 20 -> 20, of which waited for: 18 -> 18; matrix products, arithmetic and copies ran while one was open for 8% -> 9% of each run, Pallas kernels for 0% -> 0%
where the time goes in v8:
time: 135 us
  waiting for transfers between devices  77.3 us (57%)
  Pallas kernels  22.5 us (17%)
  other arithmetic  17.1 us (13%)
  starting transfers between devices  11.7 us (9%)
  local copies, waits for them, and re-layouts  4.71 us (3%)
    ppermute x14, waiting for transfers between devices, allreduce(): value = value + lax.ppermute(value, name, pairs)  50.5 us
    ppermute x2, waiting for transfers between devices, extended(): lax.ppermute(head, axis, [((i + 1) % count, i) for i in range(ends)])  13.7 us
    ppermute x2, waiting for transfers between devices, extended(): lax.ppermute(tail, axis, [(i, (i + 1) % count) for i in range(ends)])  13 us
    pallas_call x1, Pallas kernels, project(): pl.pallas_call(project_kernel, grid=(nk // tk,), in_specs=[pl.BlockSpec((...  10 us
    ppermute x2, starting transfers between devices, extended(): lax.ppermute(head, axis, [((i + 1) % count, i) for i in range(ends)])  9.19 us
    pallas_call x1, Pallas kernels, residual(): pl.pallas_call(residual_kernel, grid=(nr // block_rows,), in_specs=[pl.Bl...  9 us
    mul x2, other arithmetic, local_terms(): viscosity * (second_diff(ypadded, center, 2, ny_loc) + second_diff(zpadde...  5.23 us
    pallas_call x1, Pallas kernels, apply_inverse(): pl.pallas_call(directions_kernel, grid=(nr // block_rows,), in_specs=[pl....  3.51 us
  transfers between devices with their start and end apart: 20, of which 18 were waited for; matrix products, arithmetic and copies ran while one was open for 9% of the time, Pallas kernels for 0%

profile of v8, /device:TPU:0, one launch (start us, length us, event | category | flops | bytes accessed | tf_op | source)
XLA Modules:
  0.0 134.9 jit_solution(2277381235896685769)
XLA Ops:
  0.6 0.0 copy-start.2
  0.6 8.8 %collective-permute-start = (f32[4,2,64,256]{3,2,1,0:T(8,128)}, f32[4,2,64,256]{3,2,1,0:T(8,128)S(1)}, u32[]{:S(2)}, u32[]{:S(2)}) collective-permute-start(f32[4,2,64,256]{3,2,1,0:T(8,128)} %param.5), channel_id=1, source_target_pairs={{1,0},{2,1},{3,2},{4,3},{5,4},{6,5},{7,6},{8,7},{9,8},{10,9},{11,1... | collective-permute-start | bytes 1572872 | tf_op jit(solution)/shard_map/ppermute | solution.py:32
  9.5 0.0 collective-permute-start.1
  9.5 0.9 slice_select_fusion.1
  10.4 0.1 collective-permute-start.2
  10.5 1.2 fusion.50
  11.7 0.7 negate_multiply_fusion
  12.4 0.7 dynamic_slice.7
  13.1 0.0 collective-permute-done.2
  13.1 4.4 %fusion.15 = f32[4,2,64,256]{3,2,1,0:T(8,128)S(1)} fusion(f32[4,2,2,256]{3,2,1,0:T(2,128)S(1)} %get-tuple-element.27, f32[4,2,64,256]{3,2,1,0:T(8,128)} %param.5, f32[4,2,2,256]{3,2,1,0:T(2,128)S(1)} %get-tuple-element.26, f32[4,2,64,2]{3,2,1,0:T(8,128)S(1)} %get-tuple-element.23, f32[4,2,64,2]{3,2,1,0:T(8,128)S(1)} %get-tuple-element.22), kind=kLoop, calls=%fused_computation.33 | loop fusion | flops 3276800 | bytes 1089536 | tf_op jit(solution)/shard_map/mul | solution.py:215
  17.6 1.0 slice_subtract_fusion
  18.6 2.4 %collective-permute-done = f32[4,2,64,256]{3,2,1,0:T(8,128)S(1)} collective-permute-done((f32[4,2,64,256]{3,2,1,0:T(8,128)}, f32[4,2,64,256]{3,2,1,0:T(8,128)S(1)}, u32[]{:S(2)}, u32[]{:S(2)}) %collective-permute-start) | collective-permute-done | bytes 524320 | tf_op jit(solution)/shard_map/ppermute | solution.py:32
  21.0 7.5 %collective-permute-done.1 = f32[4,2,64,256]{3,2,1,0:T(8,128)S(1)} collective-permute-done((f32[4,2,64,256]{3,2,1,0:T(8,128)}, f32[4,2,64,256]{3,2,1,0:T(8,128)S(1)}, u32[]{:S(2)}, u32[]{:S(2)}) %collective-permute-start.1) | collective-permute-done | bytes 524320 | tf_op jit(solution)/shard_map/ppermute | solution.py:30
  28.5 1.6 %multiply_add_fusion = (f32[4,2,64,256]{3,2,1,0:T(8,128)S(1)}, f32[4,2,64,256]{3,2,1,0:T(8,128)S(1)}) fusion(f32[4,2,64,256]{3,2,1,0:T(8,128)} %param.5, f32[3,2,64,256]{3,2,1,0:T(8,128)S(1)} %slice.183, f32[1,2,64,256]{3,2,1,0:T(8,128)S(1)} %slice_subtract_fusion, f32[4,2,64,256]{3,2,1,0:T(8,128)S(1)} %collective-permute-done.1, ...), kind=kLoop, calls=%fused_computation.76 | loop fusion | flops 2883584 | bytes 3145984 | tf_op jit(solution)/shard_map/add | solution.py:245
  30.1 0.1 collective-permute-start.5
  30.2 0.1 fusion.49
  30.4 0.4 collective-permute-start.3
  30.7 1.7 %collective-permute-start.4 = (f32[4,2,64,256]{3,2,1,0:T(8,128)S(1)}, f32[4,2,64,256]{3,2,1,0:T(8,128)S(1)}, u32[]{:S(2)}, u32[]{:S(2)}) collective-permute-start(f32[4,2,64,256]{3,2,1,0:T(8,128)S(1)} %get-tuple-element.18), channel_id=1, source_target_pairs={{0,1},{1,2},{2,3},{3,4},{4,5},{5,6},{6,7},{7,8},{8,9},{9,10},{10,1... | collective-permute-start | bytes 1572872 | tf_op jit(solution)/shard_map/ppermute | solution.py:30
  32.5 0.0 collective-permute-done.5
  32.5 0.8 fusion.5
  33.4 0.1 fusion.44
  33.4 11.3 %collective-permute-done.3 = f32[4,2,64,256]{3,2,1,0:T(8,128)S(1)} collective-permute-done((f32[4,2,64,256]{3,2,1,0:T(8,128)S(1)}, f32[4,2,64,256]{3,2,1,0:T(8,128)S(1)}, u32[]{:S(2)}, u32[]{:S(2)}) %collective-permute-start.3) | collective-permute-done | bytes 524320 | tf_op jit(solution)/shard_map/ppermute | solution.py:32
  44.8 5.5 %collective-permute-done.4 = f32[4,2,64,256]{3,2,1,0:T(8,128)S(1)} collective-permute-done((f32[4,2,64,256]{3,2,1,0:T(8,128)S(1)}, f32[4,2,64,256]{3,2,1,0:T(8,128)S(1)}, u32[]{:S(2)}, u32[]{:S(2)}) %collective-permute-start.4) | collective-permute-done | bytes 524320 | tf_op jit(solution)/shard_map/ppermute | solution.py:30
  50.3 1.2 fusion.43
  51.5 10.0 %shard_map.84 = f32[256,8]{1,0:T(8,128)} custom-call(bf16[256,128,256]{2,1,0:T(8,128)(2,1)} %bitcast.19, f32[4,128,256]{2,1,0:T(8,128)} %bitcast.21, f32[4,128,256]{2,1,0:T(8,128)} %bitcast.22), custom_call_target="tpu_custom_call" | custom-call | flops 2147483648 | bytes 17833984 | tf_op jit(solution)/shard_map/pallas_call | solution.py:96
  61.5 1.0 copy.17
  62.4 0.1 collective-permute-start.6
  62.5 1.2 collective-permute-done.6
  63.7 0.0 collective-permute-start.7
  63.7 3.6 %collective-permute-done.7 = f32[256,8]{0,1:T(8,128)S(1)} collective-permute-done((f32[256,8]{0,1:T(8,128)S(1)}, f32[256,8]{0,1:T(8,128)S(1)}, u32[]{:S(2)}, u32[]{:S(2)}) %collective-permute-start.7) | collective-permute-done | bytes 8224 | tf_op jit(solution)/shard_map/ppermute | solution.py:69
  67.3 0.0 collective-permute-start.8
  67.3 4.9 %collective-permute-done.8 = f32[256,8]{0,1:T(8,128)S(1)} collective-permute-done((f32[256,8]{0,1:T(8,128)S(1)}, f32[256,8]{0,1:T(8,128)S(1)}, u32[]{:S(2)}, u32[]{:S(2)}) %collective-permute-start.8) | collective-permute-done | bytes 8224 | tf_op jit(solution)/shard_map/ppermute | solution.py:69
  72.2 3.6 %collective-permute-done.9 = f32[256,8]{0,1:T(8,128)S(1)} collective-permute-done((f32[256,8]{0,1:T(8,128)S(1)}, f32[256,8]{0,1:T(8,128)S(1)}, u32[]{:S(2)}, u32[]{:S(2)}) %collective-permute-start.9) | collective-permute-done | bytes 8224 | tf_op jit(solution)/shard_map/ppermute | solution.py:69
  75.9 4.9 %collective-permute-done.10 = f32[256,8]{0,1:T(8,128)S(1)} collective-permute-done((f32[256,8]{0,1:T(8,128)S(1)}, f32[256,8]{0,1:T(8,128)S(1)}, u32[]{:S(2)}, u32[]{:S(2)}) %collective-permute-start.10) | collective-permute-done | bytes 8224 | tf_op jit(solution)/shard_map/ppermute | solution.py:69
  80.7 0.0 collective-permute-start.11
  80.7 3.6 %collective-permute-done.11 = f32[256,8]{0,1:T(8,128)S(1)} collective-permute-done((f32[256,8]{0,1:T(8,128)S(1)}, f32[256,8]{0,1:T(8,128)S(1)}, u32[]{:S(2)}, u32[]{:S(2)}) %collective-permute-start.11) | collective-permute-done | bytes 8224 | tf_op jit(solution)/shard_map/ppermute | solution.py:69
  84.4 0.0 collective-permute-start.12
  84.4 2.1 %pad_maximum_fusion = f32[8,2,64,256]{3,2,1,0:T(8,128)} fusion(f32[4,2,64,256]{3,2,1,0:T(8,128)S(1)} %copy-done.1, f32[4,2,64,256]{3,2,1,0:T(8,128)} %copy-done), kind=kLoop, calls=%fused_computation.1 | loop fusion | flops 262144 | bytes 2097152 | tf_op jit(solution)/shard_map/concatenate | solution.py:248
  86.5 2.8 %collective-permute-done.12 = f32[256,8]{0,1:T(8,128)S(1)} collective-permute-done((f32[256,8]{0,1:T(8,128)S(1)}, f32[256,8]{0,1:T(8,128)S(1)}, u32[]{:S(2)}, u32[]{:S(2)}) %collective-permute-start.12) | collective-permute-done | bytes 8224 | tf_op jit(solution)/shard_map/ppermute | solution.py:69
  89.2 0.6 convert_bitcast_fusion
  89.8 9.0 %shard_map.85 = (f32[8,128,256]{2,1,0:T(8,128)}, f32[36,256]{1,0:T(8,128)}) custom-call(bf16[8,256]{1,0:T(8,128)(2,1)} %get-tuple-element.16.c_ref, bf16[256,128,256]{2,1,0:T(8,128)(2,1)} %bitcast.20, f32[8,128,256]{2,1,0:T(8,128)} %bitcast.23), custom_call_target="tpu_custom_call" | custom-call | flops 2147483648 | bytes 18874368 | tf_op jit(solution)/shard_map/pallas_call | solution.py:171
  98.8 0.9 reduce_sum.9
  99.7 0.8 gather_fusion
  100.5 0.1 reshape.44
  100.6 0.1 copy.19
  100.7 1.2 collective-permute-done.13
  101.8 3.6 %collective-permute-done.14 = f32[8,8]{0,1:T(8,128)S(1)} collective-permute-done((f32[8,8]{0,1:T(8,128)S(1)}, f32[8,8]{0,1:T(8,128)S(1)}, u32[]{:S(2)}, u32[]{:S(2)}) %collective-permute-start.14) | collective-permute-done | bytes 288 | tf_op jit(solution)/shard_map/ppermute | solution.py:69
  105.5 4.8 %collective-permute-done.15 = f32[8,8]{0,1:T(8,128)S(1)} collective-permute-done((f32[8,8]{0,1:T(8,128)S(1)}, f32[8,8]{0,1:T(8,128)S(1)}, u32[]{:S(2)}, u32[]{:S(2)}) %collective-permute-start.15) | collective-permute-done | bytes 288 | tf_op jit(solution)/shard_map/ppermute | solution.py:69
  110.3 0.0 collective-permute-start.16
  110.3 3.6 %collective-permute-done.16 = f32[8,8]{0,1:T(8,128)S(1)} collective-permute-done((f32[8,8]{0,1:T(8,128)S(1)}, f32[8,8]{0,1:T(8,128)S(1)}, u32[]{:S(2)}, u32[]{:S(2)}) %collective-permute-start.16) | collective-permute-done | bytes 288 | tf_op jit(solution)/shard_map/ppermute | solution.py:69
  113.9 0.0 collective-permute-start.17
  113.9 4.8 %collective-permute-done.17 = f32[8,8]{0,1:T(8,128)S(1)} collective-permute-done((f32[8,8]{0,1:T(8,128)S(1)}, f32[8,8]{0,1:T(8,128)S(1)}, u32[]{:S(2)}, u32[]{:S(2)}) %collective-permute-start.17) | collective-permute-done | bytes 288 | tf_op jit(solution)/shard_map/ppermute | solution.py:69
  118.7 0.0 collective-permute-start.18
  118.7 3.6 %collective-permute-done.18 = f32[8,8]{0,1:T(8,128)S(1)} collective-permute-done((f32[8,8]{0,1:T(8,128)S(1)}, f32[8,8]{0,1:T(8,128)S(1)}, u32[]{:S(2)}, u32[]{:S(2)}) %collective-permute-start.18) | collective-permute-done | bytes 288 | tf_op jit(solution)/shard_map/ppermute | solution.py:69
  122.3 0.5 collective-permute-start.19
  122.8 4.3 %collective-permute-done.19 = f32[8,8]{0,1:T(8,128)S(1)} collective-permute-done((f32[8,8]{0,1:T(8,128)S(1)}, f32[8,8]{0,1:T(8,128)S(1)}, u32[]{:S(2)}, u32[]{:S(2)}) %collective-permute-start.19) | collective-permute-done | bytes 288 | tf_op jit(solution)/shard_map/ppermute | solution.py:69
  127.1 0.1 copy.20
  127.2 0.7 cholesky.20
  128.0 0.6 compare_reduce_fusion
  128.6 0.6 select_bitcast_fusion
  129.3 0.6 custom-call.7
  129.9 0.8 fusion.45.l_ref
  130.7 0.7 copy.22
  131.4 3.5 %shard_map.86 = f32[8,128,256]{2,1,0:T(8,128)} custom-call(f32[8,8]{1,0:T(8,128)} %fusion.45.l_ref, f32[8,128,256]{2,1,0:T(8,128)} %get-tuple-element.7.w_ref), custom_call_target="tpu_custom_call" | custom-call | flops 2097152 | bytes 2097152 | tf_op jit(solution)/shard_map/pallas_call | solution.py:120
  (31 shorter events, 0.2 us)
Async XLA Ops:
  0.6 80.1 %copy-start.2 = (s32[64]{0:T(128)S(1)}, s32[64]{0:T(128)}, u32[]{:S(2)}) copy-start(s32[64]{0:T(128)} %constant.99) | copy-start | bytes 772
  0.6 20.3 %collective-permute-start = (f32[4,2,64,256]{3,2,1,0:T(8,128)}, f32[4,2,64,256]{3,2,1,0:T(8,128)S(1)}, u32[]{:S(2)}, u32[]{:S(2)}) collective-permute-start(f32[4,2,64,256]{3,2,1,0:T(8,128)} %param.5), channel_id=1, source_target_pairs={{1,0},{2,1},{3,2},{4,3},{5,4},{6,5},{7,6},{8,7},{9,8},{10,9},{11,1... | collective-permute-start | bytes 1572872 | tf_op jit(solution)/shard_map/ppermute | solution.py:32
  9.5 19.0 %collective-permute-start.1 = (f32[4,2,64,256]{3,2,1,0:T(8,128)}, f32[4,2,64,256]{3,2,1,0:T(8,128)S(1)}, u32[]{:S(2)}, u32[]{:S(2)}) collective-permute-start(f32[4,2,64,256]{3,2,1,0:T(8,128)} %param.5), channel_id=1, source_target_pairs={{0,1},{1,2},{2,3},{3,4},{4,5},{5,6},{6,7},{7,8},{8,9},{9,10},{10,1... | collective-permute-start | bytes 1572872 | tf_op jit(solution)/shard_map/ppermute | solution.py:30
  10.4 2.7 %collective-permute-start.2 = (f32[4,2,2,256]{3,2,1,0:T(2,128)S(1)}, f32[4,2,2,256]{3,2,1,0:T(2,128)S(1)}, u32[]{:S(2)}, u32[]{:S(2)}) collective-permute-start(f32[4,2,2,256]{3,2,1,0:T(2,128)S(1)} %slice_select_fusion.1), channel_id=1, source_target_pairs={{0,64},{64,0},{1,65},{65,1},{2,66},{66,2},{3,67},{67,3},{4,68},{68... | collective-permute-start | bytes 49160 | tf_op jit(solution)/shard_map/ppermute | solution.py:22
  30.1 21.4 %copy-start = (f32[4,2,64,256]{3,2,1,0:T(8,128)}, f32[4,2,64,256]{3,2,1,0:T(8,128)S(1)}, u32[]{:S(2)}) copy-start(f32[4,2,64,256]{3,2,1,0:T(8,128)S(1)} %get-tuple-element.18) | copy-start | bytes 1572868
  30.1 2.3 %collective-permute-start.5 = (f32[4,2,2,256]{3,2,1,0:T(2,128)S(1)}, f32[4,2,2,256]{3,2,1,0:T(2,128)S(1)}, u32[]{:S(2)}, u32[]{:S(2)}) collective-permute-start(f32[4,2,2,256]{3,2,1,0:T(2,128)S(1)} %slice_select_fusion), channel_id=1, source_target_pairs={{0,64},{64,0},{1,65},{65,1},{2,66},{66,2},{3,67},{67,3},{4,68},{68... | collective-permute-start | bytes 49160 | tf_op jit(solution)/shard_map/ppermute | solution.py:22
  30.4 14.4 %collective-permute-start.3 = (f32[4,2,64,256]{3,2,1,0:T(8,128)S(1)}, f32[4,2,64,256]{3,2,1,0:T(8,128)S(1)}, u32[]{:S(2)}, u32[]{:S(2)}) collective-permute-start(f32[4,2,64,256]{3,2,1,0:T(8,128)S(1)} %get-tuple-element.18), channel_id=1, source_target_pairs={{1,0},{2,1},{3,2},{4,3},{5,4},{6,5},{7,6},{8,7},{9,8},{10,9},{11,1... | collective-permute-start | bytes 1572872 | tf_op jit(solution)/shard_map/ppermute | solution.py:32
  30.7 19.6 %collective-permute-start.4 = (f32[4,2,64,256]{3,2,1,0:T(8,128)S(1)}, f32[4,2,64,256]{3,2,1,0:T(8,128)S(1)}, u32[]{:S(2)}, u32[]{:S(2)}) collective-permute-start(f32[4,2,64,256]{3,2,1,0:T(8,128)S(1)} %get-tuple-element.18), channel_id=1, source_target_pairs={{0,1},{1,2},{2,3},{3,4},{4,5},{5,6},{6,7},{7,8},{8,9},{9,10},{10,1... | collective-permute-start | bytes 1572872 | tf_op jit(solution)/shard_map/ppermute | solution.py:30
  51.5 32.9 %copy-start.1 = (f32[4,2,64,256]{3,2,1,0:T(8,128)S(1)}, f32[4,2,64,256]{3,2,1,0:T(8,128)}, u32[]{:S(2)}) copy-start(f32[4,2,64,256]{3,2,1,0:T(8,128)} %fusion.43) | copy-start | bytes 1572868
  62.4 1.2 collective-permute-start.6
  63.7 3.7 %collective-permute-start.7 = (f32[256,8]{0,1:T(8,128)S(1)}, f32[256,8]{0,1:T(8,128)S(1)}, u32[]{:S(2)}, u32[]{:S(2)}) collective-permute-start(f32[256,8]{0,1:T(8,128)S(1)} %add.161), channel_id=1, source_target_pairs={{0,1},{1,0},{2,3},{3,2},{4,5},{5,4},{6,7},{7,6},{8,9},{9,8},{10,11... | collective-permute-start | bytes 24584 | tf_op jit(solution)/shard_map/ppermute | solution.py:69
  67.3 4.9 %collective-permute-start.8 = (f32[256,8]{0,1:T(8,128)S(1)}, f32[256,8]{0,1:T(8,128)S(1)}, u32[]{:S(2)}, u32[]{:S(2)}) collective-permute-start(f32[256,8]{0,1:T(8,128)S(1)} %add.162), channel_id=1, source_target_pairs={{0,3},{1,2},{2,1},{3,0},{4,7},{5,6},{6,5},{7,4},{8,11},{9,10},{10,... | collective-permute-start | bytes 24584 | tf_op jit(solution)/shard_map/ppermute | solution.py:69
  72.2 3.7 %collective-permute-start.9 = (f32[256,8]{0,1:T(8,128)S(1)}, f32[256,8]{0,1:T(8,128)S(1)}, u32[]{:S(2)}, u32[]{:S(2)}) collective-permute-start(f32[256,8]{0,1:T(8,128)S(1)} %add.163), channel_id=1, source_target_pairs={{0,4},{1,5},{2,6},{3,7},{4,0},{5,1},{6,2},{7,3},{8,12},{9,13},{10,... | collective-permute-start | bytes 24584 | tf_op jit(solution)/shard_map/ppermute | solution.py:69
  75.9 4.9 %collective-permute-start.10 = (f32[256,8]{0,1:T(8,128)S(1)}, f32[256,8]{0,1:T(8,128)S(1)}, u32[]{:S(2)}, u32[]{:S(2)}) collective-permute-start(f32[256,8]{0,1:T(8,128)S(1)} %add.164), channel_id=1, source_target_pairs={{0,12},{1,13},{2,14},{3,15},{4,8},{5,9},{6,10},{7,11},{8,4},{9,5},... | collective-permute-start | bytes 24584 | tf_op jit(solution)/shard_map/ppermute | solution.py:69
  80.7 3.7 %collective-permute-start.11 = (f32[256,8]{0,1:T(8,128)S(1)}, f32[256,8]{0,1:T(8,128)S(1)}, u32[]{:S(2)}, u32[]{:S(2)}) collective-permute-start(f32[256,8]{0,1:T(8,128)S(1)} %add.165), channel_id=1, source_target_pairs={{0,16},{1,17},{2,18},{3,19},{4,20},{5,21},{6,22},{7,23},{8,24},{9,... | collective-permute-start | bytes 24584 | tf_op jit(solution)/shard_map/ppermute | solution.py:69
  84.4 4.9 %collective-permute-start.12 = (f32[256,8]{0,1:T(8,128)S(1)}, f32[256,8]{0,1:T(8,128)S(1)}, u32[]{:S(2)}, u32[]{:S(2)}) collective-permute-start(f32[256,8]{0,1:T(8,128)S(1)} %add.166), channel_id=1, source_target_pairs={{0,48},{1,49},{2,50},{3,51},{4,52},{5,53},{6,54},{7,55},{8,56},{9,... | collective-permute-start | bytes 24584 | tf_op jit(solution)/shard_map/ppermute | solution.py:69
  100.7 1.2 collective-permute-start.13
  101.8 3.6 %collective-permute-start.14 = (f32[8,8]{0,1:T(8,128)S(1)}, f32[8,8]{0,1:T(8,128)S(1)}, u32[]{:S(2)}, u32[]{:S(2)}) collective-permute-start(f32[8,8]{0,1:T(8,128)S(1)} %add.170), channel_id=1, source_target_pairs={{0,1},{1,0},{2,3},{3,2},{4,5},{5,4},{6,7},{7,6},{8,9},{9,8},{10,11... | collective-permute-start | bytes 776 | tf_op jit(solution)/shard_map/ppermute | solution.py:69
  105.5 4.8 %collective-permute-start.15 = (f32[8,8]{0,1:T(8,128)S(1)}, f32[8,8]{0,1:T(8,128)S(1)}, u32[]{:S(2)}, u32[]{:S(2)}) collective-permute-start(f32[8,8]{0,1:T(8,128)S(1)} %add.171), channel_id=1, source_target_pairs={{0,3},{1,2},{2,1},{3,0},{4,7},{5,6},{6,5},{7,4},{8,11},{9,10},{10,... | collective-permute-start | bytes 776 | tf_op jit(solution)/shard_map/ppermute | solution.py:69
  110.3 3.6 %collective-permute-start.16 = (f32[8,8]{0,1:T(8,128)S(1)}, f32[8,8]{0,1:T(8,128)S(1)}, u32[]{:S(2)}, u32[]{:S(2)}) collective-permute-start(f32[8,8]{0,1:T(8,128)S(1)} %add.172), channel_id=1, source_target_pairs={{0,4},{1,5},{2,6},{3,7},{4,0},{5,1},{6,2},{7,3},{8,12},{9,13},{10,... | collective-permute-start | bytes 776 | tf_op jit(solution)/shard_map/ppermute | solution.py:69
  113.9 4.8 %collective-permute-start.17 = (f32[8,8]{0,1:T(8,128)S(1)}, f32[8,8]{0,1:T(8,128)S(1)}, u32[]{:S(2)}, u32[]{:S(2)}) collective-permute-start(f32[8,8]{0,1:T(8,128)S(1)} %add.173), channel_id=1, source_target_pairs={{0,12},{1,13},{2,14},{3,15},{4,8},{5,9},{6,10},{7,11},{8,4},{9,5},... | collective-permute-start | bytes 776 | tf_op jit(solution)/shard_map/ppermute | solution.py:69
  118.7 3.6 %collective-permute-start.18 = (f32[8,8]{0,1:T(8,128)S(1)}, f32[8,8]{0,1:T(8,128)S(1)}, u32[]{:S(2)}, u32[]{:S(2)}) collective-permute-start(f32[8,8]{0,1:T(8,128)S(1)} %add.174), channel_id=1, source_target_pairs={{0,16},{1,17},{2,18},{3,19},{4,20},{5,21},{6,22},{7,23},{8,24},{9,... | collective-permute-start | bytes 776 | tf_op jit(solution)/shard_map/ppermute | solution.py:69
  122.3 4.8 %collective-permute-start.19 = (f32[8,8]{0,1:T(8,128)S(1)}, f32[8,8]{0,1:T(8,128)S(1)}, u32[]{:S(2)}, u32[]{:S(2)}) collective-permute-start(f32[8,8]{0,1:T(8,128)S(1)} %add.175), channel_id=1, source_target_pairs={{0,48},{1,49},{2,50},{3,51},{4,52},{5,53},{6,54},{7,55},{8,56},{9,... | collective-permute-start | bytes 776 | tf_op jit(solution)/shard_map/ppermute | solution.py:69

commit v9 on v7

--- a/solution.py
+++ b/solution.py
@@ -82,23 +82,27 @@
     row_t = lax.broadcasted_iota(jnp.int32, acc.shape, 0) % ROWS
     col_t = lax.broadcasted_iota(jnp.int32, acc.shape, 1) % ROWS
     acc = jnp.where(row_t == col_t, acc, 0.0)
-    o_ref[...] = jnp.sum(acc.reshape(tk, ROWS, ns * ROWS), axis=1)
-
-
-def project(basis3, snaps3, tk=64):
+    lanes = jnp.sum(acc.reshape(tk, ROWS, ns * ROWS), axis=1)
+    group = lax.broadcasted_iota(jnp.int32, (ns, ns * ROWS), 1) // ROWS
+    snapshot = lax.broadcasted_iota(jnp.int32, (ns, ns * ROWS), 0)
+    gather = jnp.where(group == snapshot, 1.0, 0.0)
+    o_ref[...] = lax.dot_general(gather, lanes, (((1,), (1,)), ((), ())),
+                                 precision=lax.Precision.HIGHEST, preferred_element_type=jnp.float32)
+
+
+def project(basis3, snaps3, tk=128):
     nk, nr, nz = basis3.shape
     ns = snaps3.shape[0]
-    out = pl.pallas_call(
+    return pl.pallas_call(
         project_kernel,
         grid=(nk // tk,),
         in_specs=[pl.BlockSpec((tk, nr, nz), lambda i: (i, 0, 0)),
                   pl.BlockSpec((ns, nr, nz), lambda i: (0, 0, 0))],
-        out_specs=pl.BlockSpec((tk, ns * ROWS), lambda i: (i, 0)),
-        out_shape=jax.ShapeDtypeStruct((nk, ns * ROWS), jnp.float32),
+        out_specs=pl.BlockSpec((ns, tk), lambda i: (0, i)),
+        out_shape=jax.ShapeDtypeStruct((ns, nk), jnp.float32),
         cost_estimate=pl.CostEstimate(flops=2 * nk * nr * nz * ns * ROWS, transcendentals=0,
-                                      bytes_accessed=nk * nr * nz * 2 + ns * nr * nz * 2 + nk * ns * ROWS * 4),
+                                      bytes_accessed=nk * nr * nz * 2 + ns * nr * nz * 2 + nk * ns * 4),
     )(basis3, snaps3)
-    return jnp.sum(out.reshape(nk, ns, ROWS), axis=2)
 
 
 def residual_kernel(c_ref, b_ref, s_ref, o_ref, g_ref, spread_ref, acc_ref):
@@ -112,7 +116,7 @@
         col = lax.broadcasted_iota(jnp.int32, (nk, nk * rows), 1)
         row = lax.broadcasted_iota(jnp.int32, (nk, nk * rows), 0)
         expand = jnp.where(col // rows == row, 1.0, 0.0).astype(jnp.bfloat16)
-        wide = jnp.dot(c_ref[...], expand, preferred_element_type=jnp.float32)
+        wide = jnp.dot(c_ref[...].astype(jnp.bfloat16), expand, preferred_element_type=jnp.float32)
         tall = jnp.broadcast_to(wide[:, None, :], (ns, rows, nk * rows)).reshape(ns * rows, nk * rows)
         r_t = lax.broadcasted_iota(jnp.int32, tall.shape, 0) % rows
         c_t = lax.broadcasted_iota(jnp.int32, tall.shape, 1) % rows
@@ -137,7 +141,7 @@
         g_ref[...] = jnp.sum(acc_ref[...], axis=1)
 
 
-def residual(coeffs_bf, basis3, snaps3, block_rows=2 * ROWS):
+def residual(coeffs_t, basis3, snaps3, block_rows=2 * ROWS):
     nk, nr, nz = basis3.shape
     ns = snaps3.shape[0]
     pairs = ns * (ns + 1) // 2
@@ -156,7 +160,7 @@
         compiler_params=pltpu.CompilerParams(dimension_semantics=("arbitrary",)),
         cost_estimate=pl.CostEstimate(flops=2 * ns * ROWS * nk * ROWS * nz * (nr // ROWS), transcendentals=0,
                                       bytes_accessed=nk * nr * nz * 2 + 2 * ns * nr * nz * 4),
-    )(coeffs_bf.T, basis3, snaps3)
+    )(coeffs_t, basis3, snaps3)
     sums = jnp.sum(g, axis=1)
     table = np.zeros((ns, ns), np.int32)
     p = 0
@@ -223,9 +227,9 @@
     snaps3 = snapshots.reshape(ns, -1, snapshots.shape[3])
     basis3 = basis.reshape(basis.shape[0], -1, basis.shape[3])
     partial_proj = project(basis3, snaps3.astype(jnp.bfloat16))
-    coeffs = allreduce(partial_proj, ("role", "slab"))
-    coeffs_bf = coeffs.astype(jnp.bfloat16)
-    residual3, local_gram = residual(coeffs_bf, basis3, snaps3)
+    coeffs_t = allreduce(partial_proj, ("role", "slab"))
+    coeffs = coeffs_t.T
+    residual3, local_gram = residual(coeffs_t, basis3, snaps3)
     total_gram = allreduce(local_gram, ("role", "slab"))
     lower_factor = jnp.linalg.cholesky(total_gram)
     inverse_factor = jax.scipy.linalg.solve_triangular(lower_factor, jnp.eye(ns, dtype=jnp.float32), lower=True)

time: 134 us -> 134 us (level)
  no operation moved by 1% of the time
where the time goes in v9:
time: 134 us; the launch traced here: 133 us
  waiting for transfers between devices  80.1 us (60%)
  other arithmetic  18.9 us (14%)
  Pallas kernels  18.5 us (14%)
  starting transfers between devices  11.1 us (8%)
  local copies, waits for them, and re-layouts  3.77 us (3%)
    ppermute x14, waiting for transfers between devices, allreduce(): value = value + lax.ppermute(value, name, pairs)  53.3 us
    ppermute x2, waiting for transfers between devices, extended(): lax.ppermute(head, axis, [((i + 1) % count, i) for i in range(ends)])  13.7 us
    ppermute x2, waiting for transfers between devices, extended(): lax.ppermute(tail, axis, [(i, (i + 1) % count) for i in range(ends)])  13 us
    pallas_call x1, Pallas kernels, project(): pl.pallas_call(project_kernel, grid=(nk // tk,), in_specs=[pl.BlockSpec((...  9.49 us
    ppermute x2, starting transfers between devices, extended(): lax.ppermute(head, axis, [((i + 1) % count, i) for i in range(ends)])  9.19 us
    pallas_call x1, Pallas kernels, residual(): pl.pallas_call(residual_kernel, grid=(nr // block_rows,), in_specs=[pl.Bl...  8.97 us
    mul x2, other arithmetic, local_terms(): viscosity * (second_diff(ypadded, center, 2, ny_loc) + second_diff(zpadde...  5.22 us
    reduce_sum x1, other arithmetic, on_device(): jnp.sum(inverse_factor[:, :, None, None] * residual3[None], axis=1)  2.96 us
  transfers between devices with their start and end apart: 20, of which 18 were waited for; matrix products, arithmetic and copies ran while one was open for 8% of the time, Pallas kernels for 0%

profile of v9, /device:TPU:0, one launch (start us, length us, event | category | flops | bytes accessed | tf_op | source)
XLA Modules:
  0.0 133.4 jit_solution(7980978080095361599)
XLA Ops:
  0.6 8.8 %collective-permute-start = (f32[4,2,64,256]{3,2,1,0:T(8,128)}, f32[4,2,64,256]{3,2,1,0:T(8,128)S(1)}, u32[]{:S(2)}, u32[]{:S(2)}) collective-permute-start(f32[4,2,64,256]{3,2,1,0:T(8,128)} %param.5), channel_id=1, source_target_pairs={{1,0},{2,1},{3,2},{4,3},{5,4},{6,5},{7,6},{8,7},{9,8},{10,9},{11,1... | collective-permute-start | bytes 1572872 | tf_op jit(solution)/shard_map/ppermute | solution.py:32
  9.5 0.0 collective-permute-start.1
  9.5 0.9 slice_select_fusion.1
  10.4 0.1 collective-permute-start.2
  10.5 1.2 fusion.50
  11.6 0.7 negate_multiply_fusion
  12.4 0.7 dynamic_slice.7
  13.1 0.0 collective-permute-done.2
  13.1 4.4 %fusion.15 = f32[4,2,64,256]{3,2,1,0:T(8,128)S(1)} fusion(f32[4,2,2,256]{3,2,1,0:T(2,128)S(1)} %get-tuple-element.29, f32[4,2,64,256]{3,2,1,0:T(8,128)} %param.5, f32[4,2,2,256]{3,2,1,0:T(2,128)S(1)} %get-tuple-element.28, f32[4,2,64,2]{3,2,1,0:T(8,128)S(1)} %get-tuple-element.25, f32[4,2,64,2]{3,2,1,0:T(8,128)S(1)} %get-tuple-element.24), kind=kLoop, calls=%fused_computation.34 | loop fusion | flops 3276800 | bytes 1089536 | tf_op jit(solution)/shard_map/mul | solution.py:192
  17.6 1.0 slice_subtract_fusion
  18.6 2.4 %collective-permute-done = f32[4,2,64,256]{3,2,1,0:T(8,128)S(1)} collective-permute-done((f32[4,2,64,256]{3,2,1,0:T(8,128)}, f32[4,2,64,256]{3,2,1,0:T(8,128)S(1)}, u32[]{:S(2)}, u32[]{:S(2)}) %collective-permute-start) | collective-permute-done | bytes 524320 | tf_op jit(solution)/shard_map/ppermute | solution.py:32
  21.0 7.5 %collective-permute-done.1 = f32[4,2,64,256]{3,2,1,0:T(8,128)S(1)} collective-permute-done((f32[4,2,64,256]{3,2,1,0:T(8,128)}, f32[4,2,64,256]{3,2,1,0:T(8,128)S(1)}, u32[]{:S(2)}, u32[]{:S(2)}) %collective-permute-start.1) | collective-permute-done | bytes 524320 | tf_op jit(solution)/shard_map/ppermute | solution.py:30
  28.5 1.6 %multiply_add_fusion = (f32[4,2,64,256]{3,2,1,0:T(8,128)S(1)}, f32[4,2,64,256]{3,2,1,0:T(8,128)S(1)}) fusion(f32[4,2,64,256]{3,2,1,0:T(8,128)} %param.5, f32[3,2,64,256]{3,2,1,0:T(8,128)S(1)} %slice.183, f32[1,2,64,256]{3,2,1,0:T(8,128)S(1)} %slice_subtract_fusion, f32[4,2,64,256]{3,2,1,0:T(8,128)S(1)} %collective-permute-done.1, ...), kind=kLoop, calls=%fused_computation.77 | loop fusion | flops 2883584 | bytes 3145984 | tf_op jit(solution)/shard_map/add | solution.py:222
  30.1 0.1 collective-permute-start.5
  30.2 0.1 fusion.49
  30.3 0.4 collective-permute-start.3
  30.7 1.7 %collective-permute-start.4 = (f32[4,2,64,256]{3,2,1,0:T(8,128)S(1)}, f32[4,2,64,256]{3,2,1,0:T(8,128)S(1)}, u32[]{:S(2)}, u32[]{:S(2)}) collective-permute-start(f32[4,2,64,256]{3,2,1,0:T(8,128)S(1)} %get-tuple-element.20), channel_id=1, source_target_pairs={{0,1},{1,2},{2,3},{3,4},{4,5},{5,6},{6,7},{7,8},{8,9},{9,10},{10,1... | collective-permute-start | bytes 1572872 | tf_op jit(solution)/shard_map/ppermute | solution.py:30
  32.5 0.8 fusion.5
  33.3 0.1 fusion.44
  33.4 11.3 %collective-permute-done.3 = f32[4,2,64,256]{3,2,1,0:T(8,128)S(1)} collective-permute-done((f32[4,2,64,256]{3,2,1,0:T(8,128)S(1)}, f32[4,2,64,256]{3,2,1,0:T(8,128)S(1)}, u32[]{:S(2)}, u32[]{:S(2)}) %collective-permute-start.3) | collective-permute-done | bytes 524320 | tf_op jit(solution)/shard_map/ppermute | solution.py:32
  44.7 5.5 %collective-permute-done.4 = f32[4,2,64,256]{3,2,1,0:T(8,128)S(1)} collective-permute-done((f32[4,2,64,256]{3,2,1,0:T(8,128)S(1)}, f32[4,2,64,256]{3,2,1,0:T(8,128)S(1)}, u32[]{:S(2)}, u32[]{:S(2)}) %collective-permute-start.4) | collective-permute-done | bytes 524320 | tf_op jit(solution)/shard_map/ppermute | solution.py:30
  50.3 0.4 fusion.43
  50.7 0.0 copy-start.1
  50.7 0.1 pad_maximum_fusion
  50.8 0.0 copy-start
  50.8 1.0 bitcast_convert_fusion.s_ref
  51.8 9.5 %shard_map.84 = f32[8,256]{1,0:T(8,128)} custom-call(bf16[256,128,256]{2,1,0:T(8,128)(2,1)} %bitcast.17, bf16[8,128,256]{2,1,0:T(8,128)(2,1)} %bitcast_convert_fusion.s_ref), custom_call_target="tpu_custom_call" | custom-call | flops 2147483648 | bytes 17309696 | tf_op jit(solution)/shard_map/pallas_call | solution.py:96
  61.3 0.0 collective-permute-start.6
  61.3 1.4 %collective-permute-done.6 = f32[8,256]{1,0:T(8,128)S(1)} collective-permute-done((f32[8,256]{1,0:T(8,128)}, f32[8,256]{1,0:T(8,128)S(1)}, u32[]{:S(2)}, u32[]{:S(2)}) %collective-permute-start.6) | collective-permute-done | bytes 8224 | tf_op jit(solution)/shard_map/ppermute | solution.py:69
  62.7 0.7 add.161
  63.4 0.0 collective-permute-start.7
  63.4 3.6 %collective-permute-done.7 = f32[8,256]{1,0:T(8,128)S(1)} collective-permute-done((f32[8,256]{1,0:T(8,128)S(1)}, f32[8,256]{1,0:T(8,128)S(1)}, u32[]{:S(2)}, u32[]{:S(2)}) %collective-permute-start.7) | collective-permute-done | bytes 8224 | tf_op jit(solution)/shard_map/ppermute | solution.py:69
  67.0 4.9 %collective-permute-done.8 = f32[8,256]{1,0:T(8,128)S(1)} collective-permute-done((f32[8,256]{1,0:T(8,128)S(1)}, f32[8,256]{1,0:T(8,128)S(1)}, u32[]{:S(2)}, u32[]{:S(2)}) %collective-permute-start.8) | collective-permute-done | bytes 8224 | tf_op jit(solution)/shard_map/ppermute | solution.py:69
  71.9 0.0 collective-permute-start.9
  71.9 3.6 %collective-permute-done.9 = f32[8,256]{1,0:T(8,128)S(1)} collective-permute-done((f32[8,256]{1,0:T(8,128)S(1)}, f32[8,256]{1,0:T(8,128)S(1)}, u32[]{:S(2)}, u32[]{:S(2)}) %collective-permute-start.9) | collective-permute-done | bytes 8224 | tf_op jit(solution)/shard_map/ppermute | solution.py:69
  75.5 0.0 collective-permute-start.10
  75.5 4.9 %collective-permute-done.10 = f32[8,256]{1,0:T(8,128)S(1)} collective-permute-done((f32[8,256]{1,0:T(8,128)S(1)}, f32[8,256]{1,0:T(8,128)S(1)}, u32[]{:S(2)}, u32[]{:S(2)}) %collective-permute-start.10) | collective-permute-done | bytes 8224 | tf_op jit(solution)/shard_map/ppermute | solution.py:69
  80.4 3.6 %collective-permute-done.11 = f32[8,256]{1,0:T(8,128)S(1)} collective-permute-done((f32[8,256]{1,0:T(8,128)S(1)}, f32[8,256]{1,0:T(8,128)S(1)}, u32[]{:S(2)}, u32[]{:S(2)}) %collective-permute-start.11) | collective-permute-done | bytes 8224 | tf_op jit(solution)/shard_map/ppermute | solution.py:69
  84.1 4.8 %collective-permute-done.12 = f32[8,256]{1,0:T(8,128)S(1)} collective-permute-done((f32[8,256]{1,0:T(8,128)S(1)}, f32[8,256]{1,0:T(8,128)S(1)}, u32[]{:S(2)}, u32[]{:S(2)}) %collective-permute-start.12) | collective-permute-done | bytes 8224 | tf_op jit(solution)/shard_map/ppermute | solution.py:69
  88.9 0.6 add.167.c_ref
  89.5 9.0 %shard_map.85 = (f32[8,128,256]{2,1,0:T(8,128)}, f32[36,256]{1,0:T(8,128)}) custom-call(f32[8,256]{1,0:T(8,128)} %add.167.c_ref, bf16[256,128,256]{2,1,0:T(8,128)(2,1)} %bitcast.18, f32[8,128,256]{2,1,0:T(8,128)} %bitcast.19), custom_call_target="tpu_custom_call" | custom-call | flops 2147483648 | bytes 18874368 | tf_op jit(solution)/shard_map/pallas_call | solution.py:148
  98.5 0.9 reduce_sum.18
  99.4 0.8 gather_fusion
  100.2 0.1 reshape.38
  100.2 0.1 copy.20
  100.3 0.0 collective-permute-start.13
  100.3 1.2 collective-permute-done.13
  101.5 0.0 collective-permute-start.14
  101.5 3.6 %collective-permute-done.14 = f32[8,8]{0,1:T(8,128)S(1)} collective-permute-done((f32[8,8]{0,1:T(8,128)S(1)}, f32[8,8]{0,1:T(8,128)S(1)}, u32[]{:S(2)}, u32[]{:S(2)}) %collective-permute-start.14) | collective-permute-done | bytes 288 | tf_op jit(solution)/shard_map/ppermute | solution.py:69
  105.1 0.0 collective-permute-start.15
  105.1 4.8 %collective-permute-done.15 = f32[8,8]{0,1:T(8,128)S(1)} collective-permute-done((f32[8,8]{0,1:T(8,128)S(1)}, f32[8,8]{0,1:T(8,128)S(1)}, u32[]{:S(2)}, u32[]{:S(2)}) %collective-permute-start.15) | collective-permute-done | bytes 288 | tf_op jit(solution)/shard_map/ppermute | solution.py:69
  109.9 3.6 %collective-permute-done.16 = f32[8,8]{0,1:T(8,128)S(1)} collective-permute-done((f32[8,8]{0,1:T(8,128)S(1)}, f32[8,8]{0,1:T(8,128)S(1)}, u32[]{:S(2)}, u32[]{:S(2)}) %collective-permute-start.16) | collective-permute-done | bytes 288 | tf_op jit(solution)/shard_map/ppermute | solution.py:69
  113.5 0.0 collective-permute-start.17
  113.5 4.8 %collective-permute-done.17 = f32[8,8]{0,1:T(8,128)S(1)} collective-permute-done((f32[8,8]{0,1:T(8,128)S(1)}, f32[8,8]{0,1:T(8,128)S(1)}, u32[]{:S(2)}, u32[]{:S(2)}) %collective-permute-start.17) | collective-permute-done | bytes 288 | tf_op jit(solution)/shard_map/ppermute | solution.py:69
  118.4 3.6 %collective-permute-done.18 = f32[8,8]{0,1:T(8,128)S(1)} collective-permute-done((f32[8,8]{0,1:T(8,128)S(1)}, f32[8,8]{0,1:T(8,128)S(1)}, u32[]{:S(2)}, u32[]{:S(2)}) %collective-permute-start.18) | collective-permute-done | bytes 288 | tf_op jit(solution)/shard_map/ppermute | solution.py:69
  122.0 4.8 %collective-permute-done.19 = f32[8,8]{0,1:T(8,128)S(1)} collective-permute-done((f32[8,8]{0,1:T(8,128)S(1)}, f32[8,8]{0,1:T(8,128)S(1)}, u32[]{:S(2)}, u32[]{:S(2)}) %collective-permute-start.19) | collective-permute-done | bytes 288 | tf_op jit(solution)/shard_map/ppermute | solution.py:69
  126.8 0.1 copy.21
  126.9 0.7 cholesky.20
  127.6 0.6 compare_reduce_fusion
  128.3 0.6 select_bitcast_fusion
  128.9 0.6 custom-call.7
  129.5 0.2 fusion.45
  129.7 0.7 copy.23
  130.4 3.0 %multiply_reduce_fusion = f32[8,128,256]{2,1,0:T(8,128)} fusion(f32[8,128,256]{2,1,0:T(8,128)} %get-tuple-element.7, f32[8,8]{1,0:T(8,128)S(1)} %fusion.45), kind=kLoop, calls=%fused_computation.1 | loop fusion | flops 3932160 | bytes 2097408 | tf_op jit(solution)/shard_map/reduce_sum | solution.py:236
  (31 shorter events, 0.2 us)
Async XLA Ops:
  0.6 20.3 %collective-permute-start = (f32[4,2,64,256]{3,2,1,0:T(8,128)}, f32[4,2,64,256]{3,2,1,0:T(8,128)S(1)}, u32[]{:S(2)}, u32[]{:S(2)}) collective-permute-start(f32[4,2,64,256]{3,2,1,0:T(8,128)} %param.5), channel_id=1, source_target_pairs={{1,0},{2,1},{3,2},{4,3},{5,4},{6,5},{7,6},{8,7},{9,8},{10,9},{11,1... | collective-permute-start | bytes 1572872 | tf_op jit(solution)/shard_map/ppermute | solution.py:32
  9.5 19.0 %collective-permute-start.1 = (f32[4,2,64,256]{3,2,1,0:T(8,128)}, f32[4,2,64,256]{3,2,1,0:T(8,128)S(1)}, u32[]{:S(2)}, u32[]{:S(2)}) collective-permute-start(f32[4,2,64,256]{3,2,1,0:T(8,128)} %param.5), channel_id=1, source_target_pairs={{0,1},{1,2},{2,3},{3,4},{4,5},{5,6},{6,7},{7,8},{8,9},{9,10},{10,1... | collective-permute-start | bytes 1572872 | tf_op jit(solution)/shard_map/ppermute | solution.py:30
  10.4 2.7 %collective-permute-start.2 = (f32[4,2,2,256]{3,2,1,0:T(2,128)S(1)}, f32[4,2,2,256]{3,2,1,0:T(2,128)S(1)}, u32[]{:S(2)}, u32[]{:S(2)}) collective-permute-start(f32[4,2,2,256]{3,2,1,0:T(2,128)S(1)} %slice_select_fusion.1), channel_id=1, source_target_pairs={{0,64},{64,0},{1,65},{65,1},{2,66},{66,2},{3,67},{67,3},{4,68},{68... | collective-permute-start | bytes 49160 | tf_op jit(solution)/shard_map/ppermute | solution.py:22
  30.1 2.3 %collective-permute-start.5 = (f32[4,2,2,256]{3,2,1,0:T(2,128)S(1)}, f32[4,2,2,256]{3,2,1,0:T(2,128)S(1)}, u32[]{:S(2)}, u32[]{:S(2)}) collective-permute-start(f32[4,2,2,256]{3,2,1,0:T(2,128)S(1)} %slice_select_fusion), channel_id=1, source_target_pairs={{0,64},{64,0},{1,65},{65,1},{2,66},{66,2},{3,67},{67,3},{4,68},{68... | collective-permute-start | bytes 49160 | tf_op jit(solution)/shard_map/ppermute | solution.py:22
  30.3 14.4 %collective-permute-start.3 = (f32[4,2,64,256]{3,2,1,0:T(8,128)S(1)}, f32[4,2,64,256]{3,2,1,0:T(8,128)S(1)}, u32[]{:S(2)}, u32[]{:S(2)}) collective-permute-start(f32[4,2,64,256]{3,2,1,0:T(8,128)S(1)} %get-tuple-element.20), channel_id=1, source_target_pairs={{1,0},{2,1},{3,2},{4,3},{5,4},{6,5},{7,6},{8,7},{9,8},{10,9},{11,1... | collective-permute-start | bytes 1572872 | tf_op jit(solution)/shard_map/ppermute | solution.py:32
  30.7 19.6 %collective-permute-start.4 = (f32[4,2,64,256]{3,2,1,0:T(8,128)S(1)}, f32[4,2,64,256]{3,2,1,0:T(8,128)S(1)}, u32[]{:S(2)}, u32[]{:S(2)}) collective-permute-start(f32[4,2,64,256]{3,2,1,0:T(8,128)S(1)} %get-tuple-element.20), channel_id=1, source_target_pairs={{0,1},{1,2},{2,3},{3,4},{4,5},{5,6},{6,7},{7,8},{8,9},{9,10},{10,1... | collective-permute-start | bytes 1572872 | tf_op jit(solution)/shard_map/ppermute | solution.py:30
  50.7 10.6 %copy-start.1 = (f32[4,2,64,256]{3,2,1,0:T(8,128)}, f32[4,2,64,256]{3,2,1,0:T(8,128)S(1)}, u32[]{:S(2)}) copy-start(f32[4,2,64,256]{3,2,1,0:T(8,128)S(1)} %fusion.43) | copy-start | bytes 1572868
  50.8 10.5 %copy-start = (f32[8,2,64,256]{3,2,1,0:T(8,128)}, f32[8,2,64,256]{3,2,1,0:T(8,128)S(1)}, u32[]{:S(2)}) copy-start(f32[8,2,64,256]{3,2,1,0:T(8,128)S(1)} %pad_maximum_fusion) | copy-start | bytes 3145732
  51.8 32.3 %copy-start.2 = (s32[64]{0:T(128)S(1)}, s32[64]{0:T(128)}, u32[]{:S(2)}) copy-start(s32[64]{0:T(128)} %constant.99) | copy-start | bytes 772
  61.3 1.4 %collective-permute-start.6 = (f32[8,256]{1,0:T(8,128)}, f32[8,256]{1,0:T(8,128)S(1)}, u32[]{:S(2)}, u32[]{:S(2)}) collective-permute-start(f32[8,256]{1,0:T(8,128)} %shard_map.84), channel_id=1, source_target_pairs={{0,64},{64,0},{1,65},{65,1},{2,66},{66,2},{3,67},{67,3},{4,68},{68... | collective-permute-start | bytes 24584 | tf_op jit(solution)/shard_map/ppermute | solution.py:69
  63.4 3.7 %collective-permute-start.7 = (f32[8,256]{1,0:T(8,128)S(1)}, f32[8,256]{1,0:T(8,128)S(1)}, u32[]{:S(2)}, u32[]{:S(2)}) collective-permute-start(f32[8,256]{1,0:T(8,128)S(1)} %add.161), channel_id=1, source_target_pairs={{0,1},{1,0},{2,3},{3,2},{4,5},{5,4},{6,7},{7,6},{8,9},{9,8},{10,11... | collective-permute-start | bytes 24584 | tf_op jit(solution)/shard_map/ppermute | solution.py:69
  67.0 4.9 %collective-permute-start.8 = (f32[8,256]{1,0:T(8,128)S(1)}, f32[8,256]{1,0:T(8,128)S(1)}, u32[]{:S(2)}, u32[]{:S(2)}) collective-permute-start(f32[8,256]{1,0:T(8,128)S(1)} %add.162), channel_id=1, source_target_pairs={{0,3},{1,2},{2,1},{3,0},{4,7},{5,6},{6,5},{7,4},{8,11},{9,10},{10,... | collective-permute-start | bytes 24584 | tf_op jit(solution)/shard_map/ppermute | solution.py:69
  71.9 3.7 %collective-permute-start.9 = (f32[8,256]{1,0:T(8,128)S(1)}, f32[8,256]{1,0:T(8,128)S(1)}, u32[]{:S(2)}, u32[]{:S(2)}) collective-permute-start(f32[8,256]{1,0:T(8,128)S(1)} %add.163), channel_id=1, source_target_pairs={{0,4},{1,5},{2,6},{3,7},{4,0},{5,1},{6,2},{7,3},{8,12},{9,13},{10,... | collective-permute-start | bytes 24584 | tf_op jit(solution)/shard_map/ppermute | solution.py:69
  75.5 4.9 %collective-permute-start.10 = (f32[8,256]{1,0:T(8,128)S(1)}, f32[8,256]{1,0:T(8,128)S(1)}, u32[]{:S(2)}, u32[]{:S(2)}) collective-permute-start(f32[8,256]{1,0:T(8,128)S(1)} %add.164), channel_id=1, source_target_pairs={{0,12},{1,13},{2,14},{3,15},{4,8},{5,9},{6,10},{7,11},{8,4},{9,5},... | collective-permute-start | bytes 24584 | tf_op jit(solution)/shard_map/ppermute | solution.py:69
  80.4 3.7 %collective-permute-start.11 = (f32[8,256]{1,0:T(8,128)S(1)}, f32[8,256]{1,0:T(8,128)S(1)}, u32[]{:S(2)}, u32[]{:S(2)}) collective-permute-start(f32[8,256]{1,0:T(8,128)S(1)} %add.165), channel_id=1, source_target_pairs={{0,16},{1,17},{2,18},{3,19},{4,20},{5,21},{6,22},{7,23},{8,24},{9,... | collective-permute-start | bytes 24584 | tf_op jit(solution)/shard_map/ppermute | solution.py:69
  84.0 4.9 %collective-permute-start.12 = (f32[8,256]{1,0:T(8,128)S(1)}, f32[8,256]{1,0:T(8,128)S(1)}, u32[]{:S(2)}, u32[]{:S(2)}) collective-permute-start(f32[8,256]{1,0:T(8,128)S(1)} %add.166), channel_id=1, source_target_pairs={{0,48},{1,49},{2,50},{3,51},{4,52},{5,53},{6,54},{7,55},{8,56},{9,... | collective-permute-start | bytes 24584 | tf_op jit(solution)/shard_map/ppermute | solution.py:69
  100.3 1.2 collective-permute-start.13
  101.5 3.6 %collective-permute-start.14 = (f32[8,8]{0,1:T(8,128)S(1)}, f32[8,8]{0,1:T(8,128)S(1)}, u32[]{:S(2)}, u32[]{:S(2)}) collective-permute-start(f32[8,8]{0,1:T(8,128)S(1)} %add.170), channel_id=1, source_target_pairs={{0,1},{1,0},{2,3},{3,2},{4,5},{5,4},{6,7},{7,6},{8,9},{9,8},{10,11... | collective-permute-start | bytes 776 | tf_op jit(solution)/shard_map/ppermute | solution.py:69
  105.1 4.8 %collective-permute-start.15 = (f32[8,8]{0,1:T(8,128)S(1)}, f32[8,8]{0,1:T(8,128)S(1)}, u32[]{:S(2)}, u32[]{:S(2)}) collective-permute-start(f32[8,8]{0,1:T(8,128)S(1)} %add.171), channel_id=1, source_target_pairs={{0,3},{1,2},{2,1},{3,0},{4,7},{5,6},{6,5},{7,4},{8,11},{9,10},{10,... | collective-permute-start | bytes 776 | tf_op jit(solution)/shard_map/ppermute | solution.py:69
  109.9 3.6 %collective-permute-start.16 = (f32[8,8]{0,1:T(8,128)S(1)}, f32[8,8]{0,1:T(8,128)S(1)}, u32[]{:S(2)}, u32[]{:S(2)}) collective-permute-start(f32[8,8]{0,1:T(8,128)S(1)} %add.172), channel_id=1, source_target_pairs={{0,4},{1,5},{2,6},{3,7},{4,0},{5,1},{6,2},{7,3},{8,12},{9,13},{10,... | collective-permute-start | bytes 776 | tf_op jit(solution)/shard_map/ppermute | solution.py:69
  113.5 4.8 %collective-permute-start.17 = (f32[8,8]{0,1:T(8,128)S(1)}, f32[8,8]{0,1:T(8,128)S(1)}, u32[]{:S(2)}, u32[]{:S(2)}) collective-permute-start(f32[8,8]{0,1:T(8,128)S(1)} %add.173), channel_id=1, source_target_pairs={{0,12},{1,13},{2,14},{3,15},{4,8},{5,9},{6,10},{7,11},{8,4},{9,5},... | collective-permute-start | bytes 776 | tf_op jit(solution)/shard_map/ppermute | solution.py:69
  118.4 3.6 %collective-permute-start.18 = (f32[8,8]{0,1:T(8,128)S(1)}, f32[8,8]{0,1:T(8,128)S(1)}, u32[]{:S(2)}, u32[]{:S(2)}) collective-permute-start(f32[8,8]{0,1:T(8,128)S(1)} %add.174), channel_id=1, source_target_pairs={{0,16},{1,17},{2,18},{3,19},{4,20},{5,21},{6,22},{7,23},{8,24},{9,... | collective-permute-start | bytes 776 | tf_op jit(solution)/shard_map/ppermute | solution.py:69
  122.0 4.8 %collective-permute-start.19 = (f32[8,8]{0,1:T(8,128)S(1)}, f32[8,8]{0,1:T(8,128)S(1)}, u32[]{:S(2)}, u32[]{:S(2)}) collective-permute-start(f32[8,8]{0,1:T(8,128)S(1)} %add.175), channel_id=1, source_target_pairs={{0,48},{1,49},{2,50},{3,51},{4,52},{5,53},{6,54},{7,55},{8,56},{9,... | collective-permute-start | bytes 776 | tf_op jit(solution)/shard_map/ppermute | solution.py:69

commit v10 on v9

--- a/solution.py
+++ b/solution.py
@@ -138,7 +138,17 @@
 
     @pl.when(step == pl.num_programs(0) - 1)
     def _():
-        g_ref[...] = jnp.sum(acc_ref[...], axis=1)
+        row = lax.broadcasted_iota(jnp.int32, (ns, ns), 0)
+        col = lax.broadcasted_iota(jnp.int32, (ns, ns), 1)
+        gram = jnp.zeros((ns, ns), jnp.float32)
+        p = 0
+        for a in range(ns):
+            for b in range(a, ns):
+                total = jnp.sum(acc_ref[p])
+                hit = ((row == a) & (col == b)) | ((row == b) & (col == a))
+                gram = jnp.where(hit, total, gram)
+                p += 1
+        g_ref[...] = gram
 
 
 def residual(coeffs_t, basis3, snaps3, block_rows=2 * ROWS):
@@ -152,23 +162,16 @@
                   pl.BlockSpec((nk, block_rows, nz), lambda j: (0, j, 0)),
                   pl.BlockSpec((ns, block_rows, nz), lambda j: (0, j, 0))],
         out_specs=[pl.BlockSpec((ns, block_rows, nz), lambda j: (0, j, 0)),
-                   pl.BlockSpec((pairs, nz), lambda j: (0, 0))],
+                   pl.BlockSpec((ns, ns), lambda j: (0, 0))],
         out_shape=[jax.ShapeDtypeStruct((ns, nr, nz), jnp.float32),
-                   jax.ShapeDtypeStruct((pairs, nz), jnp.float32)],
+                   jax.ShapeDtypeStruct((ns, ns), jnp.float32)],
         scratch_shapes=[pltpu.VMEM((ns * ROWS, nk * ROWS), jnp.bfloat16),
                         pltpu.VMEM((pairs, ROWS // 2, nz), jnp.float32)],
         compiler_params=pltpu.CompilerParams(dimension_semantics=("arbitrary",)),
         cost_estimate=pl.CostEstimate(flops=2 * ns * ROWS * nk * ROWS * nz * (nr // ROWS), transcendentals=0,
                                       bytes_accessed=nk * nr * nz * 2 + 2 * ns * nr * nz * 4),
     )(coeffs_t, basis3, snaps3)
-    sums = jnp.sum(g, axis=1)
-    table = np.zeros((ns, ns), np.int32)
-    p = 0
-    for a in range(ns):
-        for b in range(a, ns):
-            table[a, b] = p; table[b, a] = p; p += 1
-    gram = sums[jnp.asarray(table)]
-    return w, gram
+    return w, g
 
 
 def offset_slice(padded, offset, dimension, length):

time: 134 us -> 126 us (0.940)
  waiting for transfers between devices: 80.1 us -> 60.1 us
  starting transfers between devices: 11.1 us -> 24.3 us
    ppermute x2, waiting for transfers between devices: 13.7 us -> 0.01 us  [extended(): lax.ppermute(head, axis, [((i + 1) % count, i) for i in range(ends)])]
    ppermute x14, starting transfers between devices: 0.04 us -> 7.67 us  [allreduce(): value = value + lax.ppermute(value, name, pairs)]
    ppermute x14, waiting for transfers between devices: 53.3 us -> 45.7 us  [allreduce(): value = value + lax.ppermute(value, name, pairs)]
    ppermute x2, starting transfers between devices: 9.19 us -> 14.3 us  [extended(): lax.ppermute(head, axis, [((i + 1) % count, i) for i in range(ends)])]
  transfers between devices with their start and end apart: 20 -> 20, of which waited for: 18 -> 16; matrix products, arithmetic and copies ran while one was open for 8% -> 8% of each run, Pallas kernels for 0% -> 0%
where the time goes in v10:
time: 126 us; the launch traced here: 125 us
  waiting for transfers between devices  60.1 us (48%)
  starting transfers between devices  24.3 us (19%)
  Pallas kernels  18.6 us (15%)
  other arithmetic  18 us (14%)
  local copies, waits for them, and re-layouts  3.59 us (3%)
    ppermute x14, waiting for transfers between devices, allreduce(): value = value + lax.ppermute(value, name, pairs)  45.7 us
    ppermute x2, waiting for transfers between devices, extended(): lax.ppermute(tail, axis, [(i, (i + 1) % count) for i in range(ends)])  14.4 us
    ppermute x2, starting transfers between devices, extended(): lax.ppermute(head, axis, [((i + 1) % count, i) for i in range(ends)])  14.3 us
    pallas_call x1, Pallas kernels, project(): pl.pallas_call(project_kernel, grid=(nk // tk,), in_specs=[pl.BlockSpec((...  9.48 us
    pallas_call x1, Pallas kernels, residual(): pl.pallas_call(residual_kernel, grid=(nr // block_rows,), in_specs=[pl.Bl...  9.09 us
    ppermute x14, starting transfers between devices, allreduce(): value = value + lax.ppermute(value, name, pairs)  7.67 us
    mul x2, other arithmetic, local_terms(): viscosity * (second_diff(ypadded, center, 2, ny_loc) + second_diff(zpadde...  5.22 us
    reduce_sum x1, other arithmetic, on_device(): jnp.sum(inverse_factor[:, :, None, None] * residual3[None], axis=1)  2.96 us
  transfers between devices with their start and end apart: 20, of which 16 were waited for; matrix products, arithmetic and copies ran while one was open for 8% of the time, Pallas kernels for 0%

profile of v10, /device:TPU:0, one launch (start us, length us, event | category | flops | bytes accessed | tf_op | source)
XLA Modules:
  0.0 125.5 jit_solution(16379800374079841892)
XLA Ops:
  0.6 2.1 %collective-permute-start.1 = (f32[4,2,64,256]{3,2,1,0:T(8,128)}, f32[4,2,64,256]{3,2,1,0:T(8,128)S(1)}, u32[]{:S(2)}, u32[]{:S(2)}) collective-permute-start(f32[4,2,64,256]{3,2,1,0:T(8,128)} %param.4), channel_id=1, source_target_pairs={{0,1},{1,2},{2,3},{3,4},{4,5},{5,6},{6,7},{7,8},{8,9},{9,10},{10,1... | collective-permute-start | bytes 1572872 | tf_op jit(solution)/shard_map/ppermute | solution.py:30
  2.7 6.8 %collective-permute-start = (f32[4,2,64,256]{3,2,1,0:T(8,128)}, f32[4,2,64,256]{3,2,1,0:T(8,128)S(1)}, u32[]{:S(2)}, u32[]{:S(2)}) collective-permute-start(f32[4,2,64,256]{3,2,1,0:T(8,128)} %param.4), channel_id=1, source_target_pairs={{1,0},{2,1},{3,2},{4,3},{5,4},{6,5},{7,6},{8,7},{9,8},{10,9},{11,1... | collective-permute-start | bytes 1572872 | tf_op jit(solution)/shard_map/ppermute | solution.py:32
  9.5 0.9 slice_select_fusion.1
  10.4 0.1 collective-permute-start.2
  10.5 1.2 fusion.50
  11.7 0.7 negate_multiply_fusion
  12.4 0.7 dynamic_slice.7
  13.2 0.0 collective-permute-done.2
  13.2 4.4 %fusion.15 = f32[4,2,64,256]{3,2,1,0:T(8,128)S(1)} fusion(f32[4,2,2,256]{3,2,1,0:T(2,128)S(1)} %get-tuple-element.25, f32[4,2,64,256]{3,2,1,0:T(8,128)} %param.4, f32[4,2,2,256]{3,2,1,0:T(2,128)S(1)} %get-tuple-element.24, f32[4,2,64,2]{3,2,1,0:T(8,128)S(1)} %get-tuple-element.21, f32[4,2,64,2]{3,2,1,0:T(8,128)S(1)} %get-tuple-element.20), kind=kLoop, calls=%fused_computation.33 | loop fusion | flops 3276800 | bytes 1089536 | tf_op jit(solution)/shard_map/mul | solution.py:195
  17.6 1.0 slice_subtract_fusion
  18.6 3.0 %collective-permute-done.1 = f32[4,2,64,256]{3,2,1,0:T(8,128)S(1)} collective-permute-done((f32[4,2,64,256]{3,2,1,0:T(8,128)}, f32[4,2,64,256]{3,2,1,0:T(8,128)S(1)}, u32[]{:S(2)}, u32[]{:S(2)}) %collective-permute-start.1) | collective-permute-done | bytes 524320 | tf_op jit(solution)/shard_map/ppermute | solution.py:30
  21.6 0.0 collective-permute-done
  21.6 1.6 %multiply_add_fusion = (f32[4,2,64,256]{3,2,1,0:T(8,128)S(1)}, f32[4,2,64,256]{3,2,1,0:T(8,128)S(1)}) fusion(f32[4,2,64,256]{3,2,1,0:T(8,128)} %param.4, f32[3,2,64,256]{3,2,1,0:T(8,128)S(1)} %slice.181, f32[1,2,64,256]{3,2,1,0:T(8,128)S(1)} %slice_subtract_fusion, f32[4,2,64,256]{3,2,1,0:T(8,128)S(1)} %collective-permute-done.1, ...), kind=kLoop, calls=%fused_computation.76 | loop fusion | flops 2883584 | bytes 3145984 | tf_op jit(solution)/shard_map/add | solution.py:225
  23.2 0.1 collective-permute-start.5
  23.3 0.1 fusion.49
  23.5 0.1 collective-permute-start.4
  23.5 7.5 %collective-permute-start.3 = (f32[4,2,64,256]{3,2,1,0:T(8,128)S(1)}, f32[4,2,64,256]{3,2,1,0:T(8,128)S(1)}, u32[]{:S(2)}, u32[]{:S(2)}) collective-permute-start(f32[4,2,64,256]{3,2,1,0:T(8,128)S(1)} %get-tuple-element.16), channel_id=1, source_target_pairs={{1,0},{2,1},{3,2},{4,3},{5,4},{6,5},{7,6},{8,7},{9,8},{10,9},{11,1... | collective-permute-start | bytes 1572872 | tf_op jit(solution)/shard_map/ppermute | solution.py:32
  31.0 0.0 collective-permute-done.5
  31.0 0.8 fusion.5
  31.9 0.1 fusion.44
  32.0 11.4 %collective-permute-done.4 = f32[4,2,64,256]{3,2,1,0:T(8,128)S(1)} collective-permute-done((f32[4,2,64,256]{3,2,1,0:T(8,128)S(1)}, f32[4,2,64,256]{3,2,1,0:T(8,128)S(1)}, u32[]{:S(2)}, u32[]{:S(2)}) %collective-permute-start.4) | collective-permute-done | bytes 524320 | tf_op jit(solution)/shard_map/ppermute | solution.py:30
  43.4 0.0 collective-permute-done.3
  43.4 0.4 fusion.43
  43.8 0.0 copy-start.1
  43.8 0.1 pad_maximum_fusion
  43.9 0.0 copy-start
  43.9 1.0 bitcast_convert_fusion.s_ref
  44.9 9.5 %shard_map.75 = f32[8,256]{1,0:T(8,128)} custom-call(bf16[256,128,256]{2,1,0:T(8,128)(2,1)} %bitcast.17, bf16[8,128,256]{2,1,0:T(8,128)(2,1)} %bitcast_convert_fusion.s_ref), custom_call_target="tpu_custom_call" | custom-call | flops 2147483648 | bytes 17309696 | tf_op jit(solution)/shard_map/pallas_call | solution.py:96
  54.3 1.4 %collective-permute-done.6 = f32[8,256]{1,0:T(8,128)S(1)} collective-permute-done((f32[8,256]{1,0:T(8,128)}, f32[8,256]{1,0:T(8,128)S(1)}, u32[]{:S(2)}, u32[]{:S(2)}) %collective-permute-start.6) | collective-permute-done | bytes 8224 | tf_op jit(solution)/shard_map/ppermute | solution.py:69
  55.7 0.7 add.155
  56.4 0.0 collective-permute-start.7
  56.4 3.6 %collective-permute-done.7 = f32[8,256]{1,0:T(8,128)S(1)} collective-permute-done((f32[8,256]{1,0:T(8,128)S(1)}, f32[8,256]{1,0:T(8,128)S(1)}, u32[]{:S(2)}, u32[]{:S(2)}) %collective-permute-start.7) | collective-permute-done | bytes 8224 | tf_op jit(solution)/shard_map/ppermute | solution.py:69
  60.1 0.0 collective-permute-start.8
  60.1 4.9 %collective-permute-done.8 = f32[8,256]{1,0:T(8,128)S(1)} collective-permute-done((f32[8,256]{1,0:T(8,128)S(1)}, f32[8,256]{1,0:T(8,128)S(1)}, u32[]{:S(2)}, u32[]{:S(2)}) %collective-permute-start.8) | collective-permute-done | bytes 8224 | tf_op jit(solution)/shard_map/ppermute | solution.py:69
  64.9 3.6 %collective-permute-done.9 = f32[8,256]{1,0:T(8,128)S(1)} collective-permute-done((f32[8,256]{1,0:T(8,128)S(1)}, f32[8,256]{1,0:T(8,128)S(1)}, u32[]{:S(2)}, u32[]{:S(2)}) %collective-permute-start.9) | collective-permute-done | bytes 8224 | tf_op jit(solution)/shard_map/ppermute | solution.py:69
  68.6 4.9 %collective-permute-done.10 = f32[8,256]{1,0:T(8,128)S(1)} collective-permute-done((f32[8,256]{1,0:T(8,128)S(1)}, f32[8,256]{1,0:T(8,128)S(1)}, u32[]{:S(2)}, u32[]{:S(2)}) %collective-permute-start.10) | collective-permute-done | bytes 8224 | tf_op jit(solution)/shard_map/ppermute | solution.py:69
  73.5 0.0 collective-permute-start.11
  73.5 3.6 %collective-permute-done.11 = f32[8,256]{1,0:T(8,128)S(1)} collective-permute-done((f32[8,256]{1,0:T(8,128)S(1)}, f32[8,256]{1,0:T(8,128)S(1)}, u32[]{:S(2)}, u32[]{:S(2)}) %collective-permute-start.11) | collective-permute-done | bytes 8224 | tf_op jit(solution)/shard_map/ppermute | solution.py:69
  77.1 1.9 %collective-permute-start.12 = (f32[8,256]{1,0:T(8,128)S(1)}, f32[8,256]{1,0:T(8,128)S(1)}, u32[]{:S(2)}, u32[]{:S(2)}) collective-permute-start(f32[8,256]{1,0:T(8,128)S(1)} %add.160), channel_id=1, source_target_pairs={{0,48},{1,49},{2,50},{3,51},{4,52},{5,53},{6,54},{7,55},{8,56},{9,... | collective-permute-start | bytes 24584 | tf_op jit(solution)/shard_map/ppermute | solution.py:69
  79.0 3.0 %collective-permute-done.12 = f32[8,256]{1,0:T(8,128)S(1)} collective-permute-done((f32[8,256]{1,0:T(8,128)S(1)}, f32[8,256]{1,0:T(8,128)S(1)}, u32[]{:S(2)}, u32[]{:S(2)}) %collective-permute-start.12) | collective-permute-done | bytes 8224 | tf_op jit(solution)/shard_map/ppermute | solution.py:69
  82.0 0.6 add.161.c_ref
  82.6 9.1 %shard_map.76 = (f32[8,128,256]{2,1,0:T(8,128)}, f32[8,8]{1,0:T(8,128)}) custom-call(f32[8,256]{1,0:T(8,128)} %add.161.c_ref, bf16[256,128,256]{2,1,0:T(8,128)(2,1)} %bitcast.18, f32[8,128,256]{2,1,0:T(8,128)} %bitcast.19), custom_call_target="tpu_custom_call" | custom-call | flops 2147483648 | bytes 18874368 | tf_op jit(solution)/shard_map/pallas_call | solution.py:158
  91.7 0.8 copy.14
  92.4 1.2 collective-permute-done.13
  93.6 0.0 collective-permute-start.14
  93.6 3.6 %collective-permute-done.14 = f32[8,8]{0,1:T(8,128)S(1)} collective-permute-done((f32[8,8]{0,1:T(8,128)S(1)}, f32[8,8]{0,1:T(8,128)S(1)}, u32[]{:S(2)}, u32[]{:S(2)}) %collective-permute-start.14) | collective-permute-done | bytes 288 | tf_op jit(solution)/shard_map/ppermute | solution.py:69
  97.2 1.9 %collective-permute-start.15 = (f32[8,8]{0,1:T(8,128)S(1)}, f32[8,8]{0,1:T(8,128)S(1)}, u32[]{:S(2)}, u32[]{:S(2)}) collective-permute-start(f32[8,8]{0,1:T(8,128)S(1)} %add.163), channel_id=1, source_target_pairs={{0,3},{1,2},{2,1},{3,0},{4,7},{5,6},{6,5},{7,4},{8,11},{9,10},{10,... | collective-permute-start | bytes 776 | tf_op jit(solution)/shard_map/ppermute | solution.py:69
  99.1 2.9 %collective-permute-done.15 = f32[8,8]{0,1:T(8,128)S(1)} collective-permute-done((f32[8,8]{0,1:T(8,128)S(1)}, f32[8,8]{0,1:T(8,128)S(1)}, u32[]{:S(2)}, u32[]{:S(2)}) %collective-permute-start.15) | collective-permute-done | bytes 288 | tf_op jit(solution)/shard_map/ppermute | solution.py:69
  102.0 0.0 collective-permute-start.16
  102.0 3.6 %collective-permute-done.16 = f32[8,8]{0,1:T(8,128)S(1)} collective-permute-done((f32[8,8]{0,1:T(8,128)S(1)}, f32[8,8]{0,1:T(8,128)S(1)}, u32[]{:S(2)}, u32[]{:S(2)}) %collective-permute-start.16) | collective-permute-done | bytes 288 | tf_op jit(solution)/shard_map/ppermute | solution.py:69
  105.7 1.9 %collective-permute-start.17 = (f32[8,8]{0,1:T(8,128)S(1)}, f32[8,8]{0,1:T(8,128)S(1)}, u32[]{:S(2)}, u32[]{:S(2)}) collective-permute-start(f32[8,8]{0,1:T(8,128)S(1)} %add.165), channel_id=1, source_target_pairs={{0,12},{1,13},{2,14},{3,15},{4,8},{5,9},{6,10},{7,11},{8,4},{9,5},... | collective-permute-start | bytes 776 | tf_op jit(solution)/shard_map/ppermute | solution.py:69
  107.6 2.9 %collective-permute-done.17 = f32[8,8]{0,1:T(8,128)S(1)} collective-permute-done((f32[8,8]{0,1:T(8,128)S(1)}, f32[8,8]{0,1:T(8,128)S(1)}, u32[]{:S(2)}, u32[]{:S(2)}) %collective-permute-start.17) | collective-permute-done | bytes 288 | tf_op jit(solution)/shard_map/ppermute | solution.py:69
  110.5 0.0 collective-permute-start.18
  110.5 3.6 %collective-permute-done.18 = f32[8,8]{0,1:T(8,128)S(1)} collective-permute-done((f32[8,8]{0,1:T(8,128)S(1)}, f32[8,8]{0,1:T(8,128)S(1)}, u32[]{:S(2)}, u32[]{:S(2)}) %collective-permute-start.18) | collective-permute-done | bytes 288 | tf_op jit(solution)/shard_map/ppermute | solution.py:69
  114.1 1.9 %collective-permute-start.19 = (f32[8,8]{0,1:T(8,128)S(1)}, f32[8,8]{0,1:T(8,128)S(1)}, u32[]{:S(2)}, u32[]{:S(2)}) collective-permute-start(f32[8,8]{0,1:T(8,128)S(1)} %add.167), channel_id=1, source_target_pairs={{0,48},{1,49},{2,50},{3,51},{4,52},{5,53},{6,54},{7,55},{8,56},{9,... | collective-permute-start | bytes 776 | tf_op jit(solution)/shard_map/ppermute | solution.py:69
  116.0 2.9 %collective-permute-done.19 = f32[8,8]{0,1:T(8,128)S(1)} collective-permute-done((f32[8,8]{0,1:T(8,128)S(1)}, f32[8,8]{0,1:T(8,128)S(1)}, u32[]{:S(2)}, u32[]{:S(2)}) %collective-permute-start.19) | collective-permute-done | bytes 288 | tf_op jit(solution)/shard_map/ppermute | solution.py:69
  118.9 0.1 copy.15
  119.0 0.7 cholesky.20
  119.7 0.6 compare_reduce_fusion
  120.4 0.6 select_bitcast_fusion
  121.0 0.6 custom-call.7
  121.7 0.2 fusion.45
  121.8 0.7 copy.17
  122.5 3.0 %multiply_reduce_fusion = f32[8,128,256]{2,1,0:T(8,128)} fusion(f32[8,128,256]{2,1,0:T(8,128)} %get-tuple-element.7, f32[8,8]{1,0:T(8,128)S(1)} %fusion.45), kind=kLoop, calls=%fused_computation | loop fusion | flops 3932160 | bytes 2097408 | tf_op jit(solution)/shard_map/reduce_sum | solution.py:239
  (25 shorter events, 0.2 us)
Async XLA Ops:
  0.6 21.0 %collective-permute-start.1 = (f32[4,2,64,256]{3,2,1,0:T(8,128)}, f32[4,2,64,256]{3,2,1,0:T(8,128)S(1)}, u32[]{:S(2)}, u32[]{:S(2)}) collective-permute-start(f32[4,2,64,256]{3,2,1,0:T(8,128)} %param.4), channel_id=1, source_target_pairs={{0,1},{1,2},{2,3},{3,4},{4,5},{5,6},{6,7},{7,8},{8,9},{9,10},{10,1... | collective-permute-start | bytes 1572872 | tf_op jit(solution)/shard_map/ppermute | solution.py:30
  2.7 18.9 %collective-permute-start = (f32[4,2,64,256]{3,2,1,0:T(8,128)}, f32[4,2,64,256]{3,2,1,0:T(8,128)S(1)}, u32[]{:S(2)}, u32[]{:S(2)}) collective-permute-start(f32[4,2,64,256]{3,2,1,0:T(8,128)} %param.4), channel_id=1, source_target_pairs={{1,0},{2,1},{3,2},{4,3},{5,4},{6,5},{7,6},{8,7},{9,8},{10,9},{11,1... | collective-permute-start | bytes 1572872 | tf_op jit(solution)/shard_map/ppermute | solution.py:32
  10.4 2.7 %collective-permute-start.2 = (f32[4,2,2,256]{3,2,1,0:T(2,128)S(1)}, f32[4,2,2,256]{3,2,1,0:T(2,128)S(1)}, u32[]{:S(2)}, u32[]{:S(2)}) collective-permute-start(f32[4,2,2,256]{3,2,1,0:T(2,128)S(1)} %slice_select_fusion.1), channel_id=1, source_target_pairs={{0,64},{64,0},{1,65},{65,1},{2,66},{66,2},{3,67},{67,3},{4,68},{68... | collective-permute-start | bytes 49160 | tf_op jit(solution)/shard_map/ppermute | solution.py:22
  23.2 7.8 %collective-permute-start.5 = (f32[4,2,2,256]{3,2,1,0:T(2,128)S(1)}, f32[4,2,2,256]{3,2,1,0:T(2,128)S(1)}, u32[]{:S(2)}, u32[]{:S(2)}) collective-permute-start(f32[4,2,2,256]{3,2,1,0:T(2,128)S(1)} %slice_select_fusion), channel_id=1, source_target_pairs={{0,64},{64,0},{1,65},{65,1},{2,66},{66,2},{3,67},{67,3},{4,68},{68... | collective-permute-start | bytes 49160 | tf_op jit(solution)/shard_map/ppermute | solution.py:22
  23.5 19.9 %collective-permute-start.4 = (f32[4,2,64,256]{3,2,1,0:T(8,128)S(1)}, f32[4,2,64,256]{3,2,1,0:T(8,128)S(1)}, u32[]{:S(2)}, u32[]{:S(2)}) collective-permute-start(f32[4,2,64,256]{3,2,1,0:T(8,128)S(1)} %get-tuple-element.16), channel_id=1, source_target_pairs={{0,1},{1,2},{2,3},{3,4},{4,5},{5,6},{6,7},{7,8},{8,9},{9,10},{10,1... | collective-permute-start | bytes 1572872 | tf_op jit(solution)/shard_map/ppermute | solution.py:30
  23.5 19.8 %collective-permute-start.3 = (f32[4,2,64,256]{3,2,1,0:T(8,128)S(1)}, f32[4,2,64,256]{3,2,1,0:T(8,128)S(1)}, u32[]{:S(2)}, u32[]{:S(2)}) collective-permute-start(f32[4,2,64,256]{3,2,1,0:T(8,128)S(1)} %get-tuple-element.16), channel_id=1, source_target_pairs={{1,0},{2,1},{3,2},{4,3},{5,4},{6,5},{7,6},{8,7},{9,8},{10,9},{11,1... | collective-permute-start | bytes 1572872 | tf_op jit(solution)/shard_map/ppermute | solution.py:32
  43.8 10.6 %copy-start.1 = (f32[4,2,64,256]{3,2,1,0:T(8,128)}, f32[4,2,64,256]{3,2,1,0:T(8,128)S(1)}, u32[]{:S(2)}) copy-start(f32[4,2,64,256]{3,2,1,0:T(8,128)S(1)} %fusion.43) | copy-start | bytes 1572868
  43.9 10.5 %copy-start = (f32[8,2,64,256]{3,2,1,0:T(8,128)}, f32[8,2,64,256]{3,2,1,0:T(8,128)S(1)}, u32[]{:S(2)}) copy-start(f32[8,2,64,256]{3,2,1,0:T(8,128)S(1)} %pad_maximum_fusion) | copy-start | bytes 3145732
  54.3 1.4 %collective-permute-start.6 = (f32[8,256]{1,0:T(8,128)}, f32[8,256]{1,0:T(8,128)S(1)}, u32[]{:S(2)}, u32[]{:S(2)}) collective-permute-start(f32[8,256]{1,0:T(8,128)} %shard_map.75), channel_id=1, source_target_pairs={{0,64},{64,0},{1,65},{65,1},{2,66},{66,2},{3,67},{67,3},{4,68},{68... | collective-permute-start | bytes 24584 | tf_op jit(solution)/shard_map/ppermute | solution.py:69
  56.4 3.7 %collective-permute-start.7 = (f32[8,256]{1,0:T(8,128)S(1)}, f32[8,256]{1,0:T(8,128)S(1)}, u32[]{:S(2)}, u32[]{:S(2)}) collective-permute-start(f32[8,256]{1,0:T(8,128)S(1)} %add.155), channel_id=1, source_target_pairs={{0,1},{1,0},{2,3},{3,2},{4,5},{5,4},{6,7},{7,6},{8,9},{9,8},{10,11... | collective-permute-start | bytes 24584 | tf_op jit(solution)/shard_map/ppermute | solution.py:69
  60.1 4.9 %collective-permute-start.8 = (f32[8,256]{1,0:T(8,128)S(1)}, f32[8,256]{1,0:T(8,128)S(1)}, u32[]{:S(2)}, u32[]{:S(2)}) collective-permute-start(f32[8,256]{1,0:T(8,128)S(1)} %add.156), channel_id=1, source_target_pairs={{0,3},{1,2},{2,1},{3,0},{4,7},{5,6},{6,5},{7,4},{8,11},{9,10},{10,... | collective-permute-start | bytes 24584 | tf_op jit(solution)/shard_map/ppermute | solution.py:69
  64.9 3.7 %collective-permute-start.9 = (f32[8,256]{1,0:T(8,128)S(1)}, f32[8,256]{1,0:T(8,128)S(1)}, u32[]{:S(2)}, u32[]{:S(2)}) collective-permute-start(f32[8,256]{1,0:T(8,128)S(1)} %add.157), channel_id=1, source_target_pairs={{0,4},{1,5},{2,6},{3,7},{4,0},{5,1},{6,2},{7,3},{8,12},{9,13},{10,... | collective-permute-start | bytes 24584 | tf_op jit(solution)/shard_map/ppermute | solution.py:69
  68.6 4.9 %collective-permute-start.10 = (f32[8,256]{1,0:T(8,128)S(1)}, f32[8,256]{1,0:T(8,128)S(1)}, u32[]{:S(2)}, u32[]{:S(2)}) collective-permute-start(f32[8,256]{1,0:T(8,128)S(1)} %add.158), channel_id=1, source_target_pairs={{0,12},{1,13},{2,14},{3,15},{4,8},{5,9},{6,10},{7,11},{8,4},{9,5},... | collective-permute-start | bytes 24584 | tf_op jit(solution)/shard_map/ppermute | solution.py:69
  73.5 3.7 %collective-permute-start.11 = (f32[8,256]{1,0:T(8,128)S(1)}, f32[8,256]{1,0:T(8,128)S(1)}, u32[]{:S(2)}, u32[]{:S(2)}) collective-permute-start(f32[8,256]{1,0:T(8,128)S(1)} %add.159), channel_id=1, source_target_pairs={{0,16},{1,17},{2,18},{3,19},{4,20},{5,21},{6,22},{7,23},{8,24},{9,... | collective-permute-start | bytes 24584 | tf_op jit(solution)/shard_map/ppermute | solution.py:69
  77.1 4.9 %collective-permute-start.12 = (f32[8,256]{1,0:T(8,128)S(1)}, f32[8,256]{1,0:T(8,128)S(1)}, u32[]{:S(2)}, u32[]{:S(2)}) collective-permute-start(f32[8,256]{1,0:T(8,128)S(1)} %add.160), channel_id=1, source_target_pairs={{0,48},{1,49},{2,50},{3,51},{4,52},{5,53},{6,54},{7,55},{8,56},{9,... | collective-permute-start | bytes 24584 | tf_op jit(solution)/shard_map/ppermute | solution.py:69
  92.4 1.2 collective-permute-start.13
  93.6 3.6 %collective-permute-start.14 = (f32[8,8]{0,1:T(8,128)S(1)}, f32[8,8]{0,1:T(8,128)S(1)}, u32[]{:S(2)}, u32[]{:S(2)}) collective-permute-start(f32[8,8]{0,1:T(8,128)S(1)} %add.162), channel_id=1, source_target_pairs={{0,1},{1,0},{2,3},{3,2},{4,5},{5,4},{6,7},{7,6},{8,9},{9,8},{10,11... | collective-permute-start | bytes 776 | tf_op jit(solution)/shard_map/ppermute | solution.py:69
  97.2 4.8 %collective-permute-start.15 = (f32[8,8]{0,1:T(8,128)S(1)}, f32[8,8]{0,1:T(8,128)S(1)}, u32[]{:S(2)}, u32[]{:S(2)}) collective-permute-start(f32[8,8]{0,1:T(8,128)S(1)} %add.163), channel_id=1, source_target_pairs={{0,3},{1,2},{2,1},{3,0},{4,7},{5,6},{6,5},{7,4},{8,11},{9,10},{10,... | collective-permute-start | bytes 776 | tf_op jit(solution)/shard_map/ppermute | solution.py:69
  102.0 3.6 %collective-permute-start.16 = (f32[8,8]{0,1:T(8,128)S(1)}, f32[8,8]{0,1:T(8,128)S(1)}, u32[]{:S(2)}, u32[]{:S(2)}) collective-permute-start(f32[8,8]{0,1:T(8,128)S(1)} %add.164), channel_id=1, source_target_pairs={{0,4},{1,5},{2,6},{3,7},{4,0},{5,1},{6,2},{7,3},{8,12},{9,13},{10,... | collective-permute-start | bytes 776 | tf_op jit(solution)/shard_map/ppermute | solution.py:69
  105.7 4.8 %collective-permute-start.17 = (f32[8,8]{0,1:T(8,128)S(1)}, f32[8,8]{0,1:T(8,128)S(1)}, u32[]{:S(2)}, u32[]{:S(2)}) collective-permute-start(f32[8,8]{0,1:T(8,128)S(1)} %add.165), channel_id=1, source_target_pairs={{0,12},{1,13},{2,14},{3,15},{4,8},{5,9},{6,10},{7,11},{8,4},{9,5},... | collective-permute-start | bytes 776 | tf_op jit(solution)/shard_map/ppermute | solution.py:69
  110.5 3.6 %collective-permute-start.18 = (f32[8,8]{0,1:T(8,128)S(1)}, f32[8,8]{0,1:T(8,128)S(1)}, u32[]{:S(2)}, u32[]{:S(2)}) collective-permute-start(f32[8,8]{0,1:T(8,128)S(1)} %add.166), channel_id=1, source_target_pairs={{0,16},{1,17},{2,18},{3,19},{4,20},{5,21},{6,22},{7,23},{8,24},{9,... | collective-permute-start | bytes 776 | tf_op jit(solution)/shard_map/ppermute | solution.py:69
  114.1 4.8 %collective-permute-start.19 = (f32[8,8]{0,1:T(8,128)S(1)}, f32[8,8]{0,1:T(8,128)S(1)}, u32[]{:S(2)}, u32[]{:S(2)}) collective-permute-start(f32[8,8]{0,1:T(8,128)S(1)} %add.167), channel_id=1, source_target_pairs={{0,48},{1,49},{2,50},{3,51},{4,52},{5,53},{6,54},{7,55},{8,56},{9,... | collective-permute-start | bytes 776 | tf_op jit(solution)/shard_map/ppermute | solution.py:69

commit v11 on v10

--- a/solution.py
+++ b/solution.py
@@ -174,6 +174,45 @@
     return w, g
 
 
+def factor_kernel(g_ref, w_ref, u_ref, d_ref):
+    ns = g_ref.shape[0]
+    gram = g_ref[...]
+    row = lax.broadcasted_iota(jnp.int32, (ns, ns), 0)
+    col = lax.broadcasted_iota(jnp.int32, (ns, ns), 1)
+    upper = jnp.zeros((ns, ns), jnp.float32)
+    for j in range(ns):
+        grow = jnp.sum(jnp.where(row == j, gram, 0.0), axis=0, keepdims=True)
+        ucol = jnp.sum(jnp.where(col == j, upper, 0.0), axis=1, keepdims=True)
+        v = grow - jnp.sum(upper * ucol, axis=0, keepdims=True)
+        root = jnp.sqrt(jnp.sum(jnp.where(col[:1] == j, v, 0.0)))
+        newrow = jnp.where(col[:1] > j, v / root, jnp.where(col[:1] == j, root, 0.0))
+        upper = jnp.where(row == j, newrow, upper)
+    u_ref[...] = upper
+
+    def entry(s, t):
+        return jnp.sum(jnp.where((row == t) & (col == s), upper, 0.0))
+
+    for s in range(ns):
+        acc = w_ref[s]
+        for t in range(s):
+            acc = acc - entry(s, t) * d_ref[t]
+        d_ref[s] = acc / entry(s, s)
+
+
+def factor_and_solve(gram, residual3):
+    ns = gram.shape[0]
+    vmem = pl.BlockSpec(memory_space=pltpu.VMEM)
+    return pl.pallas_call(
+        factor_kernel,
+        in_specs=[vmem, vmem],
+        out_specs=[vmem, vmem],
+        out_shape=[jax.ShapeDtypeStruct((ns, ns), jnp.float32),
+                   jax.ShapeDtypeStruct(residual3.shape, jnp.float32)],
+        cost_estimate=pl.CostEstimate(flops=ns * ns * residual3[0].size, transcendentals=ns,
+                                      bytes_accessed=2 * residual3.size * 4),
+    )(gram, residual3)
+
+
 def offset_slice(padded, offset, dimension, length):
     return lax.slice_in_dim(padded, 2 + offset, 2 + offset + length, axis=dimension)
 
@@ -234,10 +273,8 @@
     coeffs = coeffs_t.T
     residual3, local_gram = residual(coeffs_t, basis3, snaps3)
     total_gram = allreduce(local_gram, ("role", "slab"))
-    lower_factor = jnp.linalg.cholesky(total_gram)
-    inverse_factor = jax.scipy.linalg.solve_triangular(lower_factor, jnp.eye(ns, dtype=jnp.float32), lower=True)
-    directions = jnp.sum(inverse_factor[:, :, None, None] * residual3[None], axis=1)
-    return (advanced, coeffs, lower_factor.T, directions.reshape(snapshots.shape))
+    upper_factor, directions = factor_and_solve(total_gram, residual3)
+    return (advanced, coeffs, upper_factor, directions.reshape(snapshots.shape))
 
 
 def solution(mesh):

time: 126 us -> 125 us (level)
  Pallas kernels: 18.6 us -> 23.4 us
  other arithmetic: 18 us -> 13.6 us
  local copies, waits for them, and re-layouts: 3.59 us -> 2.08 us
    pallas_call x0 -> x1, Pallas kernels: none -> 4.79 us  [factor_and_solve(): pl.pallas_call(factor_kernel, in_specs=[vmem, vmem], out_specs=[vmem, vme...]
    reduce_sum x1 -> x0, other arithmetic: 2.96 us -> none  [on_device(): jnp.sum(inverse_factor[:, :, None, None] * residual3[None], axis=1)]
    another operation x5 -> x0, other arithmetic: 2.67 us -> none  [the longest x3 1.39 us: on_device(): lower_factor = jnp.linalg.cholesky(total_gram)]
    add x14, other arithmetic: 1.34 us -> 2.61 us  [allreduce(): value = value + lax.ppermute(value, name, pairs)]
where the time goes in v11:
time: 125 us; the launch traced here: 124 us
  waiting for transfers between devices  60.3 us (48%)
  starting transfers between devices  24.3 us (19%)
  Pallas kernels  23.4 us (19%)
  other arithmetic  13.6 us (11%)
  local copies, waits for them, and re-layouts  2.08 us (2%)
    ppermute x14, waiting for transfers between devices, allreduce(): value = value + lax.ppermute(value, name, pairs)  45.9 us
    ppermute x2, waiting for transfers between devices, extended(): lax.ppermute(tail, axis, [(i, (i + 1) % count) for i in range(ends)])  14.4 us
    ppermute x2, starting transfers between devices, extended(): lax.ppermute(head, axis, [((i + 1) % count, i) for i in range(ends)])  14.3 us
    pallas_call x1, Pallas kernels, project(): pl.pallas_call(project_kernel, grid=(nk // tk,), in_specs=[pl.BlockSpec((...  9.48 us
    pallas_call x1, Pallas kernels, residual(): pl.pallas_call(residual_kernel, grid=(nr // block_rows,), in_specs=[pl.Bl...  9.11 us
    ppermute x14, starting transfers between devices, allreduce(): value = value + lax.ppermute(value, name, pairs)  7.68 us
    mul x2, other arithmetic, local_terms(): viscosity * (second_diff(ypadded, center, 2, ny_loc) + second_diff(zpadde...  5.22 us
    pallas_call x1, Pallas kernels, factor_and_solve(): pl.pallas_call(factor_kernel, in_specs=[vmem, vmem], out_specs=[vmem, vme...  4.79 us
  transfers between devices with their start and end apart: 20, of which 16 were waited for; matrix products, arithmetic and copies ran while one was open for 8% of the time, Pallas kernels for 0%

profile of v11, /device:TPU:0, one launch (start us, length us, event | category | flops | bytes accessed | tf_op | source)
XLA Modules:
  0.0 124.5 jit_solution(13149611546795344864)
XLA Ops:
  0.6 2.1 %collective-permute-start.1 = (f32[4,2,64,256]{3,2,1,0:T(8,128)}, f32[4,2,64,256]{3,2,1,0:T(8,128)S(1)}, u32[]{:S(2)}, u32[]{:S(2)}) collective-permute-start(f32[4,2,64,256]{3,2,1,0:T(8,128)} %param.4), channel_id=1, source_target_pairs={{0,1},{1,2},{2,3},{3,4},{4,5},{5,6},{6,7},{7,8},{8,9},{9,10},{10,1... | collective-permute-start | bytes 1572872 | tf_op jit(solution)/shard_map/ppermute | solution.py:30
  2.7 6.8 %collective-permute-start = (f32[4,2,64,256]{3,2,1,0:T(8,128)}, f32[4,2,64,256]{3,2,1,0:T(8,128)S(1)}, u32[]{:S(2)}, u32[]{:S(2)}) collective-permute-start(f32[4,2,64,256]{3,2,1,0:T(8,128)} %param.4), channel_id=1, source_target_pairs={{1,0},{2,1},{3,2},{4,3},{5,4},{6,5},{7,6},{8,7},{9,8},{10,9},{11,1... | collective-permute-start | bytes 1572872 | tf_op jit(solution)/shard_map/ppermute | solution.py:32
  9.5 0.9 slice_select_fusion.1
  10.4 0.1 collective-permute-start.2
  10.5 1.2 fusion.46
  11.7 0.7 negate_multiply_fusion
  12.4 0.7 dynamic_slice.7
  13.2 0.0 collective-permute-done.2
  13.2 4.4 %fusion.15 = f32[4,2,64,256]{3,2,1,0:T(8,128)S(1)} fusion(f32[4,2,2,256]{3,2,1,0:T(2,128)S(1)} %get-tuple-element.21, f32[4,2,64,256]{3,2,1,0:T(8,128)} %param.4, f32[4,2,2,256]{3,2,1,0:T(2,128)S(1)} %get-tuple-element.20, f32[4,2,64,2]{3,2,1,0:T(8,128)S(1)} %get-tuple-element.17, f32[4,2,64,2]{3,2,1,0:T(8,128)S(1)} %get-tuple-element.16), kind=kLoop, calls=%fused_computation.32 | loop fusion | flops 3276800 | bytes 1089536 | tf_op jit(solution)/shard_map/mul | solution.py:234
  17.6 1.0 slice_subtract_fusion
  18.6 3.0 %collective-permute-done.1 = f32[4,2,64,256]{3,2,1,0:T(8,128)S(1)} collective-permute-done((f32[4,2,64,256]{3,2,1,0:T(8,128)}, f32[4,2,64,256]{3,2,1,0:T(8,128)S(1)}, u32[]{:S(2)}, u32[]{:S(2)}) %collective-permute-start.1) | collective-permute-done | bytes 524320 | tf_op jit(solution)/shard_map/ppermute | solution.py:30
  21.6 0.0 collective-permute-done
  21.6 1.6 %multiply_add_fusion = (f32[4,2,64,256]{3,2,1,0:T(8,128)S(1)}, f32[4,2,64,256]{3,2,1,0:T(8,128)S(1)}) fusion(f32[4,2,64,256]{3,2,1,0:T(8,128)} %param.4, f32[3,2,64,256]{3,2,1,0:T(8,128)S(1)} %slice.169, f32[1,2,64,256]{3,2,1,0:T(8,128)S(1)} %slice_subtract_fusion, f32[4,2,64,256]{3,2,1,0:T(8,128)S(1)} %collective-permute-done.1, ...), kind=kLoop, calls=%fused_computation.75 | loop fusion | flops 2883584 | bytes 3145984 | tf_op jit(solution)/shard_map/add | solution.py:264
  23.2 0.1 collective-permute-start.5
  23.3 0.1 fusion.45
  23.5 0.1 collective-permute-start.4
  23.5 7.5 %collective-permute-start.3 = (f32[4,2,64,256]{3,2,1,0:T(8,128)S(1)}, f32[4,2,64,256]{3,2,1,0:T(8,128)S(1)}, u32[]{:S(2)}, u32[]{:S(2)}) collective-permute-start(f32[4,2,64,256]{3,2,1,0:T(8,128)S(1)} %get-tuple-element.12), channel_id=1, source_target_pairs={{1,0},{2,1},{3,2},{4,3},{5,4},{6,5},{7,6},{8,7},{9,8},{10,9},{11,1... | collective-permute-start | bytes 1572872 | tf_op jit(solution)/shard_map/ppermute | solution.py:32
  31.0 0.0 collective-permute-done.5
  31.0 0.8 fusion.5
  31.9 0.1 fusion.44
  32.0 11.4 %collective-permute-done.4 = f32[4,2,64,256]{3,2,1,0:T(8,128)S(1)} collective-permute-done((f32[4,2,64,256]{3,2,1,0:T(8,128)S(1)}, f32[4,2,64,256]{3,2,1,0:T(8,128)S(1)}, u32[]{:S(2)}, u32[]{:S(2)}) %collective-permute-start.4) | collective-permute-done | bytes 524320 | tf_op jit(solution)/shard_map/ppermute | solution.py:30
  43.4 0.0 collective-permute-done.3
  43.4 0.4 fusion.43
  43.8 0.0 copy-start.1
  43.8 0.1 pad_maximum_fusion
  43.9 0.0 copy-start
  43.9 1.0 bitcast_convert_fusion.s_ref
  44.9 9.5 %shard_map.75 = f32[8,256]{1,0:T(8,128)} custom-call(bf16[256,128,256]{2,1,0:T(8,128)(2,1)} %bitcast.5, bf16[8,128,256]{2,1,0:T(8,128)(2,1)} %bitcast_convert_fusion.s_ref), custom_call_target="tpu_custom_call" | custom-call | flops 2147483648 | bytes 17309696 | tf_op jit(solution)/shard_map/pallas_call | solution.py:96
  54.3 0.0 collective-permute-start.6
  54.3 1.4 %collective-permute-done.6 = f32[8,256]{1,0:T(8,128)S(1)} collective-permute-done((f32[8,256]{1,0:T(8,128)}, f32[8,256]{1,0:T(8,128)S(1)}, u32[]{:S(2)}, u32[]{:S(2)}) %collective-permute-start.6) | collective-permute-done | bytes 8224 | tf_op jit(solution)/shard_map/ppermute | solution.py:69
  55.7 0.7 add.143
  56.4 0.0 collective-permute-start.7
  56.4 3.6 %collective-permute-done.7 = f32[8,256]{1,0:T(8,128)S(1)} collective-permute-done((f32[8,256]{1,0:T(8,128)S(1)}, f32[8,256]{1,0:T(8,128)S(1)}, u32[]{:S(2)}, u32[]{:S(2)}) %collective-permute-start.7) | collective-permute-done | bytes 8224 | tf_op jit(solution)/shard_map/ppermute | solution.py:69
  60.1 0.0 collective-permute-start.8
  60.1 4.9 %collective-permute-done.8 = f32[8,256]{1,0:T(8,128)S(1)} collective-permute-done((f32[8,256]{1,0:T(8,128)S(1)}, f32[8,256]{1,0:T(8,128)S(1)}, u32[]{:S(2)}, u32[]{:S(2)}) %collective-permute-start.8) | collective-permute-done | bytes 8224 | tf_op jit(solution)/shard_map/ppermute | solution.py:69
  64.9 0.0 collective-permute-start.9
  64.9 3.6 %collective-permute-done.9 = f32[8,256]{1,0:T(8,128)S(1)} collective-permute-done((f32[8,256]{1,0:T(8,128)S(1)}, f32[8,256]{1,0:T(8,128)S(1)}, u32[]{:S(2)}, u32[]{:S(2)}) %collective-permute-start.9) | collective-permute-done | bytes 8224 | tf_op jit(solution)/shard_map/ppermute | solution.py:69
  68.6 0.0 collective-permute-start.10
  68.6 4.9 %collective-permute-done.10 = f32[8,256]{1,0:T(8,128)S(1)} collective-permute-done((f32[8,256]{1,0:T(8,128)S(1)}, f32[8,256]{1,0:T(8,128)S(1)}, u32[]{:S(2)}, u32[]{:S(2)}) %collective-permute-start.10) | collective-permute-done | bytes 8224 | tf_op jit(solution)/shard_map/ppermute | solution.py:69
  73.5 0.0 collective-permute-start.11
  73.5 3.6 %collective-permute-done.11 = f32[8,256]{1,0:T(8,128)S(1)} collective-permute-done((f32[8,256]{1,0:T(8,128)S(1)}, f32[8,256]{1,0:T(8,128)S(1)}, u32[]{:S(2)}, u32[]{:S(2)}) %collective-permute-start.11) | collective-permute-done | bytes 8224 | tf_op jit(solution)/shard_map/ppermute | solution.py:69
  77.1 1.9 %collective-permute-start.12 = (f32[8,256]{1,0:T(8,128)S(1)}, f32[8,256]{1,0:T(8,128)S(1)}, u32[]{:S(2)}, u32[]{:S(2)}) collective-permute-start(f32[8,256]{1,0:T(8,128)S(1)} %add.148), channel_id=1, source_target_pairs={{0,48},{1,49},{2,50},{3,51},{4,52},{5,53},{6,54},{7,55},{8,56},{9,... | collective-permute-start | bytes 24584 | tf_op jit(solution)/shard_map/ppermute | solution.py:69
  79.0 3.0 %collective-permute-done.12 = f32[8,256]{1,0:T(8,128)S(1)} collective-permute-done((f32[8,256]{1,0:T(8,128)S(1)}, f32[8,256]{1,0:T(8,128)S(1)}, u32[]{:S(2)}, u32[]{:S(2)}) %collective-permute-start.12) | collective-permute-done | bytes 8224 | tf_op jit(solution)/shard_map/ppermute | solution.py:69
  82.0 0.6 add.149.c_ref
  82.6 0.0 copy-done
  82.6 9.1 %shard_map.76 = (f32[8,128,256]{2,1,0:T(8,128)}, f32[8,8]{1,0:T(8,128)}) custom-call(f32[8,256]{1,0:T(8,128)} %add.149.c_ref, bf16[256,128,256]{2,1,0:T(8,128)(2,1)} %bitcast.6, f32[8,128,256]{2,1,0:T(8,128)} %bitcast.7), custom_call_target="tpu_custom_call" | custom-call | flops 2147483648 | bytes 18874368 | tf_op jit(solution)/shard_map/pallas_call | solution.py:158
  91.7 0.0 copy-done.1
  91.7 0.0 collective-permute-start.13
  91.7 1.4 %collective-permute-done.13 = f32[8,8]{1,0:T(8,128)S(1)} collective-permute-done((f32[8,8]{1,0:T(8,128)}, f32[8,8]{1,0:T(8,128)S(1)}, u32[]{:S(2)}, u32[]{:S(2)}) %collective-permute-start.13) | collective-permute-done | bytes 288 | tf_op jit(solution)/shard_map/ppermute | solution.py:69
  93.1 0.7 add.150
  93.8 0.0 collective-permute-start.14
  93.8 3.6 %collective-permute-done.14 = f32[8,8]{1,0:T(8,128)S(1)} collective-permute-done((f32[8,8]{1,0:T(8,128)S(1)}, f32[8,8]{1,0:T(8,128)S(1)}, u32[]{:S(2)}, u32[]{:S(2)}) %collective-permute-start.14) | collective-permute-done | bytes 288 | tf_op jit(solution)/shard_map/ppermute | solution.py:69
  97.4 1.9 %collective-permute-start.15 = (f32[8,8]{1,0:T(8,128)S(1)}, f32[8,8]{1,0:T(8,128)S(1)}, u32[]{:S(2)}, u32[]{:S(2)}) collective-permute-start(f32[8,8]{1,0:T(8,128)S(1)} %add.151), channel_id=1, source_target_pairs={{0,3},{1,2},{2,1},{3,0},{4,7},{5,6},{6,5},{7,4},{8,11},{9,10},{10,... | collective-permute-start | bytes 776 | tf_op jit(solution)/shard_map/ppermute | solution.py:69
  99.3 2.9 %collective-permute-done.15 = f32[8,8]{1,0:T(8,128)S(1)} collective-permute-done((f32[8,8]{1,0:T(8,128)S(1)}, f32[8,8]{1,0:T(8,128)S(1)}, u32[]{:S(2)}, u32[]{:S(2)}) %collective-permute-start.15) | collective-permute-done | bytes 288 | tf_op jit(solution)/shard_map/ppermute | solution.py:69
  102.2 0.0 collective-permute-start.16
  102.2 3.6 %collective-permute-done.16 = f32[8,8]{1,0:T(8,128)S(1)} collective-permute-done((f32[8,8]{1,0:T(8,128)S(1)}, f32[8,8]{1,0:T(8,128)S(1)}, u32[]{:S(2)}, u32[]{:S(2)}) %collective-permute-start.16) | collective-permute-done | bytes 288 | tf_op jit(solution)/shard_map/ppermute | solution.py:69
  105.8 1.9 %collective-permute-start.17 = (f32[8,8]{1,0:T(8,128)S(1)}, f32[8,8]{1,0:T(8,128)S(1)}, u32[]{:S(2)}, u32[]{:S(2)}) collective-permute-start(f32[8,8]{1,0:T(8,128)S(1)} %add.153), channel_id=1, source_target_pairs={{0,12},{1,13},{2,14},{3,15},{4,8},{5,9},{6,10},{7,11},{8,4},{9,5},... | collective-permute-start | bytes 776 | tf_op jit(solution)/shard_map/ppermute | solution.py:69
  107.8 2.9 %collective-permute-done.17 = f32[8,8]{1,0:T(8,128)S(1)} collective-permute-done((f32[8,8]{1,0:T(8,128)S(1)}, f32[8,8]{1,0:T(8,128)S(1)}, u32[]{:S(2)}, u32[]{:S(2)}) %collective-permute-start.17) | collective-permute-done | bytes 288 | tf_op jit(solution)/shard_map/ppermute | solution.py:69
  110.7 0.0 collective-permute-start.18
  110.7 3.6 %collective-permute-done.18 = f32[8,8]{1,0:T(8,128)S(1)} collective-permute-done((f32[8,8]{1,0:T(8,128)S(1)}, f32[8,8]{1,0:T(8,128)S(1)}, u32[]{:S(2)}, u32[]{:S(2)}) %collective-permute-start.18) | collective-permute-done | bytes 288 | tf_op jit(solution)/shard_map/ppermute | solution.py:69
  114.3 1.9 %collective-permute-start.19 = (f32[8,8]{1,0:T(8,128)S(1)}, f32[8,8]{1,0:T(8,128)S(1)}, u32[]{:S(2)}, u32[]{:S(2)}) collective-permute-start(f32[8,8]{1,0:T(8,128)S(1)} %add.155), channel_id=1, source_target_pairs={{0,48},{1,49},{2,50},{3,51},{4,52},{5,53},{6,54},{7,55},{8,56},{9,... | collective-permute-start | bytes 776 | tf_op jit(solution)/shard_map/ppermute | solution.py:69
  116.2 2.9 %collective-permute-done.19 = f32[8,8]{1,0:T(8,128)S(1)} collective-permute-done((f32[8,8]{1,0:T(8,128)S(1)}, f32[8,8]{1,0:T(8,128)S(1)}, u32[]{:S(2)}, u32[]{:S(2)}) %collective-permute-start.19) | collective-permute-done | bytes 288 | tf_op jit(solution)/shard_map/ppermute | solution.py:69
  119.1 0.6 add.156.g_ref
  119.7 4.8 %shard_map.77 = (f32[8,8]{1,0:T(8,128)}, f32[8,128,256]{2,1,0:T(8,128)}) custom-call(f32[8,8]{1,0:T(8,128)} %add.156.g_ref, f32[8,128,256]{2,1,0:T(8,128)} %get-tuple-element.9.w_ref), custom_call_target="tpu_custom_call" | custom-call | flops 2097152 | bytes 2097152 | tf_op jit(solution)/shard_map/pallas_call | solution.py:205
  (15 shorter events, 0.1 us)
Async XLA Ops:
  0.6 21.0 %collective-permute-start.1 = (f32[4,2,64,256]{3,2,1,0:T(8,128)}, f32[4,2,64,256]{3,2,1,0:T(8,128)S(1)}, u32[]{:S(2)}, u32[]{:S(2)}) collective-permute-start(f32[4,2,64,256]{3,2,1,0:T(8,128)} %param.4), channel_id=1, source_target_pairs={{0,1},{1,2},{2,3},{3,4},{4,5},{5,6},{6,7},{7,8},{8,9},{9,10},{10,1... | collective-permute-start | bytes 1572872 | tf_op jit(solution)/shard_map/ppermute | solution.py:30
  2.7 18.9 %collective-permute-start = (f32[4,2,64,256]{3,2,1,0:T(8,128)}, f32[4,2,64,256]{3,2,1,0:T(8,128)S(1)}, u32[]{:S(2)}, u32[]{:S(2)}) collective-permute-start(f32[4,2,64,256]{3,2,1,0:T(8,128)} %param.4), channel_id=1, source_target_pairs={{1,0},{2,1},{3,2},{4,3},{5,4},{6,5},{7,6},{8,7},{9,8},{10,9},{11,1... | collective-permute-start | bytes 1572872 | tf_op jit(solution)/shard_map/ppermute | solution.py:32
  10.4 2.7 %collective-permute-start.2 = (f32[4,2,2,256]{3,2,1,0:T(2,128)S(1)}, f32[4,2,2,256]{3,2,1,0:T(2,128)S(1)}, u32[]{:S(2)}, u32[]{:S(2)}) collective-permute-start(f32[4,2,2,256]{3,2,1,0:T(2,128)S(1)} %slice_select_fusion.1), channel_id=1, source_target_pairs={{0,64},{64,0},{1,65},{65,1},{2,66},{66,2},{3,67},{67,3},{4,68},{68... | collective-permute-start | bytes 49160 | tf_op jit(solution)/shard_map/ppermute | solution.py:22
  23.2 7.8 %collective-permute-start.5 = (f32[4,2,2,256]{3,2,1,0:T(2,128)S(1)}, f32[4,2,2,256]{3,2,1,0:T(2,128)S(1)}, u32[]{:S(2)}, u32[]{:S(2)}) collective-permute-start(f32[4,2,2,256]{3,2,1,0:T(2,128)S(1)} %slice_select_fusion), channel_id=1, source_target_pairs={{0,64},{64,0},{1,65},{65,1},{2,66},{66,2},{3,67},{67,3},{4,68},{68... | collective-permute-start | bytes 49160 | tf_op jit(solution)/shard_map/ppermute | solution.py:22
  23.5 19.9 %collective-permute-start.4 = (f32[4,2,64,256]{3,2,1,0:T(8,128)S(1)}, f32[4,2,64,256]{3,2,1,0:T(8,128)S(1)}, u32[]{:S(2)}, u32[]{:S(2)}) collective-permute-start(f32[4,2,64,256]{3,2,1,0:T(8,128)S(1)} %get-tuple-element.12), channel_id=1, source_target_pairs={{0,1},{1,2},{2,3},{3,4},{4,5},{5,6},{6,7},{7,8},{8,9},{9,10},{10,1... | collective-permute-start | bytes 1572872 | tf_op jit(solution)/shard_map/ppermute | solution.py:30
  23.5 19.8 %collective-permute-start.3 = (f32[4,2,64,256]{3,2,1,0:T(8,128)S(1)}, f32[4,2,64,256]{3,2,1,0:T(8,128)S(1)}, u32[]{:S(2)}, u32[]{:S(2)}) collective-permute-start(f32[4,2,64,256]{3,2,1,0:T(8,128)S(1)} %get-tuple-element.12), channel_id=1, source_target_pairs={{1,0},{2,1},{3,2},{4,3},{5,4},{6,5},{7,6},{8,7},{9,8},{10,9},{11,1... | collective-permute-start | bytes 1572872 | tf_op jit(solution)/shard_map/ppermute | solution.py:32
  43.8 47.9 %copy-start.1 = (f32[4,2,64,256]{3,2,1,0:T(8,128)}, f32[4,2,64,256]{3,2,1,0:T(8,128)S(1)}, u32[]{:S(2)}) copy-start(f32[4,2,64,256]{3,2,1,0:T(8,128)S(1)} %fusion.43) | copy-start | bytes 1572868
  43.9 38.7 %copy-start = (f32[8,2,64,256]{3,2,1,0:T(8,128)}, f32[8,2,64,256]{3,2,1,0:T(8,128)S(1)}, u32[]{:S(2)}) copy-start(f32[8,2,64,256]{3,2,1,0:T(8,128)S(1)} %pad_maximum_fusion) | copy-start | bytes 3145732
  54.3 1.4 %collective-permute-start.6 = (f32[8,256]{1,0:T(8,128)}, f32[8,256]{1,0:T(8,128)S(1)}, u32[]{:S(2)}, u32[]{:S(2)}) collective-permute-start(f32[8,256]{1,0:T(8,128)} %shard_map.75), channel_id=1, source_target_pairs={{0,64},{64,0},{1,65},{65,1},{2,66},{66,2},{3,67},{67,3},{4,68},{68... | collective-permute-start | bytes 24584 | tf_op jit(solution)/shard_map/ppermute | solution.py:69
  56.4 3.7 %collective-permute-start.7 = (f32[8,256]{1,0:T(8,128)S(1)}, f32[8,256]{1,0:T(8,128)S(1)}, u32[]{:S(2)}, u32[]{:S(2)}) collective-permute-start(f32[8,256]{1,0:T(8,128)S(1)} %add.143), channel_id=1, source_target_pairs={{0,1},{1,0},{2,3},{3,2},{4,5},{5,4},{6,7},{7,6},{8,9},{9,8},{10,11... | collective-permute-start | bytes 24584 | tf_op jit(solution)/shard_map/ppermute | solution.py:69
  60.1 4.9 %collective-permute-start.8 = (f32[8,256]{1,0:T(8,128)S(1)}, f32[8,256]{1,0:T(8,128)S(1)}, u32[]{:S(2)}, u32[]{:S(2)}) collective-permute-start(f32[8,256]{1,0:T(8,128)S(1)} %add.144), channel_id=1, source_target_pairs={{0,3},{1,2},{2,1},{3,0},{4,7},{5,6},{6,5},{7,4},{8,11},{9,10},{10,... | collective-permute-start | bytes 24584 | tf_op jit(solution)/shard_map/ppermute | solution.py:69
  64.9 3.7 %collective-permute-start.9 = (f32[8,256]{1,0:T(8,128)S(1)}, f32[8,256]{1,0:T(8,128)S(1)}, u32[]{:S(2)}, u32[]{:S(2)}) collective-permute-start(f32[8,256]{1,0:T(8,128)S(1)} %add.145), channel_id=1, source_target_pairs={{0,4},{1,5},{2,6},{3,7},{4,0},{5,1},{6,2},{7,3},{8,12},{9,13},{10,... | collective-permute-start | bytes 24584 | tf_op jit(solution)/shard_map/ppermute | solution.py:69
  68.6 4.9 %collective-permute-start.10 = (f32[8,256]{1,0:T(8,128)S(1)}, f32[8,256]{1,0:T(8,128)S(1)}, u32[]{:S(2)}, u32[]{:S(2)}) collective-permute-start(f32[8,256]{1,0:T(8,128)S(1)} %add.146), channel_id=1, source_target_pairs={{0,12},{1,13},{2,14},{3,15},{4,8},{5,9},{6,10},{7,11},{8,4},{9,5},... | collective-permute-start | bytes 24584 | tf_op jit(solution)/shard_map/ppermute | solution.py:69
  73.5 3.7 %collective-permute-start.11 = (f32[8,256]{1,0:T(8,128)S(1)}, f32[8,256]{1,0:T(8,128)S(1)}, u32[]{:S(2)}, u32[]{:S(2)}) collective-permute-start(f32[8,256]{1,0:T(8,128)S(1)} %add.147), channel_id=1, source_target_pairs={{0,16},{1,17},{2,18},{3,19},{4,20},{5,21},{6,22},{7,23},{8,24},{9,... | collective-permute-start | bytes 24584 | tf_op jit(solution)/shard_map/ppermute | solution.py:69
  77.1 4.9 %collective-permute-start.12 = (f32[8,256]{1,0:T(8,128)S(1)}, f32[8,256]{1,0:T(8,128)S(1)}, u32[]{:S(2)}, u32[]{:S(2)}) collective-permute-start(f32[8,256]{1,0:T(8,128)S(1)} %add.148), channel_id=1, source_target_pairs={{0,48},{1,49},{2,50},{3,51},{4,52},{5,53},{6,54},{7,55},{8,56},{9,... | collective-permute-start | bytes 24584 | tf_op jit(solution)/shard_map/ppermute | solution.py:69
  91.7 1.4 %collective-permute-start.13 = (f32[8,8]{1,0:T(8,128)}, f32[8,8]{1,0:T(8,128)S(1)}, u32[]{:S(2)}, u32[]{:S(2)}) collective-permute-start(f32[8,8]{1,0:T(8,128)} %get-tuple-element.8), channel_id=1, source_target_pairs={{0,64},{64,0},{1,65},{65,1},{2,66},{66,2},{3,67},{67,3},{4,68},{68... | collective-permute-start | bytes 776 | tf_op jit(solution)/shard_map/ppermute | solution.py:69
  93.8 3.6 %collective-permute-start.14 = (f32[8,8]{1,0:T(8,128)S(1)}, f32[8,8]{1,0:T(8,128)S(1)}, u32[]{:S(2)}, u32[]{:S(2)}) collective-permute-start(f32[8,8]{1,0:T(8,128)S(1)} %add.150), channel_id=1, source_target_pairs={{0,1},{1,0},{2,3},{3,2},{4,5},{5,4},{6,7},{7,6},{8,9},{9,8},{10,11... | collective-permute-start | bytes 776 | tf_op jit(solution)/shard_map/ppermute | solution.py:69
  97.4 4.8 %collective-permute-start.15 = (f32[8,8]{1,0:T(8,128)S(1)}, f32[8,8]{1,0:T(8,128)S(1)}, u32[]{:S(2)}, u32[]{:S(2)}) collective-permute-start(f32[8,8]{1,0:T(8,128)S(1)} %add.151), channel_id=1, source_target_pairs={{0,3},{1,2},{2,1},{3,0},{4,7},{5,6},{6,5},{7,4},{8,11},{9,10},{10,... | collective-permute-start | bytes 776 | tf_op jit(solution)/shard_map/ppermute | solution.py:69
  102.2 3.6 %collective-permute-start.16 = (f32[8,8]{1,0:T(8,128)S(1)}, f32[8,8]{1,0:T(8,128)S(1)}, u32[]{:S(2)}, u32[]{:S(2)}) collective-permute-start(f32[8,8]{1,0:T(8,128)S(1)} %add.152), channel_id=1, source_target_pairs={{0,4},{1,5},{2,6},{3,7},{4,0},{5,1},{6,2},{7,3},{8,12},{9,13},{10,... | collective-permute-start | bytes 776 | tf_op jit(solution)/shard_map/ppermute | solution.py:69
  105.8 4.8 %collective-permute-start.17 = (f32[8,8]{1,0:T(8,128)S(1)}, f32[8,8]{1,0:T(8,128)S(1)}, u32[]{:S(2)}, u32[]{:S(2)}) collective-permute-start(f32[8,8]{1,0:T(8,128)S(1)} %add.153), channel_id=1, source_target_pairs={{0,12},{1,13},{2,14},{3,15},{4,8},{5,9},{6,10},{7,11},{8,4},{9,5},... | collective-permute-start | bytes 776 | tf_op jit(solution)/shard_map/ppermute | solution.py:69
  110.7 3.6 %collective-permute-start.18 = (f32[8,8]{1,0:T(8,128)S(1)}, f32[8,8]{1,0:T(8,128)S(1)}, u32[]{:S(2)}, u32[]{:S(2)}) collective-permute-start(f32[8,8]{1,0:T(8,128)S(1)} %add.154), channel_id=1, source_target_pairs={{0,16},{1,17},{2,18},{3,19},{4,20},{5,21},{6,22},{7,23},{8,24},{9,... | collective-permute-start | bytes 776 | tf_op jit(solution)/shard_map/ppermute | solution.py:69
  114.3 4.8 %collective-permute-start.19 = (f32[8,8]{1,0:T(8,128)S(1)}, f32[8,8]{1,0:T(8,128)S(1)}, u32[]{:S(2)}, u32[]{:S(2)}) collective-permute-start(f32[8,8]{1,0:T(8,128)S(1)} %add.155), channel_id=1, source_target_pairs={{0,48},{1,49},{2,50},{3,51},{4,52},{5,53},{6,54},{7,55},{8,56},{9,... | collective-permute-start | bytes 776 | tf_op jit(solution)/shard_map/ppermute | solution.py:69

commit v12 on v11

--- a/solution.py
+++ b/solution.py
@@ -196,7 +196,7 @@
         acc = w_ref[s]
         for t in range(s):
             acc = acc - entry(s, t) * d_ref[t]
-        d_ref[s] = acc / entry(s, s)
+        d_ref[s] = acc * (1.0 / entry(s, s))
 
 
 def factor_and_solve(gram, residual3):

time: 125 us -> 125 us (level)
  no operation moved by 1% of the time
where the time goes in v12:
time: 125 us
  waiting for transfers between devices  60.3 us (48%)
  starting transfers between devices  24.3 us (19%)
  Pallas kernels  23.5 us (19%)
  other arithmetic  13.6 us (11%)
  local copies, waits for them, and re-layouts  2.08 us (2%)
    ppermute x14, waiting for transfers between devices, allreduce(): value = value + lax.ppermute(value, name, pairs)  45.9 us
    ppermute x2, waiting for transfers between devices, extended(): lax.ppermute(tail, axis, [(i, (i + 1) % count) for i in range(ends)])  14.4 us
    ppermute x2, starting transfers between devices, extended(): lax.ppermute(head, axis, [((i + 1) % count, i) for i in range(ends)])  14.3 us
    pallas_call x1, Pallas kernels, project(): pl.pallas_call(project_kernel, grid=(nk // tk,), in_specs=[pl.BlockSpec((...  9.48 us
    pallas_call x1, Pallas kernels, residual(): pl.pallas_call(residual_kernel, grid=(nr // block_rows,), in_specs=[pl.Bl...  9.11 us
    ppermute x14, starting transfers between devices, allreduce(): value = value + lax.ppermute(value, name, pairs)  7.68 us
    mul x2, other arithmetic, local_terms(): viscosity * (second_diff(ypadded, center, 2, ny_loc) + second_diff(zpadde...  5.22 us
    pallas_call x1, Pallas kernels, factor_and_solve(): pl.pallas_call(factor_kernel, in_specs=[vmem, vmem], out_specs=[vmem, vme...  4.89 us
  transfers between devices with their start and end apart: 20, of which 16 were waited for; matrix products, arithmetic and copies ran while one was open for 8% of the time, Pallas kernels for 0%

profile of v12, /device:TPU:0, one launch (start us, length us, event | category | flops | bytes accessed | tf_op | source)
XLA Modules:
  0.0 124.6 jit_solution(7049510502576491337)
XLA Ops:
  0.6 2.1 %collective-permute-start.1 = (f32[4,2,64,256]{3,2,1,0:T(8,128)}, f32[4,2,64,256]{3,2,1,0:T(8,128)S(1)}, u32[]{:S(2)}, u32[]{:S(2)}) collective-permute-start(f32[4,2,64,256]{3,2,1,0:T(8,128)} %param.4), channel_id=1, source_target_pairs={{0,1},{1,2},{2,3},{3,4},{4,5},{5,6},{6,7},{7,8},{8,9},{9,10},{10,1... | collective-permute-start | bytes 1572872 | tf_op jit(solution)/shard_map/ppermute | solution.py:30
  2.7 6.8 %collective-permute-start = (f32[4,2,64,256]{3,2,1,0:T(8,128)}, f32[4,2,64,256]{3,2,1,0:T(8,128)S(1)}, u32[]{:S(2)}, u32[]{:S(2)}) collective-permute-start(f32[4,2,64,256]{3,2,1,0:T(8,128)} %param.4), channel_id=1, source_target_pairs={{1,0},{2,1},{3,2},{4,3},{5,4},{6,5},{7,6},{8,7},{9,8},{10,9},{11,1... | collective-permute-start | bytes 1572872 | tf_op jit(solution)/shard_map/ppermute | solution.py:32
  9.5 0.9 slice_select_fusion.1
  10.4 0.1 collective-permute-start.2
  10.5 1.2 fusion.46
  11.7 0.7 negate_multiply_fusion
  12.4 0.7 dynamic_slice.7
  13.2 0.0 collective-permute-done.2
  13.2 4.4 %fusion.15 = f32[4,2,64,256]{3,2,1,0:T(8,128)S(1)} fusion(f32[4,2,2,256]{3,2,1,0:T(2,128)S(1)} %get-tuple-element.21, f32[4,2,64,256]{3,2,1,0:T(8,128)} %param.4, f32[4,2,2,256]{3,2,1,0:T(2,128)S(1)} %get-tuple-element.20, f32[4,2,64,2]{3,2,1,0:T(8,128)S(1)} %get-tuple-element.17, f32[4,2,64,2]{3,2,1,0:T(8,128)S(1)} %get-tuple-element.16), kind=kLoop, calls=%fused_computation.32 | loop fusion | flops 3276800 | bytes 1089536 | tf_op jit(solution)/shard_map/mul | solution.py:234
  17.6 1.0 slice_subtract_fusion
  18.6 3.0 %collective-permute-done.1 = f32[4,2,64,256]{3,2,1,0:T(8,128)S(1)} collective-permute-done((f32[4,2,64,256]{3,2,1,0:T(8,128)}, f32[4,2,64,256]{3,2,1,0:T(8,128)S(1)}, u32[]{:S(2)}, u32[]{:S(2)}) %collective-permute-start.1) | collective-permute-done | bytes 524320 | tf_op jit(solution)/shard_map/ppermute | solution.py:30
  21.6 0.0 collective-permute-done
  21.6 1.6 %multiply_add_fusion = (f32[4,2,64,256]{3,2,1,0:T(8,128)S(1)}, f32[4,2,64,256]{3,2,1,0:T(8,128)S(1)}) fusion(f32[4,2,64,256]{3,2,1,0:T(8,128)} %param.4, f32[3,2,64,256]{3,2,1,0:T(8,128)S(1)} %slice.169, f32[1,2,64,256]{3,2,1,0:T(8,128)S(1)} %slice_subtract_fusion, f32[4,2,64,256]{3,2,1,0:T(8,128)S(1)} %collective-permute-done.1, ...), kind=kLoop, calls=%fused_computation.75 | loop fusion | flops 2883584 | bytes 3145984 | tf_op jit(solution)/shard_map/add | solution.py:264
  23.2 0.1 collective-permute-start.5
  23.3 0.1 fusion.45
  23.5 0.1 collective-permute-start.4
  23.5 7.5 %collective-permute-start.3 = (f32[4,2,64,256]{3,2,1,0:T(8,128)S(1)}, f32[4,2,64,256]{3,2,1,0:T(8,128)S(1)}, u32[]{:S(2)}, u32[]{:S(2)}) collective-permute-start(f32[4,2,64,256]{3,2,1,0:T(8,128)S(1)} %get-tuple-element.12), channel_id=1, source_target_pairs={{1,0},{2,1},{3,2},{4,3},{5,4},{6,5},{7,6},{8,7},{9,8},{10,9},{11,1... | collective-permute-start | bytes 1572872 | tf_op jit(solution)/shard_map/ppermute | solution.py:32
  31.0 0.0 collective-permute-done.5
  31.0 0.8 fusion.5
  31.9 0.1 fusion.44
  32.0 11.4 %collective-permute-done.4 = f32[4,2,64,256]{3,2,1,0:T(8,128)S(1)} collective-permute-done((f32[4,2,64,256]{3,2,1,0:T(8,128)S(1)}, f32[4,2,64,256]{3,2,1,0:T(8,128)S(1)}, u32[]{:S(2)}, u32[]{:S(2)}) %collective-permute-start.4) | collective-permute-done | bytes 524320 | tf_op jit(solution)/shard_map/ppermute | solution.py:30
  43.4 0.0 collective-permute-done.3
  43.4 0.4 fusion.43
  43.8 0.0 copy-start.1
  43.8 0.1 pad_maximum_fusion
  43.9 0.0 copy-start
  43.9 1.0 bitcast_convert_fusion.s_ref
  44.9 9.5 %shard_map.75 = f32[8,256]{1,0:T(8,128)} custom-call(bf16[256,128,256]{2,1,0:T(8,128)(2,1)} %bitcast.5, bf16[8,128,256]{2,1,0:T(8,128)(2,1)} %bitcast_convert_fusion.s_ref), custom_call_target="tpu_custom_call" | custom-call | flops 2147483648 | bytes 17309696 | tf_op jit(solution)/shard_map/pallas_call | solution.py:96
  54.3 0.0 collective-permute-start.6
  54.3 1.4 %collective-permute-done.6 = f32[8,256]{1,0:T(8,128)S(1)} collective-permute-done((f32[8,256]{1,0:T(8,128)}, f32[8,256]{1,0:T(8,128)S(1)}, u32[]{:S(2)}, u32[]{:S(2)}) %collective-permute-start.6) | collective-permute-done | bytes 8224 | tf_op jit(solution)/shard_map/ppermute | solution.py:69
  55.7 0.7 add.143
  56.4 0.0 collective-permute-start.7
  56.4 3.6 %collective-permute-done.7 = f32[8,256]{1,0:T(8,128)S(1)} collective-permute-done((f32[8,256]{1,0:T(8,128)S(1)}, f32[8,256]{1,0:T(8,128)S(1)}, u32[]{:S(2)}, u32[]{:S(2)}) %collective-permute-start.7) | collective-permute-done | bytes 8224 | tf_op jit(solution)/shard_map/ppermute | solution.py:69
  60.1 0.0 collective-permute-start.8
  60.1 4.9 %collective-permute-done.8 = f32[8,256]{1,0:T(8,128)S(1)} collective-permute-done((f32[8,256]{1,0:T(8,128)S(1)}, f32[8,256]{1,0:T(8,128)S(1)}, u32[]{:S(2)}, u32[]{:S(2)}) %collective-permute-start.8) | collective-permute-done | bytes 8224 | tf_op jit(solution)/shard_map/ppermute | solution.py:69
  64.9 0.0 collective-permute-start.9
  64.9 3.6 %collective-permute-done.9 = f32[8,256]{1,0:T(8,128)S(1)} collective-permute-done((f32[8,256]{1,0:T(8,128)S(1)}, f32[8,256]{1,0:T(8,128)S(1)}, u32[]{:S(2)}, u32[]{:S(2)}) %collective-permute-start.9) | collective-permute-done | bytes 8224 | tf_op jit(solution)/shard_map/ppermute | solution.py:69
  68.6 0.0 collective-permute-start.10
  68.6 4.9 %collective-permute-done.10 = f32[8,256]{1,0:T(8,128)S(1)} collective-permute-done((f32[8,256]{1,0:T(8,128)S(1)}, f32[8,256]{1,0:T(8,128)S(1)}, u32[]{:S(2)}, u32[]{:S(2)}) %collective-permute-start.10) | collective-permute-done | bytes 8224 | tf_op jit(solution)/shard_map/ppermute | solution.py:69
  73.5 0.0 collective-permute-start.11
  73.5 3.6 %collective-permute-done.11 = f32[8,256]{1,0:T(8,128)S(1)} collective-permute-done((f32[8,256]{1,0:T(8,128)S(1)}, f32[8,256]{1,0:T(8,128)S(1)}, u32[]{:S(2)}, u32[]{:S(2)}) %collective-permute-start.11) | collective-permute-done | bytes 8224 | tf_op jit(solution)/shard_map/ppermute | solution.py:69
  77.1 1.9 %collective-permute-start.12 = (f32[8,256]{1,0:T(8,128)S(1)}, f32[8,256]{1,0:T(8,128)S(1)}, u32[]{:S(2)}, u32[]{:S(2)}) collective-permute-start(f32[8,256]{1,0:T(8,128)S(1)} %add.148), channel_id=1, source_target_pairs={{0,48},{1,49},{2,50},{3,51},{4,52},{5,53},{6,54},{7,55},{8,56},{9,... | collective-permute-start | bytes 24584 | tf_op jit(solution)/shard_map/ppermute | solution.py:69
  79.0 3.0 %collective-permute-done.12 = f32[8,256]{1,0:T(8,128)S(1)} collective-permute-done((f32[8,256]{1,0:T(8,128)S(1)}, f32[8,256]{1,0:T(8,128)S(1)}, u32[]{:S(2)}, u32[]{:S(2)}) %collective-permute-start.12) | collective-permute-done | bytes 8224 | tf_op jit(solution)/shard_map/ppermute | solution.py:69
  82.0 0.6 add.149.c_ref
  82.6 0.0 copy-done
  82.6 9.1 %shard_map.76 = (f32[8,128,256]{2,1,0:T(8,128)}, f32[8,8]{1,0:T(8,128)}) custom-call(f32[8,256]{1,0:T(8,128)} %add.149.c_ref, bf16[256,128,256]{2,1,0:T(8,128)(2,1)} %bitcast.6, f32[8,128,256]{2,1,0:T(8,128)} %bitcast.7), custom_call_target="tpu_custom_call" | custom-call | flops 2147483648 | bytes 18874368 | tf_op jit(solution)/shard_map/pallas_call | solution.py:158
  91.7 0.0 copy-done.1
  91.7 0.0 collective-permute-start.13
  91.7 1.4 %collective-permute-done.13 = f32[8,8]{1,0:T(8,128)S(1)} collective-permute-done((f32[8,8]{1,0:T(8,128)}, f32[8,8]{1,0:T(8,128)S(1)}, u32[]{:S(2)}, u32[]{:S(2)}) %collective-permute-start.13) | collective-permute-done | bytes 288 | tf_op jit(solution)/shard_map/ppermute | solution.py:69
  93.1 0.7 add.150
  93.8 0.0 collective-permute-start.14
  93.8 3.6 %collective-permute-done.14 = f32[8,8]{1,0:T(8,128)S(1)} collective-permute-done((f32[8,8]{1,0:T(8,128)S(1)}, f32[8,8]{1,0:T(8,128)S(1)}, u32[]{:S(2)}, u32[]{:S(2)}) %collective-permute-start.14) | collective-permute-done | bytes 288 | tf_op jit(solution)/shard_map/ppermute | solution.py:69
  97.4 1.9 %collective-permute-start.15 = (f32[8,8]{1,0:T(8,128)S(1)}, f32[8,8]{1,0:T(8,128)S(1)}, u32[]{:S(2)}, u32[]{:S(2)}) collective-permute-start(f32[8,8]{1,0:T(8,128)S(1)} %add.151), channel_id=1, source_target_pairs={{0,3},{1,2},{2,1},{3,0},{4,7},{5,6},{6,5},{7,4},{8,11},{9,10},{10,... | collective-permute-start | bytes 776 | tf_op jit(solution)/shard_map/ppermute | solution.py:69
  99.3 2.9 %collective-permute-done.15 = f32[8,8]{1,0:T(8,128)S(1)} collective-permute-done((f32[8,8]{1,0:T(8,128)S(1)}, f32[8,8]{1,0:T(8,128)S(1)}, u32[]{:S(2)}, u32[]{:S(2)}) %collective-permute-start.15) | collective-permute-done | bytes 288 | tf_op jit(solution)/shard_map/ppermute | solution.py:69
  102.2 0.0 collective-permute-start.16
  102.2 3.6 %collective-permute-done.16 = f32[8,8]{1,0:T(8,128)S(1)} collective-permute-done((f32[8,8]{1,0:T(8,128)S(1)}, f32[8,8]{1,0:T(8,128)S(1)}, u32[]{:S(2)}, u32[]{:S(2)}) %collective-permute-start.16) | collective-permute-done | bytes 288 | tf_op jit(solution)/shard_map/ppermute | solution.py:69
  105.8 1.9 %collective-permute-start.17 = (f32[8,8]{1,0:T(8,128)S(1)}, f32[8,8]{1,0:T(8,128)S(1)}, u32[]{:S(2)}, u32[]{:S(2)}) collective-permute-start(f32[8,8]{1,0:T(8,128)S(1)} %add.153), channel_id=1, source_target_pairs={{0,12},{1,13},{2,14},{3,15},{4,8},{5,9},{6,10},{7,11},{8,4},{9,5},... | collective-permute-start | bytes 776 | tf_op jit(solution)/shard_map/ppermute | solution.py:69
  107.8 2.9 %collective-permute-done.17 = f32[8,8]{1,0:T(8,128)S(1)} collective-permute-done((f32[8,8]{1,0:T(8,128)S(1)}, f32[8,8]{1,0:T(8,128)S(1)}, u32[]{:S(2)}, u32[]{:S(2)}) %collective-permute-start.17) | collective-permute-done | bytes 288 | tf_op jit(solution)/shard_map/ppermute | solution.py:69
  110.7 0.0 collective-permute-start.18
  110.7 3.6 %collective-permute-done.18 = f32[8,8]{1,0:T(8,128)S(1)} collective-permute-done((f32[8,8]{1,0:T(8,128)S(1)}, f32[8,8]{1,0:T(8,128)S(1)}, u32[]{:S(2)}, u32[]{:S(2)}) %collective-permute-start.18) | collective-permute-done | bytes 288 | tf_op jit(solution)/shard_map/ppermute | solution.py:69
  114.3 1.9 %collective-permute-start.19 = (f32[8,8]{1,0:T(8,128)S(1)}, f32[8,8]{1,0:T(8,128)S(1)}, u32[]{:S(2)}, u32[]{:S(2)}) collective-permute-start(f32[8,8]{1,0:T(8,128)S(1)} %add.155), channel_id=1, source_target_pairs={{0,48},{1,49},{2,50},{3,51},{4,52},{5,53},{6,54},{7,55},{8,56},{9,... | collective-permute-start | bytes 776 | tf_op jit(solution)/shard_map/ppermute | solution.py:69
  116.2 2.9 %collective-permute-done.19 = f32[8,8]{1,0:T(8,128)S(1)} collective-permute-done((f32[8,8]{1,0:T(8,128)S(1)}, f32[8,8]{1,0:T(8,128)S(1)}, u32[]{:S(2)}, u32[]{:S(2)}) %collective-permute-start.19) | collective-permute-done | bytes 288 | tf_op jit(solution)/shard_map/ppermute | solution.py:69
  119.1 0.6 add.156.g_ref
  119.7 4.9 %shard_map.77 = (f32[8,8]{1,0:T(8,128)}, f32[8,128,256]{2,1,0:T(8,128)}) custom-call(f32[8,8]{1,0:T(8,128)} %add.156.g_ref, f32[8,128,256]{2,1,0:T(8,128)} %get-tuple-element.9.w_ref), custom_call_target="tpu_custom_call" | custom-call | flops 2097152 | bytes 2097152 | tf_op jit(solution)/shard_map/pallas_call | solution.py:205
  (15 shorter events, 0.1 us)
Async XLA Ops:
  0.6 21.0 %collective-permute-start.1 = (f32[4,2,64,256]{3,2,1,0:T(8,128)}, f32[4,2,64,256]{3,2,1,0:T(8,128)S(1)}, u32[]{:S(2)}, u32[]{:S(2)}) collective-permute-start(f32[4,2,64,256]{3,2,1,0:T(8,128)} %param.4), channel_id=1, source_target_pairs={{0,1},{1,2},{2,3},{3,4},{4,5},{5,6},{6,7},{7,8},{8,9},{9,10},{10,1... | collective-permute-start | bytes 1572872 | tf_op jit(solution)/shard_map/ppermute | solution.py:30
  2.7 18.9 %collective-permute-start = (f32[4,2,64,256]{3,2,1,0:T(8,128)}, f32[4,2,64,256]{3,2,1,0:T(8,128)S(1)}, u32[]{:S(2)}, u32[]{:S(2)}) collective-permute-start(f32[4,2,64,256]{3,2,1,0:T(8,128)} %param.4), channel_id=1, source_target_pairs={{1,0},{2,1},{3,2},{4,3},{5,4},{6,5},{7,6},{8,7},{9,8},{10,9},{11,1... | collective-permute-start | bytes 1572872 | tf_op jit(solution)/shard_map/ppermute | solution.py:32
  10.4 2.7 %collective-permute-start.2 = (f32[4,2,2,256]{3,2,1,0:T(2,128)S(1)}, f32[4,2,2,256]{3,2,1,0:T(2,128)S(1)}, u32[]{:S(2)}, u32[]{:S(2)}) collective-permute-start(f32[4,2,2,256]{3,2,1,0:T(2,128)S(1)} %slice_select_fusion.1), channel_id=1, source_target_pairs={{0,64},{64,0},{1,65},{65,1},{2,66},{66,2},{3,67},{67,3},{4,68},{68... | collective-permute-start | bytes 49160 | tf_op jit(solution)/shard_map/ppermute | solution.py:22
  23.2 7.8 %collective-permute-start.5 = (f32[4,2,2,256]{3,2,1,0:T(2,128)S(1)}, f32[4,2,2,256]{3,2,1,0:T(2,128)S(1)}, u32[]{:S(2)}, u32[]{:S(2)}) collective-permute-start(f32[4,2,2,256]{3,2,1,0:T(2,128)S(1)} %slice_select_fusion), channel_id=1, source_target_pairs={{0,64},{64,0},{1,65},{65,1},{2,66},{66,2},{3,67},{67,3},{4,68},{68... | collective-permute-start | bytes 49160 | tf_op jit(solution)/shard_map/ppermute | solution.py:22
  23.5 19.9 %collective-permute-start.4 = (f32[4,2,64,256]{3,2,1,0:T(8,128)S(1)}, f32[4,2,64,256]{3,2,1,0:T(8,128)S(1)}, u32[]{:S(2)}, u32[]{:S(2)}) collective-permute-start(f32[4,2,64,256]{3,2,1,0:T(8,128)S(1)} %get-tuple-element.12), channel_id=1, source_target_pairs={{0,1},{1,2},{2,3},{3,4},{4,5},{5,6},{6,7},{7,8},{8,9},{9,10},{10,1... | collective-permute-start | bytes 1572872 | tf_op jit(solution)/shard_map/ppermute | solution.py:30
  23.5 19.8 %collective-permute-start.3 = (f32[4,2,64,256]{3,2,1,0:T(8,128)S(1)}, f32[4,2,64,256]{3,2,1,0:T(8,128)S(1)}, u32[]{:S(2)}, u32[]{:S(2)}) collective-permute-start(f32[4,2,64,256]{3,2,1,0:T(8,128)S(1)} %get-tuple-element.12), channel_id=1, source_target_pairs={{1,0},{2,1},{3,2},{4,3},{5,4},{6,5},{7,6},{8,7},{9,8},{10,9},{11,1... | collective-permute-start | bytes 1572872 | tf_op jit(solution)/shard_map/ppermute | solution.py:32
  43.8 47.9 %copy-start.1 = (f32[4,2,64,256]{3,2,1,0:T(8,128)}, f32[4,2,64,256]{3,2,1,0:T(8,128)S(1)}, u32[]{:S(2)}) copy-start(f32[4,2,64,256]{3,2,1,0:T(8,128)S(1)} %fusion.43) | copy-start | bytes 1572868
  43.9 38.7 %copy-start = (f32[8,2,64,256]{3,2,1,0:T(8,128)}, f32[8,2,64,256]{3,2,1,0:T(8,128)S(1)}, u32[]{:S(2)}) copy-start(f32[8,2,64,256]{3,2,1,0:T(8,128)S(1)} %pad_maximum_fusion) | copy-start | bytes 3145732
  54.3 1.4 %collective-permute-start.6 = (f32[8,256]{1,0:T(8,128)}, f32[8,256]{1,0:T(8,128)S(1)}, u32[]{:S(2)}, u32[]{:S(2)}) collective-permute-start(f32[8,256]{1,0:T(8,128)} %shard_map.75), channel_id=1, source_target_pairs={{0,64},{64,0},{1,65},{65,1},{2,66},{66,2},{3,67},{67,3},{4,68},{68... | collective-permute-start | bytes 24584 | tf_op jit(solution)/shard_map/ppermute | solution.py:69
  56.4 3.7 %collective-permute-start.7 = (f32[8,256]{1,0:T(8,128)S(1)}, f32[8,256]{1,0:T(8,128)S(1)}, u32[]{:S(2)}, u32[]{:S(2)}) collective-permute-start(f32[8,256]{1,0:T(8,128)S(1)} %add.143), channel_id=1, source_target_pairs={{0,1},{1,0},{2,3},{3,2},{4,5},{5,4},{6,7},{7,6},{8,9},{9,8},{10,11... | collective-permute-start | bytes 24584 | tf_op jit(solution)/shard_map/ppermute | solution.py:69
  60.1 4.9 %collective-permute-start.8 = (f32[8,256]{1,0:T(8,128)S(1)}, f32[8,256]{1,0:T(8,128)S(1)}, u32[]{:S(2)}, u32[]{:S(2)}) collective-permute-start(f32[8,256]{1,0:T(8,128)S(1)} %add.144), channel_id=1, source_target_pairs={{0,3},{1,2},{2,1},{3,0},{4,7},{5,6},{6,5},{7,4},{8,11},{9,10},{10,... | collective-permute-start | bytes 24584 | tf_op jit(solution)/shard_map/ppermute | solution.py:69
  64.9 3.7 %collective-permute-start.9 = (f32[8,256]{1,0:T(8,128)S(1)}, f32[8,256]{1,0:T(8,128)S(1)}, u32[]{:S(2)}, u32[]{:S(2)}) collective-permute-start(f32[8,256]{1,0:T(8,128)S(1)} %add.145), channel_id=1, source_target_pairs={{0,4},{1,5},{2,6},{3,7},{4,0},{5,1},{6,2},{7,3},{8,12},{9,13},{10,... | collective-permute-start | bytes 24584 | tf_op jit(solution)/shard_map/ppermute | solution.py:69
  68.6 4.9 %collective-permute-start.10 = (f32[8,256]{1,0:T(8,128)S(1)}, f32[8,256]{1,0:T(8,128)S(1)}, u32[]{:S(2)}, u32[]{:S(2)}) collective-permute-start(f32[8,256]{1,0:T(8,128)S(1)} %add.146), channel_id=1, source_target_pairs={{0,12},{1,13},{2,14},{3,15},{4,8},{5,9},{6,10},{7,11},{8,4},{9,5},... | collective-permute-start | bytes 24584 | tf_op jit(solution)/shard_map/ppermute | solution.py:69
  73.5 3.7 %collective-permute-start.11 = (f32[8,256]{1,0:T(8,128)S(1)}, f32[8,256]{1,0:T(8,128)S(1)}, u32[]{:S(2)}, u32[]{:S(2)}) collective-permute-start(f32[8,256]{1,0:T(8,128)S(1)} %add.147), channel_id=1, source_target_pairs={{0,16},{1,17},{2,18},{3,19},{4,20},{5,21},{6,22},{7,23},{8,24},{9,... | collective-permute-start | bytes 24584 | tf_op jit(solution)/shard_map/ppermute | solution.py:69
  77.1 4.9 %collective-permute-start.12 = (f32[8,256]{1,0:T(8,128)S(1)}, f32[8,256]{1,0:T(8,128)S(1)}, u32[]{:S(2)}, u32[]{:S(2)}) collective-permute-start(f32[8,256]{1,0:T(8,128)S(1)} %add.148), channel_id=1, source_target_pairs={{0,48},{1,49},{2,50},{3,51},{4,52},{5,53},{6,54},{7,55},{8,56},{9,... | collective-permute-start | bytes 24584 | tf_op jit(solution)/shard_map/ppermute | solution.py:69
  91.7 1.4 %collective-permute-start.13 = (f32[8,8]{1,0:T(8,128)}, f32[8,8]{1,0:T(8,128)S(1)}, u32[]{:S(2)}, u32[]{:S(2)}) collective-permute-start(f32[8,8]{1,0:T(8,128)} %get-tuple-element.8), channel_id=1, source_target_pairs={{0,64},{64,0},{1,65},{65,1},{2,66},{66,2},{3,67},{67,3},{4,68},{68... | collective-permute-start | bytes 776 | tf_op jit(solution)/shard_map/ppermute | solution.py:69
  93.8 3.6 %collective-permute-start.14 = (f32[8,8]{1,0:T(8,128)S(1)}, f32[8,8]{1,0:T(8,128)S(1)}, u32[]{:S(2)}, u32[]{:S(2)}) collective-permute-start(f32[8,8]{1,0:T(8,128)S(1)} %add.150), channel_id=1, source_target_pairs={{0,1},{1,0},{2,3},{3,2},{4,5},{5,4},{6,7},{7,6},{8,9},{9,8},{10,11... | collective-permute-start | bytes 776 | tf_op jit(solution)/shard_map/ppermute | solution.py:69
  97.4 4.8 %collective-permute-start.15 = (f32[8,8]{1,0:T(8,128)S(1)}, f32[8,8]{1,0:T(8,128)S(1)}, u32[]{:S(2)}, u32[]{:S(2)}) collective-permute-start(f32[8,8]{1,0:T(8,128)S(1)} %add.151), channel_id=1, source_target_pairs={{0,3},{1,2},{2,1},{3,0},{4,7},{5,6},{6,5},{7,4},{8,11},{9,10},{10,... | collective-permute-start | bytes 776 | tf_op jit(solution)/shard_map/ppermute | solution.py:69
  102.2 3.6 %collective-permute-start.16 = (f32[8,8]{1,0:T(8,128)S(1)}, f32[8,8]{1,0:T(8,128)S(1)}, u32[]{:S(2)}, u32[]{:S(2)}) collective-permute-start(f32[8,8]{1,0:T(8,128)S(1)} %add.152), channel_id=1, source_target_pairs={{0,4},{1,5},{2,6},{3,7},{4,0},{5,1},{6,2},{7,3},{8,12},{9,13},{10,... | collective-permute-start | bytes 776 | tf_op jit(solution)/shard_map/ppermute | solution.py:69
  105.8 4.8 %collective-permute-start.17 = (f32[8,8]{1,0:T(8,128)S(1)}, f32[8,8]{1,0:T(8,128)S(1)}, u32[]{:S(2)}, u32[]{:S(2)}) collective-permute-start(f32[8,8]{1,0:T(8,128)S(1)} %add.153), channel_id=1, source_target_pairs={{0,12},{1,13},{2,14},{3,15},{4,8},{5,9},{6,10},{7,11},{8,4},{9,5},... | collective-permute-start | bytes 776 | tf_op jit(solution)/shard_map/ppermute | solution.py:69
  110.7 3.6 %collective-permute-start.18 = (f32[8,8]{1,0:T(8,128)S(1)}, f32[8,8]{1,0:T(8,128)S(1)}, u32[]{:S(2)}, u32[]{:S(2)}) collective-permute-start(f32[8,8]{1,0:T(8,128)S(1)} %add.154), channel_id=1, source_target_pairs={{0,16},{1,17},{2,18},{3,19},{4,20},{5,21},{6,22},{7,23},{8,24},{9,... | collective-permute-start | bytes 776 | tf_op jit(solution)/shard_map/ppermute | solution.py:69
  114.3 4.8 %collective-permute-start.19 = (f32[8,8]{1,0:T(8,128)S(1)}, f32[8,8]{1,0:T(8,128)S(1)}, u32[]{:S(2)}, u32[]{:S(2)}) collective-permute-start(f32[8,8]{1,0:T(8,128)S(1)} %add.155), channel_id=1, source_target_pairs={{0,48},{1,49},{2,50},{3,51},{4,52},{5,53},{6,54},{7,55},{8,56},{9,... | collective-permute-start | bytes 776 | tf_op jit(solution)/shard_map/ppermute | solution.py:69

commit v13 on v12

--- a/solution.py
+++ b/solution.py
@@ -70,14 +70,14 @@
     return value
 
 
-def project_kernel(b_ref, s_ref, o_ref):
+def project_kernel(b_ref, first_ref, second_ref, o_ref):
     tk, nr, nz = b_ref.shape
-    ns = s_ref.shape[0]
+    ns = first_ref.shape[0] + second_ref.shape[0]
     acc = jnp.zeros((tk * ROWS, ns * ROWS), jnp.float32)
     for j in range(nr // ROWS):
         rows = pl.ds(j * ROWS, ROWS)
         lhs = b_ref[:, rows, :].reshape(tk * ROWS, nz)
-        rhs = s_ref[:, rows, :].reshape(ns * ROWS, nz)
+        rhs = jnp.concatenate([first_ref[:, rows, :], second_ref[:, rows, :]], axis=0).reshape(ns * ROWS, nz)
         acc = acc + lax.dot_general(lhs, rhs, (((1,), (1,)), ((), ())), preferred_element_type=jnp.float32)
     row_t = lax.broadcasted_iota(jnp.int32, acc.shape, 0) % ROWS
     col_t = lax.broadcasted_iota(jnp.int32, acc.shape, 1) % ROWS
@@ -90,19 +90,20 @@
                                  precision=lax.Precision.HIGHEST, preferred_element_type=jnp.float32)
 
 
-def project(basis3, snaps3, tk=128):
+def project(basis3, first3, second3, tk=128):
     nk, nr, nz = basis3.shape
-    ns = snaps3.shape[0]
+    ns = first3.shape[0] + second3.shape[0]
     return pl.pallas_call(
         project_kernel,
         grid=(nk // tk,),
         in_specs=[pl.BlockSpec((tk, nr, nz), lambda i: (i, 0, 0)),
-                  pl.BlockSpec((ns, nr, nz), lambda i: (0, 0, 0))],
+                  pl.BlockSpec(first3.shape, lambda i: (0, 0, 0)),
+                  pl.BlockSpec(second3.shape, lambda i: (0, 0, 0))],
         out_specs=pl.BlockSpec((ns, tk), lambda i: (0, i)),
         out_shape=jax.ShapeDtypeStruct((ns, nk), jnp.float32),
         cost_estimate=pl.CostEstimate(flops=2 * nk * nr * nz * ns * ROWS, transcendentals=0,
                                       bytes_accessed=nk * nr * nz * 2 + ns * nr * nz * 2 + nk * ns * 4),
-    )(basis3, snaps3)
+    )(basis3, first3, second3)
 
 
 def residual_kernel(c_ref, b_ref, s_ref, o_ref, g_ref, spread_ref, acc_ref):
@@ -268,7 +269,9 @@
     ns = snapshots.shape[0]
     snaps3 = snapshots.reshape(ns, -1, snapshots.shape[3])
     basis3 = basis.reshape(basis.shape[0], -1, basis.shape[3])
-    partial_proj = project(basis3, snaps3.astype(jnp.bfloat16))
+    first3 = segment_one.reshape(segment_one.shape[0], -1, segment_one.shape[3]).astype(jnp.bfloat16)
+    second3 = advanced.reshape(advanced.shape[0], -1, advanced.shape[3]).astype(jnp.bfloat16)
+    partial_proj = project(basis3, first3, second3)
     coeffs_t = allreduce(partial_proj, ("role", "slab"))
     coeffs = coeffs_t.T
     residual3, local_gram = residual(coeffs_t, basis3, snaps3)

time: 125 us -> 125 us (level)
  other arithmetic: 13.6 us -> 15.1 us
    convert_element_type x1 -> x2, other arithmetic: 0.98 us -> 3.45 us  [the longest x1 2.32 us: on_device(): segment_one.reshape(segment_one.shape[0], -1, segment_one.shape[3])]
    add x2 -> x0, other arithmetic: 2.01 us -> none  [the longest x1 1.61 us: on_device(): segment_one = velocity + time_step * (8.0 / 15.0) * tend_zero]
  transfers between devices with their start and end apart: 20 -> 20, of which waited for: 16 -> 16; matrix products, arithmetic and copies ran while one was open for 8% -> 9% of each run, Pallas kernels for 0% -> 0%
where the time goes in v13:
time: 125 us
  waiting for transfers between devices  59.2 us (47%)
  starting transfers between devices  24.3 us (19%)
  Pallas kernels  23.7 us (19%)
  other arithmetic  15.1 us (12%)
  local copies, waits for them, and re-layouts  2.07 us (2%)
    ppermute x14, waiting for transfers between devices, allreduce(): value = value + lax.ppermute(value, name, pairs)  44.8 us
    ppermute x2, waiting for transfers between devices, extended(): lax.ppermute(tail, axis, [(i, (i + 1) % count) for i in range(ends)])  14.4 us
    ppermute x2, starting transfers between devices, extended(): lax.ppermute(head, axis, [((i + 1) % count, i) for i in range(ends)])  14.3 us
    pallas_call x1, Pallas kernels, project(): pl.pallas_call(project_kernel, grid=(nk // tk,), in_specs=[pl.BlockSpec((...  9.65 us
    pallas_call x1, Pallas kernels, residual(): pl.pallas_call(residual_kernel, grid=(nr // block_rows,), in_specs=[pl.Bl...  9.12 us
    ppermute x14, starting transfers between devices, allreduce(): value = value + lax.ppermute(value, name, pairs)  7.69 us
    mul x2, other arithmetic, local_terms(): viscosity * (second_diff(ypadded, center, 2, ny_loc) + second_diff(zpadde...  5.24 us
    pallas_call x1, Pallas kernels, factor_and_solve(): pl.pallas_call(factor_kernel, in_specs=[vmem, vmem], out_specs=[vmem, vme...  4.89 us
  transfers between devices with their start and end apart: 20, of which 16 were waited for; matrix products, arithmetic and copies ran while one was open for 9% of the time, Pallas kernels for 0%

profile of v13, /device:TPU:0, one launch (start us, length us, event | category | flops | bytes accessed | tf_op | source)
XLA Modules:
  0.0 125.1 jit_solution(16809432116302598543)
XLA Ops:
  0.6 2.1 %collective-permute-start.1 = (f32[4,2,64,256]{3,2,1,0:T(8,128)}, f32[4,2,64,256]{3,2,1,0:T(8,128)S(1)}, u32[]{:S(2)}, u32[]{:S(2)}) collective-permute-start(f32[4,2,64,256]{3,2,1,0:T(8,128)} %param.4), channel_id=1, source_target_pairs={{0,1},{1,2},{2,3},{3,4},{4,5},{5,6},{6,7},{7,8},{8,9},{9,10},{10,1... | collective-permute-start | bytes 1572872 | tf_op jit(solution)/shard_map/ppermute | solution.py:30
  2.7 6.8 %collective-permute-start = (f32[4,2,64,256]{3,2,1,0:T(8,128)}, f32[4,2,64,256]{3,2,1,0:T(8,128)S(1)}, u32[]{:S(2)}, u32[]{:S(2)}) collective-permute-start(f32[4,2,64,256]{3,2,1,0:T(8,128)} %param.4), channel_id=1, source_target_pairs={{1,0},{2,1},{3,2},{4,3},{5,4},{6,5},{7,6},{8,7},{9,8},{10,9},{11,1... | collective-permute-start | bytes 1572872 | tf_op jit(solution)/shard_map/ppermute | solution.py:32
  9.5 0.9 slice_select_fusion.1
  10.4 0.1 collective-permute-start.2
  10.5 1.2 fusion.49
  11.7 0.7 negate_multiply_fusion
  12.4 0.7 dynamic_slice.7
  13.2 0.0 collective-permute-done.2
  13.2 4.4 %fusion.15 = f32[4,2,64,256]{3,2,1,0:T(8,128)S(1)} fusion(f32[4,2,2,256]{3,2,1,0:T(2,128)S(1)} %get-tuple-element.24, f32[4,2,64,256]{3,2,1,0:T(8,128)} %param.4, f32[4,2,2,256]{3,2,1,0:T(2,128)S(1)} %get-tuple-element.23, f32[4,2,64,2]{3,2,1,0:T(8,128)S(1)} %get-tuple-element.20, f32[4,2,64,2]{3,2,1,0:T(8,128)S(1)} %get-tuple-element.19), kind=kLoop, calls=%fused_computation.32 | loop fusion | flops 3276800 | bytes 1089536 | tf_op jit(solution)/shard_map/mul | solution.py:235
  17.6 1.0 slice_subtract_fusion
  18.6 3.0 %collective-permute-done.1 = f32[4,2,64,256]{3,2,1,0:T(8,128)S(1)} collective-permute-done((f32[4,2,64,256]{3,2,1,0:T(8,128)}, f32[4,2,64,256]{3,2,1,0:T(8,128)S(1)}, u32[]{:S(2)}, u32[]{:S(2)}) %collective-permute-start.1) | collective-permute-done | bytes 524320 | tf_op jit(solution)/shard_map/ppermute | solution.py:30
  21.6 0.0 collective-permute-done
  21.6 2.3 %fusion.47 = (bf16[4,2,64,256]{3,2,1,0:T(8,128)(2,1)}, f32[4,2,64,256]{3,2,1,0:T(8,128)S(1)}, f32[4,2,64,256]{3,2,1,0:T(8,128)S(1)}) fusion(f32[4,2,64,256]{3,2,1,0:T(8,128)} %param.4, f32[3,2,64,256]{3,2,1,0:T(8,128)S(1)} %slice.169, f32[1,2,64,256]{3,2,1,0:T(8,128)S(1)} %slice_subtract_fusion, f32[4,2,64,256]{3,2,1,0:T(8,128)S(1)} %collective-permute-done.1, ...), kind=kLoop, calls=%fused_computation.87 | loop fusion | flops 3014656 | bytes 3408128 | tf_op jit(solution)/shard_map/convert_element_type | solution.py:272
  23.9 0.1 collective-permute-start.5
  24.0 0.1 fusion.48
  24.2 0.1 collective-permute-start.4
  24.2 7.5 %collective-permute-start.3 = (f32[4,2,64,256]{3,2,1,0:T(8,128)S(1)}, f32[4,2,64,256]{3,2,1,0:T(8,128)S(1)}, u32[]{:S(2)}, u32[]{:S(2)}) collective-permute-start(f32[4,2,64,256]{3,2,1,0:T(8,128)S(1)} %get-tuple-element.15), channel_id=1, source_target_pairs={{1,0},{2,1},{3,2},{4,3},{5,4},{6,5},{7,6},{8,7},{9,8},{10,9},{11,1... | collective-permute-start | bytes 1572872 | tf_op jit(solution)/shard_map/ppermute | solution.py:32
  31.7 0.0 collective-permute-done.5
  31.7 0.8 fusion.5
  32.6 0.1 fusion.44
  32.7 11.4 %collective-permute-done.4 = f32[4,2,64,256]{3,2,1,0:T(8,128)S(1)} collective-permute-done((f32[4,2,64,256]{3,2,1,0:T(8,128)S(1)}, f32[4,2,64,256]{3,2,1,0:T(8,128)S(1)}, u32[]{:S(2)}, u32[]{:S(2)}) %collective-permute-start.4) | collective-permute-done | bytes 524320 | tf_op jit(solution)/shard_map/ppermute | solution.py:30
  44.1 0.0 collective-permute-done.3
  44.1 1.1 fusion.45
  45.2 0.0 copy-start
  45.2 9.7 %shard_map.75 = f32[8,256]{1,0:T(8,128)} custom-call(bf16[256,128,256]{2,1,0:T(8,128)(2,1)} %bitcast.6, bf16[4,128,256]{2,1,0:T(8,128)(2,1)} %bitcast.9, bf16[4,128,256]{2,1,0:T(8,128)(2,1)} %bitcast.10), custom_call_target="tpu_custom_call" | custom-call | flops 2147483648 | bytes 17309696 | tf_op jit(solution)/shard_map/pallas_call | solution.py:96
  54.9 0.0 collective-permute-start.6
  54.9 1.4 %collective-permute-done.6 = f32[8,256]{1,0:T(8,128)S(1)} collective-permute-done((f32[8,256]{1,0:T(8,128)}, f32[8,256]{1,0:T(8,128)S(1)}, u32[]{:S(2)}, u32[]{:S(2)}) %collective-permute-start.6) | collective-permute-done | bytes 8224 | tf_op jit(solution)/shard_map/ppermute | solution.py:69
  56.2 0.7 add.143
  56.9 0.0 collective-permute-start.7
  56.9 3.6 %collective-permute-done.7 = f32[8,256]{1,0:T(8,128)S(1)} collective-permute-done((f32[8,256]{1,0:T(8,128)S(1)}, f32[8,256]{1,0:T(8,128)S(1)}, u32[]{:S(2)}, u32[]{:S(2)}) %collective-permute-start.7) | collective-permute-done | bytes 8224 | tf_op jit(solution)/shard_map/ppermute | solution.py:69
  60.6 0.0 collective-permute-start.8
  60.6 4.9 %collective-permute-done.8 = f32[8,256]{1,0:T(8,128)S(1)} collective-permute-done((f32[8,256]{1,0:T(8,128)S(1)}, f32[8,256]{1,0:T(8,128)S(1)}, u32[]{:S(2)}, u32[]{:S(2)}) %collective-permute-start.8) | collective-permute-done | bytes 8224 | tf_op jit(solution)/shard_map/ppermute | solution.py:69
  65.5 0.0 collective-permute-start.9
  65.5 3.6 %collective-permute-done.9 = f32[8,256]{1,0:T(8,128)S(1)} collective-permute-done((f32[8,256]{1,0:T(8,128)S(1)}, f32[8,256]{1,0:T(8,128)S(1)}, u32[]{:S(2)}, u32[]{:S(2)}) %collective-permute-start.9) | collective-permute-done | bytes 8224 | tf_op jit(solution)/shard_map/ppermute | solution.py:69
  69.1 0.0 collective-permute-start.10
  69.1 4.9 %collective-permute-done.10 = f32[8,256]{1,0:T(8,128)S(1)} collective-permute-done((f32[8,256]{1,0:T(8,128)S(1)}, f32[8,256]{1,0:T(8,128)S(1)}, u32[]{:S(2)}, u32[]{:S(2)}) %collective-permute-start.10) | collective-permute-done | bytes 8224 | tf_op jit(solution)/shard_map/ppermute | solution.py:69
  74.0 0.0 collective-permute-start.11
  74.0 3.6 %collective-permute-done.11 = f32[8,256]{1,0:T(8,128)S(1)} collective-permute-done((f32[8,256]{1,0:T(8,128)S(1)}, f32[8,256]{1,0:T(8,128)S(1)}, u32[]{:S(2)}, u32[]{:S(2)}) %collective-permute-start.11) | collective-permute-done | bytes 8224 | tf_op jit(solution)/shard_map/ppermute | solution.py:69
  77.6 1.9 %collective-permute-start.12 = (f32[8,256]{1,0:T(8,128)S(1)}, f32[8,256]{1,0:T(8,128)S(1)}, u32[]{:S(2)}, u32[]{:S(2)}) collective-permute-start(f32[8,256]{1,0:T(8,128)S(1)} %add.148), channel_id=1, source_target_pairs={{0,48},{1,49},{2,50},{3,51},{4,52},{5,53},{6,54},{7,55},{8,56},{9,... | collective-permute-start | bytes 24584 | tf_op jit(solution)/shard_map/ppermute | solution.py:69
  79.5 1.1 pad_maximum_fusion
  80.6 1.9 %collective-permute-done.12 = f32[8,256]{1,0:T(8,128)S(1)} collective-permute-done((f32[8,256]{1,0:T(8,128)S(1)}, f32[8,256]{1,0:T(8,128)S(1)}, u32[]{:S(2)}, u32[]{:S(2)}) %collective-permute-start.12) | collective-permute-done | bytes 8224 | tf_op jit(solution)/shard_map/ppermute | solution.py:69
  82.5 0.6 add.149.c_ref
  83.1 9.1 %shard_map.76 = (f32[8,128,256]{2,1,0:T(8,128)}, f32[8,8]{1,0:T(8,128)}) custom-call(f32[8,256]{1,0:T(8,128)} %add.149.c_ref, bf16[256,128,256]{2,1,0:T(8,128)(2,1)} %bitcast.7, f32[8,128,256]{2,1,0:T(8,128)} %bitcast.8), custom_call_target="tpu_custom_call" | custom-call | flops 2147483648 | bytes 18874368 | tf_op jit(solution)/shard_map/pallas_call | solution.py:159
  92.2 0.0 copy-done
  92.2 0.0 collective-permute-start.13
  92.3 1.4 %collective-permute-done.13 = f32[8,8]{1,0:T(8,128)S(1)} collective-permute-done((f32[8,8]{1,0:T(8,128)}, f32[8,8]{1,0:T(8,128)S(1)}, u32[]{:S(2)}, u32[]{:S(2)}) %collective-permute-start.13) | collective-permute-done | bytes 288 | tf_op jit(solution)/shard_map/ppermute | solution.py:69
  93.6 0.7 add.150
  94.3 0.0 collective-permute-start.14
  94.3 3.6 %collective-permute-done.14 = f32[8,8]{1,0:T(8,128)S(1)} collective-permute-done((f32[8,8]{1,0:T(8,128)S(1)}, f32[8,8]{1,0:T(8,128)S(1)}, u32[]{:S(2)}, u32[]{:S(2)}) %collective-permute-start.14) | collective-permute-done | bytes 288 | tf_op jit(solution)/shard_map/ppermute | solution.py:69
  97.9 1.9 %collective-permute-start.15 = (f32[8,8]{1,0:T(8,128)S(1)}, f32[8,8]{1,0:T(8,128)S(1)}, u32[]{:S(2)}, u32[]{:S(2)}) collective-permute-start(f32[8,8]{1,0:T(8,128)S(1)} %add.151), channel_id=1, source_target_pairs={{0,3},{1,2},{2,1},{3,0},{4,7},{5,6},{6,5},{7,4},{8,11},{9,10},{10,... | collective-permute-start | bytes 776 | tf_op jit(solution)/shard_map/ppermute | solution.py:69
  99.8 2.9 %collective-permute-done.15 = f32[8,8]{1,0:T(8,128)S(1)} collective-permute-done((f32[8,8]{1,0:T(8,128)S(1)}, f32[8,8]{1,0:T(8,128)S(1)}, u32[]{:S(2)}, u32[]{:S(2)}) %collective-permute-start.15) | collective-permute-done | bytes 288 | tf_op jit(solution)/shard_map/ppermute | solution.py:69
  102.7 0.0 collective-permute-start.16
  102.7 3.6 %collective-permute-done.16 = f32[8,8]{1,0:T(8,128)S(1)} collective-permute-done((f32[8,8]{1,0:T(8,128)S(1)}, f32[8,8]{1,0:T(8,128)S(1)}, u32[]{:S(2)}, u32[]{:S(2)}) %collective-permute-start.16) | collective-permute-done | bytes 288 | tf_op jit(solution)/shard_map/ppermute | solution.py:69
  106.4 1.9 %collective-permute-start.17 = (f32[8,8]{1,0:T(8,128)S(1)}, f32[8,8]{1,0:T(8,128)S(1)}, u32[]{:S(2)}, u32[]{:S(2)}) collective-permute-start(f32[8,8]{1,0:T(8,128)S(1)} %add.153), channel_id=1, source_target_pairs={{0,12},{1,13},{2,14},{3,15},{4,8},{5,9},{6,10},{7,11},{8,4},{9,5},... | collective-permute-start | bytes 776 | tf_op jit(solution)/shard_map/ppermute | solution.py:69
  108.3 2.9 %collective-permute-done.17 = f32[8,8]{1,0:T(8,128)S(1)} collective-permute-done((f32[8,8]{1,0:T(8,128)S(1)}, f32[8,8]{1,0:T(8,128)S(1)}, u32[]{:S(2)}, u32[]{:S(2)}) %collective-permute-start.17) | collective-permute-done | bytes 288 | tf_op jit(solution)/shard_map/ppermute | solution.py:69
  111.2 0.0 collective-permute-start.18
  111.2 3.6 %collective-permute-done.18 = f32[8,8]{1,0:T(8,128)S(1)} collective-permute-done((f32[8,8]{1,0:T(8,128)S(1)}, f32[8,8]{1,0:T(8,128)S(1)}, u32[]{:S(2)}, u32[]{:S(2)}) %collective-permute-start.18) | collective-permute-done | bytes 288 | tf_op jit(solution)/shard_map/ppermute | solution.py:69
  114.8 1.9 %collective-permute-start.19 = (f32[8,8]{1,0:T(8,128)S(1)}, f32[8,8]{1,0:T(8,128)S(1)}, u32[]{:S(2)}, u32[]{:S(2)}) collective-permute-start(f32[8,8]{1,0:T(8,128)S(1)} %add.155), channel_id=1, source_target_pairs={{0,48},{1,49},{2,50},{3,51},{4,52},{5,53},{6,54},{7,55},{8,56},{9,... | collective-permute-start | bytes 776 | tf_op jit(solution)/shard_map/ppermute | solution.py:69
  116.7 2.9 %collective-permute-done.19 = f32[8,8]{1,0:T(8,128)S(1)} collective-permute-done((f32[8,8]{1,0:T(8,128)S(1)}, f32[8,8]{1,0:T(8,128)S(1)}, u32[]{:S(2)}, u32[]{:S(2)}) %collective-permute-start.19) | collective-permute-done | bytes 288 | tf_op jit(solution)/shard_map/ppermute | solution.py:69
  119.6 0.6 add.156.g_ref
  120.2 4.9 %shard_map.77 = (f32[8,8]{1,0:T(8,128)}, f32[8,128,256]{2,1,0:T(8,128)}) custom-call(f32[8,8]{1,0:T(8,128)} %add.156.g_ref, f32[8,128,256]{2,1,0:T(8,128)} %get-tuple-element.9.w_ref), custom_call_target="tpu_custom_call" | custom-call | flops 2097152 | bytes 2097152 | tf_op jit(solution)/shard_map/pallas_call | solution.py:206
  (15 shorter events, 0.1 us)
Async XLA Ops:
  0.6 21.0 %collective-permute-start.1 = (f32[4,2,64,256]{3,2,1,0:T(8,128)}, f32[4,2,64,256]{3,2,1,0:T(8,128)S(1)}, u32[]{:S(2)}, u32[]{:S(2)}) collective-permute-start(f32[4,2,64,256]{3,2,1,0:T(8,128)} %param.4), channel_id=1, source_target_pairs={{0,1},{1,2},{2,3},{3,4},{4,5},{5,6},{6,7},{7,8},{8,9},{9,10},{10,1... | collective-permute-start | bytes 1572872 | tf_op jit(solution)/shard_map/ppermute | solution.py:30
  2.7 18.9 %collective-permute-start = (f32[4,2,64,256]{3,2,1,0:T(8,128)}, f32[4,2,64,256]{3,2,1,0:T(8,128)S(1)}, u32[]{:S(2)}, u32[]{:S(2)}) collective-permute-start(f32[4,2,64,256]{3,2,1,0:T(8,128)} %param.4), channel_id=1, source_target_pairs={{1,0},{2,1},{3,2},{4,3},{5,4},{6,5},{7,6},{8,7},{9,8},{10,9},{11,1... | collective-permute-start | bytes 1572872 | tf_op jit(solution)/shard_map/ppermute | solution.py:32
  10.4 2.7 %collective-permute-start.2 = (f32[4,2,2,256]{3,2,1,0:T(2,128)S(1)}, f32[4,2,2,256]{3,2,1,0:T(2,128)S(1)}, u32[]{:S(2)}, u32[]{:S(2)}) collective-permute-start(f32[4,2,2,256]{3,2,1,0:T(2,128)S(1)} %slice_select_fusion.1), channel_id=1, source_target_pairs={{0,64},{64,0},{1,65},{65,1},{2,66},{66,2},{3,67},{67,3},{4,68},{68... | collective-permute-start | bytes 49160 | tf_op jit(solution)/shard_map/ppermute | solution.py:22
  23.9 7.8 %collective-permute-start.5 = (f32[4,2,2,256]{3,2,1,0:T(2,128)S(1)}, f32[4,2,2,256]{3,2,1,0:T(2,128)S(1)}, u32[]{:S(2)}, u32[]{:S(2)}) collective-permute-start(f32[4,2,2,256]{3,2,1,0:T(2,128)S(1)} %slice_select_fusion), channel_id=1, source_target_pairs={{0,64},{64,0},{1,65},{65,1},{2,66},{66,2},{3,67},{67,3},{4,68},{68... | collective-permute-start | bytes 49160 | tf_op jit(solution)/shard_map/ppermute | solution.py:22
  24.2 19.9 %collective-permute-start.4 = (f32[4,2,64,256]{3,2,1,0:T(8,128)S(1)}, f32[4,2,64,256]{3,2,1,0:T(8,128)S(1)}, u32[]{:S(2)}, u32[]{:S(2)}) collective-permute-start(f32[4,2,64,256]{3,2,1,0:T(8,128)S(1)} %get-tuple-element.15), channel_id=1, source_target_pairs={{0,1},{1,2},{2,3},{3,4},{4,5},{5,6},{6,7},{7,8},{8,9},{9,10},{10,1... | collective-permute-start | bytes 1572872 | tf_op jit(solution)/shard_map/ppermute | solution.py:30
  24.2 19.8 %collective-permute-start.3 = (f32[4,2,64,256]{3,2,1,0:T(8,128)S(1)}, f32[4,2,64,256]{3,2,1,0:T(8,128)S(1)}, u32[]{:S(2)}, u32[]{:S(2)}) collective-permute-start(f32[4,2,64,256]{3,2,1,0:T(8,128)S(1)} %get-tuple-element.15), channel_id=1, source_target_pairs={{1,0},{2,1},{3,2},{4,3},{5,4},{6,5},{7,6},{8,7},{9,8},{10,9},{11,1... | collective-permute-start | bytes 1572872 | tf_op jit(solution)/shard_map/ppermute | solution.py:32
  45.2 47.0 %copy-start = (f32[4,2,64,256]{3,2,1,0:T(8,128)}, f32[4,2,64,256]{3,2,1,0:T(8,128)S(1)}, u32[]{:S(2)}) copy-start(f32[4,2,64,256]{3,2,1,0:T(8,128)S(1)} %get-tuple-element.13) | copy-start | bytes 1572868
  54.9 1.4 %collective-permute-start.6 = (f32[8,256]{1,0:T(8,128)}, f32[8,256]{1,0:T(8,128)S(1)}, u32[]{:S(2)}, u32[]{:S(2)}) collective-permute-start(f32[8,256]{1,0:T(8,128)} %shard_map.75), channel_id=1, source_target_pairs={{0,64},{64,0},{1,65},{65,1},{2,66},{66,2},{3,67},{67,3},{4,68},{68... | collective-permute-start | bytes 24584 | tf_op jit(solution)/shard_map/ppermute | solution.py:69
  56.9 3.7 %collective-permute-start.7 = (f32[8,256]{1,0:T(8,128)S(1)}, f32[8,256]{1,0:T(8,128)S(1)}, u32[]{:S(2)}, u32[]{:S(2)}) collective-permute-start(f32[8,256]{1,0:T(8,128)S(1)} %add.143), channel_id=1, source_target_pairs={{0,1},{1,0},{2,3},{3,2},{4,5},{5,4},{6,7},{7,6},{8,9},{9,8},{10,11... | collective-permute-start | bytes 24584 | tf_op jit(solution)/shard_map/ppermute | solution.py:69
  60.6 4.9 %collective-permute-start.8 = (f32[8,256]{1,0:T(8,128)S(1)}, f32[8,256]{1,0:T(8,128)S(1)}, u32[]{:S(2)}, u32[]{:S(2)}) collective-permute-start(f32[8,256]{1,0:T(8,128)S(1)} %add.144), channel_id=1, source_target_pairs={{0,3},{1,2},{2,1},{3,0},{4,7},{5,6},{6,5},{7,4},{8,11},{9,10},{10,... | collective-permute-start | bytes 24584 | tf_op jit(solution)/shard_map/ppermute | solution.py:69
  65.5 3.7 %collective-permute-start.9 = (f32[8,256]{1,0:T(8,128)S(1)}, f32[8,256]{1,0:T(8,128)S(1)}, u32[]{:S(2)}, u32[]{:S(2)}) collective-permute-start(f32[8,256]{1,0:T(8,128)S(1)} %add.145), channel_id=1, source_target_pairs={{0,4},{1,5},{2,6},{3,7},{4,0},{5,1},{6,2},{7,3},{8,12},{9,13},{10,... | collective-permute-start | bytes 24584 | tf_op jit(solution)/shard_map/ppermute | solution.py:69
  69.1 4.9 %collective-permute-start.10 = (f32[8,256]{1,0:T(8,128)S(1)}, f32[8,256]{1,0:T(8,128)S(1)}, u32[]{:S(2)}, u32[]{:S(2)}) collective-permute-start(f32[8,256]{1,0:T(8,128)S(1)} %add.146), channel_id=1, source_target_pairs={{0,12},{1,13},{2,14},{3,15},{4,8},{5,9},{6,10},{7,11},{8,4},{9,5},... | collective-permute-start | bytes 24584 | tf_op jit(solution)/shard_map/ppermute | solution.py:69
  74.0 3.7 %collective-permute-start.11 = (f32[8,256]{1,0:T(8,128)S(1)}, f32[8,256]{1,0:T(8,128)S(1)}, u32[]{:S(2)}, u32[]{:S(2)}) collective-permute-start(f32[8,256]{1,0:T(8,128)S(1)} %add.147), channel_id=1, source_target_pairs={{0,16},{1,17},{2,18},{3,19},{4,20},{5,21},{6,22},{7,23},{8,24},{9,... | collective-permute-start | bytes 24584 | tf_op jit(solution)/shard_map/ppermute | solution.py:69
  77.6 4.9 %collective-permute-start.12 = (f32[8,256]{1,0:T(8,128)S(1)}, f32[8,256]{1,0:T(8,128)S(1)}, u32[]{:S(2)}, u32[]{:S(2)}) collective-permute-start(f32[8,256]{1,0:T(8,128)S(1)} %add.148), channel_id=1, source_target_pairs={{0,48},{1,49},{2,50},{3,51},{4,52},{5,53},{6,54},{7,55},{8,56},{9,... | collective-permute-start | bytes 24584 | tf_op jit(solution)/shard_map/ppermute | solution.py:69
  92.2 1.4 %collective-permute-start.13 = (f32[8,8]{1,0:T(8,128)}, f32[8,8]{1,0:T(8,128)S(1)}, u32[]{:S(2)}, u32[]{:S(2)}) collective-permute-start(f32[8,8]{1,0:T(8,128)} %get-tuple-element.8), channel_id=1, source_target_pairs={{0,64},{64,0},{1,65},{65,1},{2,66},{66,2},{3,67},{67,3},{4,68},{68... | collective-permute-start | bytes 776 | tf_op jit(solution)/shard_map/ppermute | solution.py:69
  94.3 3.6 %collective-permute-start.14 = (f32[8,8]{1,0:T(8,128)S(1)}, f32[8,8]{1,0:T(8,128)S(1)}, u32[]{:S(2)}, u32[]{:S(2)}) collective-permute-start(f32[8,8]{1,0:T(8,128)S(1)} %add.150), channel_id=1, source_target_pairs={{0,1},{1,0},{2,3},{3,2},{4,5},{5,4},{6,7},{7,6},{8,9},{9,8},{10,11... | collective-permute-start | bytes 776 | tf_op jit(solution)/shard_map/ppermute | solution.py:69
  97.9 4.8 %collective-permute-start.15 = (f32[8,8]{1,0:T(8,128)S(1)}, f32[8,8]{1,0:T(8,128)S(1)}, u32[]{:S(2)}, u32[]{:S(2)}) collective-permute-start(f32[8,8]{1,0:T(8,128)S(1)} %add.151), channel_id=1, source_target_pairs={{0,3},{1,2},{2,1},{3,0},{4,7},{5,6},{6,5},{7,4},{8,11},{9,10},{10,... | collective-permute-start | bytes 776 | tf_op jit(solution)/shard_map/ppermute | solution.py:69
  102.7 3.6 %collective-permute-start.16 = (f32[8,8]{1,0:T(8,128)S(1)}, f32[8,8]{1,0:T(8,128)S(1)}, u32[]{:S(2)}, u32[]{:S(2)}) collective-permute-start(f32[8,8]{1,0:T(8,128)S(1)} %add.152), channel_id=1, source_target_pairs={{0,4},{1,5},{2,6},{3,7},{4,0},{5,1},{6,2},{7,3},{8,12},{9,13},{10,... | collective-permute-start | bytes 776 | tf_op jit(solution)/shard_map/ppermute | solution.py:69
  106.4 4.8 %collective-permute-start.17 = (f32[8,8]{1,0:T(8,128)S(1)}, f32[8,8]{1,0:T(8,128)S(1)}, u32[]{:S(2)}, u32[]{:S(2)}) collective-permute-start(f32[8,8]{1,0:T(8,128)S(1)} %add.153), channel_id=1, source_target_pairs={{0,12},{1,13},{2,14},{3,15},{4,8},{5,9},{6,10},{7,11},{8,4},{9,5},... | collective-permute-start | bytes 776 | tf_op jit(solution)/shard_map/ppermute | solution.py:69
  111.2 3.6 %collective-permute-start.18 = (f32[8,8]{1,0:T(8,128)S(1)}, f32[8,8]{1,0:T(8,128)S(1)}, u32[]{:S(2)}, u32[]{:S(2)}) collective-permute-start(f32[8,8]{1,0:T(8,128)S(1)} %add.154), channel_id=1, source_target_pairs={{0,16},{1,17},{2,18},{3,19},{4,20},{5,21},{6,22},{7,23},{8,24},{9,... | collective-permute-start | bytes 776 | tf_op jit(solution)/shard_map/ppermute | solution.py:69
  114.8 4.8 %collective-permute-start.19 = (f32[8,8]{1,0:T(8,128)S(1)}, f32[8,8]{1,0:T(8,128)S(1)}, u32[]{:S(2)}, u32[]{:S(2)}) collective-permute-start(f32[8,8]{1,0:T(8,128)S(1)} %add.155), channel_id=1, source_target_pairs={{0,48},{1,49},{2,50},{3,51},{4,52},{5,53},{6,54},{7,55},{8,56},{9,... | collective-permute-start | bytes 776 | tf_op jit(solution)/shard_map/ppermute | solution.py:69

commit v14 on v11

--- a/solution.py
+++ b/solution.py
@@ -60,14 +60,15 @@
     return [(axis, pairs) for pairs in rounds]
 
 
-def allreduce(value, axes):
+def allreduce_halves(value, axes):
     sizes = [lax.axis_size(axis) for axis in axes]
     if any(size & (size - 1) for size in sizes):
-        return lax.psum(value, axes)
-    for axis, size in zip(axes, sizes):
-        for name, pairs in exchange_rounds(axis, size):
-            value = value + lax.ppermute(value, name, pairs)
-    return value
+        return lax.psum(value, axes), jnp.zeros_like(value)
+    rounds = [step for axis, size in zip(axes, sizes) for step in exchange_rounds(axis, size)]
+    for name, pairs in rounds[:-1]:
+        value = value + lax.ppermute(value, name, pairs)
+    name, pairs = rounds[-1]
+    return value, lax.ppermute(value, name, pairs)
 
 
 def project_kernel(b_ref, s_ref, o_ref):
@@ -105,7 +106,7 @@
     )(basis3, snaps3)
 
 
-def residual_kernel(c_ref, b_ref, s_ref, o_ref, g_ref, spread_ref, acc_ref):
+def residual_kernel(c_ref, d_ref, b_ref, s_ref, o_ref, g_ref, spread_ref, acc_ref):
     nk, _, nz = b_ref.shape
     ns = s_ref.shape[0]
     rows = ROWS
@@ -116,7 +117,7 @@
         col = lax.broadcasted_iota(jnp.int32, (nk, nk * rows), 1)
         row = lax.broadcasted_iota(jnp.int32, (nk, nk * rows), 0)
         expand = jnp.where(col // rows == row, 1.0, 0.0).astype(jnp.bfloat16)
-        wide = jnp.dot(c_ref[...].astype(jnp.bfloat16), expand, preferred_element_type=jnp.float32)
+        wide = jnp.dot((c_ref[...] + d_ref[...]).astype(jnp.bfloat16), expand, preferred_element_type=jnp.float32)
         tall = jnp.broadcast_to(wide[:, None, :], (ns, rows, nk * rows)).reshape(ns * rows, nk * rows)
         r_t = lax.broadcasted_iota(jnp.int32, tall.shape, 0) % rows
         c_t = lax.broadcasted_iota(jnp.int32, tall.shape, 1) % rows
@@ -151,7 +152,7 @@
         g_ref[...] = gram
 
 
-def residual(coeffs_t, basis3, snaps3, block_rows=2 * ROWS):
+def residual(coeffs_t, coeffs_other, basis3, snaps3, block_rows=2 * ROWS):
     nk, nr, nz = basis3.shape
     ns = snaps3.shape[0]
     pairs = ns * (ns + 1) // 2
@@ -159,6 +160,7 @@
         residual_kernel,
         grid=(nr // block_rows,),
         in_specs=[pl.BlockSpec((ns, nk), lambda j: (0, 0)),
+                  pl.BlockSpec((ns, nk), lambda j: (0, 0)),
                   pl.BlockSpec((nk, block_rows, nz), lambda j: (0, j, 0)),
                   pl.BlockSpec((ns, block_rows, nz), lambda j: (0, j, 0))],
         out_specs=[pl.BlockSpec((ns, block_rows, nz), lambda j: (0, j, 0)),
@@ -170,13 +172,13 @@
         compiler_params=pltpu.CompilerParams(dimension_semantics=("arbitrary",)),
         cost_estimate=pl.CostEstimate(flops=2 * ns * ROWS * nk * ROWS * nz * (nr // ROWS), transcendentals=0,
                                       bytes_accessed=nk * nr * nz * 2 + 2 * ns * nr * nz * 4),
-    )(coeffs_t, basis3, snaps3)
+    )(coeffs_t, coeffs_other, basis3, snaps3)
     return w, g
 
 
-def factor_kernel(g_ref, w_ref, u_ref, d_ref):
+def factor_kernel(g_ref, h_ref, w_ref, u_ref, d_ref):
     ns = g_ref.shape[0]
-    gram = g_ref[...]
+    gram = g_ref[...] + h_ref[...]
     row = lax.broadcasted_iota(jnp.int32, (ns, ns), 0)
     col = lax.broadcasted_iota(jnp.int32, (ns, ns), 1)
     upper = jnp.zeros((ns, ns), jnp.float32)
@@ -199,18 +201,18 @@
         d_ref[s] = acc / entry(s, s)
 
 
-def factor_and_solve(gram, residual3):
+def factor_and_solve(gram, gram_other, residual3):
     ns = gram.shape[0]
     vmem = pl.BlockSpec(memory_space=pltpu.VMEM)
     return pl.pallas_call(
         factor_kernel,
-        in_specs=[vmem, vmem],
+        in_specs=[vmem, vmem, vmem],
         out_specs=[vmem, vmem],
         out_shape=[jax.ShapeDtypeStruct((ns, ns), jnp.float32),
                    jax.ShapeDtypeStruct(residual3.shape, jnp.float32)],
         cost_estimate=pl.CostEstimate(flops=ns * ns * residual3[0].size, transcendentals=ns,
                                       bytes_accessed=2 * residual3.size * 4),
-    )(gram, residual3)
+    )(gram, gram_other, residual3)
 
 
 def offset_slice(padded, offset, dimension, length):
@@ -269,11 +271,11 @@
     snaps3 = snapshots.reshape(ns, -1, snapshots.shape[3])
     basis3 = basis.reshape(basis.shape[0], -1, basis.shape[3])
     partial_proj = project(basis3, snaps3.astype(jnp.bfloat16))
-    coeffs_t = allreduce(partial_proj, ("role", "slab"))
-    coeffs = coeffs_t.T
-    residual3, local_gram = residual(coeffs_t, basis3, snaps3)
-    total_gram = allreduce(local_gram, ("role", "slab"))
-    upper_factor, directions = factor_and_solve(total_gram, residual3)
+    coeffs_t, coeffs_other = allreduce_halves(partial_proj, ("role", "slab"))
+    coeffs = (coeffs_t + coeffs_other).T
+    residual3, local_gram = residual(coeffs_t, coeffs_other, basis3, snaps3)
+    gram, gram_other = allreduce_halves(local_gram, ("role", "slab"))
+    upper_factor, directions = factor_and_solve(gram, gram_other, residual3)
     return (advanced, coeffs, upper_factor, directions.reshape(snapshots.shape))
 
 

time: 125 us -> 125 us (level)
  waiting for transfers between devices: 60.3 us -> 59 us
    transpose x0 -> x1, other arithmetic: none -> 1.31 us  [on_device(): coeffs = (coeffs_t + coeffs_other).T]
    ppermute x14, waiting for transfers between devices: 45.9 us -> 44.6 us  [the longest x12 40 us: allreduce_halves(): value = value + lax.ppermute(value, name, pairs)]
    add x14 -> x12, other arithmetic: 2.61 us -> 1.42 us  [allreduce_halves(): value = value + lax.ppermute(value, name, pairs)]
  transfers between devices with their start and end apart: 20 -> 20, of which waited for: 16 -> 16; matrix products, arithmetic and copies ran while one was open for 8% -> 9% of each run, Pallas kernels for 0% -> 0%
where the time goes in v14:
time: 125 us; the launch traced here: 124 us
  waiting for transfers between devices  59 us (47%)
  starting transfers between devices  24.3 us (19%)
  Pallas kernels  23.3 us (19%)
  other arithmetic  13.8 us (11%)
  local copies, waits for them, and re-layouts  3.27 us (3%)
    ppermute x12, waiting for transfers between devices, allreduce_halves(): value = value + lax.ppermute(value, name, pairs)  40 us
    ppermute x2, waiting for transfers between devices, extended(): lax.ppermute(tail, axis, [(i, (i + 1) % count) for i in range(ends)])  14.4 us
    ppermute x2, starting transfers between devices, extended(): lax.ppermute(head, axis, [((i + 1) % count, i) for i in range(ends)])  14.3 us
    pallas_call x1, Pallas kernels, project(): pl.pallas_call(project_kernel, grid=(nk // tk,), in_specs=[pl.BlockSpec((...  9.48 us
    pallas_call x1, Pallas kernels, residual(): pl.pallas_call(residual_kernel, grid=(nr // block_rows,), in_specs=[pl.Bl...  9.07 us
    mul x2, other arithmetic, local_terms(): viscosity * (second_diff(ypadded, center, 2, ny_loc) + second_diff(zpadde...  5.22 us
    pallas_call x1, Pallas kernels, factor_and_solve(): pl.pallas_call(factor_kernel, in_specs=[vmem, vmem, vmem], out_specs=[vme...  4.79 us
    ppermute x2, waiting for transfers between devices, allreduce_halves(): return (value, lax.ppermute(value, name, pairs))  4.56 us
  transfers between devices with their start and end apart: 20, of which 16 were waited for; matrix products, arithmetic and copies ran while one was open for 9% of the time, Pallas kernels for 0%

profile of v14, /device:TPU:0, one launch (start us, length us, event | category | flops | bytes accessed | tf_op | source)
XLA Modules:
  0.0 124.5 jit_solution(6775084876104300711)
XLA Ops:
  0.6 2.1 %collective-permute-start.1 = (f32[4,2,64,256]{3,2,1,0:T(8,128)}, f32[4,2,64,256]{3,2,1,0:T(8,128)S(1)}, u32[]{:S(2)}, u32[]{:S(2)}) collective-permute-start(f32[4,2,64,256]{3,2,1,0:T(8,128)} %param.4), channel_id=1, source_target_pairs={{0,1},{1,2},{2,3},{3,4},{4,5},{5,6},{6,7},{7,8},{8,9},{9,10},{10,1... | collective-permute-start | bytes 1572872 | tf_op jit(solution)/shard_map/ppermute | solution.py:30
  2.7 6.8 %collective-permute-start = (f32[4,2,64,256]{3,2,1,0:T(8,128)}, f32[4,2,64,256]{3,2,1,0:T(8,128)S(1)}, u32[]{:S(2)}, u32[]{:S(2)}) collective-permute-start(f32[4,2,64,256]{3,2,1,0:T(8,128)} %param.4), channel_id=1, source_target_pairs={{1,0},{2,1},{3,2},{4,3},{5,4},{6,5},{7,6},{8,7},{9,8},{10,9},{11,1... | collective-permute-start | bytes 1572872 | tf_op jit(solution)/shard_map/ppermute | solution.py:32
  9.5 0.9 slice_select_fusion.1
  10.4 0.1 collective-permute-start.2
  10.5 1.2 fusion.46
  11.7 0.7 negate_multiply_fusion
  12.4 0.7 dynamic_slice.7
  13.2 0.0 collective-permute-done.2
  13.2 4.4 %fusion.15 = f32[4,2,64,256]{3,2,1,0:T(8,128)S(1)} fusion(f32[4,2,2,256]{3,2,1,0:T(2,128)S(1)} %get-tuple-element.21, f32[4,2,64,256]{3,2,1,0:T(8,128)} %param.4, f32[4,2,2,256]{3,2,1,0:T(2,128)S(1)} %get-tuple-element.20, f32[4,2,64,2]{3,2,1,0:T(8,128)S(1)} %get-tuple-element.17, f32[4,2,64,2]{3,2,1,0:T(8,128)S(1)} %get-tuple-element.16), kind=kLoop, calls=%fused_computation.32 | loop fusion | flops 3276800 | bytes 1089536 | tf_op jit(solution)/shard_map/mul | solution.py:236
  17.6 1.0 slice_subtract_fusion
  18.6 3.0 %collective-permute-done.1 = f32[4,2,64,256]{3,2,1,0:T(8,128)S(1)} collective-permute-done((f32[4,2,64,256]{3,2,1,0:T(8,128)}, f32[4,2,64,256]{3,2,1,0:T(8,128)S(1)}, u32[]{:S(2)}, u32[]{:S(2)}) %collective-permute-start.1) | collective-permute-done | bytes 524320 | tf_op jit(solution)/shard_map/ppermute | solution.py:30
  21.6 0.0 collective-permute-done
  21.6 1.6 %multiply_add_fusion = (f32[4,2,64,256]{3,2,1,0:T(8,128)S(1)}, f32[4,2,64,256]{3,2,1,0:T(8,128)S(1)}) fusion(f32[4,2,64,256]{3,2,1,0:T(8,128)} %param.4, f32[3,2,64,256]{3,2,1,0:T(8,128)S(1)} %slice.169, f32[1,2,64,256]{3,2,1,0:T(8,128)S(1)} %slice_subtract_fusion, f32[4,2,64,256]{3,2,1,0:T(8,128)S(1)} %collective-permute-done.1, ...), kind=kLoop, calls=%fused_computation.75 | loop fusion | flops 2883584 | bytes 3145984 | tf_op jit(solution)/shard_map/add | solution.py:266
  23.2 0.1 collective-permute-start.5
  23.3 0.1 fusion.45
  23.5 0.1 collective-permute-start.4
  23.5 7.5 %collective-permute-start.3 = (f32[4,2,64,256]{3,2,1,0:T(8,128)S(1)}, f32[4,2,64,256]{3,2,1,0:T(8,128)S(1)}, u32[]{:S(2)}, u32[]{:S(2)}) collective-permute-start(f32[4,2,64,256]{3,2,1,0:T(8,128)S(1)} %get-tuple-element.12), channel_id=1, source_target_pairs={{1,0},{2,1},{3,2},{4,3},{5,4},{6,5},{7,6},{8,7},{9,8},{10,9},{11,1... | collective-permute-start | bytes 1572872 | tf_op jit(solution)/shard_map/ppermute | solution.py:32
  31.0 0.0 collective-permute-done.5
  31.0 0.8 fusion.5
  31.9 0.1 fusion.44
  32.0 11.4 %collective-permute-done.4 = f32[4,2,64,256]{3,2,1,0:T(8,128)S(1)} collective-permute-done((f32[4,2,64,256]{3,2,1,0:T(8,128)S(1)}, f32[4,2,64,256]{3,2,1,0:T(8,128)S(1)}, u32[]{:S(2)}, u32[]{:S(2)}) %collective-permute-start.4) | collective-permute-done | bytes 524320 | tf_op jit(solution)/shard_map/ppermute | solution.py:30
  43.4 0.0 collective-permute-done.3
  43.4 0.4 fusion.43
  43.8 0.0 copy-start.1
  43.8 0.1 pad_maximum_fusion
  43.9 0.0 copy-start
  43.9 1.0 bitcast_convert_fusion.s_ref
  44.9 9.5 %shard_map.75 = f32[8,256]{1,0:T(8,128)} custom-call(bf16[256,128,256]{2,1,0:T(8,128)(2,1)} %bitcast.6, bf16[8,128,256]{2,1,0:T(8,128)(2,1)} %bitcast_convert_fusion.s_ref), custom_call_target="tpu_custom_call" | custom-call | flops 2147483648 | bytes 17309696 | tf_op jit(solution)/shard_map/pallas_call | solution.py:97
  54.3 0.0 collective-permute-start.6
  54.3 1.4 %collective-permute-done.6 = f32[8,256]{1,0:T(8,128)S(1)} collective-permute-done((f32[8,256]{1,0:T(8,128)}, f32[8,256]{1,0:T(8,128)S(1)}, u32[]{:S(2)}, u32[]{:S(2)}) %collective-permute-start.6) | collective-permute-done | bytes 8224 | tf_op jit(solution)/shard_map/ppermute | solution.py:69
  55.7 0.7 add.140
  56.4 0.0 collective-permute-start.7
  56.4 3.6 %collective-permute-done.7 = f32[8,256]{1,0:T(8,128)S(1)} collective-permute-done((f32[8,256]{1,0:T(8,128)S(1)}, f32[8,256]{1,0:T(8,128)S(1)}, u32[]{:S(2)}, u32[]{:S(2)}) %collective-permute-start.7) | collective-permute-done | bytes 8224 | tf_op jit(solution)/shard_map/ppermute | solution.py:69
  60.1 0.0 collective-permute-start.8
  60.1 4.9 %collective-permute-done.8 = f32[8,256]{1,0:T(8,128)S(1)} collective-permute-done((f32[8,256]{1,0:T(8,128)S(1)}, f32[8,256]{1,0:T(8,128)S(1)}, u32[]{:S(2)}, u32[]{:S(2)}) %collective-permute-start.8) | collective-permute-done | bytes 8224 | tf_op jit(solution)/shard_map/ppermute | solution.py:69
  64.9 0.0 collective-permute-start.9
  64.9 3.6 %collective-permute-done.9 = f32[8,256]{1,0:T(8,128)S(1)} collective-permute-done((f32[8,256]{1,0:T(8,128)S(1)}, f32[8,256]{1,0:T(8,128)S(1)}, u32[]{:S(2)}, u32[]{:S(2)}) %collective-permute-start.9) | collective-permute-done | bytes 8224 | tf_op jit(solution)/shard_map/ppermute | solution.py:69
  68.6 0.0 collective-permute-start.10
  68.6 4.9 %collective-permute-done.10 = f32[8,256]{1,0:T(8,128)S(1)} collective-permute-done((f32[8,256]{1,0:T(8,128)S(1)}, f32[8,256]{1,0:T(8,128)S(1)}, u32[]{:S(2)}, u32[]{:S(2)}) %collective-permute-start.10) | collective-permute-done | bytes 8224 | tf_op jit(solution)/shard_map/ppermute | solution.py:69
  73.5 0.0 collective-permute-start.11
  73.5 3.6 %collective-permute-done.11 = f32[8,256]{1,0:T(8,128)S(1)} collective-permute-done((f32[8,256]{1,0:T(8,128)S(1)}, f32[8,256]{1,0:T(8,128)S(1)}, u32[]{:S(2)}, u32[]{:S(2)}) %collective-permute-start.11) | collective-permute-done | bytes 8224 | tf_op jit(solution)/shard_map/ppermute | solution.py:69
  77.1 1.9 %collective-permute-start.12 = (f32[8,256]{1,0:T(8,128)S(1)}, f32[8,256]{1,0:T(8,128)S(1)}, u32[]{:S(2)}, u32[]{:S(2)}) collective-permute-start(f32[8,256]{1,0:T(8,128)S(1)} %add.145.c_ref), channel_id=1, source_target_pairs={{0,48},{1,49},{2,50},{3,51},{4,52},{5,53},{6,54},{7,55},{8,56},{9,... | collective-permute-start | bytes 24584 | tf_op jit(solution)/shard_map/ppermute | solution.py:71
  79.0 3.0 %collective-permute-done.12.d_ref = f32[8,256]{1,0:T(8,128)S(1)} collective-permute-done((f32[8,256]{1,0:T(8,128)S(1)}, f32[8,256]{1,0:T(8,128)S(1)}, u32[]{:S(2)}, u32[]{:S(2)}) %collective-permute-start.12) | collective-permute-done | bytes 8224 | tf_op jit(solution)/shard_map/ppermute | solution.py:71
  82.0 0.0 copy-done
  82.0 0.6 copy-done.3
  82.6 9.1 %shard_map.76 = (f32[8,128,256]{2,1,0:T(8,128)}, f32[8,8]{1,0:T(8,128)}) custom-call(f32[8,256]{1,0:T(8,128)} %copy-done.2, f32[8,256]{1,0:T(8,128)} %copy-done.3, bf16[256,128,256]{2,1,0:T(8,128)(2,1)} %bitcast.7, f32[8,128,256]{2,1,0:T(8,128)} %bitcast.8), custom_call_target="tpu_custom_call" | custom-call | flops 2147483648 | bytes 18874368 | tf_op jit(solution)/shard_map/pallas_call | solution.py:159
  91.7 0.1 collective-permute-start.13
  91.7 1.4 %collective-permute-done.13 = f32[8,8]{1,0:T(8,128)S(1)} collective-permute-done((f32[8,8]{1,0:T(8,128)}, f32[8,8]{1,0:T(8,128)S(1)}, u32[]{:S(2)}, u32[]{:S(2)}) %collective-permute-start.13) | collective-permute-done | bytes 288 | tf_op jit(solution)/shard_map/ppermute | solution.py:69
  93.1 0.7 add.147
  93.8 0.0 collective-permute-start.14
  93.8 3.6 %collective-permute-done.14 = f32[8,8]{1,0:T(8,128)S(1)} collective-permute-done((f32[8,8]{1,0:T(8,128)S(1)}, f32[8,8]{1,0:T(8,128)S(1)}, u32[]{:S(2)}, u32[]{:S(2)}) %collective-permute-start.14) | collective-permute-done | bytes 288 | tf_op jit(solution)/shard_map/ppermute | solution.py:69
  97.4 1.9 %collective-permute-start.15 = (f32[8,8]{1,0:T(8,128)S(1)}, f32[8,8]{1,0:T(8,128)S(1)}, u32[]{:S(2)}, u32[]{:S(2)}) collective-permute-start(f32[8,8]{1,0:T(8,128)S(1)} %add.148), channel_id=1, source_target_pairs={{0,3},{1,2},{2,1},{3,0},{4,7},{5,6},{6,5},{7,4},{8,11},{9,10},{10,... | collective-permute-start | bytes 776 | tf_op jit(solution)/shard_map/ppermute | solution.py:69
  99.3 2.9 %collective-permute-done.15 = f32[8,8]{1,0:T(8,128)S(1)} collective-permute-done((f32[8,8]{1,0:T(8,128)S(1)}, f32[8,8]{1,0:T(8,128)S(1)}, u32[]{:S(2)}, u32[]{:S(2)}) %collective-permute-start.15) | collective-permute-done | bytes 288 | tf_op jit(solution)/shard_map/ppermute | solution.py:69
  102.2 0.0 collective-permute-start.16
  102.2 3.6 %collective-permute-done.16 = f32[8,8]{1,0:T(8,128)S(1)} collective-permute-done((f32[8,8]{1,0:T(8,128)S(1)}, f32[8,8]{1,0:T(8,128)S(1)}, u32[]{:S(2)}, u32[]{:S(2)}) %collective-permute-start.16) | collective-permute-done | bytes 288 | tf_op jit(solution)/shard_map/ppermute | solution.py:69
  105.8 1.9 %collective-permute-start.17 = (f32[8,8]{1,0:T(8,128)S(1)}, f32[8,8]{1,0:T(8,128)S(1)}, u32[]{:S(2)}, u32[]{:S(2)}) collective-permute-start(f32[8,8]{1,0:T(8,128)S(1)} %add.150), channel_id=1, source_target_pairs={{0,12},{1,13},{2,14},{3,15},{4,8},{5,9},{6,10},{7,11},{8,4},{9,5},... | collective-permute-start | bytes 776 | tf_op jit(solution)/shard_map/ppermute | solution.py:69
  107.7 2.9 %collective-permute-done.17 = f32[8,8]{1,0:T(8,128)S(1)} collective-permute-done((f32[8,8]{1,0:T(8,128)S(1)}, f32[8,8]{1,0:T(8,128)S(1)}, u32[]{:S(2)}, u32[]{:S(2)}) %collective-permute-start.17) | collective-permute-done | bytes 288 | tf_op jit(solution)/shard_map/ppermute | solution.py:69
  110.7 0.0 collective-permute-start.18
  110.7 3.6 %collective-permute-done.18 = f32[8,8]{1,0:T(8,128)S(1)} collective-permute-done((f32[8,8]{1,0:T(8,128)S(1)}, f32[8,8]{1,0:T(8,128)S(1)}, u32[]{:S(2)}, u32[]{:S(2)}) %collective-permute-start.18) | collective-permute-done | bytes 288 | tf_op jit(solution)/shard_map/ppermute | solution.py:69
  114.3 1.9 %collective-permute-start.19 = (f32[8,8]{1,0:T(8,128)S(1)}, f32[8,8]{1,0:T(8,128)S(1)}, u32[]{:S(2)}, u32[]{:S(2)}) collective-permute-start(f32[8,8]{1,0:T(8,128)S(1)} %add.152.g_ref), channel_id=1, source_target_pairs={{0,48},{1,49},{2,50},{3,51},{4,52},{5,53},{6,54},{7,55},{8,56},{9,... | collective-permute-start | bytes 776 | tf_op jit(solution)/shard_map/ppermute | solution.py:71
  116.2 1.3 %add_bitcast_fusion = f32[256,8]{0,1:T(8,128)} fusion(f32[8,256]{1,0:T(8,128)} %copy-done.2, f32[8,256]{1,0:T(8,128)} %copy-done.3), kind=kLoop, calls=%fused_computation.85 | loop fusion | flops 2048 | bytes 24576 | tf_op jit(solution)/shard_map/transpose | solution.py:275
  117.5 1.6 %collective-permute-done.19.h_ref = f32[8,8]{1,0:T(8,128)S(1)} collective-permute-done((f32[8,8]{1,0:T(8,128)S(1)}, f32[8,8]{1,0:T(8,128)S(1)}, u32[]{:S(2)}, u32[]{:S(2)}) %collective-permute-start.19) | collective-permute-done | bytes 288 | tf_op jit(solution)/shard_map/ppermute | solution.py:71
  119.1 0.6 copy-done.5
  119.7 4.8 %shard_map.77 = (f32[8,8]{1,0:T(8,128)}, f32[8,128,256]{2,1,0:T(8,128)}) custom-call(f32[8,8]{1,0:T(8,128)} %copy-done.4, f32[8,8]{1,0:T(8,128)} %copy-done.5, f32[8,128,256]{2,1,0:T(8,128)} %get-tuple-element.9.w_ref), custom_call_target="tpu_custom_call" | custom-call | flops 2097152 | bytes 2097152 | tf_op jit(solution)/shard_map/pallas_call | solution.py:207
  (22 shorter events, 0.1 us)
Async XLA Ops:
  0.6 21.0 %collective-permute-start.1 = (f32[4,2,64,256]{3,2,1,0:T(8,128)}, f32[4,2,64,256]{3,2,1,0:T(8,128)S(1)}, u32[]{:S(2)}, u32[]{:S(2)}) collective-permute-start(f32[4,2,64,256]{3,2,1,0:T(8,128)} %param.4), channel_id=1, source_target_pairs={{0,1},{1,2},{2,3},{3,4},{4,5},{5,6},{6,7},{7,8},{8,9},{9,10},{10,1... | collective-permute-start | bytes 1572872 | tf_op jit(solution)/shard_map/ppermute | solution.py:30
  2.7 18.9 %collective-permute-start = (f32[4,2,64,256]{3,2,1,0:T(8,128)}, f32[4,2,64,256]{3,2,1,0:T(8,128)S(1)}, u32[]{:S(2)}, u32[]{:S(2)}) collective-permute-start(f32[4,2,64,256]{3,2,1,0:T(8,128)} %param.4), channel_id=1, source_target_pairs={{1,0},{2,1},{3,2},{4,3},{5,4},{6,5},{7,6},{8,7},{9,8},{10,9},{11,1... | collective-permute-start | bytes 1572872 | tf_op jit(solution)/shard_map/ppermute | solution.py:32
  10.4 2.7 %collective-permute-start.2 = (f32[4,2,2,256]{3,2,1,0:T(2,128)S(1)}, f32[4,2,2,256]{3,2,1,0:T(2,128)S(1)}, u32[]{:S(2)}, u32[]{:S(2)}) collective-permute-start(f32[4,2,2,256]{3,2,1,0:T(2,128)S(1)} %slice_select_fusion.1), channel_id=1, source_target_pairs={{0,64},{64,0},{1,65},{65,1},{2,66},{66,2},{3,67},{67,3},{4,68},{68... | collective-permute-start | bytes 49160 | tf_op jit(solution)/shard_map/ppermute | solution.py:22
  23.2 7.8 %collective-permute-start.5 = (f32[4,2,2,256]{3,2,1,0:T(2,128)S(1)}, f32[4,2,2,256]{3,2,1,0:T(2,128)S(1)}, u32[]{:S(2)}, u32[]{:S(2)}) collective-permute-start(f32[4,2,2,256]{3,2,1,0:T(2,128)S(1)} %slice_select_fusion), channel_id=1, source_target_pairs={{0,64},{64,0},{1,65},{65,1},{2,66},{66,2},{3,67},{67,3},{4,68},{68... | collective-permute-start | bytes 49160 | tf_op jit(solution)/shard_map/ppermute | solution.py:22
  23.5 19.9 %collective-permute-start.4 = (f32[4,2,64,256]{3,2,1,0:T(8,128)S(1)}, f32[4,2,64,256]{3,2,1,0:T(8,128)S(1)}, u32[]{:S(2)}, u32[]{:S(2)}) collective-permute-start(f32[4,2,64,256]{3,2,1,0:T(8,128)S(1)} %get-tuple-element.12), channel_id=1, source_target_pairs={{0,1},{1,2},{2,3},{3,4},{4,5},{5,6},{6,7},{7,8},{8,9},{9,10},{10,1... | collective-permute-start | bytes 1572872 | tf_op jit(solution)/shard_map/ppermute | solution.py:30
  23.5 19.8 %collective-permute-start.3 = (f32[4,2,64,256]{3,2,1,0:T(8,128)S(1)}, f32[4,2,64,256]{3,2,1,0:T(8,128)S(1)}, u32[]{:S(2)}, u32[]{:S(2)}) collective-permute-start(f32[4,2,64,256]{3,2,1,0:T(8,128)S(1)} %get-tuple-element.12), channel_id=1, source_target_pairs={{1,0},{2,1},{3,2},{4,3},{5,4},{6,5},{7,6},{8,7},{9,8},{10,9},{11,1... | collective-permute-start | bytes 1572872 | tf_op jit(solution)/shard_map/ppermute | solution.py:32
  43.8 47.9 %copy-start.1 = (f32[4,2,64,256]{3,2,1,0:T(8,128)}, f32[4,2,64,256]{3,2,1,0:T(8,128)S(1)}, u32[]{:S(2)}) copy-start(f32[4,2,64,256]{3,2,1,0:T(8,128)S(1)} %fusion.43) | copy-start | bytes 1572868
  43.9 38.1 %copy-start = (f32[8,2,64,256]{3,2,1,0:T(8,128)}, f32[8,2,64,256]{3,2,1,0:T(8,128)S(1)}, u32[]{:S(2)}) copy-start(f32[8,2,64,256]{3,2,1,0:T(8,128)S(1)} %pad_maximum_fusion) | copy-start | bytes 3145732
  54.3 1.4 %collective-permute-start.6 = (f32[8,256]{1,0:T(8,128)}, f32[8,256]{1,0:T(8,128)S(1)}, u32[]{:S(2)}, u32[]{:S(2)}) collective-permute-start(f32[8,256]{1,0:T(8,128)} %shard_map.75), channel_id=1, source_target_pairs={{0,64},{64,0},{1,65},{65,1},{2,66},{66,2},{3,67},{67,3},{4,68},{68... | collective-permute-start | bytes 24584 | tf_op jit(solution)/shard_map/ppermute | solution.py:69
  56.4 3.7 %collective-permute-start.7 = (f32[8,256]{1,0:T(8,128)S(1)}, f32[8,256]{1,0:T(8,128)S(1)}, u32[]{:S(2)}, u32[]{:S(2)}) collective-permute-start(f32[8,256]{1,0:T(8,128)S(1)} %add.140), channel_id=1, source_target_pairs={{0,1},{1,0},{2,3},{3,2},{4,5},{5,4},{6,7},{7,6},{8,9},{9,8},{10,11... | collective-permute-start | bytes 24584 | tf_op jit(solution)/shard_map/ppermute | solution.py:69
  60.1 4.9 %collective-permute-start.8 = (f32[8,256]{1,0:T(8,128)S(1)}, f32[8,256]{1,0:T(8,128)S(1)}, u32[]{:S(2)}, u32[]{:S(2)}) collective-permute-start(f32[8,256]{1,0:T(8,128)S(1)} %add.141), channel_id=1, source_target_pairs={{0,3},{1,2},{2,1},{3,0},{4,7},{5,6},{6,5},{7,4},{8,11},{9,10},{10,... | collective-permute-start | bytes 24584 | tf_op jit(solution)/shard_map/ppermute | solution.py:69
  64.9 3.7 %collective-permute-start.9 = (f32[8,256]{1,0:T(8,128)S(1)}, f32[8,256]{1,0:T(8,128)S(1)}, u32[]{:S(2)}, u32[]{:S(2)}) collective-permute-start(f32[8,256]{1,0:T(8,128)S(1)} %add.142), channel_id=1, source_target_pairs={{0,4},{1,5},{2,6},{3,7},{4,0},{5,1},{6,2},{7,3},{8,12},{9,13},{10,... | collective-permute-start | bytes 24584 | tf_op jit(solution)/shard_map/ppermute | solution.py:69
  68.6 4.9 %collective-permute-start.10 = (f32[8,256]{1,0:T(8,128)S(1)}, f32[8,256]{1,0:T(8,128)S(1)}, u32[]{:S(2)}, u32[]{:S(2)}) collective-permute-start(f32[8,256]{1,0:T(8,128)S(1)} %add.143), channel_id=1, source_target_pairs={{0,12},{1,13},{2,14},{3,15},{4,8},{5,9},{6,10},{7,11},{8,4},{9,5},... | collective-permute-start | bytes 24584 | tf_op jit(solution)/shard_map/ppermute | solution.py:69
  73.5 3.7 %collective-permute-start.11 = (f32[8,256]{1,0:T(8,128)S(1)}, f32[8,256]{1,0:T(8,128)S(1)}, u32[]{:S(2)}, u32[]{:S(2)}) collective-permute-start(f32[8,256]{1,0:T(8,128)S(1)} %add.144), channel_id=1, source_target_pairs={{0,16},{1,17},{2,18},{3,19},{4,20},{5,21},{6,22},{7,23},{8,24},{9,... | collective-permute-start | bytes 24584 | tf_op jit(solution)/shard_map/ppermute | solution.py:69
  77.1 4.9 %copy-start.2 = (f32[8,256]{1,0:T(8,128)}, f32[8,256]{1,0:T(8,128)S(1)}, u32[]{:S(2)}) copy-start(f32[8,256]{1,0:T(8,128)S(1)} %add.145.c_ref) | copy-start | bytes 24580
  77.1 4.9 %collective-permute-start.12 = (f32[8,256]{1,0:T(8,128)S(1)}, f32[8,256]{1,0:T(8,128)S(1)}, u32[]{:S(2)}, u32[]{:S(2)}) collective-permute-start(f32[8,256]{1,0:T(8,128)S(1)} %add.145.c_ref), channel_id=1, source_target_pairs={{0,48},{1,49},{2,50},{3,51},{4,52},{5,53},{6,54},{7,55},{8,56},{9,... | collective-permute-start | bytes 24584 | tf_op jit(solution)/shard_map/ppermute | solution.py:71
  82.0 0.6 copy-start.3
  91.7 1.4 %collective-permute-start.13 = (f32[8,8]{1,0:T(8,128)}, f32[8,8]{1,0:T(8,128)S(1)}, u32[]{:S(2)}, u32[]{:S(2)}) collective-permute-start(f32[8,8]{1,0:T(8,128)} %get-tuple-element.8), channel_id=1, source_target_pairs={{0,64},{64,0},{1,65},{65,1},{2,66},{66,2},{3,67},{67,3},{4,68},{68... | collective-permute-start | bytes 776 | tf_op jit(solution)/shard_map/ppermute | solution.py:69
  93.8 3.6 %collective-permute-start.14 = (f32[8,8]{1,0:T(8,128)S(1)}, f32[8,8]{1,0:T(8,128)S(1)}, u32[]{:S(2)}, u32[]{:S(2)}) collective-permute-start(f32[8,8]{1,0:T(8,128)S(1)} %add.147), channel_id=1, source_target_pairs={{0,1},{1,0},{2,3},{3,2},{4,5},{5,4},{6,7},{7,6},{8,9},{9,8},{10,11... | collective-permute-start | bytes 776 | tf_op jit(solution)/shard_map/ppermute | solution.py:69
  97.4 4.8 %collective-permute-start.15 = (f32[8,8]{1,0:T(8,128)S(1)}, f32[8,8]{1,0:T(8,128)S(1)}, u32[]{:S(2)}, u32[]{:S(2)}) collective-permute-start(f32[8,8]{1,0:T(8,128)S(1)} %add.148), channel_id=1, source_target_pairs={{0,3},{1,2},{2,1},{3,0},{4,7},{5,6},{6,5},{7,4},{8,11},{9,10},{10,... | collective-permute-start | bytes 776 | tf_op jit(solution)/shard_map/ppermute | solution.py:69
  102.2 3.6 %collective-permute-start.16 = (f32[8,8]{1,0:T(8,128)S(1)}, f32[8,8]{1,0:T(8,128)S(1)}, u32[]{:S(2)}, u32[]{:S(2)}) collective-permute-start(f32[8,8]{1,0:T(8,128)S(1)} %add.149), channel_id=1, source_target_pairs={{0,4},{1,5},{2,6},{3,7},{4,0},{5,1},{6,2},{7,3},{8,12},{9,13},{10,... | collective-permute-start | bytes 776 | tf_op jit(solution)/shard_map/ppermute | solution.py:69
  105.8 4.8 %collective-permute-start.17 = (f32[8,8]{1,0:T(8,128)S(1)}, f32[8,8]{1,0:T(8,128)S(1)}, u32[]{:S(2)}, u32[]{:S(2)}) collective-permute-start(f32[8,8]{1,0:T(8,128)S(1)} %add.150), channel_id=1, source_target_pairs={{0,12},{1,13},{2,14},{3,15},{4,8},{5,9},{6,10},{7,11},{8,4},{9,5},... | collective-permute-start | bytes 776 | tf_op jit(solution)/shard_map/ppermute | solution.py:69
  110.7 3.6 %collective-permute-start.18 = (f32[8,8]{1,0:T(8,128)S(1)}, f32[8,8]{1,0:T(8,128)S(1)}, u32[]{:S(2)}, u32[]{:S(2)}) collective-permute-start(f32[8,8]{1,0:T(8,128)S(1)} %add.151), channel_id=1, source_target_pairs={{0,16},{1,17},{2,18},{3,19},{4,20},{5,21},{6,22},{7,23},{8,24},{9,... | collective-permute-start | bytes 776 | tf_op jit(solution)/shard_map/ppermute | solution.py:69
  114.3 4.8 %copy-start.4 = (f32[8,8]{1,0:T(8,128)}, f32[8,8]{1,0:T(8,128)S(1)}, u32[]{:S(2)}) copy-start(f32[8,8]{1,0:T(8,128)S(1)} %add.152.g_ref) | copy-start | bytes 772
  114.3 4.8 %collective-permute-start.19 = (f32[8,8]{1,0:T(8,128)S(1)}, f32[8,8]{1,0:T(8,128)S(1)}, u32[]{:S(2)}, u32[]{:S(2)}) collective-permute-start(f32[8,8]{1,0:T(8,128)S(1)} %add.152.g_ref), channel_id=1, source_target_pairs={{0,48},{1,49},{2,50},{3,51},{4,52},{5,53},{6,54},{7,55},{8,56},{9,... | collective-permute-start | bytes 776 | tf_op jit(solution)/shard_map/ppermute | solution.py:71
  119.1 0.6 copy-start.5

commit v15 on v11

--- a/solution.py
+++ b/solution.py
@@ -60,14 +60,47 @@
     return [(axis, pairs) for pairs in rounds]
 
 
+def mirror(index, strides, flips):
+    for bit, stride in enumerate(strides):
+        if flips >> bit & 1:
+            digit = (index // stride) % 4
+            index += (3 - 2 * digit) * stride
+    return index
+
+
 def allreduce(value, axes):
     sizes = [lax.axis_size(axis) for axis in axes]
     if any(size & (size - 1) for size in sizes):
         return lax.psum(value, axes)
-    for axis, size in zip(axes, sizes):
+    *pair_axes, ring_axis = axes
+    for axis, size in zip(pair_axes, sizes):
         for name, pairs in exchange_rounds(axis, size):
             value = value + lax.ppermute(value, name, pairs)
-    return value
+    count = sizes[-1]
+    strides = []
+    stride = 1
+    while stride < count and count % (stride * 4) == 0:
+        strides.append(stride)
+        stride *= 4
+    if stride != count or not strides:
+        for name, pairs in exchange_rounds(ring_axis, count):
+            value = value + lax.ppermute(value, name, pairs)
+        return value
+    for stride in strides:
+        value = value + lax.ppermute(value, ring_axis, ring_pairs(4, stride, count, False))
+    groups = 1 << len(strides)
+    gathered = [value] + [
+        lax.ppermute(value, ring_axis, [(i, mirror(i, strides, flips)) for i in range(count)])
+        for flips in range(1, groups)
+    ]
+    stacked = jnp.stack(gathered)
+    index = lax.axis_index(ring_axis)
+    own = sum(((index // stride) % 4 // 2) << bit for bit, stride in enumerate(strides))
+    total = None
+    for group in range(groups):
+        term = lax.dynamic_index_in_dim(stacked, group ^ own, 0, keepdims=False)
+        total = term if total is None else total + term
+    return total
 
 
 def project_kernel(b_ref, s_ref, o_ref):

time: 125 us -> 140 us (1.12)
  starting transfers between devices: 24.3 us -> 49.9 us
  waiting for transfers between devices: 60.3 us -> 49.5 us
    ppermute x14 -> x2, waiting for transfers between devices: 45.9 us -> 2.74 us  [allreduce(): value = value + lax.ppermute(value, name, pairs)]
    ppermute x0 -> x20, starting transfers between devices: none -> 33.2 us  [the longest x14 33.2 us: allreduce(): lax.ppermute(value, ring_axis, [(i, mirror(i, strides, flips)) for i in r...]
    ppermute x0 -> x20, waiting for transfers between devices: none -> 32.3 us  [the longest x6 21.8 us: allreduce(): lax.ppermute(value, ring_axis, ring_pairs(4, stride, count, False))]
    ppermute x14 -> x2, starting transfers between devices: 7.68 us -> 0.06 us  [allreduce(): value = value + lax.ppermute(value, name, pairs)]
  transfers between devices with their start and end apart: 20 -> 28, of which waited for: 16 -> 13; matrix products, arithmetic and copies ran while one was open for 8% -> 8% of each run, Pallas kernels for 0% -> 0%
where the time goes in v15:
time: 140 us
  starting transfers between devices  49.9 us (36%)
  waiting for transfers between devices  49.5 us (35%)
  Pallas kernels  23.3 us (17%)
  other arithmetic  14.2 us (10%)
  local copies, waits for them, and re-layouts  2.11 us (2%)
    ppermute x14, starting transfers between devices, allreduce(): lax.ppermute(value, ring_axis, [(i, mirror(i, strides, flips)) for i in r...  33.2 us
    ppermute x6, waiting for transfers between devices, allreduce(): lax.ppermute(value, ring_axis, ring_pairs(4, stride, count, False))  21.8 us
    ppermute x2, waiting for transfers between devices, extended(): lax.ppermute(tail, axis, [(i, (i + 1) % count) for i in range(ends)])  14.4 us
    ppermute x2, starting transfers between devices, extended(): lax.ppermute(head, axis, [((i + 1) % count, i) for i in range(ends)])  14.3 us
    ppermute x14, waiting for transfers between devices, allreduce(): lax.ppermute(value, ring_axis, [(i, mirror(i, strides, flips)) for i in r...  10.6 us
    pallas_call x1, Pallas kernels, project(): pl.pallas_call(project_kernel, grid=(nk // tk,), in_specs=[pl.BlockSpec((...  9.48 us
    pallas_call x1, Pallas kernels, residual(): pl.pallas_call(residual_kernel, grid=(nr // block_rows,), in_specs=[pl.Bl...  9.08 us
    mul x2, other arithmetic, local_terms(): viscosity * (second_diff(ypadded, center, 2, ny_loc) + second_diff(zpadde...  5.23 us
  transfers between devices with their start and end apart: 28, of which 13 were waited for; matrix products, arithmetic and copies ran while one was open for 8% of the time, Pallas kernels for 0%

profile of v15, /device:TPU:0, one launch (start us, length us, event | category | flops | bytes accessed | tf_op | source)
XLA Modules:
  0.0 139.9 jit_solution(16411566678245935273)
XLA Ops:
  0.6 2.1 %collective-permute-start.1 = (f32[4,2,64,256]{3,2,1,0:T(8,128)}, f32[4,2,64,256]{3,2,1,0:T(8,128)S(1)}, u32[]{:S(2)}, u32[]{:S(2)}) collective-permute-start(f32[4,2,64,256]{3,2,1,0:T(8,128)} %param.4), channel_id=1, source_target_pairs={{0,1},{1,2},{2,3},{3,4},{4,5},{5,6},{6,7},{7,8},{8,9},{9,10},{10,1... | collective-permute-start | bytes 1572872 | tf_op jit(solution)/shard_map/ppermute | solution.py:30
  2.7 6.8 %collective-permute-start = (f32[4,2,64,256]{3,2,1,0:T(8,128)}, f32[4,2,64,256]{3,2,1,0:T(8,128)S(1)}, u32[]{:S(2)}, u32[]{:S(2)}) collective-permute-start(f32[4,2,64,256]{3,2,1,0:T(8,128)} %param.4), channel_id=1, source_target_pairs={{1,0},{2,1},{3,2},{4,3},{5,4},{6,5},{7,6},{8,7},{9,8},{10,9},{11,1... | collective-permute-start | bytes 1572872 | tf_op jit(solution)/shard_map/ppermute | solution.py:32
  9.5 0.9 slice_select_fusion.1
  10.4 0.1 collective-permute-start.2
  10.5 1.2 fusion.46
  11.7 0.7 negate_multiply_fusion
  12.4 0.7 dynamic_slice.57
  13.2 0.0 collective-permute-done.2
  13.2 4.4 %fusion.15 = f32[4,2,64,256]{3,2,1,0:T(8,128)S(1)} fusion(f32[4,2,2,256]{3,2,1,0:T(2,128)S(1)} %get-tuple-element.25, f32[4,2,64,256]{3,2,1,0:T(8,128)} %param.4, f32[4,2,2,256]{3,2,1,0:T(2,128)S(1)} %get-tuple-element.24, f32[4,2,64,2]{3,2,1,0:T(8,128)S(1)} %get-tuple-element.21, f32[4,2,64,2]{3,2,1,0:T(8,128)S(1)} %get-tuple-element.20), kind=kLoop, calls=%fused_computation.32 | loop fusion | flops 3276800 | bytes 1089536 | tf_op jit(solution)/shard_map/mul | solution.py:267
  17.6 1.0 slice_subtract_fusion
  18.6 3.0 %collective-permute-done.1 = f32[4,2,64,256]{3,2,1,0:T(8,128)S(1)} collective-permute-done((f32[4,2,64,256]{3,2,1,0:T(8,128)}, f32[4,2,64,256]{3,2,1,0:T(8,128)S(1)}, u32[]{:S(2)}, u32[]{:S(2)}) %collective-permute-start.1) | collective-permute-done | bytes 524320 | tf_op jit(solution)/shard_map/ppermute | solution.py:30
  21.6 1.6 %multiply_add_fusion = (f32[4,2,64,256]{3,2,1,0:T(8,128)S(1)}, f32[4,2,64,256]{3,2,1,0:T(8,128)S(1)}) fusion(f32[4,2,64,256]{3,2,1,0:T(8,128)} %param.4, f32[3,2,64,256]{3,2,1,0:T(8,128)S(1)} %slice.169, f32[1,2,64,256]{3,2,1,0:T(8,128)S(1)} %slice_subtract_fusion, f32[4,2,64,256]{3,2,1,0:T(8,128)S(1)} %collective-permute-done.1, ...), kind=kLoop, calls=%fused_computation.75 | loop fusion | flops 2883584 | bytes 3145984 | tf_op jit(solution)/shard_map/add | solution.py:297
  23.2 0.1 collective-permute-start.5
  23.3 0.1 fusion.45
  23.5 0.1 collective-permute-start.4
  23.5 7.5 %collective-permute-start.3 = (f32[4,2,64,256]{3,2,1,0:T(8,128)S(1)}, f32[4,2,64,256]{3,2,1,0:T(8,128)S(1)}, u32[]{:S(2)}, u32[]{:S(2)}) collective-permute-start(f32[4,2,64,256]{3,2,1,0:T(8,128)S(1)} %get-tuple-element.16), channel_id=1, source_target_pairs={{1,0},{2,1},{3,2},{4,3},{5,4},{6,5},{7,6},{8,7},{9,8},{10,9},{11,1... | collective-permute-start | bytes 1572872 | tf_op jit(solution)/shard_map/ppermute | solution.py:32
  31.0 0.8 fusion.5
  31.9 0.1 fusion.44
  32.0 11.4 %collective-permute-done.4 = f32[4,2,64,256]{3,2,1,0:T(8,128)S(1)} collective-permute-done((f32[4,2,64,256]{3,2,1,0:T(8,128)S(1)}, f32[4,2,64,256]{3,2,1,0:T(8,128)S(1)}, u32[]{:S(2)}, u32[]{:S(2)}) %collective-permute-start.4) | collective-permute-done | bytes 524320 | tf_op jit(solution)/shard_map/ppermute | solution.py:30
  43.4 0.4 fusion.43
  43.8 0.0 copy-start.1
  43.8 0.1 pad_maximum_fusion
  43.9 0.0 copy-start
  43.9 1.0 bitcast_convert_fusion.s_ref
  44.8 9.5 %shard_map.75 = f32[8,256]{1,0:T(8,128)} custom-call(bf16[256,128,256]{2,1,0:T(8,128)(2,1)} %bitcast.43, bf16[8,128,256]{2,1,0:T(8,128)(2,1)} %bitcast_convert_fusion.s_ref), custom_call_target="tpu_custom_call" | custom-call | flops 2147483648 | bytes 17309696 | tf_op jit(solution)/shard_map/pallas_call | solution.py:129
  54.3 0.0 collective-permute-start.6
  54.3 1.4 collective-permute-done.6
  55.7 0.7 add.240
  56.4 0.0 collective-permute-start.7
  56.4 3.6 %collective-permute-done.7 = f32[8,256]{1,0:T(8,128)S(1)} collective-permute-done((f32[8,256]{1,0:T(8,128)S(1)}, f32[8,256]{1,0:T(8,128)S(1)}, u32[]{:S(2)}, u32[]{:S(2)}) %collective-permute-start.7) | collective-permute-done | bytes 8224 | tf_op jit(solution)/shard_map/ppermute | solution.py:90
  60.1 3.6 %collective-permute-done.8 = f32[8,256]{1,0:T(8,128)S(1)} collective-permute-done((f32[8,256]{1,0:T(8,128)S(1)}, f32[8,256]{1,0:T(8,128)S(1)}, u32[]{:S(2)}, u32[]{:S(2)}) %collective-permute-start.8) | collective-permute-done | bytes 8224 | tf_op jit(solution)/shard_map/ppermute | solution.py:90
  63.7 3.6 %collective-permute-done.9 = f32[8,256]{1,0:T(8,128)S(1)} collective-permute-done((f32[8,256]{1,0:T(8,128)S(1)}, f32[8,256]{1,0:T(8,128)S(1)}, u32[]{:S(2)}, u32[]{:S(2)}) %collective-permute-start.9) | collective-permute-done | bytes 8224 | tf_op jit(solution)/shard_map/ppermute | solution.py:90
  67.4 0.0 collective-permute-start.10
  67.4 3.2 %collective-permute-start.11 = (f32[8,256]{1,0:T(8,128)S(1)}, f32[8,256]{1,0:T(8,128)S(1)}, u32[]{:S(2)}, u32[]{:S(2)}) collective-permute-start(f32[8,256]{1,0:T(8,128)S(1)} %get-tuple-element.15), channel_id=1, source_target_pairs={{0,12},{1,13},{2,14},{3,15},{4,8},{5,9},{6,10},{7,11},{8,4},{9,5},... | collective-permute-start | bytes 24584 | tf_op jit(solution)/shard_map/ppermute | solution.py:93
  70.6 2.7 %collective-permute-start.12 = (f32[8,256]{1,0:T(8,128)S(1)}, f32[8,256]{1,0:T(8,128)S(1)}, u32[]{:S(2)}, u32[]{:S(2)}) collective-permute-start(f32[8,256]{1,0:T(8,128)S(1)} %get-tuple-element.15), channel_id=1, source_target_pairs={{0,15},{1,14},{2,13},{3,12},{4,11},{5,10},{6,9},{7,8},{8,7},{9,6},... | collective-permute-start | bytes 24584 | tf_op jit(solution)/shard_map/ppermute | solution.py:93
  73.3 2.5 %collective-permute-start.13 = (f32[8,256]{1,0:T(8,128)S(1)}, f32[8,256]{1,0:T(8,128)S(1)}, u32[]{:S(2)}, u32[]{:S(2)}) collective-permute-start(f32[8,256]{1,0:T(8,128)S(1)} %get-tuple-element.15), channel_id=1, source_target_pairs={{0,48},{1,49},{2,50},{3,51},{4,52},{5,53},{6,54},{7,55},{8,56},{9,... | collective-permute-start | bytes 24584 | tf_op jit(solution)/shard_map/ppermute | solution.py:93
  75.8 2.1 %collective-permute-start.14 = (f32[8,256]{1,0:T(8,128)S(1)}, f32[8,256]{1,0:T(8,128)S(1)}, u32[]{:S(2)}, u32[]{:S(2)}) collective-permute-start(f32[8,256]{1,0:T(8,128)S(1)} %get-tuple-element.15), channel_id=1, source_target_pairs={{0,51},{1,50},{2,49},{3,48},{4,55},{5,54},{6,53},{7,52},{8,59},{9,... | collective-permute-start | bytes 24584 | tf_op jit(solution)/shard_map/ppermute | solution.py:93
  77.9 5.9 %collective-permute-start.15 = (f32[8,256]{1,0:T(8,128)S(1)}, f32[8,256]{1,0:T(8,128)S(1)}, u32[]{:S(2)}, u32[]{:S(2)}) collective-permute-start(f32[8,256]{1,0:T(8,128)S(1)} %get-tuple-element.15), channel_id=1, source_target_pairs={{0,60},{1,61},{2,62},{3,63},{4,56},{5,57},{6,58},{7,59},{8,52},{9,... | collective-permute-start | bytes 24584 | tf_op jit(solution)/shard_map/ppermute | solution.py:93
  83.8 0.0 collective-permute-done.11
  83.8 0.2 collective-permute-start.16
  84.0 1.4 %collective-permute-done.15 = f32[8,256]{1,0:T(8,128)S(1)} collective-permute-done((f32[8,256]{1,0:T(8,128)S(1)}, f32[8,256]{1,0:T(8,128)S(1)}, u32[]{:S(2)}, u32[]{:S(2)}) %collective-permute-start.15) | collective-permute-done | bytes 8224 | tf_op jit(solution)/shard_map/ppermute | solution.py:93
  85.5 7.4 %collective-permute-done.16 = f32[8,256]{1,0:T(8,128)S(1)} collective-permute-done((f32[8,256]{1,0:T(8,128)S(1)}, f32[8,256]{1,0:T(8,128)S(1)}, u32[]{:S(2)}, u32[]{:S(2)}) %collective-permute-start.16) | collective-permute-done | bytes 8224 | tf_op jit(solution)/shard_map/ppermute | solution.py:93
  92.9 0.6 fusion.47.c_ref
  93.5 9.1 %shard_map.76 = (f32[8,128,256]{2,1,0:T(8,128)}, f32[8,8]{1,0:T(8,128)}) custom-call(f32[8,256]{1,0:T(8,128)} %fusion.47.c_ref, bf16[256,128,256]{2,1,0:T(8,128)(2,1)} %bitcast.44, f32[8,128,256]{2,1,0:T(8,128)} %bitcast.45), custom_call_target="tpu_custom_call" | custom-call | flops 2147483648 | bytes 18874368 | tf_op jit(solution)/shard_map/pallas_call | solution.py:191
  102.6 0.1 collective-permute-start.17
  102.6 1.4 collective-permute-done.17
  104.0 0.7 add.265
  104.7 3.6 %collective-permute-done.18 = f32[8,8]{1,0:T(8,128)S(1)} collective-permute-done((f32[8,8]{1,0:T(8,128)S(1)}, f32[8,8]{1,0:T(8,128)S(1)}, u32[]{:S(2)}, u32[]{:S(2)}) %collective-permute-start.18) | collective-permute-done | bytes 288 | tf_op jit(solution)/shard_map/ppermute | solution.py:90
  108.3 3.6 %collective-permute-done.19 = f32[8,8]{1,0:T(8,128)S(1)} collective-permute-done((f32[8,8]{1,0:T(8,128)S(1)}, f32[8,8]{1,0:T(8,128)S(1)}, u32[]{:S(2)}, u32[]{:S(2)}) %collective-permute-start.19) | collective-permute-done | bytes 288 | tf_op jit(solution)/shard_map/ppermute | solution.py:90
  111.9 3.6 %collective-permute-done.20 = f32[8,8]{1,0:T(8,128)S(1)} collective-permute-done((f32[8,8]{1,0:T(8,128)S(1)}, f32[8,8]{1,0:T(8,128)S(1)}, u32[]{:S(2)}, u32[]{:S(2)}) %collective-permute-start.20) | collective-permute-done | bytes 288 | tf_op jit(solution)/shard_map/ppermute | solution.py:90
  115.5 0.6 fusion.48
  116.1 0.6 collective-permute-start.22
  116.7 5.3 %collective-permute-start.23 = (f32[8,8]{1,0:T(8,128)S(1)}, f32[8,8]{1,0:T(8,128)S(1)}, u32[]{:S(2)}, u32[]{:S(2)}) collective-permute-start(f32[8,8]{1,0:T(8,128)S(1)} %get-tuple-element.13), channel_id=1, source_target_pairs={{0,15},{1,14},{2,13},{3,12},{4,11},{5,10},{6,9},{7,8},{8,7},{9,6},... | collective-permute-start | bytes 776 | tf_op jit(solution)/shard_map/ppermute | solution.py:93
  122.0 0.0 collective-permute-start.24
  122.0 2.7 %collective-permute-start.25 = (f32[8,8]{1,0:T(8,128)S(1)}, f32[8,8]{1,0:T(8,128)S(1)}, u32[]{:S(2)}, u32[]{:S(2)}) collective-permute-start(f32[8,8]{1,0:T(8,128)S(1)} %get-tuple-element.13), channel_id=1, source_target_pairs={{0,51},{1,50},{2,49},{3,48},{4,55},{5,54},{6,53},{7,52},{8,59},{9,... | collective-permute-start | bytes 776 | tf_op jit(solution)/shard_map/ppermute | solution.py:93
  124.7 0.8 collective-permute-start.26
  125.5 7.2 %collective-permute-start.27 = (f32[8,8]{1,0:T(8,128)S(1)}, f32[8,8]{1,0:T(8,128)S(1)}, u32[]{:S(2)}, u32[]{:S(2)}) collective-permute-start(f32[8,8]{1,0:T(8,128)S(1)} %get-tuple-element.13), channel_id=1, source_target_pairs={{0,63},{1,62},{2,61},{3,60},{4,59},{5,58},{6,57},{7,56},{8,55},{9,... | collective-permute-start | bytes 776 | tf_op jit(solution)/shard_map/ppermute | solution.py:93
  132.7 0.0 collective-permute-done.23
  132.7 0.0 collective-permute-done.24
  132.8 0.0 collective-permute-done.25
  132.8 0.0 collective-permute-done.26
  132.8 1.7 %collective-permute-done.27 = f32[8,8]{1,0:T(8,128)S(1)} collective-permute-done((f32[8,8]{1,0:T(8,128)S(1)}, f32[8,8]{1,0:T(8,128)S(1)}, u32[]{:S(2)}, u32[]{:S(2)}) %collective-permute-start.27) | collective-permute-done | bytes 288 | tf_op jit(solution)/shard_map/ppermute | solution.py:93
  134.5 0.6 add_bitcast_fusion.g_ref
  135.1 4.8 %shard_map.77 = (f32[8,8]{1,0:T(8,128)}, f32[8,128,256]{2,1,0:T(8,128)}) custom-call(f32[8,8]{1,0:T(8,128)} %add_bitcast_fusion.g_ref, f32[8,128,256]{2,1,0:T(8,128)} %get-tuple-element.9.w_ref), custom_call_target="tpu_custom_call" | custom-call | flops 2097152 | bytes 2097152 | tf_op jit(solution)/shard_map/pallas_call | solution.py:238
  (42 shorter events, 0.2 us)
Async XLA Ops:
  0.6 21.0 %collective-permute-start.1 = (f32[4,2,64,256]{3,2,1,0:T(8,128)}, f32[4,2,64,256]{3,2,1,0:T(8,128)S(1)}, u32[]{:S(2)}, u32[]{:S(2)}) collective-permute-start(f32[4,2,64,256]{3,2,1,0:T(8,128)} %param.4), channel_id=1, source_target_pairs={{0,1},{1,2},{2,3},{3,4},{4,5},{5,6},{6,7},{7,8},{8,9},{9,10},{10,1... | collective-permute-start | bytes 1572872 | tf_op jit(solution)/shard_map/ppermute | solution.py:30
  2.7 18.9 %collective-permute-start = (f32[4,2,64,256]{3,2,1,0:T(8,128)}, f32[4,2,64,256]{3,2,1,0:T(8,128)S(1)}, u32[]{:S(2)}, u32[]{:S(2)}) collective-permute-start(f32[4,2,64,256]{3,2,1,0:T(8,128)} %param.4), channel_id=1, source_target_pairs={{1,0},{2,1},{3,2},{4,3},{5,4},{6,5},{7,6},{8,7},{9,8},{10,9},{11,1... | collective-permute-start | bytes 1572872 | tf_op jit(solution)/shard_map/ppermute | solution.py:32
  10.4 2.7 %collective-permute-start.2 = (f32[4,2,2,256]{3,2,1,0:T(2,128)S(1)}, f32[4,2,2,256]{3,2,1,0:T(2,128)S(1)}, u32[]{:S(2)}, u32[]{:S(2)}) collective-permute-start(f32[4,2,2,256]{3,2,1,0:T(2,128)S(1)} %slice_select_fusion.1), channel_id=1, source_target_pairs={{0,64},{64,0},{1,65},{65,1},{2,66},{66,2},{3,67},{67,3},{4,68},{68... | collective-permute-start | bytes 49160 | tf_op jit(solution)/shard_map/ppermute | solution.py:22
  23.2 7.8 %collective-permute-start.5 = (f32[4,2,2,256]{3,2,1,0:T(2,128)S(1)}, f32[4,2,2,256]{3,2,1,0:T(2,128)S(1)}, u32[]{:S(2)}, u32[]{:S(2)}) collective-permute-start(f32[4,2,2,256]{3,2,1,0:T(2,128)S(1)} %slice_select_fusion), channel_id=1, source_target_pairs={{0,64},{64,0},{1,65},{65,1},{2,66},{66,2},{3,67},{67,3},{4,68},{68... | collective-permute-start | bytes 49160 | tf_op jit(solution)/shard_map/ppermute | solution.py:22
  23.5 19.9 %collective-permute-start.4 = (f32[4,2,64,256]{3,2,1,0:T(8,128)S(1)}, f32[4,2,64,256]{3,2,1,0:T(8,128)S(1)}, u32[]{:S(2)}, u32[]{:S(2)}) collective-permute-start(f32[4,2,64,256]{3,2,1,0:T(8,128)S(1)} %get-tuple-element.16), channel_id=1, source_target_pairs={{0,1},{1,2},{2,3},{3,4},{4,5},{5,6},{6,7},{7,8},{8,9},{9,10},{10,1... | collective-permute-start | bytes 1572872 | tf_op jit(solution)/shard_map/ppermute | solution.py:30
  23.5 19.8 %collective-permute-start.3 = (f32[4,2,64,256]{3,2,1,0:T(8,128)S(1)}, f32[4,2,64,256]{3,2,1,0:T(8,128)S(1)}, u32[]{:S(2)}, u32[]{:S(2)}) collective-permute-start(f32[4,2,64,256]{3,2,1,0:T(8,128)S(1)} %get-tuple-element.16), channel_id=1, source_target_pairs={{1,0},{2,1},{3,2},{4,3},{5,4},{6,5},{7,6},{8,7},{9,8},{10,9},{11,1... | collective-permute-start | bytes 1572872 | tf_op jit(solution)/shard_map/ppermute | solution.py:32
  43.8 58.8 %copy-start.1 = (f32[4,2,64,256]{3,2,1,0:T(8,128)}, f32[4,2,64,256]{3,2,1,0:T(8,128)S(1)}, u32[]{:S(2)}) copy-start(f32[4,2,64,256]{3,2,1,0:T(8,128)S(1)} %fusion.43) | copy-start | bytes 1572868
  43.9 49.6 %copy-start = (f32[8,2,64,256]{3,2,1,0:T(8,128)}, f32[8,2,64,256]{3,2,1,0:T(8,128)S(1)}, u32[]{:S(2)}) copy-start(f32[8,2,64,256]{3,2,1,0:T(8,128)S(1)} %pad_maximum_fusion) | copy-start | bytes 3145732
  54.3 1.4 collective-permute-start.6
  56.4 3.7 %collective-permute-start.7 = (f32[8,256]{1,0:T(8,128)S(1)}, f32[8,256]{1,0:T(8,128)S(1)}, u32[]{:S(2)}, u32[]{:S(2)}) collective-permute-start(f32[8,256]{1,0:T(8,128)S(1)} %add.240), channel_id=1, source_target_pairs={{0,1},{1,0},{2,3},{3,2},{4,5},{5,4},{6,7},{7,6},{8,9},{9,8},{10,11... | collective-permute-start | bytes 24584 | tf_op jit(solution)/shard_map/ppermute | solution.py:90
  60.1 3.7 %collective-permute-start.8 = (f32[8,256]{1,0:T(8,128)S(1)}, f32[8,256]{1,0:T(8,128)S(1)}, u32[]{:S(2)}, u32[]{:S(2)}) collective-permute-start(f32[8,256]{1,0:T(8,128)S(1)} %add.241), channel_id=1, source_target_pairs={{0,4},{1,5},{2,6},{3,7},{4,0},{5,1},{6,2},{7,3},{8,12},{9,13},{10,... | collective-permute-start | bytes 24584 | tf_op jit(solution)/shard_map/ppermute | solution.py:90
  63.7 3.7 %collective-permute-start.9 = (f32[8,256]{1,0:T(8,128)S(1)}, f32[8,256]{1,0:T(8,128)S(1)}, u32[]{:S(2)}, u32[]{:S(2)}) collective-permute-start(f32[8,256]{1,0:T(8,128)S(1)} %add.242), channel_id=1, source_target_pairs={{0,16},{1,17},{2,18},{3,19},{4,20},{5,21},{6,22},{7,23},{8,24},{9,... | collective-permute-start | bytes 24584 | tf_op jit(solution)/shard_map/ppermute | solution.py:90
  67.4 10.5 %collective-permute-start.10 = (f32[8,256]{1,0:T(8,128)S(1)}, f32[8,256]{1,0:T(8,128)S(1)}, u32[]{:S(2)}, u32[]{:S(2)}) collective-permute-start(f32[8,256]{1,0:T(8,128)S(1)} %get-tuple-element.15), channel_id=1, source_target_pairs={{0,3},{1,2},{2,1},{3,0},{4,7},{5,6},{6,5},{7,4},{8,11},{9,10},{10,... | collective-permute-start | bytes 24584 | tf_op jit(solution)/shard_map/ppermute | solution.py:93
  67.4 16.4 %collective-permute-start.11 = (f32[8,256]{1,0:T(8,128)S(1)}, f32[8,256]{1,0:T(8,128)S(1)}, u32[]{:S(2)}, u32[]{:S(2)}) collective-permute-start(f32[8,256]{1,0:T(8,128)S(1)} %get-tuple-element.15), channel_id=1, source_target_pairs={{0,12},{1,13},{2,14},{3,15},{4,8},{5,9},{6,10},{7,11},{8,4},{9,5},... | collective-permute-start | bytes 24584 | tf_op jit(solution)/shard_map/ppermute | solution.py:93
  70.6 13.4 %collective-permute-start.12 = (f32[8,256]{1,0:T(8,128)S(1)}, f32[8,256]{1,0:T(8,128)S(1)}, u32[]{:S(2)}, u32[]{:S(2)}) collective-permute-start(f32[8,256]{1,0:T(8,128)S(1)} %get-tuple-element.15), channel_id=1, source_target_pairs={{0,15},{1,14},{2,13},{3,12},{4,11},{5,10},{6,9},{7,8},{8,7},{9,6},... | collective-permute-start | bytes 24584 | tf_op jit(solution)/shard_map/ppermute | solution.py:93
  73.3 10.7 %collective-permute-start.13 = (f32[8,256]{1,0:T(8,128)S(1)}, f32[8,256]{1,0:T(8,128)S(1)}, u32[]{:S(2)}, u32[]{:S(2)}) collective-permute-start(f32[8,256]{1,0:T(8,128)S(1)} %get-tuple-element.15), channel_id=1, source_target_pairs={{0,48},{1,49},{2,50},{3,51},{4,52},{5,53},{6,54},{7,55},{8,56},{9,... | collective-permute-start | bytes 24584 | tf_op jit(solution)/shard_map/ppermute | solution.py:93
  75.8 8.3 %collective-permute-start.14 = (f32[8,256]{1,0:T(8,128)S(1)}, f32[8,256]{1,0:T(8,128)S(1)}, u32[]{:S(2)}, u32[]{:S(2)}) collective-permute-start(f32[8,256]{1,0:T(8,128)S(1)} %get-tuple-element.15), channel_id=1, source_target_pairs={{0,51},{1,50},{2,49},{3,48},{4,55},{5,54},{6,53},{7,52},{8,59},{9,... | collective-permute-start | bytes 24584 | tf_op jit(solution)/shard_map/ppermute | solution.py:93
  77.9 7.6 %collective-permute-start.15 = (f32[8,256]{1,0:T(8,128)S(1)}, f32[8,256]{1,0:T(8,128)S(1)}, u32[]{:S(2)}, u32[]{:S(2)}) collective-permute-start(f32[8,256]{1,0:T(8,128)S(1)} %get-tuple-element.15), channel_id=1, source_target_pairs={{0,60},{1,61},{2,62},{3,63},{4,56},{5,57},{6,58},{7,59},{8,52},{9,... | collective-permute-start | bytes 24584 | tf_op jit(solution)/shard_map/ppermute | solution.py:93
  83.8 9.1 %collective-permute-start.16 = (f32[8,256]{1,0:T(8,128)S(1)}, f32[8,256]{1,0:T(8,128)S(1)}, u32[]{:S(2)}, u32[]{:S(2)}) collective-permute-start(f32[8,256]{1,0:T(8,128)S(1)} %get-tuple-element.15), channel_id=1, source_target_pairs={{0,63},{1,62},{2,61},{3,60},{4,59},{5,58},{6,57},{7,56},{8,55},{9,... | collective-permute-start | bytes 24584 | tf_op jit(solution)/shard_map/ppermute | solution.py:93
  102.6 1.4 %collective-permute-start.17 = (f32[8,8]{1,0:T(8,128)}, f32[8,8]{1,0:T(8,128)S(1)}, u32[]{:S(2)}, u32[]{:S(2)}) collective-permute-start(f32[8,8]{1,0:T(8,128)} %get-tuple-element.8), channel_id=1, source_target_pairs={{0,64},{64,0},{1,65},{65,1},{2,66},{66,2},{3,67},{67,3},{4,68},{68... | collective-permute-start | bytes 776 | tf_op jit(solution)/shard_map/ppermute | solution.py:78
  104.7 3.6 %collective-permute-start.18 = (f32[8,8]{1,0:T(8,128)S(1)}, f32[8,8]{1,0:T(8,128)S(1)}, u32[]{:S(2)}, u32[]{:S(2)}) collective-permute-start(f32[8,8]{1,0:T(8,128)S(1)} %add.265), channel_id=1, source_target_pairs={{0,1},{1,0},{2,3},{3,2},{4,5},{5,4},{6,7},{7,6},{8,9},{9,8},{10,11... | collective-permute-start | bytes 776 | tf_op jit(solution)/shard_map/ppermute | solution.py:90
  108.3 3.6 %collective-permute-start.19 = (f32[8,8]{1,0:T(8,128)S(1)}, f32[8,8]{1,0:T(8,128)S(1)}, u32[]{:S(2)}, u32[]{:S(2)}) collective-permute-start(f32[8,8]{1,0:T(8,128)S(1)} %add.266), channel_id=1, source_target_pairs={{0,4},{1,5},{2,6},{3,7},{4,0},{5,1},{6,2},{7,3},{8,12},{9,13},{10,... | collective-permute-start | bytes 776 | tf_op jit(solution)/shard_map/ppermute | solution.py:90
  111.9 3.6 %collective-permute-start.20 = (f32[8,8]{1,0:T(8,128)S(1)}, f32[8,8]{1,0:T(8,128)S(1)}, u32[]{:S(2)}, u32[]{:S(2)}) collective-permute-start(f32[8,8]{1,0:T(8,128)S(1)} %add.267), channel_id=1, source_target_pairs={{0,16},{1,17},{2,18},{3,19},{4,20},{5,21},{6,22},{7,23},{8,24},{9,... | collective-permute-start | bytes 776 | tf_op jit(solution)/shard_map/ppermute | solution.py:90
  115.5 9.2 %collective-permute-start.21 = (f32[8,8]{1,0:T(8,128)S(1)}, f32[8,8]{1,0:T(8,128)S(1)}, u32[]{:S(2)}, u32[]{:S(2)}) collective-permute-start(f32[8,8]{1,0:T(8,128)S(1)} %get-tuple-element.13), channel_id=1, source_target_pairs={{0,3},{1,2},{2,1},{3,0},{4,7},{5,6},{6,5},{7,4},{8,11},{9,10},{10,... | collective-permute-start | bytes 776 | tf_op jit(solution)/shard_map/ppermute | solution.py:93
  116.1 9.4 %collective-permute-start.22 = (f32[8,8]{1,0:T(8,128)S(1)}, f32[8,8]{1,0:T(8,128)S(1)}, u32[]{:S(2)}, u32[]{:S(2)}) collective-permute-start(f32[8,8]{1,0:T(8,128)S(1)} %get-tuple-element.13), channel_id=1, source_target_pairs={{0,12},{1,13},{2,14},{3,15},{4,8},{5,9},{6,10},{7,11},{8,4},{9,5},... | collective-permute-start | bytes 776 | tf_op jit(solution)/shard_map/ppermute | solution.py:93
  116.7 16.0 %collective-permute-start.23 = (f32[8,8]{1,0:T(8,128)S(1)}, f32[8,8]{1,0:T(8,128)S(1)}, u32[]{:S(2)}, u32[]{:S(2)}) collective-permute-start(f32[8,8]{1,0:T(8,128)S(1)} %get-tuple-element.13), channel_id=1, source_target_pairs={{0,15},{1,14},{2,13},{3,12},{4,11},{5,10},{6,9},{7,8},{8,7},{9,6},... | collective-permute-start | bytes 776 | tf_op jit(solution)/shard_map/ppermute | solution.py:93
  122.0 10.7 %collective-permute-start.24 = (f32[8,8]{1,0:T(8,128)S(1)}, f32[8,8]{1,0:T(8,128)S(1)}, u32[]{:S(2)}, u32[]{:S(2)}) collective-permute-start(f32[8,8]{1,0:T(8,128)S(1)} %get-tuple-element.13), channel_id=1, source_target_pairs={{0,48},{1,49},{2,50},{3,51},{4,52},{5,53},{6,54},{7,55},{8,56},{9,... | collective-permute-start | bytes 776 | tf_op jit(solution)/shard_map/ppermute | solution.py:93
  122.0 10.7 %collective-permute-start.25 = (f32[8,8]{1,0:T(8,128)S(1)}, f32[8,8]{1,0:T(8,128)S(1)}, u32[]{:S(2)}, u32[]{:S(2)}) collective-permute-start(f32[8,8]{1,0:T(8,128)S(1)} %get-tuple-element.13), channel_id=1, source_target_pairs={{0,51},{1,50},{2,49},{3,48},{4,55},{5,54},{6,53},{7,52},{8,59},{9,... | collective-permute-start | bytes 776 | tf_op jit(solution)/shard_map/ppermute | solution.py:93
  124.7 8.1 %collective-permute-start.26 = (f32[8,8]{1,0:T(8,128)S(1)}, f32[8,8]{1,0:T(8,128)S(1)}, u32[]{:S(2)}, u32[]{:S(2)}) collective-permute-start(f32[8,8]{1,0:T(8,128)S(1)} %get-tuple-element.13), channel_id=1, source_target_pairs={{0,60},{1,61},{2,62},{3,63},{4,56},{5,57},{6,58},{7,59},{8,52},{9,... | collective-permute-start | bytes 776 | tf_op jit(solution)/shard_map/ppermute | solution.py:93
  125.5 9.0 %collective-permute-start.27 = (f32[8,8]{1,0:T(8,128)S(1)}, f32[8,8]{1,0:T(8,128)S(1)}, u32[]{:S(2)}, u32[]{:S(2)}) collective-permute-start(f32[8,8]{1,0:T(8,128)S(1)} %get-tuple-element.13), channel_id=1, source_target_pairs={{0,63},{1,62},{2,61},{3,60},{4,59},{5,58},{6,57},{7,56},{8,55},{9,... | collective-permute-start | bytes 776 | tf_op jit(solution)/shard_map/ppermute | solution.py:93

commit v16 on v11

--- a/solution.py
+++ b/solution.py
@@ -86,11 +86,17 @@
     group = lax.broadcasted_iota(jnp.int32, (ns, ns * ROWS), 1) // ROWS
     snapshot = lax.broadcasted_iota(jnp.int32, (ns, ns * ROWS), 0)
     gather = jnp.where(group == snapshot, 1.0, 0.0)
-    o_ref[...] = lax.dot_general(gather, lanes, (((1,), (1,)), ((), ())),
-                                 precision=lax.Precision.HIGHEST, preferred_element_type=jnp.float32)
-
-
-def project(basis3, snaps3, tk=128):
+    result = lax.dot_general(gather, lanes, (((1,), (1,)), ((), ())),
+                             precision=lax.Precision.HIGHEST, preferred_element_type=jnp.float32)
+    halves = o_ref.shape[1] // tk
+    step = pl.program_id(0) % halves
+    for half in range(halves):
+        @pl.when(step == half)
+        def _():
+            o_ref[:, half * tk:(half + 1) * tk] = result
+
+
+def project(basis3, snaps3, tk=64, lanes=128):
     nk, nr, nz = basis3.shape
     ns = snaps3.shape[0]
     return pl.pallas_call(
@@ -98,7 +104,7 @@
         grid=(nk // tk,),
         in_specs=[pl.BlockSpec((tk, nr, nz), lambda i: (i, 0, 0)),
                   pl.BlockSpec((ns, nr, nz), lambda i: (0, 0, 0))],
-        out_specs=pl.BlockSpec((ns, tk), lambda i: (0, i)),
+        out_specs=pl.BlockSpec((ns, lanes), lambda i: (0, i * tk // lanes)),
         out_shape=jax.ShapeDtypeStruct((ns, nk), jnp.float32),
         cost_estimate=pl.CostEstimate(flops=2 * nk * nr * nz * ns * ROWS, transcendentals=0,
                                       bytes_accessed=nk * nr * nz * 2 + ns * nr * nz * 2 + nk * ns * 4),

time: 125 us -> 125 us (level)
  no operation moved by 1% of the time
where the time goes in v16:
time: 125 us
  waiting for transfers between devices  60.3 us (48%)
  starting transfers between devices  24.3 us (19%)
  Pallas kernels  23.8 us (19%)
  other arithmetic  13.6 us (11%)
  local copies, waits for them, and re-layouts  2.08 us (2%)
    ppermute x14, waiting for transfers between devices, allreduce(): value = value + lax.ppermute(value, name, pairs)  45.9 us
    ppermute x2, waiting for transfers between devices, extended(): lax.ppermute(tail, axis, [(i, (i + 1) % count) for i in range(ends)])  14.4 us
    ppermute x2, starting transfers between devices, extended(): lax.ppermute(head, axis, [((i + 1) % count, i) for i in range(ends)])  14.3 us
    pallas_call x1, Pallas kernels, project(): pl.pallas_call(project_kernel, grid=(nk // tk,), in_specs=[pl.BlockSpec((...  9.88 us
    pallas_call x1, Pallas kernels, residual(): pl.pallas_call(residual_kernel, grid=(nr // block_rows,), in_specs=[pl.Bl...  9.12 us
    ppermute x14, starting transfers between devices, allreduce(): value = value + lax.ppermute(value, name, pairs)  7.67 us
    mul x2, other arithmetic, local_terms(): viscosity * (second_diff(ypadded, center, 2, ny_loc) + second_diff(zpadde...  5.22 us
    pallas_call x1, Pallas kernels, factor_and_solve(): pl.pallas_call(factor_kernel, in_specs=[vmem, vmem], out_specs=[vmem, vme...  4.79 us
  transfers between devices with their start and end apart: 20, of which 16 were waited for; matrix products, arithmetic and copies ran while one was open for 8% of the time, Pallas kernels for 0%

profile of v16, /device:TPU:0, one launch (start us, length us, event | category | flops | bytes accessed | tf_op | source)
XLA Modules:
  0.0 124.9 jit_solution(7009856559113580772)
XLA Ops:
  0.6 2.1 %collective-permute-start.1 = (f32[4,2,64,256]{3,2,1,0:T(8,128)}, f32[4,2,64,256]{3,2,1,0:T(8,128)S(1)}, u32[]{:S(2)}, u32[]{:S(2)}) collective-permute-start(f32[4,2,64,256]{3,2,1,0:T(8,128)} %param.4), channel_id=1, source_target_pairs={{0,1},{1,2},{2,3},{3,4},{4,5},{5,6},{6,7},{7,8},{8,9},{9,10},{10,1... | collective-permute-start | bytes 1572872 | tf_op jit(solution)/shard_map/ppermute | solution.py:30
  2.7 6.8 %collective-permute-start = (f32[4,2,64,256]{3,2,1,0:T(8,128)}, f32[4,2,64,256]{3,2,1,0:T(8,128)S(1)}, u32[]{:S(2)}, u32[]{:S(2)}) collective-permute-start(f32[4,2,64,256]{3,2,1,0:T(8,128)} %param.4), channel_id=1, source_target_pairs={{1,0},{2,1},{3,2},{4,3},{5,4},{6,5},{7,6},{8,7},{9,8},{10,9},{11,1... | collective-permute-start | bytes 1572872 | tf_op jit(solution)/shard_map/ppermute | solution.py:32
  9.5 0.9 slice_select_fusion.1
  10.4 0.1 collective-permute-start.2
  10.5 1.2 fusion.46
  11.7 0.7 negate_multiply_fusion
  12.4 0.7 dynamic_slice.7
  13.2 0.0 collective-permute-done.2
  13.2 4.4 %fusion.15 = f32[4,2,64,256]{3,2,1,0:T(8,128)S(1)} fusion(f32[4,2,2,256]{3,2,1,0:T(2,128)S(1)} %get-tuple-element.21, f32[4,2,64,256]{3,2,1,0:T(8,128)} %param.4, f32[4,2,2,256]{3,2,1,0:T(2,128)S(1)} %get-tuple-element.20, f32[4,2,64,2]{3,2,1,0:T(8,128)S(1)} %get-tuple-element.17, f32[4,2,64,2]{3,2,1,0:T(8,128)S(1)} %get-tuple-element.16), kind=kLoop, calls=%fused_computation.32 | loop fusion | flops 3276800 | bytes 1089536 | tf_op jit(solution)/shard_map/mul | solution.py:240
  17.6 1.0 slice_subtract_fusion
  18.6 3.0 %collective-permute-done.1 = f32[4,2,64,256]{3,2,1,0:T(8,128)S(1)} collective-permute-done((f32[4,2,64,256]{3,2,1,0:T(8,128)}, f32[4,2,64,256]{3,2,1,0:T(8,128)S(1)}, u32[]{:S(2)}, u32[]{:S(2)}) %collective-permute-start.1) | collective-permute-done | bytes 524320 | tf_op jit(solution)/shard_map/ppermute | solution.py:30
  21.6 0.0 collective-permute-done
  21.6 1.6 %multiply_add_fusion = (f32[4,2,64,256]{3,2,1,0:T(8,128)S(1)}, f32[4,2,64,256]{3,2,1,0:T(8,128)S(1)}) fusion(f32[4,2,64,256]{3,2,1,0:T(8,128)} %param.4, f32[3,2,64,256]{3,2,1,0:T(8,128)S(1)} %slice.169, f32[1,2,64,256]{3,2,1,0:T(8,128)S(1)} %slice_subtract_fusion, f32[4,2,64,256]{3,2,1,0:T(8,128)S(1)} %collective-permute-done.1, ...), kind=kLoop, calls=%fused_computation.75 | loop fusion | flops 2883584 | bytes 3145984 | tf_op jit(solution)/shard_map/add | solution.py:270
  23.2 0.1 collective-permute-start.5
  23.3 0.1 fusion.45
  23.5 0.1 collective-permute-start.4
  23.5 7.5 %collective-permute-start.3 = (f32[4,2,64,256]{3,2,1,0:T(8,128)S(1)}, f32[4,2,64,256]{3,2,1,0:T(8,128)S(1)}, u32[]{:S(2)}, u32[]{:S(2)}) collective-permute-start(f32[4,2,64,256]{3,2,1,0:T(8,128)S(1)} %get-tuple-element.12), channel_id=1, source_target_pairs={{1,0},{2,1},{3,2},{4,3},{5,4},{6,5},{7,6},{8,7},{9,8},{10,9},{11,1... | collective-permute-start | bytes 1572872 | tf_op jit(solution)/shard_map/ppermute | solution.py:32
  31.0 0.0 collective-permute-done.5
  31.0 0.8 fusion.5
  31.9 0.1 fusion.44
  32.0 11.4 %collective-permute-done.4 = f32[4,2,64,256]{3,2,1,0:T(8,128)S(1)} collective-permute-done((f32[4,2,64,256]{3,2,1,0:T(8,128)S(1)}, f32[4,2,64,256]{3,2,1,0:T(8,128)S(1)}, u32[]{:S(2)}, u32[]{:S(2)}) %collective-permute-start.4) | collective-permute-done | bytes 524320 | tf_op jit(solution)/shard_map/ppermute | solution.py:30
  43.4 0.0 collective-permute-done.3
  43.4 0.4 fusion.43
  43.8 0.0 copy-start.1
  43.8 0.1 pad_maximum_fusion
  43.9 0.0 copy-start
  43.9 1.0 bitcast_convert_fusion.s_ref
  44.9 9.9 %shard_map.75 = f32[8,256]{1,0:T(8,128)} custom-call(bf16[256,128,256]{2,1,0:T(8,128)(2,1)} %bitcast.5, bf16[8,128,256]{2,1,0:T(8,128)(2,1)} %bitcast_convert_fusion.s_ref), custom_call_target="tpu_custom_call" | custom-call | flops 2147483648 | bytes 17309696 | tf_op jit(solution)/shard_map/pallas_call | solution.py:102
  54.7 0.0 collective-permute-start.6
  54.7 1.4 %collective-permute-done.6 = f32[8,256]{1,0:T(8,128)S(1)} collective-permute-done((f32[8,256]{1,0:T(8,128)}, f32[8,256]{1,0:T(8,128)S(1)}, u32[]{:S(2)}, u32[]{:S(2)}) %collective-permute-start.6) | collective-permute-done | bytes 8224 | tf_op jit(solution)/shard_map/ppermute | solution.py:69
  56.1 0.7 add.143
  56.8 0.0 collective-permute-start.7
  56.8 3.6 %collective-permute-done.7 = f32[8,256]{1,0:T(8,128)S(1)} collective-permute-done((f32[8,256]{1,0:T(8,128)S(1)}, f32[8,256]{1,0:T(8,128)S(1)}, u32[]{:S(2)}, u32[]{:S(2)}) %collective-permute-start.7) | collective-permute-done | bytes 8224 | tf_op jit(solution)/shard_map/ppermute | solution.py:69
  60.5 0.0 collective-permute-start.8
  60.5 4.9 %collective-permute-done.8 = f32[8,256]{1,0:T(8,128)S(1)} collective-permute-done((f32[8,256]{1,0:T(8,128)S(1)}, f32[8,256]{1,0:T(8,128)S(1)}, u32[]{:S(2)}, u32[]{:S(2)}) %collective-permute-start.8) | collective-permute-done | bytes 8224 | tf_op jit(solution)/shard_map/ppermute | solution.py:69
  65.3 0.0 collective-permute-start.9
  65.3 3.6 %collective-permute-done.9 = f32[8,256]{1,0:T(8,128)S(1)} collective-permute-done((f32[8,256]{1,0:T(8,128)S(1)}, f32[8,256]{1,0:T(8,128)S(1)}, u32[]{:S(2)}, u32[]{:S(2)}) %collective-permute-start.9) | collective-permute-done | bytes 8224 | tf_op jit(solution)/shard_map/ppermute | solution.py:69
  69.0 0.0 collective-permute-start.10
  69.0 4.9 %collective-permute-done.10 = f32[8,256]{1,0:T(8,128)S(1)} collective-permute-done((f32[8,256]{1,0:T(8,128)S(1)}, f32[8,256]{1,0:T(8,128)S(1)}, u32[]{:S(2)}, u32[]{:S(2)}) %collective-permute-start.10) | collective-permute-done | bytes 8224 | tf_op jit(solution)/shard_map/ppermute | solution.py:69
  73.9 0.0 collective-permute-start.11
  73.9 3.6 %collective-permute-done.11 = f32[8,256]{1,0:T(8,128)S(1)} collective-permute-done((f32[8,256]{1,0:T(8,128)S(1)}, f32[8,256]{1,0:T(8,128)S(1)}, u32[]{:S(2)}, u32[]{:S(2)}) %collective-permute-start.11) | collective-permute-done | bytes 8224 | tf_op jit(solution)/shard_map/ppermute | solution.py:69
  77.5 1.9 %collective-permute-start.12 = (f32[8,256]{1,0:T(8,128)S(1)}, f32[8,256]{1,0:T(8,128)S(1)}, u32[]{:S(2)}, u32[]{:S(2)}) collective-permute-start(f32[8,256]{1,0:T(8,128)S(1)} %add.148), channel_id=1, source_target_pairs={{0,48},{1,49},{2,50},{3,51},{4,52},{5,53},{6,54},{7,55},{8,56},{9,... | collective-permute-start | bytes 24584 | tf_op jit(solution)/shard_map/ppermute | solution.py:69
  79.4 3.0 %collective-permute-done.12 = f32[8,256]{1,0:T(8,128)S(1)} collective-permute-done((f32[8,256]{1,0:T(8,128)S(1)}, f32[8,256]{1,0:T(8,128)S(1)}, u32[]{:S(2)}, u32[]{:S(2)}) %collective-permute-start.12) | collective-permute-done | bytes 8224 | tf_op jit(solution)/shard_map/ppermute | solution.py:69
  82.4 0.6 add.149.c_ref
  83.0 0.0 copy-done
  83.0 9.1 %shard_map.76 = (f32[8,128,256]{2,1,0:T(8,128)}, f32[8,8]{1,0:T(8,128)}) custom-call(f32[8,256]{1,0:T(8,128)} %add.149.c_ref, bf16[256,128,256]{2,1,0:T(8,128)(2,1)} %bitcast.6, f32[8,128,256]{2,1,0:T(8,128)} %bitcast.7), custom_call_target="tpu_custom_call" | custom-call | flops 2147483648 | bytes 18874368 | tf_op jit(solution)/shard_map/pallas_call | solution.py:164
  92.1 0.0 copy-done.1
  92.1 0.0 collective-permute-start.13
  92.1 1.4 %collective-permute-done.13 = f32[8,8]{1,0:T(8,128)S(1)} collective-permute-done((f32[8,8]{1,0:T(8,128)}, f32[8,8]{1,0:T(8,128)S(1)}, u32[]{:S(2)}, u32[]{:S(2)}) %collective-permute-start.13) | collective-permute-done | bytes 288 | tf_op jit(solution)/shard_map/ppermute | solution.py:69
  93.5 0.7 add.150
  94.2 0.0 collective-permute-start.14
  94.2 3.6 %collective-permute-done.14 = f32[8,8]{1,0:T(8,128)S(1)} collective-permute-done((f32[8,8]{1,0:T(8,128)S(1)}, f32[8,8]{1,0:T(8,128)S(1)}, u32[]{:S(2)}, u32[]{:S(2)}) %collective-permute-start.14) | collective-permute-done | bytes 288 | tf_op jit(solution)/shard_map/ppermute | solution.py:69
  97.8 1.9 %collective-permute-start.15 = (f32[8,8]{1,0:T(8,128)S(1)}, f32[8,8]{1,0:T(8,128)S(1)}, u32[]{:S(2)}, u32[]{:S(2)}) collective-permute-start(f32[8,8]{1,0:T(8,128)S(1)} %add.151), channel_id=1, source_target_pairs={{0,3},{1,2},{2,1},{3,0},{4,7},{5,6},{6,5},{7,4},{8,11},{9,10},{10,... | collective-permute-start | bytes 776 | tf_op jit(solution)/shard_map/ppermute | solution.py:69
  99.7 2.9 %collective-permute-done.15 = f32[8,8]{1,0:T(8,128)S(1)} collective-permute-done((f32[8,8]{1,0:T(8,128)S(1)}, f32[8,8]{1,0:T(8,128)S(1)}, u32[]{:S(2)}, u32[]{:S(2)}) %collective-permute-start.15) | collective-permute-done | bytes 288 | tf_op jit(solution)/shard_map/ppermute | solution.py:69
  102.6 0.0 collective-permute-start.16
  102.6 3.6 %collective-permute-done.16 = f32[8,8]{1,0:T(8,128)S(1)} collective-permute-done((f32[8,8]{1,0:T(8,128)S(1)}, f32[8,8]{1,0:T(8,128)S(1)}, u32[]{:S(2)}, u32[]{:S(2)}) %collective-permute-start.16) | collective-permute-done | bytes 288 | tf_op jit(solution)/shard_map/ppermute | solution.py:69
  106.2 1.9 %collective-permute-start.17 = (f32[8,8]{1,0:T(8,128)S(1)}, f32[8,8]{1,0:T(8,128)S(1)}, u32[]{:S(2)}, u32[]{:S(2)}) collective-permute-start(f32[8,8]{1,0:T(8,128)S(1)} %add.153), channel_id=1, source_target_pairs={{0,12},{1,13},{2,14},{3,15},{4,8},{5,9},{6,10},{7,11},{8,4},{9,5},... | collective-permute-start | bytes 776 | tf_op jit(solution)/shard_map/ppermute | solution.py:69
  108.2 2.9 %collective-permute-done.17 = f32[8,8]{1,0:T(8,128)S(1)} collective-permute-done((f32[8,8]{1,0:T(8,128)S(1)}, f32[8,8]{1,0:T(8,128)S(1)}, u32[]{:S(2)}, u32[]{:S(2)}) %collective-permute-start.17) | collective-permute-done | bytes 288 | tf_op jit(solution)/shard_map/ppermute | solution.py:69
  111.1 0.0 collective-permute-start.18
  111.1 3.6 %collective-permute-done.18 = f32[8,8]{1,0:T(8,128)S(1)} collective-permute-done((f32[8,8]{1,0:T(8,128)S(1)}, f32[8,8]{1,0:T(8,128)S(1)}, u32[]{:S(2)}, u32[]{:S(2)}) %collective-permute-start.18) | collective-permute-done | bytes 288 | tf_op jit(solution)/shard_map/ppermute | solution.py:69
  114.7 1.9 %collective-permute-start.19 = (f32[8,8]{1,0:T(8,128)S(1)}, f32[8,8]{1,0:T(8,128)S(1)}, u32[]{:S(2)}, u32[]{:S(2)}) collective-permute-start(f32[8,8]{1,0:T(8,128)S(1)} %add.155), channel_id=1, source_target_pairs={{0,48},{1,49},{2,50},{3,51},{4,52},{5,53},{6,54},{7,55},{8,56},{9,... | collective-permute-start | bytes 776 | tf_op jit(solution)/shard_map/ppermute | solution.py:69
  116.6 2.9 %collective-permute-done.19 = f32[8,8]{1,0:T(8,128)S(1)} collective-permute-done((f32[8,8]{1,0:T(8,128)S(1)}, f32[8,8]{1,0:T(8,128)S(1)}, u32[]{:S(2)}, u32[]{:S(2)}) %collective-permute-start.19) | collective-permute-done | bytes 288 | tf_op jit(solution)/shard_map/ppermute | solution.py:69
  119.5 0.6 add.156.g_ref
  120.1 4.8 %shard_map.77 = (f32[8,8]{1,0:T(8,128)}, f32[8,128,256]{2,1,0:T(8,128)}) custom-call(f32[8,8]{1,0:T(8,128)} %add.156.g_ref, f32[8,128,256]{2,1,0:T(8,128)} %get-tuple-element.9.w_ref), custom_call_target="tpu_custom_call" | custom-call | flops 2097152 | bytes 2097152 | tf_op jit(solution)/shard_map/pallas_call | solution.py:211
  (15 shorter events, 0.1 us)
Async XLA Ops:
  0.6 21.0 %collective-permute-start.1 = (f32[4,2,64,256]{3,2,1,0:T(8,128)}, f32[4,2,64,256]{3,2,1,0:T(8,128)S(1)}, u32[]{:S(2)}, u32[]{:S(2)}) collective-permute-start(f32[4,2,64,256]{3,2,1,0:T(8,128)} %param.4), channel_id=1, source_target_pairs={{0,1},{1,2},{2,3},{3,4},{4,5},{5,6},{6,7},{7,8},{8,9},{9,10},{10,1... | collective-permute-start | bytes 1572872 | tf_op jit(solution)/shard_map/ppermute | solution.py:30
  2.7 18.9 %collective-permute-start = (f32[4,2,64,256]{3,2,1,0:T(8,128)}, f32[4,2,64,256]{3,2,1,0:T(8,128)S(1)}, u32[]{:S(2)}, u32[]{:S(2)}) collective-permute-start(f32[4,2,64,256]{3,2,1,0:T(8,128)} %param.4), channel_id=1, source_target_pairs={{1,0},{2,1},{3,2},{4,3},{5,4},{6,5},{7,6},{8,7},{9,8},{10,9},{11,1... | collective-permute-start | bytes 1572872 | tf_op jit(solution)/shard_map/ppermute | solution.py:32
  10.4 2.7 %collective-permute-start.2 = (f32[4,2,2,256]{3,2,1,0:T(2,128)S(1)}, f32[4,2,2,256]{3,2,1,0:T(2,128)S(1)}, u32[]{:S(2)}, u32[]{:S(2)}) collective-permute-start(f32[4,2,2,256]{3,2,1,0:T(2,128)S(1)} %slice_select_fusion.1), channel_id=1, source_target_pairs={{0,64},{64,0},{1,65},{65,1},{2,66},{66,2},{3,67},{67,3},{4,68},{68... | collective-permute-start | bytes 49160 | tf_op jit(solution)/shard_map/ppermute | solution.py:22
  23.2 7.8 %collective-permute-start.5 = (f32[4,2,2,256]{3,2,1,0:T(2,128)S(1)}, f32[4,2,2,256]{3,2,1,0:T(2,128)S(1)}, u32[]{:S(2)}, u32[]{:S(2)}) collective-permute-start(f32[4,2,2,256]{3,2,1,0:T(2,128)S(1)} %slice_select_fusion), channel_id=1, source_target_pairs={{0,64},{64,0},{1,65},{65,1},{2,66},{66,2},{3,67},{67,3},{4,68},{68... | collective-permute-start | bytes 49160 | tf_op jit(solution)/shard_map/ppermute | solution.py:22
  23.5 19.9 %collective-permute-start.4 = (f32[4,2,64,256]{3,2,1,0:T(8,128)S(1)}, f32[4,2,64,256]{3,2,1,0:T(8,128)S(1)}, u32[]{:S(2)}, u32[]{:S(2)}) collective-permute-start(f32[4,2,64,256]{3,2,1,0:T(8,128)S(1)} %get-tuple-element.12), channel_id=1, source_target_pairs={{0,1},{1,2},{2,3},{3,4},{4,5},{5,6},{6,7},{7,8},{8,9},{9,10},{10,1... | collective-permute-start | bytes 1572872 | tf_op jit(solution)/shard_map/ppermute | solution.py:30
  23.5 19.8 %collective-permute-start.3 = (f32[4,2,64,256]{3,2,1,0:T(8,128)S(1)}, f32[4,2,64,256]{3,2,1,0:T(8,128)S(1)}, u32[]{:S(2)}, u32[]{:S(2)}) collective-permute-start(f32[4,2,64,256]{3,2,1,0:T(8,128)S(1)} %get-tuple-element.12), channel_id=1, source_target_pairs={{1,0},{2,1},{3,2},{4,3},{5,4},{6,5},{7,6},{8,7},{9,8},{10,9},{11,1... | collective-permute-start | bytes 1572872 | tf_op jit(solution)/shard_map/ppermute | solution.py:32
  43.8 48.3 %copy-start.1 = (f32[4,2,64,256]{3,2,1,0:T(8,128)}, f32[4,2,64,256]{3,2,1,0:T(8,128)S(1)}, u32[]{:S(2)}) copy-start(f32[4,2,64,256]{3,2,1,0:T(8,128)S(1)} %fusion.43) | copy-start | bytes 1572868
  43.9 39.1 %copy-start = (f32[8,2,64,256]{3,2,1,0:T(8,128)}, f32[8,2,64,256]{3,2,1,0:T(8,128)S(1)}, u32[]{:S(2)}) copy-start(f32[8,2,64,256]{3,2,1,0:T(8,128)S(1)} %pad_maximum_fusion) | copy-start | bytes 3145732
  54.7 1.4 %collective-permute-start.6 = (f32[8,256]{1,0:T(8,128)}, f32[8,256]{1,0:T(8,128)S(1)}, u32[]{:S(2)}, u32[]{:S(2)}) collective-permute-start(f32[8,256]{1,0:T(8,128)} %shard_map.75), channel_id=1, source_target_pairs={{0,64},{64,0},{1,65},{65,1},{2,66},{66,2},{3,67},{67,3},{4,68},{68... | collective-permute-start | bytes 24584 | tf_op jit(solution)/shard_map/ppermute | solution.py:69
  56.8 3.7 %collective-permute-start.7 = (f32[8,256]{1,0:T(8,128)S(1)}, f32[8,256]{1,0:T(8,128)S(1)}, u32[]{:S(2)}, u32[]{:S(2)}) collective-permute-start(f32[8,256]{1,0:T(8,128)S(1)} %add.143), channel_id=1, source_target_pairs={{0,1},{1,0},{2,3},{3,2},{4,5},{5,4},{6,7},{7,6},{8,9},{9,8},{10,11... | collective-permute-start | bytes 24584 | tf_op jit(solution)/shard_map/ppermute | solution.py:69
  60.5 4.9 %collective-permute-start.8 = (f32[8,256]{1,0:T(8,128)S(1)}, f32[8,256]{1,0:T(8,128)S(1)}, u32[]{:S(2)}, u32[]{:S(2)}) collective-permute-start(f32[8,256]{1,0:T(8,128)S(1)} %add.144), channel_id=1, source_target_pairs={{0,3},{1,2},{2,1},{3,0},{4,7},{5,6},{6,5},{7,4},{8,11},{9,10},{10,... | collective-permute-start | bytes 24584 | tf_op jit(solution)/shard_map/ppermute | solution.py:69
  65.3 3.7 %collective-permute-start.9 = (f32[8,256]{1,0:T(8,128)S(1)}, f32[8,256]{1,0:T(8,128)S(1)}, u32[]{:S(2)}, u32[]{:S(2)}) collective-permute-start(f32[8,256]{1,0:T(8,128)S(1)} %add.145), channel_id=1, source_target_pairs={{0,4},{1,5},{2,6},{3,7},{4,0},{5,1},{6,2},{7,3},{8,12},{9,13},{10,... | collective-permute-start | bytes 24584 | tf_op jit(solution)/shard_map/ppermute | solution.py:69
  69.0 4.9 %collective-permute-start.10 = (f32[8,256]{1,0:T(8,128)S(1)}, f32[8,256]{1,0:T(8,128)S(1)}, u32[]{:S(2)}, u32[]{:S(2)}) collective-permute-start(f32[8,256]{1,0:T(8,128)S(1)} %add.146), channel_id=1, source_target_pairs={{0,12},{1,13},{2,14},{3,15},{4,8},{5,9},{6,10},{7,11},{8,4},{9,5},... | collective-permute-start | bytes 24584 | tf_op jit(solution)/shard_map/ppermute | solution.py:69
  73.9 3.7 %collective-permute-start.11 = (f32[8,256]{1,0:T(8,128)S(1)}, f32[8,256]{1,0:T(8,128)S(1)}, u32[]{:S(2)}, u32[]{:S(2)}) collective-permute-start(f32[8,256]{1,0:T(8,128)S(1)} %add.147), channel_id=1, source_target_pairs={{0,16},{1,17},{2,18},{3,19},{4,20},{5,21},{6,22},{7,23},{8,24},{9,... | collective-permute-start | bytes 24584 | tf_op jit(solution)/shard_map/ppermute | solution.py:69
  77.5 4.9 %collective-permute-start.12 = (f32[8,256]{1,0:T(8,128)S(1)}, f32[8,256]{1,0:T(8,128)S(1)}, u32[]{:S(2)}, u32[]{:S(2)}) collective-permute-start(f32[8,256]{1,0:T(8,128)S(1)} %add.148), channel_id=1, source_target_pairs={{0,48},{1,49},{2,50},{3,51},{4,52},{5,53},{6,54},{7,55},{8,56},{9,... | collective-permute-start | bytes 24584 | tf_op jit(solution)/shard_map/ppermute | solution.py:69
  92.1 1.4 %collective-permute-start.13 = (f32[8,8]{1,0:T(8,128)}, f32[8,8]{1,0:T(8,128)S(1)}, u32[]{:S(2)}, u32[]{:S(2)}) collective-permute-start(f32[8,8]{1,0:T(8,128)} %get-tuple-element.8), channel_id=1, source_target_pairs={{0,64},{64,0},{1,65},{65,1},{2,66},{66,2},{3,67},{67,3},{4,68},{68... | collective-permute-start | bytes 776 | tf_op jit(solution)/shard_map/ppermute | solution.py:69
  94.2 3.6 %collective-permute-start.14 = (f32[8,8]{1,0:T(8,128)S(1)}, f32[8,8]{1,0:T(8,128)S(1)}, u32[]{:S(2)}, u32[]{:S(2)}) collective-permute-start(f32[8,8]{1,0:T(8,128)S(1)} %add.150), channel_id=1, source_target_pairs={{0,1},{1,0},{2,3},{3,2},{4,5},{5,4},{6,7},{7,6},{8,9},{9,8},{10,11... | collective-permute-start | bytes 776 | tf_op jit(solution)/shard_map/ppermute | solution.py:69
  97.8 4.8 %collective-permute-start.15 = (f32[8,8]{1,0:T(8,128)S(1)}, f32[8,8]{1,0:T(8,128)S(1)}, u32[]{:S(2)}, u32[]{:S(2)}) collective-permute-start(f32[8,8]{1,0:T(8,128)S(1)} %add.151), channel_id=1, source_target_pairs={{0,3},{1,2},{2,1},{3,0},{4,7},{5,6},{6,5},{7,4},{8,11},{9,10},{10,... | collective-permute-start | bytes 776 | tf_op jit(solution)/shard_map/ppermute | solution.py:69
  102.6 3.6 %collective-permute-start.16 = (f32[8,8]{1,0:T(8,128)S(1)}, f32[8,8]{1,0:T(8,128)S(1)}, u32[]{:S(2)}, u32[]{:S(2)}) collective-permute-start(f32[8,8]{1,0:T(8,128)S(1)} %add.152), channel_id=1, source_target_pairs={{0,4},{1,5},{2,6},{3,7},{4,0},{5,1},{6,2},{7,3},{8,12},{9,13},{10,... | collective-permute-start | bytes 776 | tf_op jit(solution)/shard_map/ppermute | solution.py:69
  106.2 4.8 %collective-permute-start.17 = (f32[8,8]{1,0:T(8,128)S(1)}, f32[8,8]{1,0:T(8,128)S(1)}, u32[]{:S(2)}, u32[]{:S(2)}) collective-permute-start(f32[8,8]{1,0:T(8,128)S(1)} %add.153), channel_id=1, source_target_pairs={{0,12},{1,13},{2,14},{3,15},{4,8},{5,9},{6,10},{7,11},{8,4},{9,5},... | collective-permute-start | bytes 776 | tf_op jit(solution)/shard_map/ppermute | solution.py:69
  111.1 3.6 %collective-permute-start.18 = (f32[8,8]{1,0:T(8,128)S(1)}, f32[8,8]{1,0:T(8,128)S(1)}, u32[]{:S(2)}, u32[]{:S(2)}) collective-permute-start(f32[8,8]{1,0:T(8,128)S(1)} %add.154), channel_id=1, source_target_pairs={{0,16},{1,17},{2,18},{3,19},{4,20},{5,21},{6,22},{7,23},{8,24},{9,... | collective-permute-start | bytes 776 | tf_op jit(solution)/shard_map/ppermute | solution.py:69
  114.7 4.8 %collective-permute-start.19 = (f32[8,8]{1,0:T(8,128)S(1)}, f32[8,8]{1,0:T(8,128)S(1)}, u32[]{:S(2)}, u32[]{:S(2)}) collective-permute-start(f32[8,8]{1,0:T(8,128)S(1)} %add.155), channel_id=1, source_target_pairs={{0,48},{1,49},{2,50},{3,51},{4,52},{5,53},{6,54},{7,55},{8,56},{9,... | collective-permute-start | bytes 776 | tf_op jit(solution)/shard_map/ppermute | solution.py:69

commit v17 on v12

--- a/solution.py
+++ b/solution.py
@@ -189,14 +189,12 @@
         upper = jnp.where(row == j, newrow, upper)
     u_ref[...] = upper
 
-    def entry(s, t):
-        return jnp.sum(jnp.where((row == t) & (col == s), upper, 0.0))
-
     for s in range(ns):
+        ucol = jnp.sum(jnp.where(col == s, upper, 0.0), axis=1, keepdims=True)
         acc = w_ref[s]
         for t in range(s):
-            acc = acc - entry(s, t) * d_ref[t]
-        d_ref[s] = acc * (1.0 / entry(s, s))
+            acc = acc - ucol[t:t + 1, :] * d_ref[t]
+        d_ref[s] = acc / ucol[s:s + 1, :]
 
 
 def factor_and_solve(gram, residual3):

time: 125 us -> 125 us (level)
  no operation moved by 1% of the time
where the time goes in v17:
time: 125 us; the launch traced here: 124 us
  waiting for transfers between devices  60.3 us (48%)
  starting transfers between devices  24.3 us (19%)
  Pallas kernels  23.3 us (19%)
  other arithmetic  13.6 us (11%)
  local copies, waits for them, and re-layouts  2.08 us (2%)
    ppermute x14, waiting for transfers between devices, allreduce(): value = value + lax.ppermute(value, name, pairs)  45.9 us
    ppermute x2, waiting for transfers between devices, extended(): lax.ppermute(tail, axis, [(i, (i + 1) % count) for i in range(ends)])  14.4 us
    ppermute x2, starting transfers between devices, extended(): lax.ppermute(head, axis, [((i + 1) % count, i) for i in range(ends)])  14.3 us
    pallas_call x1, Pallas kernels, project(): pl.pallas_call(project_kernel, grid=(nk // tk,), in_specs=[pl.BlockSpec((...  9.48 us
    pallas_call x1, Pallas kernels, residual(): pl.pallas_call(residual_kernel, grid=(nr // block_rows,), in_specs=[pl.Bl...  9.11 us
    ppermute x14, starting transfers between devices, allreduce(): value = value + lax.ppermute(value, name, pairs)  7.68 us
    mul x2, other arithmetic, local_terms(): viscosity * (second_diff(ypadded, center, 2, ny_loc) + second_diff(zpadde...  5.22 us
    pallas_call x1, Pallas kernels, factor_and_solve(): pl.pallas_call(factor_kernel, in_specs=[vmem, vmem], out_specs=[vmem, vme...  4.74 us
  transfers between devices with their start and end apart: 20, of which 16 were waited for; matrix products, arithmetic and copies ran while one was open for 8% of the time, Pallas kernels for 0%

profile of v17, /device:TPU:0, one launch (start us, length us, event | category | flops | bytes accessed | tf_op | source)
XLA Modules:
  0.0 124.4 jit_solution(1859407876354843016)
XLA Ops:
  0.6 2.1 %collective-permute-start.1 = (f32[4,2,64,256]{3,2,1,0:T(8,128)}, f32[4,2,64,256]{3,2,1,0:T(8,128)S(1)}, u32[]{:S(2)}, u32[]{:S(2)}) collective-permute-start(f32[4,2,64,256]{3,2,1,0:T(8,128)} %param.4), channel_id=1, source_target_pairs={{0,1},{1,2},{2,3},{3,4},{4,5},{5,6},{6,7},{7,8},{8,9},{9,10},{10,1... | collective-permute-start | bytes 1572872 | tf_op jit(solution)/shard_map/ppermute | solution.py:30
  2.7 6.8 %collective-permute-start = (f32[4,2,64,256]{3,2,1,0:T(8,128)}, f32[4,2,64,256]{3,2,1,0:T(8,128)S(1)}, u32[]{:S(2)}, u32[]{:S(2)}) collective-permute-start(f32[4,2,64,256]{3,2,1,0:T(8,128)} %param.4), channel_id=1, source_target_pairs={{1,0},{2,1},{3,2},{4,3},{5,4},{6,5},{7,6},{8,7},{9,8},{10,9},{11,1... | collective-permute-start | bytes 1572872 | tf_op jit(solution)/shard_map/ppermute | solution.py:32
  9.5 0.9 slice_select_fusion.1
  10.4 0.1 collective-permute-start.2
  10.5 1.2 fusion.46
  11.7 0.7 negate_multiply_fusion
  12.4 0.7 dynamic_slice.7
  13.2 0.0 collective-permute-done.2
  13.2 4.4 %fusion.15 = f32[4,2,64,256]{3,2,1,0:T(8,128)S(1)} fusion(f32[4,2,2,256]{3,2,1,0:T(2,128)S(1)} %get-tuple-element.21, f32[4,2,64,256]{3,2,1,0:T(8,128)} %param.4, f32[4,2,2,256]{3,2,1,0:T(2,128)S(1)} %get-tuple-element.20, f32[4,2,64,2]{3,2,1,0:T(8,128)S(1)} %get-tuple-element.17, f32[4,2,64,2]{3,2,1,0:T(8,128)S(1)} %get-tuple-element.16), kind=kLoop, calls=%fused_computation.32 | loop fusion | flops 3276800 | bytes 1089536 | tf_op jit(solution)/shard_map/mul | solution.py:232
  17.6 1.0 slice_subtract_fusion
  18.6 3.0 %collective-permute-done.1 = f32[4,2,64,256]{3,2,1,0:T(8,128)S(1)} collective-permute-done((f32[4,2,64,256]{3,2,1,0:T(8,128)}, f32[4,2,64,256]{3,2,1,0:T(8,128)S(1)}, u32[]{:S(2)}, u32[]{:S(2)}) %collective-permute-start.1) | collective-permute-done | bytes 524320 | tf_op jit(solution)/shard_map/ppermute | solution.py:30
  21.6 0.0 collective-permute-done
  21.6 1.6 %multiply_add_fusion = (f32[4,2,64,256]{3,2,1,0:T(8,128)S(1)}, f32[4,2,64,256]{3,2,1,0:T(8,128)S(1)}) fusion(f32[4,2,64,256]{3,2,1,0:T(8,128)} %param.4, f32[3,2,64,256]{3,2,1,0:T(8,128)S(1)} %slice.169, f32[1,2,64,256]{3,2,1,0:T(8,128)S(1)} %slice_subtract_fusion, f32[4,2,64,256]{3,2,1,0:T(8,128)S(1)} %collective-permute-done.1, ...), kind=kLoop, calls=%fused_computation.75 | loop fusion | flops 2883584 | bytes 3145984 | tf_op jit(solution)/shard_map/add | solution.py:262
  23.2 0.1 collective-permute-start.5
  23.3 0.1 fusion.45
  23.5 0.1 collective-permute-start.4
  23.5 7.5 %collective-permute-start.3 = (f32[4,2,64,256]{3,2,1,0:T(8,128)S(1)}, f32[4,2,64,256]{3,2,1,0:T(8,128)S(1)}, u32[]{:S(2)}, u32[]{:S(2)}) collective-permute-start(f32[4,2,64,256]{3,2,1,0:T(8,128)S(1)} %get-tuple-element.12), channel_id=1, source_target_pairs={{1,0},{2,1},{3,2},{4,3},{5,4},{6,5},{7,6},{8,7},{9,8},{10,9},{11,1... | collective-permute-start | bytes 1572872 | tf_op jit(solution)/shard_map/ppermute | solution.py:32
  31.0 0.0 collective-permute-done.5
  31.0 0.8 fusion.5
  31.9 0.1 fusion.44
  32.0 11.4 %collective-permute-done.4 = f32[4,2,64,256]{3,2,1,0:T(8,128)S(1)} collective-permute-done((f32[4,2,64,256]{3,2,1,0:T(8,128)S(1)}, f32[4,2,64,256]{3,2,1,0:T(8,128)S(1)}, u32[]{:S(2)}, u32[]{:S(2)}) %collective-permute-start.4) | collective-permute-done | bytes 524320 | tf_op jit(solution)/shard_map/ppermute | solution.py:30
  43.4 0.0 collective-permute-done.3
  43.4 0.4 fusion.43
  43.8 0.0 copy-start.1
  43.8 0.1 pad_maximum_fusion
  43.9 0.0 copy-start
  43.9 1.0 bitcast_convert_fusion.s_ref
  44.9 9.5 %shard_map.75 = f32[8,256]{1,0:T(8,128)} custom-call(bf16[256,128,256]{2,1,0:T(8,128)(2,1)} %bitcast.5, bf16[8,128,256]{2,1,0:T(8,128)(2,1)} %bitcast_convert_fusion.s_ref), custom_call_target="tpu_custom_call" | custom-call | flops 2147483648 | bytes 17309696 | tf_op jit(solution)/shard_map/pallas_call | solution.py:96
  54.3 0.0 collective-permute-start.6
  54.3 1.4 %collective-permute-done.6 = f32[8,256]{1,0:T(8,128)S(1)} collective-permute-done((f32[8,256]{1,0:T(8,128)}, f32[8,256]{1,0:T(8,128)S(1)}, u32[]{:S(2)}, u32[]{:S(2)}) %collective-permute-start.6) | collective-permute-done | bytes 8224 | tf_op jit(solution)/shard_map/ppermute | solution.py:69
  55.7 0.7 add.143
  56.4 0.0 collective-permute-start.7
  56.4 3.6 %collective-permute-done.7 = f32[8,256]{1,0:T(8,128)S(1)} collective-permute-done((f32[8,256]{1,0:T(8,128)S(1)}, f32[8,256]{1,0:T(8,128)S(1)}, u32[]{:S(2)}, u32[]{:S(2)}) %collective-permute-start.7) | collective-permute-done | bytes 8224 | tf_op jit(solution)/shard_map/ppermute | solution.py:69
  60.1 0.0 collective-permute-start.8
  60.1 4.9 %collective-permute-done.8 = f32[8,256]{1,0:T(8,128)S(1)} collective-permute-done((f32[8,256]{1,0:T(8,128)S(1)}, f32[8,256]{1,0:T(8,128)S(1)}, u32[]{:S(2)}, u32[]{:S(2)}) %collective-permute-start.8) | collective-permute-done | bytes 8224 | tf_op jit(solution)/shard_map/ppermute | solution.py:69
  64.9 0.0 collective-permute-start.9
  64.9 3.6 %collective-permute-done.9 = f32[8,256]{1,0:T(8,128)S(1)} collective-permute-done((f32[8,256]{1,0:T(8,128)S(1)}, f32[8,256]{1,0:T(8,128)S(1)}, u32[]{:S(2)}, u32[]{:S(2)}) %collective-permute-start.9) | collective-permute-done | bytes 8224 | tf_op jit(solution)/shard_map/ppermute | solution.py:69
  68.6 0.0 collective-permute-start.10
  68.6 4.9 %collective-permute-done.10 = f32[8,256]{1,0:T(8,128)S(1)} collective-permute-done((f32[8,256]{1,0:T(8,128)S(1)}, f32[8,256]{1,0:T(8,128)S(1)}, u32[]{:S(2)}, u32[]{:S(2)}) %collective-permute-start.10) | collective-permute-done | bytes 8224 | tf_op jit(solution)/shard_map/ppermute | solution.py:69
  73.5 0.0 collective-permute-start.11
  73.5 3.6 %collective-permute-done.11 = f32[8,256]{1,0:T(8,128)S(1)} collective-permute-done((f32[8,256]{1,0:T(8,128)S(1)}, f32[8,256]{1,0:T(8,128)S(1)}, u32[]{:S(2)}, u32[]{:S(2)}) %collective-permute-start.11) | collective-permute-done | bytes 8224 | tf_op jit(solution)/shard_map/ppermute | solution.py:69
  77.1 1.9 %collective-permute-start.12 = (f32[8,256]{1,0:T(8,128)S(1)}, f32[8,256]{1,0:T(8,128)S(1)}, u32[]{:S(2)}, u32[]{:S(2)}) collective-permute-start(f32[8,256]{1,0:T(8,128)S(1)} %add.148), channel_id=1, source_target_pairs={{0,48},{1,49},{2,50},{3,51},{4,52},{5,53},{6,54},{7,55},{8,56},{9,... | collective-permute-start | bytes 24584 | tf_op jit(solution)/shard_map/ppermute | solution.py:69
  79.0 3.0 %collective-permute-done.12 = f32[8,256]{1,0:T(8,128)S(1)} collective-permute-done((f32[8,256]{1,0:T(8,128)S(1)}, f32[8,256]{1,0:T(8,128)S(1)}, u32[]{:S(2)}, u32[]{:S(2)}) %collective-permute-start.12) | collective-permute-done | bytes 8224 | tf_op jit(solution)/shard_map/ppermute | solution.py:69
  82.0 0.6 add.149.c_ref
  82.6 0.0 copy-done
  82.6 9.1 %shard_map.76 = (f32[8,128,256]{2,1,0:T(8,128)}, f32[8,8]{1,0:T(8,128)}) custom-call(f32[8,256]{1,0:T(8,128)} %add.149.c_ref, bf16[256,128,256]{2,1,0:T(8,128)(2,1)} %bitcast.6, f32[8,128,256]{2,1,0:T(8,128)} %bitcast.7), custom_call_target="tpu_custom_call" | custom-call | flops 2147483648 | bytes 18874368 | tf_op jit(solution)/shard_map/pallas_call | solution.py:158
  91.7 0.0 copy-done.1
  91.7 0.0 collective-permute-start.13
  91.7 1.4 %collective-permute-done.13 = f32[8,8]{1,0:T(8,128)S(1)} collective-permute-done((f32[8,8]{1,0:T(8,128)}, f32[8,8]{1,0:T(8,128)S(1)}, u32[]{:S(2)}, u32[]{:S(2)}) %collective-permute-start.13) | collective-permute-done | bytes 288 | tf_op jit(solution)/shard_map/ppermute | solution.py:69
  93.1 0.7 add.150
  93.8 0.0 collective-permute-start.14
  93.8 3.6 %collective-permute-done.14 = f32[8,8]{1,0:T(8,128)S(1)} collective-permute-done((f32[8,8]{1,0:T(8,128)S(1)}, f32[8,8]{1,0:T(8,128)S(1)}, u32[]{:S(2)}, u32[]{:S(2)}) %collective-permute-start.14) | collective-permute-done | bytes 288 | tf_op jit(solution)/shard_map/ppermute | solution.py:69
  97.4 1.9 %collective-permute-start.15 = (f32[8,8]{1,0:T(8,128)S(1)}, f32[8,8]{1,0:T(8,128)S(1)}, u32[]{:S(2)}, u32[]{:S(2)}) collective-permute-start(f32[8,8]{1,0:T(8,128)S(1)} %add.151), channel_id=1, source_target_pairs={{0,3},{1,2},{2,1},{3,0},{4,7},{5,6},{6,5},{7,4},{8,11},{9,10},{10,... | collective-permute-start | bytes 776 | tf_op jit(solution)/shard_map/ppermute | solution.py:69
  99.3 2.9 %collective-permute-done.15 = f32[8,8]{1,0:T(8,128)S(1)} collective-permute-done((f32[8,8]{1,0:T(8,128)S(1)}, f32[8,8]{1,0:T(8,128)S(1)}, u32[]{:S(2)}, u32[]{:S(2)}) %collective-permute-start.15) | collective-permute-done | bytes 288 | tf_op jit(solution)/shard_map/ppermute | solution.py:69
  102.2 0.0 collective-permute-start.16
  102.2 3.6 %collective-permute-done.16 = f32[8,8]{1,0:T(8,128)S(1)} collective-permute-done((f32[8,8]{1,0:T(8,128)S(1)}, f32[8,8]{1,0:T(8,128)S(1)}, u32[]{:S(2)}, u32[]{:S(2)}) %collective-permute-start.16) | collective-permute-done | bytes 288 | tf_op jit(solution)/shard_map/ppermute | solution.py:69
  105.8 1.9 %collective-permute-start.17 = (f32[8,8]{1,0:T(8,128)S(1)}, f32[8,8]{1,0:T(8,128)S(1)}, u32[]{:S(2)}, u32[]{:S(2)}) collective-permute-start(f32[8,8]{1,0:T(8,128)S(1)} %add.153), channel_id=1, source_target_pairs={{0,12},{1,13},{2,14},{3,15},{4,8},{5,9},{6,10},{7,11},{8,4},{9,5},... | collective-permute-start | bytes 776 | tf_op jit(solution)/shard_map/ppermute | solution.py:69
  107.8 2.9 %collective-permute-done.17 = f32[8,8]{1,0:T(8,128)S(1)} collective-permute-done((f32[8,8]{1,0:T(8,128)S(1)}, f32[8,8]{1,0:T(8,128)S(1)}, u32[]{:S(2)}, u32[]{:S(2)}) %collective-permute-start.17) | collective-permute-done | bytes 288 | tf_op jit(solution)/shard_map/ppermute | solution.py:69
  110.7 0.0 collective-permute-start.18
  110.7 3.6 %collective-permute-done.18 = f32[8,8]{1,0:T(8,128)S(1)} collective-permute-done((f32[8,8]{1,0:T(8,128)S(1)}, f32[8,8]{1,0:T(8,128)S(1)}, u32[]{:S(2)}, u32[]{:S(2)}) %collective-permute-start.18) | collective-permute-done | bytes 288 | tf_op jit(solution)/shard_map/ppermute | solution.py:69
  114.3 1.9 %collective-permute-start.19 = (f32[8,8]{1,0:T(8,128)S(1)}, f32[8,8]{1,0:T(8,128)S(1)}, u32[]{:S(2)}, u32[]{:S(2)}) collective-permute-start(f32[8,8]{1,0:T(8,128)S(1)} %add.155), channel_id=1, source_target_pairs={{0,48},{1,49},{2,50},{3,51},{4,52},{5,53},{6,54},{7,55},{8,56},{9,... | collective-permute-start | bytes 776 | tf_op jit(solution)/shard_map/ppermute | solution.py:69
  116.2 2.9 %collective-permute-done.19 = f32[8,8]{1,0:T(8,128)S(1)} collective-permute-done((f32[8,8]{1,0:T(8,128)S(1)}, f32[8,8]{1,0:T(8,128)S(1)}, u32[]{:S(2)}, u32[]{:S(2)}) %collective-permute-start.19) | collective-permute-done | bytes 288 | tf_op jit(solution)/shard_map/ppermute | solution.py:69
  119.1 0.6 add.156.g_ref
  119.7 4.7 %shard_map.77 = (f32[8,8]{1,0:T(8,128)}, f32[8,128,256]{2,1,0:T(8,128)}) custom-call(f32[8,8]{1,0:T(8,128)} %add.156.g_ref, f32[8,128,256]{2,1,0:T(8,128)} %get-tuple-element.9.w_ref), custom_call_target="tpu_custom_call" | custom-call | flops 2097152 | bytes 2097152 | tf_op jit(solution)/shard_map/pallas_call | solution.py:203
  (15 shorter events, 0.1 us)
Async XLA Ops:
  0.6 21.0 %collective-permute-start.1 = (f32[4,2,64,256]{3,2,1,0:T(8,128)}, f32[4,2,64,256]{3,2,1,0:T(8,128)S(1)}, u32[]{:S(2)}, u32[]{:S(2)}) collective-permute-start(f32[4,2,64,256]{3,2,1,0:T(8,128)} %param.4), channel_id=1, source_target_pairs={{0,1},{1,2},{2,3},{3,4},{4,5},{5,6},{6,7},{7,8},{8,9},{9,10},{10,1... | collective-permute-start | bytes 1572872 | tf_op jit(solution)/shard_map/ppermute | solution.py:30
  2.7 18.9 %collective-permute-start = (f32[4,2,64,256]{3,2,1,0:T(8,128)}, f32[4,2,64,256]{3,2,1,0:T(8,128)S(1)}, u32[]{:S(2)}, u32[]{:S(2)}) collective-permute-start(f32[4,2,64,256]{3,2,1,0:T(8,128)} %param.4), channel_id=1, source_target_pairs={{1,0},{2,1},{3,2},{4,3},{5,4},{6,5},{7,6},{8,7},{9,8},{10,9},{11,1... | collective-permute-start | bytes 1572872 | tf_op jit(solution)/shard_map/ppermute | solution.py:32
  10.4 2.7 %collective-permute-start.2 = (f32[4,2,2,256]{3,2,1,0:T(2,128)S(1)}, f32[4,2,2,256]{3,2,1,0:T(2,128)S(1)}, u32[]{:S(2)}, u32[]{:S(2)}) collective-permute-start(f32[4,2,2,256]{3,2,1,0:T(2,128)S(1)} %slice_select_fusion.1), channel_id=1, source_target_pairs={{0,64},{64,0},{1,65},{65,1},{2,66},{66,2},{3,67},{67,3},{4,68},{68... | collective-permute-start | bytes 49160 | tf_op jit(solution)/shard_map/ppermute | solution.py:22
  23.2 7.8 %collective-permute-start.5 = (f32[4,2,2,256]{3,2,1,0:T(2,128)S(1)}, f32[4,2,2,256]{3,2,1,0:T(2,128)S(1)}, u32[]{:S(2)}, u32[]{:S(2)}) collective-permute-start(f32[4,2,2,256]{3,2,1,0:T(2,128)S(1)} %slice_select_fusion), channel_id=1, source_target_pairs={{0,64},{64,0},{1,65},{65,1},{2,66},{66,2},{3,67},{67,3},{4,68},{68... | collective-permute-start | bytes 49160 | tf_op jit(solution)/shard_map/ppermute | solution.py:22
  23.5 19.9 %collective-permute-start.4 = (f32[4,2,64,256]{3,2,1,0:T(8,128)S(1)}, f32[4,2,64,256]{3,2,1,0:T(8,128)S(1)}, u32[]{:S(2)}, u32[]{:S(2)}) collective-permute-start(f32[4,2,64,256]{3,2,1,0:T(8,128)S(1)} %get-tuple-element.12), channel_id=1, source_target_pairs={{0,1},{1,2},{2,3},{3,4},{4,5},{5,6},{6,7},{7,8},{8,9},{9,10},{10,1... | collective-permute-start | bytes 1572872 | tf_op jit(solution)/shard_map/ppermute | solution.py:30
  23.5 19.8 %collective-permute-start.3 = (f32[4,2,64,256]{3,2,1,0:T(8,128)S(1)}, f32[4,2,64,256]{3,2,1,0:T(8,128)S(1)}, u32[]{:S(2)}, u32[]{:S(2)}) collective-permute-start(f32[4,2,64,256]{3,2,1,0:T(8,128)S(1)} %get-tuple-element.12), channel_id=1, source_target_pairs={{1,0},{2,1},{3,2},{4,3},{5,4},{6,5},{7,6},{8,7},{9,8},{10,9},{11,1... | collective-permute-start | bytes 1572872 | tf_op jit(solution)/shard_map/ppermute | solution.py:32
  43.8 47.9 %copy-start.1 = (f32[4,2,64,256]{3,2,1,0:T(8,128)}, f32[4,2,64,256]{3,2,1,0:T(8,128)S(1)}, u32[]{:S(2)}) copy-start(f32[4,2,64,256]{3,2,1,0:T(8,128)S(1)} %fusion.43) | copy-start | bytes 1572868
  43.9 38.7 %copy-start = (f32[8,2,64,256]{3,2,1,0:T(8,128)}, f32[8,2,64,256]{3,2,1,0:T(8,128)S(1)}, u32[]{:S(2)}) copy-start(f32[8,2,64,256]{3,2,1,0:T(8,128)S(1)} %pad_maximum_fusion) | copy-start | bytes 3145732
  54.3 1.4 %collective-permute-start.6 = (f32[8,256]{1,0:T(8,128)}, f32[8,256]{1,0:T(8,128)S(1)}, u32[]{:S(2)}, u32[]{:S(2)}) collective-permute-start(f32[8,256]{1,0:T(8,128)} %shard_map.75), channel_id=1, source_target_pairs={{0,64},{64,0},{1,65},{65,1},{2,66},{66,2},{3,67},{67,3},{4,68},{68... | collective-permute-start | bytes 24584 | tf_op jit(solution)/shard_map/ppermute | solution.py:69
  56.4 3.7 %collective-permute-start.7 = (f32[8,256]{1,0:T(8,128)S(1)}, f32[8,256]{1,0:T(8,128)S(1)}, u32[]{:S(2)}, u32[]{:S(2)}) collective-permute-start(f32[8,256]{1,0:T(8,128)S(1)} %add.143), channel_id=1, source_target_pairs={{0,1},{1,0},{2,3},{3,2},{4,5},{5,4},{6,7},{7,6},{8,9},{9,8},{10,11... | collective-permute-start | bytes 24584 | tf_op jit(solution)/shard_map/ppermute | solution.py:69
  60.1 4.9 %collective-permute-start.8 = (f32[8,256]{1,0:T(8,128)S(1)}, f32[8,256]{1,0:T(8,128)S(1)}, u32[]{:S(2)}, u32[]{:S(2)}) collective-permute-start(f32[8,256]{1,0:T(8,128)S(1)} %add.144), channel_id=1, source_target_pairs={{0,3},{1,2},{2,1},{3,0},{4,7},{5,6},{6,5},{7,4},{8,11},{9,10},{10,... | collective-permute-start | bytes 24584 | tf_op jit(solution)/shard_map/ppermute | solution.py:69
  64.9 3.7 %collective-permute-start.9 = (f32[8,256]{1,0:T(8,128)S(1)}, f32[8,256]{1,0:T(8,128)S(1)}, u32[]{:S(2)}, u32[]{:S(2)}) collective-permute-start(f32[8,256]{1,0:T(8,128)S(1)} %add.145), channel_id=1, source_target_pairs={{0,4},{1,5},{2,6},{3,7},{4,0},{5,1},{6,2},{7,3},{8,12},{9,13},{10,... | collective-permute-start | bytes 24584 | tf_op jit(solution)/shard_map/ppermute | solution.py:69
  68.6 4.9 %collective-permute-start.10 = (f32[8,256]{1,0:T(8,128)S(1)}, f32[8,256]{1,0:T(8,128)S(1)}, u32[]{:S(2)}, u32[]{:S(2)}) collective-permute-start(f32[8,256]{1,0:T(8,128)S(1)} %add.146), channel_id=1, source_target_pairs={{0,12},{1,13},{2,14},{3,15},{4,8},{5,9},{6,10},{7,11},{8,4},{9,5},... | collective-permute-start | bytes 24584 | tf_op jit(solution)/shard_map/ppermute | solution.py:69
  73.5 3.7 %collective-permute-start.11 = (f32[8,256]{1,0:T(8,128)S(1)}, f32[8,256]{1,0:T(8,128)S(1)}, u32[]{:S(2)}, u32[]{:S(2)}) collective-permute-start(f32[8,256]{1,0:T(8,128)S(1)} %add.147), channel_id=1, source_target_pairs={{0,16},{1,17},{2,18},{3,19},{4,20},{5,21},{6,22},{7,23},{8,24},{9,... | collective-permute-start | bytes 24584 | tf_op jit(solution)/shard_map/ppermute | solution.py:69
  77.1 4.9 %collective-permute-start.12 = (f32[8,256]{1,0:T(8,128)S(1)}, f32[8,256]{1,0:T(8,128)S(1)}, u32[]{:S(2)}, u32[]{:S(2)}) collective-permute-start(f32[8,256]{1,0:T(8,128)S(1)} %add.148), channel_id=1, source_target_pairs={{0,48},{1,49},{2,50},{3,51},{4,52},{5,53},{6,54},{7,55},{8,56},{9,... | collective-permute-start | bytes 24584 | tf_op jit(solution)/shard_map/ppermute | solution.py:69
  91.7 1.4 %collective-permute-start.13 = (f32[8,8]{1,0:T(8,128)}, f32[8,8]{1,0:T(8,128)S(1)}, u32[]{:S(2)}, u32[]{:S(2)}) collective-permute-start(f32[8,8]{1,0:T(8,128)} %get-tuple-element.8), channel_id=1, source_target_pairs={{0,64},{64,0},{1,65},{65,1},{2,66},{66,2},{3,67},{67,3},{4,68},{68... | collective-permute-start | bytes 776 | tf_op jit(solution)/shard_map/ppermute | solution.py:69
  93.8 3.6 %collective-permute-start.14 = (f32[8,8]{1,0:T(8,128)S(1)}, f32[8,8]{1,0:T(8,128)S(1)}, u32[]{:S(2)}, u32[]{:S(2)}) collective-permute-start(f32[8,8]{1,0:T(8,128)S(1)} %add.150), channel_id=1, source_target_pairs={{0,1},{1,0},{2,3},{3,2},{4,5},{5,4},{6,7},{7,6},{8,9},{9,8},{10,11... | collective-permute-start | bytes 776 | tf_op jit(solution)/shard_map/ppermute | solution.py:69
  97.4 4.8 %collective-permute-start.15 = (f32[8,8]{1,0:T(8,128)S(1)}, f32[8,8]{1,0:T(8,128)S(1)}, u32[]{:S(2)}, u32[]{:S(2)}) collective-permute-start(f32[8,8]{1,0:T(8,128)S(1)} %add.151), channel_id=1, source_target_pairs={{0,3},{1,2},{2,1},{3,0},{4,7},{5,6},{6,5},{7,4},{8,11},{9,10},{10,... | collective-permute-start | bytes 776 | tf_op jit(solution)/shard_map/ppermute | solution.py:69
  102.2 3.6 %collective-permute-start.16 = (f32[8,8]{1,0:T(8,128)S(1)}, f32[8,8]{1,0:T(8,128)S(1)}, u32[]{:S(2)}, u32[]{:S(2)}) collective-permute-start(f32[8,8]{1,0:T(8,128)S(1)} %add.152), channel_id=1, source_target_pairs={{0,4},{1,5},{2,6},{3,7},{4,0},{5,1},{6,2},{7,3},{8,12},{9,13},{10,... | collective-permute-start | bytes 776 | tf_op jit(solution)/shard_map/ppermute | solution.py:69
  105.8 4.8 %collective-permute-start.17 = (f32[8,8]{1,0:T(8,128)S(1)}, f32[8,8]{1,0:T(8,128)S(1)}, u32[]{:S(2)}, u32[]{:S(2)}) collective-permute-start(f32[8,8]{1,0:T(8,128)S(1)} %add.153), channel_id=1, source_target_pairs={{0,12},{1,13},{2,14},{3,15},{4,8},{5,9},{6,10},{7,11},{8,4},{9,5},... | collective-permute-start | bytes 776 | tf_op jit(solution)/shard_map/ppermute | solution.py:69
  110.7 3.6 %collective-permute-start.18 = (f32[8,8]{1,0:T(8,128)S(1)}, f32[8,8]{1,0:T(8,128)S(1)}, u32[]{:S(2)}, u32[]{:S(2)}) collective-permute-start(f32[8,8]{1,0:T(8,128)S(1)} %add.154), channel_id=1, source_target_pairs={{0,16},{1,17},{2,18},{3,19},{4,20},{5,21},{6,22},{7,23},{8,24},{9,... | collective-permute-start | bytes 776 | tf_op jit(solution)/shard_map/ppermute | solution.py:69
  114.3 4.8 %collective-permute-start.19 = (f32[8,8]{1,0:T(8,128)S(1)}, f32[8,8]{1,0:T(8,128)S(1)}, u32[]{:S(2)}, u32[]{:S(2)}) collective-permute-start(f32[8,8]{1,0:T(8,128)S(1)} %add.155), channel_id=1, source_target_pairs={{0,48},{1,49},{2,50},{3,51},{4,52},{5,53},{6,54},{7,55},{8,56},{9,... | collective-permute-start | bytes 776 | tf_op jit(solution)/shard_map/ppermute | solution.py:69

commit v18 on v11

--- a/solution.py
+++ b/solution.py
@@ -151,7 +151,7 @@
         g_ref[...] = gram
 
 
-def residual(coeffs_t, basis3, snaps3, block_rows=2 * ROWS):
+def residual(coeffs_t, basis3, snaps3, block_rows=4 * ROWS):
     nk, nr, nz = basis3.shape
     ns = snaps3.shape[0]
     pairs = ns * (ns + 1) // 2

time: 125 us -> 124 us (level)
  no operation moved by 1% of the time
where the time goes in v18:
time: 124 us
  waiting for transfers between devices  60.3 us (49%)
  starting transfers between devices  24.3 us (20%)
  Pallas kernels  22.7 us (18%)
  other arithmetic  13.6 us (11%)
  local copies, waits for them, and re-layouts  2.08 us (2%)
    ppermute x14, waiting for transfers between devices, allreduce(): value = value + lax.ppermute(value, name, pairs)  45.9 us
    ppermute x2, waiting for transfers between devices, extended(): lax.ppermute(tail, axis, [(i, (i + 1) % count) for i in range(ends)])  14.4 us
    ppermute x2, starting transfers between devices, extended(): lax.ppermute(head, axis, [((i + 1) % count, i) for i in range(ends)])  14.3 us
    pallas_call x1, Pallas kernels, project(): pl.pallas_call(project_kernel, grid=(nk // tk,), in_specs=[pl.BlockSpec((...  9.48 us
    pallas_call x1, Pallas kernels, residual(): pl.pallas_call(residual_kernel, grid=(nr // block_rows,), in_specs=[pl.Bl...  8.44 us
    ppermute x14, starting transfers between devices, allreduce(): value = value + lax.ppermute(value, name, pairs)  7.7 us
    mul x2, other arithmetic, local_terms(): viscosity * (second_diff(ypadded, center, 2, ny_loc) + second_diff(zpadde...  5.22 us
    pallas_call x1, Pallas kernels, factor_and_solve(): pl.pallas_call(factor_kernel, in_specs=[vmem, vmem], out_specs=[vmem, vme...  4.79 us
  transfers between devices with their start and end apart: 20, of which 16 were waited for; matrix products, arithmetic and copies ran while one was open for 8% of the time, Pallas kernels for 0%

profile of v18, /device:TPU:0, one launch (start us, length us, event | category | flops | bytes accessed | tf_op | source)
XLA Modules:
  0.0 123.8 jit_solution(5023541221284093565)
XLA Ops:
  0.6 2.1 %collective-permute-start.1 = (f32[4,2,64,256]{3,2,1,0:T(8,128)}, f32[4,2,64,256]{3,2,1,0:T(8,128)S(1)}, u32[]{:S(2)}, u32[]{:S(2)}) collective-permute-start(f32[4,2,64,256]{3,2,1,0:T(8,128)} %param.4), channel_id=1, source_target_pairs={{0,1},{1,2},{2,3},{3,4},{4,5},{5,6},{6,7},{7,8},{8,9},{9,10},{10,1... | collective-permute-start | bytes 1572872 | tf_op jit(solution)/shard_map/ppermute | solution.py:30
  2.7 6.8 %collective-permute-start = (f32[4,2,64,256]{3,2,1,0:T(8,128)}, f32[4,2,64,256]{3,2,1,0:T(8,128)S(1)}, u32[]{:S(2)}, u32[]{:S(2)}) collective-permute-start(f32[4,2,64,256]{3,2,1,0:T(8,128)} %param.4), channel_id=1, source_target_pairs={{1,0},{2,1},{3,2},{4,3},{5,4},{6,5},{7,6},{8,7},{9,8},{10,9},{11,1... | collective-permute-start | bytes 1572872 | tf_op jit(solution)/shard_map/ppermute | solution.py:32
  9.5 0.9 slice_select_fusion.1
  10.4 0.1 collective-permute-start.2
  10.5 1.2 fusion.46
  11.7 0.7 negate_multiply_fusion
  12.4 0.7 dynamic_slice.7
  13.2 0.0 collective-permute-done.2
  13.2 4.4 %fusion.15 = f32[4,2,64,256]{3,2,1,0:T(8,128)S(1)} fusion(f32[4,2,2,256]{3,2,1,0:T(2,128)S(1)} %get-tuple-element.21, f32[4,2,64,256]{3,2,1,0:T(8,128)} %param.4, f32[4,2,2,256]{3,2,1,0:T(2,128)S(1)} %get-tuple-element.20, f32[4,2,64,2]{3,2,1,0:T(8,128)S(1)} %get-tuple-element.17, f32[4,2,64,2]{3,2,1,0:T(8,128)S(1)} %get-tuple-element.16), kind=kLoop, calls=%fused_computation.32 | loop fusion | flops 3276800 | bytes 1089536 | tf_op jit(solution)/shard_map/mul | solution.py:234
  17.6 1.0 slice_subtract_fusion
  18.6 3.0 %collective-permute-done.1 = f32[4,2,64,256]{3,2,1,0:T(8,128)S(1)} collective-permute-done((f32[4,2,64,256]{3,2,1,0:T(8,128)}, f32[4,2,64,256]{3,2,1,0:T(8,128)S(1)}, u32[]{:S(2)}, u32[]{:S(2)}) %collective-permute-start.1) | collective-permute-done | bytes 524320 | tf_op jit(solution)/shard_map/ppermute | solution.py:30
  21.6 0.0 collective-permute-done
  21.6 1.6 %multiply_add_fusion = (f32[4,2,64,256]{3,2,1,0:T(8,128)S(1)}, f32[4,2,64,256]{3,2,1,0:T(8,128)S(1)}) fusion(f32[4,2,64,256]{3,2,1,0:T(8,128)} %param.4, f32[3,2,64,256]{3,2,1,0:T(8,128)S(1)} %slice.169, f32[1,2,64,256]{3,2,1,0:T(8,128)S(1)} %slice_subtract_fusion, f32[4,2,64,256]{3,2,1,0:T(8,128)S(1)} %collective-permute-done.1, ...), kind=kLoop, calls=%fused_computation.75 | loop fusion | flops 2883584 | bytes 3145984 | tf_op jit(solution)/shard_map/add | solution.py:264
  23.2 0.1 collective-permute-start.5
  23.3 0.1 fusion.45
  23.5 0.1 collective-permute-start.4
  23.5 7.5 %collective-permute-start.3 = (f32[4,2,64,256]{3,2,1,0:T(8,128)S(1)}, f32[4,2,64,256]{3,2,1,0:T(8,128)S(1)}, u32[]{:S(2)}, u32[]{:S(2)}) collective-permute-start(f32[4,2,64,256]{3,2,1,0:T(8,128)S(1)} %get-tuple-element.12), channel_id=1, source_target_pairs={{1,0},{2,1},{3,2},{4,3},{5,4},{6,5},{7,6},{8,7},{9,8},{10,9},{11,1... | collective-permute-start | bytes 1572872 | tf_op jit(solution)/shard_map/ppermute | solution.py:32
  31.0 0.0 collective-permute-done.5
  31.0 0.8 fusion.5
  31.9 0.1 fusion.44
  32.0 11.4 %collective-permute-done.4 = f32[4,2,64,256]{3,2,1,0:T(8,128)S(1)} collective-permute-done((f32[4,2,64,256]{3,2,1,0:T(8,128)S(1)}, f32[4,2,64,256]{3,2,1,0:T(8,128)S(1)}, u32[]{:S(2)}, u32[]{:S(2)}) %collective-permute-start.4) | collective-permute-done | bytes 524320 | tf_op jit(solution)/shard_map/ppermute | solution.py:30
  43.4 0.0 collective-permute-done.3
  43.4 0.4 fusion.43
  43.8 0.0 copy-start.1
  43.8 0.1 pad_maximum_fusion
  43.9 0.0 copy-start
  43.9 1.0 bitcast_convert_fusion.s_ref
  44.9 9.5 %shard_map.75 = f32[8,256]{1,0:T(8,128)} custom-call(bf16[256,128,256]{2,1,0:T(8,128)(2,1)} %bitcast.5, bf16[8,128,256]{2,1,0:T(8,128)(2,1)} %bitcast_convert_fusion.s_ref), custom_call_target="tpu_custom_call" | custom-call | flops 2147483648 | bytes 17309696 | tf_op jit(solution)/shard_map/pallas_call | solution.py:96
  54.3 0.0 collective-permute-start.6
  54.3 1.4 %collective-permute-done.6 = f32[8,256]{1,0:T(8,128)S(1)} collective-permute-done((f32[8,256]{1,0:T(8,128)}, f32[8,256]{1,0:T(8,128)S(1)}, u32[]{:S(2)}, u32[]{:S(2)}) %collective-permute-start.6) | collective-permute-done | bytes 8224 | tf_op jit(solution)/shard_map/ppermute | solution.py:69
  55.7 0.7 add.143
  56.4 0.0 collective-permute-start.7
  56.4 3.6 %collective-permute-done.7 = f32[8,256]{1,0:T(8,128)S(1)} collective-permute-done((f32[8,256]{1,0:T(8,128)S(1)}, f32[8,256]{1,0:T(8,128)S(1)}, u32[]{:S(2)}, u32[]{:S(2)}) %collective-permute-start.7) | collective-permute-done | bytes 8224 | tf_op jit(solution)/shard_map/ppermute | solution.py:69
  60.1 0.0 collective-permute-start.8
  60.1 4.9 %collective-permute-done.8 = f32[8,256]{1,0:T(8,128)S(1)} collective-permute-done((f32[8,256]{1,0:T(8,128)S(1)}, f32[8,256]{1,0:T(8,128)S(1)}, u32[]{:S(2)}, u32[]{:S(2)}) %collective-permute-start.8) | collective-permute-done | bytes 8224 | tf_op jit(solution)/shard_map/ppermute | solution.py:69
  64.9 0.0 collective-permute-start.9
  64.9 3.6 %collective-permute-done.9 = f32[8,256]{1,0:T(8,128)S(1)} collective-permute-done((f32[8,256]{1,0:T(8,128)S(1)}, f32[8,256]{1,0:T(8,128)S(1)}, u32[]{:S(2)}, u32[]{:S(2)}) %collective-permute-start.9) | collective-permute-done | bytes 8224 | tf_op jit(solution)/shard_map/ppermute | solution.py:69
  68.6 0.0 collective-permute-start.10
  68.6 4.9 %collective-permute-done.10 = f32[8,256]{1,0:T(8,128)S(1)} collective-permute-done((f32[8,256]{1,0:T(8,128)S(1)}, f32[8,256]{1,0:T(8,128)S(1)}, u32[]{:S(2)}, u32[]{:S(2)}) %collective-permute-start.10) | collective-permute-done | bytes 8224 | tf_op jit(solution)/shard_map/ppermute | solution.py:69
  73.5 0.0 collective-permute-start.11
  73.5 3.6 %collective-permute-done.11 = f32[8,256]{1,0:T(8,128)S(1)} collective-permute-done((f32[8,256]{1,0:T(8,128)S(1)}, f32[8,256]{1,0:T(8,128)S(1)}, u32[]{:S(2)}, u32[]{:S(2)}) %collective-permute-start.11) | collective-permute-done | bytes 8224 | tf_op jit(solution)/shard_map/ppermute | solution.py:69
  77.1 1.9 %collective-permute-start.12 = (f32[8,256]{1,0:T(8,128)S(1)}, f32[8,256]{1,0:T(8,128)S(1)}, u32[]{:S(2)}, u32[]{:S(2)}) collective-permute-start(f32[8,256]{1,0:T(8,128)S(1)} %add.148), channel_id=1, source_target_pairs={{0,48},{1,49},{2,50},{3,51},{4,52},{5,53},{6,54},{7,55},{8,56},{9,... | collective-permute-start | bytes 24584 | tf_op jit(solution)/shard_map/ppermute | solution.py:69
  79.0 3.0 %collective-permute-done.12 = f32[8,256]{1,0:T(8,128)S(1)} collective-permute-done((f32[8,256]{1,0:T(8,128)S(1)}, f32[8,256]{1,0:T(8,128)S(1)}, u32[]{:S(2)}, u32[]{:S(2)}) %collective-permute-start.12) | collective-permute-done | bytes 8224 | tf_op jit(solution)/shard_map/ppermute | solution.py:69
  82.0 0.6 add.149.c_ref
  82.6 0.0 copy-done
  82.6 8.4 %shard_map.76 = (f32[8,128,256]{2,1,0:T(8,128)}, f32[8,8]{1,0:T(8,128)}) custom-call(f32[8,256]{1,0:T(8,128)} %add.149.c_ref, bf16[256,128,256]{2,1,0:T(8,128)(2,1)} %bitcast.6, f32[8,128,256]{2,1,0:T(8,128)} %bitcast.7), custom_call_target="tpu_custom_call" | custom-call | flops 2147483648 | bytes 18874368 | tf_op jit(solution)/shard_map/pallas_call | solution.py:158
  91.0 0.0 copy-done.1
  91.0 0.0 collective-permute-start.13
  91.1 1.4 %collective-permute-done.13 = f32[8,8]{1,0:T(8,128)S(1)} collective-permute-done((f32[8,8]{1,0:T(8,128)}, f32[8,8]{1,0:T(8,128)S(1)}, u32[]{:S(2)}, u32[]{:S(2)}) %collective-permute-start.13) | collective-permute-done | bytes 288 | tf_op jit(solution)/shard_map/ppermute | solution.py:69
  92.5 0.7 add.150
  93.1 0.0 collective-permute-start.14
  93.1 3.6 %collective-permute-done.14 = f32[8,8]{1,0:T(8,128)S(1)} collective-permute-done((f32[8,8]{1,0:T(8,128)S(1)}, f32[8,8]{1,0:T(8,128)S(1)}, u32[]{:S(2)}, u32[]{:S(2)}) %collective-permute-start.14) | collective-permute-done | bytes 288 | tf_op jit(solution)/shard_map/ppermute | solution.py:69
  96.8 1.9 %collective-permute-start.15 = (f32[8,8]{1,0:T(8,128)S(1)}, f32[8,8]{1,0:T(8,128)S(1)}, u32[]{:S(2)}, u32[]{:S(2)}) collective-permute-start(f32[8,8]{1,0:T(8,128)S(1)} %add.151), channel_id=1, source_target_pairs={{0,3},{1,2},{2,1},{3,0},{4,7},{5,6},{6,5},{7,4},{8,11},{9,10},{10,... | collective-permute-start | bytes 776 | tf_op jit(solution)/shard_map/ppermute | solution.py:69
  98.7 2.9 %collective-permute-done.15 = f32[8,8]{1,0:T(8,128)S(1)} collective-permute-done((f32[8,8]{1,0:T(8,128)S(1)}, f32[8,8]{1,0:T(8,128)S(1)}, u32[]{:S(2)}, u32[]{:S(2)}) %collective-permute-start.15) | collective-permute-done | bytes 288 | tf_op jit(solution)/shard_map/ppermute | solution.py:69
  101.6 0.0 collective-permute-start.16
  101.6 3.6 %collective-permute-done.16 = f32[8,8]{1,0:T(8,128)S(1)} collective-permute-done((f32[8,8]{1,0:T(8,128)S(1)}, f32[8,8]{1,0:T(8,128)S(1)}, u32[]{:S(2)}, u32[]{:S(2)}) %collective-permute-start.16) | collective-permute-done | bytes 288 | tf_op jit(solution)/shard_map/ppermute | solution.py:69
  105.2 1.9 %collective-permute-start.17 = (f32[8,8]{1,0:T(8,128)S(1)}, f32[8,8]{1,0:T(8,128)S(1)}, u32[]{:S(2)}, u32[]{:S(2)}) collective-permute-start(f32[8,8]{1,0:T(8,128)S(1)} %add.153), channel_id=1, source_target_pairs={{0,12},{1,13},{2,14},{3,15},{4,8},{5,9},{6,10},{7,11},{8,4},{9,5},... | collective-permute-start | bytes 776 | tf_op jit(solution)/shard_map/ppermute | solution.py:69
  107.1 2.9 %collective-permute-done.17 = f32[8,8]{1,0:T(8,128)S(1)} collective-permute-done((f32[8,8]{1,0:T(8,128)S(1)}, f32[8,8]{1,0:T(8,128)S(1)}, u32[]{:S(2)}, u32[]{:S(2)}) %collective-permute-start.17) | collective-permute-done | bytes 288 | tf_op jit(solution)/shard_map/ppermute | solution.py:69
  110.0 0.0 collective-permute-start.18
  110.0 3.6 %collective-permute-done.18 = f32[8,8]{1,0:T(8,128)S(1)} collective-permute-done((f32[8,8]{1,0:T(8,128)S(1)}, f32[8,8]{1,0:T(8,128)S(1)}, u32[]{:S(2)}, u32[]{:S(2)}) %collective-permute-start.18) | collective-permute-done | bytes 288 | tf_op jit(solution)/shard_map/ppermute | solution.py:69
  113.6 1.9 %collective-permute-start.19 = (f32[8,8]{1,0:T(8,128)S(1)}, f32[8,8]{1,0:T(8,128)S(1)}, u32[]{:S(2)}, u32[]{:S(2)}) collective-permute-start(f32[8,8]{1,0:T(8,128)S(1)} %add.155), channel_id=1, source_target_pairs={{0,48},{1,49},{2,50},{3,51},{4,52},{5,53},{6,54},{7,55},{8,56},{9,... | collective-permute-start | bytes 776 | tf_op jit(solution)/shard_map/ppermute | solution.py:69
  115.5 2.9 %collective-permute-done.19 = f32[8,8]{1,0:T(8,128)S(1)} collective-permute-done((f32[8,8]{1,0:T(8,128)S(1)}, f32[8,8]{1,0:T(8,128)S(1)}, u32[]{:S(2)}, u32[]{:S(2)}) %collective-permute-start.19) | collective-permute-done | bytes 288 | tf_op jit(solution)/shard_map/ppermute | solution.py:69
  118.4 0.6 add.156.g_ref
  119.0 4.8 %shard_map.77 = (f32[8,8]{1,0:T(8,128)}, f32[8,128,256]{2,1,0:T(8,128)}) custom-call(f32[8,8]{1,0:T(8,128)} %add.156.g_ref, f32[8,128,256]{2,1,0:T(8,128)} %get-tuple-element.9.w_ref), custom_call_target="tpu_custom_call" | custom-call | flops 2097152 | bytes 2097152 | tf_op jit(solution)/shard_map/pallas_call | solution.py:205
  (15 shorter events, 0.1 us)
Async XLA Ops:
  0.6 21.0 %collective-permute-start.1 = (f32[4,2,64,256]{3,2,1,0:T(8,128)}, f32[4,2,64,256]{3,2,1,0:T(8,128)S(1)}, u32[]{:S(2)}, u32[]{:S(2)}) collective-permute-start(f32[4,2,64,256]{3,2,1,0:T(8,128)} %param.4), channel_id=1, source_target_pairs={{0,1},{1,2},{2,3},{3,4},{4,5},{5,6},{6,7},{7,8},{8,9},{9,10},{10,1... | collective-permute-start | bytes 1572872 | tf_op jit(solution)/shard_map/ppermute | solution.py:30
  2.7 18.9 %collective-permute-start = (f32[4,2,64,256]{3,2,1,0:T(8,128)}, f32[4,2,64,256]{3,2,1,0:T(8,128)S(1)}, u32[]{:S(2)}, u32[]{:S(2)}) collective-permute-start(f32[4,2,64,256]{3,2,1,0:T(8,128)} %param.4), channel_id=1, source_target_pairs={{1,0},{2,1},{3,2},{4,3},{5,4},{6,5},{7,6},{8,7},{9,8},{10,9},{11,1... | collective-permute-start | bytes 1572872 | tf_op jit(solution)/shard_map/ppermute | solution.py:32
  10.4 2.7 %collective-permute-start.2 = (f32[4,2,2,256]{3,2,1,0:T(2,128)S(1)}, f32[4,2,2,256]{3,2,1,0:T(2,128)S(1)}, u32[]{:S(2)}, u32[]{:S(2)}) collective-permute-start(f32[4,2,2,256]{3,2,1,0:T(2,128)S(1)} %slice_select_fusion.1), channel_id=1, source_target_pairs={{0,64},{64,0},{1,65},{65,1},{2,66},{66,2},{3,67},{67,3},{4,68},{68... | collective-permute-start | bytes 49160 | tf_op jit(solution)/shard_map/ppermute | solution.py:22
  23.2 7.8 %collective-permute-start.5 = (f32[4,2,2,256]{3,2,1,0:T(2,128)S(1)}, f32[4,2,2,256]{3,2,1,0:T(2,128)S(1)}, u32[]{:S(2)}, u32[]{:S(2)}) collective-permute-start(f32[4,2,2,256]{3,2,1,0:T(2,128)S(1)} %slice_select_fusion), channel_id=1, source_target_pairs={{0,64},{64,0},{1,65},{65,1},{2,66},{66,2},{3,67},{67,3},{4,68},{68... | collective-permute-start | bytes 49160 | tf_op jit(solution)/shard_map/ppermute | solution.py:22
  23.5 19.9 %collective-permute-start.4 = (f32[4,2,64,256]{3,2,1,0:T(8,128)S(1)}, f32[4,2,64,256]{3,2,1,0:T(8,128)S(1)}, u32[]{:S(2)}, u32[]{:S(2)}) collective-permute-start(f32[4,2,64,256]{3,2,1,0:T(8,128)S(1)} %get-tuple-element.12), channel_id=1, source_target_pairs={{0,1},{1,2},{2,3},{3,4},{4,5},{5,6},{6,7},{7,8},{8,9},{9,10},{10,1... | collective-permute-start | bytes 1572872 | tf_op jit(solution)/shard_map/ppermute | solution.py:30
  23.5 19.8 %collective-permute-start.3 = (f32[4,2,64,256]{3,2,1,0:T(8,128)S(1)}, f32[4,2,64,256]{3,2,1,0:T(8,128)S(1)}, u32[]{:S(2)}, u32[]{:S(2)}) collective-permute-start(f32[4,2,64,256]{3,2,1,0:T(8,128)S(1)} %get-tuple-element.12), channel_id=1, source_target_pairs={{1,0},{2,1},{3,2},{4,3},{5,4},{6,5},{7,6},{8,7},{9,8},{10,9},{11,1... | collective-permute-start | bytes 1572872 | tf_op jit(solution)/shard_map/ppermute | solution.py:32
  43.8 47.3 %copy-start.1 = (f32[4,2,64,256]{3,2,1,0:T(8,128)}, f32[4,2,64,256]{3,2,1,0:T(8,128)S(1)}, u32[]{:S(2)}) copy-start(f32[4,2,64,256]{3,2,1,0:T(8,128)S(1)} %fusion.43) | copy-start | bytes 1572868
  43.9 38.7 %copy-start = (f32[8,2,64,256]{3,2,1,0:T(8,128)}, f32[8,2,64,256]{3,2,1,0:T(8,128)S(1)}, u32[]{:S(2)}) copy-start(f32[8,2,64,256]{3,2,1,0:T(8,128)S(1)} %pad_maximum_fusion) | copy-start | bytes 3145732
  54.3 1.4 %collective-permute-start.6 = (f32[8,256]{1,0:T(8,128)}, f32[8,256]{1,0:T(8,128)S(1)}, u32[]{:S(2)}, u32[]{:S(2)}) collective-permute-start(f32[8,256]{1,0:T(8,128)} %shard_map.75), channel_id=1, source_target_pairs={{0,64},{64,0},{1,65},{65,1},{2,66},{66,2},{3,67},{67,3},{4,68},{68... | collective-permute-start | bytes 24584 | tf_op jit(solution)/shard_map/ppermute | solution.py:69
  56.4 3.7 %collective-permute-start.7 = (f32[8,256]{1,0:T(8,128)S(1)}, f32[8,256]{1,0:T(8,128)S(1)}, u32[]{:S(2)}, u32[]{:S(2)}) collective-permute-start(f32[8,256]{1,0:T(8,128)S(1)} %add.143), channel_id=1, source_target_pairs={{0,1},{1,0},{2,3},{3,2},{4,5},{5,4},{6,7},{7,6},{8,9},{9,8},{10,11... | collective-permute-start | bytes 24584 | tf_op jit(solution)/shard_map/ppermute | solution.py:69
  60.1 4.9 %collective-permute-start.8 = (f32[8,256]{1,0:T(8,128)S(1)}, f32[8,256]{1,0:T(8,128)S(1)}, u32[]{:S(2)}, u32[]{:S(2)}) collective-permute-start(f32[8,256]{1,0:T(8,128)S(1)} %add.144), channel_id=1, source_target_pairs={{0,3},{1,2},{2,1},{3,0},{4,7},{5,6},{6,5},{7,4},{8,11},{9,10},{10,... | collective-permute-start | bytes 24584 | tf_op jit(solution)/shard_map/ppermute | solution.py:69
  64.9 3.7 %collective-permute-start.9 = (f32[8,256]{1,0:T(8,128)S(1)}, f32[8,256]{1,0:T(8,128)S(1)}, u32[]{:S(2)}, u32[]{:S(2)}) collective-permute-start(f32[8,256]{1,0:T(8,128)S(1)} %add.145), channel_id=1, source_target_pairs={{0,4},{1,5},{2,6},{3,7},{4,0},{5,1},{6,2},{7,3},{8,12},{9,13},{10,... | collective-permute-start | bytes 24584 | tf_op jit(solution)/shard_map/ppermute | solution.py:69
  68.6 4.9 %collective-permute-start.10 = (f32[8,256]{1,0:T(8,128)S(1)}, f32[8,256]{1,0:T(8,128)S(1)}, u32[]{:S(2)}, u32[]{:S(2)}) collective-permute-start(f32[8,256]{1,0:T(8,128)S(1)} %add.146), channel_id=1, source_target_pairs={{0,12},{1,13},{2,14},{3,15},{4,8},{5,9},{6,10},{7,11},{8,4},{9,5},... | collective-permute-start | bytes 24584 | tf_op jit(solution)/shard_map/ppermute | solution.py:69
  73.5 3.7 %collective-permute-start.11 = (f32[8,256]{1,0:T(8,128)S(1)}, f32[8,256]{1,0:T(8,128)S(1)}, u32[]{:S(2)}, u32[]{:S(2)}) collective-permute-start(f32[8,256]{1,0:T(8,128)S(1)} %add.147), channel_id=1, source_target_pairs={{0,16},{1,17},{2,18},{3,19},{4,20},{5,21},{6,22},{7,23},{8,24},{9,... | collective-permute-start | bytes 24584 | tf_op jit(solution)/shard_map/ppermute | solution.py:69
  77.1 4.9 %collective-permute-start.12 = (f32[8,256]{1,0:T(8,128)S(1)}, f32[8,256]{1,0:T(8,128)S(1)}, u32[]{:S(2)}, u32[]{:S(2)}) collective-permute-start(f32[8,256]{1,0:T(8,128)S(1)} %add.148), channel_id=1, source_target_pairs={{0,48},{1,49},{2,50},{3,51},{4,52},{5,53},{6,54},{7,55},{8,56},{9,... | collective-permute-start | bytes 24584 | tf_op jit(solution)/shard_map/ppermute | solution.py:69
  91.0 1.4 %collective-permute-start.13 = (f32[8,8]{1,0:T(8,128)}, f32[8,8]{1,0:T(8,128)S(1)}, u32[]{:S(2)}, u32[]{:S(2)}) collective-permute-start(f32[8,8]{1,0:T(8,128)} %get-tuple-element.8), channel_id=1, source_target_pairs={{0,64},{64,0},{1,65},{65,1},{2,66},{66,2},{3,67},{67,3},{4,68},{68... | collective-permute-start | bytes 776 | tf_op jit(solution)/shard_map/ppermute | solution.py:69
  93.1 3.6 %collective-permute-start.14 = (f32[8,8]{1,0:T(8,128)S(1)}, f32[8,8]{1,0:T(8,128)S(1)}, u32[]{:S(2)}, u32[]{:S(2)}) collective-permute-start(f32[8,8]{1,0:T(8,128)S(1)} %add.150), channel_id=1, source_target_pairs={{0,1},{1,0},{2,3},{3,2},{4,5},{5,4},{6,7},{7,6},{8,9},{9,8},{10,11... | collective-permute-start | bytes 776 | tf_op jit(solution)/shard_map/ppermute | solution.py:69
  96.8 4.8 %collective-permute-start.15 = (f32[8,8]{1,0:T(8,128)S(1)}, f32[8,8]{1,0:T(8,128)S(1)}, u32[]{:S(2)}, u32[]{:S(2)}) collective-permute-start(f32[8,8]{1,0:T(8,128)S(1)} %add.151), channel_id=1, source_target_pairs={{0,3},{1,2},{2,1},{3,0},{4,7},{5,6},{6,5},{7,4},{8,11},{9,10},{10,... | collective-permute-start | bytes 776 | tf_op jit(solution)/shard_map/ppermute | solution.py:69
  101.6 3.6 %collective-permute-start.16 = (f32[8,8]{1,0:T(8,128)S(1)}, f32[8,8]{1,0:T(8,128)S(1)}, u32[]{:S(2)}, u32[]{:S(2)}) collective-permute-start(f32[8,8]{1,0:T(8,128)S(1)} %add.152), channel_id=1, source_target_pairs={{0,4},{1,5},{2,6},{3,7},{4,0},{5,1},{6,2},{7,3},{8,12},{9,13},{10,... | collective-permute-start | bytes 776 | tf_op jit(solution)/shard_map/ppermute | solution.py:69
  105.2 4.8 %collective-permute-start.17 = (f32[8,8]{1,0:T(8,128)S(1)}, f32[8,8]{1,0:T(8,128)S(1)}, u32[]{:S(2)}, u32[]{:S(2)}) collective-permute-start(f32[8,8]{1,0:T(8,128)S(1)} %add.153), channel_id=1, source_target_pairs={{0,12},{1,13},{2,14},{3,15},{4,8},{5,9},{6,10},{7,11},{8,4},{9,5},... | collective-permute-start | bytes 776 | tf_op jit(solution)/shard_map/ppermute | solution.py:69
  110.0 3.6 %collective-permute-start.18 = (f32[8,8]{1,0:T(8,128)S(1)}, f32[8,8]{1,0:T(8,128)S(1)}, u32[]{:S(2)}, u32[]{:S(2)}) collective-permute-start(f32[8,8]{1,0:T(8,128)S(1)} %add.154), channel_id=1, source_target_pairs={{0,16},{1,17},{2,18},{3,19},{4,20},{5,21},{6,22},{7,23},{8,24},{9,... | collective-permute-start | bytes 776 | tf_op jit(solution)/shard_map/ppermute | solution.py:69
  113.6 4.8 %collective-permute-start.19 = (f32[8,8]{1,0:T(8,128)S(1)}, f32[8,8]{1,0:T(8,128)S(1)}, u32[]{:S(2)}, u32[]{:S(2)}) collective-permute-start(f32[8,8]{1,0:T(8,128)S(1)} %add.155), channel_id=1, source_target_pairs={{0,48},{1,49},{2,50},{3,51},{4,52},{5,53},{6,54},{7,55},{8,56},{9,... | collective-permute-start | bytes 776 | tf_op jit(solution)/shard_map/ppermute | solution.py:69

commit v19 on v14

--- a/solution.py
+++ b/solution.py
@@ -152,7 +152,7 @@
         g_ref[...] = gram
 
 
-def residual(coeffs_t, coeffs_other, basis3, snaps3, block_rows=2 * ROWS):
+def residual(coeffs_t, coeffs_other, basis3, snaps3, block_rows=4 * ROWS):
     nk, nr, nz = basis3.shape
     ns = snaps3.shape[0]
     pairs = ns * (ns + 1) // 2

time: 125 us -> 124 us (level)
  no operation moved by 1% of the time
where the time goes in v19:
time: 124 us
  waiting for transfers between devices  59 us (48%)
  starting transfers between devices  24.3 us (20%)
  Pallas kernels  22.8 us (18%)
  other arithmetic  13.8 us (11%)
  local copies, waits for them, and re-layouts  3.27 us (3%)
    ppermute x12, waiting for transfers between devices, allreduce_halves(): value = value + lax.ppermute(value, name, pairs)  40 us
    ppermute x2, waiting for transfers between devices, extended(): lax.ppermute(tail, axis, [(i, (i + 1) % count) for i in range(ends)])  14.4 us
    ppermute x2, starting transfers between devices, extended(): lax.ppermute(head, axis, [((i + 1) % count, i) for i in range(ends)])  14.3 us
    pallas_call x1, Pallas kernels, project(): pl.pallas_call(project_kernel, grid=(nk // tk,), in_specs=[pl.BlockSpec((...  9.48 us
    pallas_call x1, Pallas kernels, residual(): pl.pallas_call(residual_kernel, grid=(nr // block_rows,), in_specs=[pl.Bl...  8.48 us
    mul x2, other arithmetic, local_terms(): viscosity * (second_diff(ypadded, center, 2, ny_loc) + second_diff(zpadde...  5.22 us
    pallas_call x1, Pallas kernels, factor_and_solve(): pl.pallas_call(factor_kernel, in_specs=[vmem, vmem, vmem], out_specs=[vme...  4.79 us
    ppermute x2, waiting for transfers between devices, allreduce_halves(): return (value, lax.ppermute(value, name, pairs))  4.55 us
  transfers between devices with their start and end apart: 20, of which 16 were waited for; matrix products, arithmetic and copies ran while one was open for 9% of the time, Pallas kernels for 0%

profile of v19, /device:TPU:0, one launch (start us, length us, event | category | flops | bytes accessed | tf_op | source)
XLA Modules:
  0.0 123.9 jit_solution(13502827898177509518)
XLA Ops:
  0.6 2.1 %collective-permute-start.1 = (f32[4,2,64,256]{3,2,1,0:T(8,128)}, f32[4,2,64,256]{3,2,1,0:T(8,128)S(1)}, u32[]{:S(2)}, u32[]{:S(2)}) collective-permute-start(f32[4,2,64,256]{3,2,1,0:T(8,128)} %param.4), channel_id=1, source_target_pairs={{0,1},{1,2},{2,3},{3,4},{4,5},{5,6},{6,7},{7,8},{8,9},{9,10},{10,1... | collective-permute-start | bytes 1572872 | tf_op jit(solution)/shard_map/ppermute | solution.py:30
  2.7 6.8 %collective-permute-start = (f32[4,2,64,256]{3,2,1,0:T(8,128)}, f32[4,2,64,256]{3,2,1,0:T(8,128)S(1)}, u32[]{:S(2)}, u32[]{:S(2)}) collective-permute-start(f32[4,2,64,256]{3,2,1,0:T(8,128)} %param.4), channel_id=1, source_target_pairs={{1,0},{2,1},{3,2},{4,3},{5,4},{6,5},{7,6},{8,7},{9,8},{10,9},{11,1... | collective-permute-start | bytes 1572872 | tf_op jit(solution)/shard_map/ppermute | solution.py:32
  9.5 0.9 slice_select_fusion.1
  10.4 0.1 collective-permute-start.2
  10.5 1.2 fusion.46
  11.7 0.7 negate_multiply_fusion
  12.4 0.7 dynamic_slice.7
  13.2 0.0 collective-permute-done.2
  13.2 4.4 %fusion.15 = f32[4,2,64,256]{3,2,1,0:T(8,128)S(1)} fusion(f32[4,2,2,256]{3,2,1,0:T(2,128)S(1)} %get-tuple-element.21, f32[4,2,64,256]{3,2,1,0:T(8,128)} %param.4, f32[4,2,2,256]{3,2,1,0:T(2,128)S(1)} %get-tuple-element.20, f32[4,2,64,2]{3,2,1,0:T(8,128)S(1)} %get-tuple-element.17, f32[4,2,64,2]{3,2,1,0:T(8,128)S(1)} %get-tuple-element.16), kind=kLoop, calls=%fused_computation.32 | loop fusion | flops 3276800 | bytes 1089536 | tf_op jit(solution)/shard_map/mul | solution.py:236
  17.6 1.0 slice_subtract_fusion
  18.6 3.0 %collective-permute-done.1 = f32[4,2,64,256]{3,2,1,0:T(8,128)S(1)} collective-permute-done((f32[4,2,64,256]{3,2,1,0:T(8,128)}, f32[4,2,64,256]{3,2,1,0:T(8,128)S(1)}, u32[]{:S(2)}, u32[]{:S(2)}) %collective-permute-start.1) | collective-permute-done | bytes 524320 | tf_op jit(solution)/shard_map/ppermute | solution.py:30
  21.6 0.0 collective-permute-done
  21.6 1.6 %multiply_add_fusion = (f32[4,2,64,256]{3,2,1,0:T(8,128)S(1)}, f32[4,2,64,256]{3,2,1,0:T(8,128)S(1)}) fusion(f32[4,2,64,256]{3,2,1,0:T(8,128)} %param.4, f32[3,2,64,256]{3,2,1,0:T(8,128)S(1)} %slice.169, f32[1,2,64,256]{3,2,1,0:T(8,128)S(1)} %slice_subtract_fusion, f32[4,2,64,256]{3,2,1,0:T(8,128)S(1)} %collective-permute-done.1, ...), kind=kLoop, calls=%fused_computation.75 | loop fusion | flops 2883584 | bytes 3145984 | tf_op jit(solution)/shard_map/add | solution.py:266
  23.2 0.1 collective-permute-start.5
  23.3 0.1 fusion.45
  23.5 0.1 collective-permute-start.4
  23.5 7.5 %collective-permute-start.3 = (f32[4,2,64,256]{3,2,1,0:T(8,128)S(1)}, f32[4,2,64,256]{3,2,1,0:T(8,128)S(1)}, u32[]{:S(2)}, u32[]{:S(2)}) collective-permute-start(f32[4,2,64,256]{3,2,1,0:T(8,128)S(1)} %get-tuple-element.12), channel_id=1, source_target_pairs={{1,0},{2,1},{3,2},{4,3},{5,4},{6,5},{7,6},{8,7},{9,8},{10,9},{11,1... | collective-permute-start | bytes 1572872 | tf_op jit(solution)/shard_map/ppermute | solution.py:32
  31.0 0.0 collective-permute-done.5
  31.0 0.8 fusion.5
  31.9 0.1 fusion.44
  32.0 11.4 %collective-permute-done.4 = f32[4,2,64,256]{3,2,1,0:T(8,128)S(1)} collective-permute-done((f32[4,2,64,256]{3,2,1,0:T(8,128)S(1)}, f32[4,2,64,256]{3,2,1,0:T(8,128)S(1)}, u32[]{:S(2)}, u32[]{:S(2)}) %collective-permute-start.4) | collective-permute-done | bytes 524320 | tf_op jit(solution)/shard_map/ppermute | solution.py:30
  43.4 0.0 collective-permute-done.3
  43.4 0.4 fusion.43
  43.8 0.0 copy-start.1
  43.8 0.1 pad_maximum_fusion
  43.9 0.0 copy-start
  43.9 1.0 bitcast_convert_fusion.s_ref
  44.9 9.5 %shard_map.75 = f32[8,256]{1,0:T(8,128)} custom-call(bf16[256,128,256]{2,1,0:T(8,128)(2,1)} %bitcast.6, bf16[8,128,256]{2,1,0:T(8,128)(2,1)} %bitcast_convert_fusion.s_ref), custom_call_target="tpu_custom_call" | custom-call | flops 2147483648 | bytes 17309696 | tf_op jit(solution)/shard_map/pallas_call | solution.py:97
  54.3 0.0 collective-permute-start.6
  54.3 1.4 %collective-permute-done.6 = f32[8,256]{1,0:T(8,128)S(1)} collective-permute-done((f32[8,256]{1,0:T(8,128)}, f32[8,256]{1,0:T(8,128)S(1)}, u32[]{:S(2)}, u32[]{:S(2)}) %collective-permute-start.6) | collective-permute-done | bytes 8224 | tf_op jit(solution)/shard_map/ppermute | solution.py:69
  55.7 0.7 add.140
  56.4 0.0 collective-permute-start.7
  56.4 3.6 %collective-permute-done.7 = f32[8,256]{1,0:T(8,128)S(1)} collective-permute-done((f32[8,256]{1,0:T(8,128)S(1)}, f32[8,256]{1,0:T(8,128)S(1)}, u32[]{:S(2)}, u32[]{:S(2)}) %collective-permute-start.7) | collective-permute-done | bytes 8224 | tf_op jit(solution)/shard_map/ppermute | solution.py:69
  60.1 0.0 collective-permute-start.8
  60.1 4.9 %collective-permute-done.8 = f32[8,256]{1,0:T(8,128)S(1)} collective-permute-done((f32[8,256]{1,0:T(8,128)S(1)}, f32[8,256]{1,0:T(8,128)S(1)}, u32[]{:S(2)}, u32[]{:S(2)}) %collective-permute-start.8) | collective-permute-done | bytes 8224 | tf_op jit(solution)/shard_map/ppermute | solution.py:69
  64.9 0.0 collective-permute-start.9
  64.9 3.6 %collective-permute-done.9 = f32[8,256]{1,0:T(8,128)S(1)} collective-permute-done((f32[8,256]{1,0:T(8,128)S(1)}, f32[8,256]{1,0:T(8,128)S(1)}, u32[]{:S(2)}, u32[]{:S(2)}) %collective-permute-start.9) | collective-permute-done | bytes 8224 | tf_op jit(solution)/shard_map/ppermute | solution.py:69
  68.6 0.0 collective-permute-start.10
  68.6 4.9 %collective-permute-done.10 = f32[8,256]{1,0:T(8,128)S(1)} collective-permute-done((f32[8,256]{1,0:T(8,128)S(1)}, f32[8,256]{1,0:T(8,128)S(1)}, u32[]{:S(2)}, u32[]{:S(2)}) %collective-permute-start.10) | collective-permute-done | bytes 8224 | tf_op jit(solution)/shard_map/ppermute | solution.py:69
  73.5 0.0 collective-permute-start.11
  73.5 3.6 %collective-permute-done.11 = f32[8,256]{1,0:T(8,128)S(1)} collective-permute-done((f32[8,256]{1,0:T(8,128)S(1)}, f32[8,256]{1,0:T(8,128)S(1)}, u32[]{:S(2)}, u32[]{:S(2)}) %collective-permute-start.11) | collective-permute-done | bytes 8224 | tf_op jit(solution)/shard_map/ppermute | solution.py:69
  77.1 1.9 %collective-permute-start.12 = (f32[8,256]{1,0:T(8,128)S(1)}, f32[8,256]{1,0:T(8,128)S(1)}, u32[]{:S(2)}, u32[]{:S(2)}) collective-permute-start(f32[8,256]{1,0:T(8,128)S(1)} %add.145.c_ref), channel_id=1, source_target_pairs={{0,48},{1,49},{2,50},{3,51},{4,52},{5,53},{6,54},{7,55},{8,56},{9,... | collective-permute-start | bytes 24584 | tf_op jit(solution)/shard_map/ppermute | solution.py:71
  79.0 3.0 %collective-permute-done.12.d_ref = f32[8,256]{1,0:T(8,128)S(1)} collective-permute-done((f32[8,256]{1,0:T(8,128)S(1)}, f32[8,256]{1,0:T(8,128)S(1)}, u32[]{:S(2)}, u32[]{:S(2)}) %collective-permute-start.12) | collective-permute-done | bytes 8224 | tf_op jit(solution)/shard_map/ppermute | solution.py:71
  82.0 0.6 copy-done.3
  82.6 8.5 %shard_map.76 = (f32[8,128,256]{2,1,0:T(8,128)}, f32[8,8]{1,0:T(8,128)}) custom-call(f32[8,256]{1,0:T(8,128)} %copy-done.2, f32[8,256]{1,0:T(8,128)} %copy-done.3, bf16[256,128,256]{2,1,0:T(8,128)(2,1)} %bitcast.7, f32[8,128,256]{2,1,0:T(8,128)} %bitcast.8), custom_call_target="tpu_custom_call" | custom-call | flops 2147483648 | bytes 18874368 | tf_op jit(solution)/shard_map/pallas_call | solution.py:159
  91.1 0.1 collective-permute-start.13
  91.1 1.4 %collective-permute-done.13 = f32[8,8]{1,0:T(8,128)S(1)} collective-permute-done((f32[8,8]{1,0:T(8,128)}, f32[8,8]{1,0:T(8,128)S(1)}, u32[]{:S(2)}, u32[]{:S(2)}) %collective-permute-start.13) | collective-permute-done | bytes 288 | tf_op jit(solution)/shard_map/ppermute | solution.py:69
  92.5 0.7 add.147
  93.2 0.0 collective-permute-start.14
  93.2 3.6 %collective-permute-done.14 = f32[8,8]{1,0:T(8,128)S(1)} collective-permute-done((f32[8,8]{1,0:T(8,128)S(1)}, f32[8,8]{1,0:T(8,128)S(1)}, u32[]{:S(2)}, u32[]{:S(2)}) %collective-permute-start.14) | collective-permute-done | bytes 288 | tf_op jit(solution)/shard_map/ppermute | solution.py:69
  96.8 1.9 %collective-permute-start.15 = (f32[8,8]{1,0:T(8,128)S(1)}, f32[8,8]{1,0:T(8,128)S(1)}, u32[]{:S(2)}, u32[]{:S(2)}) collective-permute-start(f32[8,8]{1,0:T(8,128)S(1)} %add.148), channel_id=1, source_target_pairs={{0,3},{1,2},{2,1},{3,0},{4,7},{5,6},{6,5},{7,4},{8,11},{9,10},{10,... | collective-permute-start | bytes 776 | tf_op jit(solution)/shard_map/ppermute | solution.py:69
  98.7 2.9 %collective-permute-done.15 = f32[8,8]{1,0:T(8,128)S(1)} collective-permute-done((f32[8,8]{1,0:T(8,128)S(1)}, f32[8,8]{1,0:T(8,128)S(1)}, u32[]{:S(2)}, u32[]{:S(2)}) %collective-permute-start.15) | collective-permute-done | bytes 288 | tf_op jit(solution)/shard_map/ppermute | solution.py:69
  101.6 0.0 collective-permute-start.16
  101.6 3.6 %collective-permute-done.16 = f32[8,8]{1,0:T(8,128)S(1)} collective-permute-done((f32[8,8]{1,0:T(8,128)S(1)}, f32[8,8]{1,0:T(8,128)S(1)}, u32[]{:S(2)}, u32[]{:S(2)}) %collective-permute-start.16) | collective-permute-done | bytes 288 | tf_op jit(solution)/shard_map/ppermute | solution.py:69
  105.2 1.9 %collective-permute-start.17 = (f32[8,8]{1,0:T(8,128)S(1)}, f32[8,8]{1,0:T(8,128)S(1)}, u32[]{:S(2)}, u32[]{:S(2)}) collective-permute-start(f32[8,8]{1,0:T(8,128)S(1)} %add.150), channel_id=1, source_target_pairs={{0,12},{1,13},{2,14},{3,15},{4,8},{5,9},{6,10},{7,11},{8,4},{9,5},... | collective-permute-start | bytes 776 | tf_op jit(solution)/shard_map/ppermute | solution.py:69
  107.1 2.9 %collective-permute-done.17 = f32[8,8]{1,0:T(8,128)S(1)} collective-permute-done((f32[8,8]{1,0:T(8,128)S(1)}, f32[8,8]{1,0:T(8,128)S(1)}, u32[]{:S(2)}, u32[]{:S(2)}) %collective-permute-start.17) | collective-permute-done | bytes 288 | tf_op jit(solution)/shard_map/ppermute | solution.py:69
  110.0 0.0 collective-permute-start.18
  110.1 3.6 %collective-permute-done.18 = f32[8,8]{1,0:T(8,128)S(1)} collective-permute-done((f32[8,8]{1,0:T(8,128)S(1)}, f32[8,8]{1,0:T(8,128)S(1)}, u32[]{:S(2)}, u32[]{:S(2)}) %collective-permute-start.18) | collective-permute-done | bytes 288 | tf_op jit(solution)/shard_map/ppermute | solution.py:69
  113.7 1.9 %collective-permute-start.19 = (f32[8,8]{1,0:T(8,128)S(1)}, f32[8,8]{1,0:T(8,128)S(1)}, u32[]{:S(2)}, u32[]{:S(2)}) collective-permute-start(f32[8,8]{1,0:T(8,128)S(1)} %add.152.g_ref), channel_id=1, source_target_pairs={{0,48},{1,49},{2,50},{3,51},{4,52},{5,53},{6,54},{7,55},{8,56},{9,... | collective-permute-start | bytes 776 | tf_op jit(solution)/shard_map/ppermute | solution.py:71
  115.6 1.3 %add_bitcast_fusion = f32[256,8]{0,1:T(8,128)} fusion(f32[8,256]{1,0:T(8,128)} %copy-done.2, f32[8,256]{1,0:T(8,128)} %copy-done.3), kind=kLoop, calls=%fused_computation.85 | loop fusion | flops 2048 | bytes 24576 | tf_op jit(solution)/shard_map/transpose | solution.py:275
  116.9 1.6 %collective-permute-done.19.h_ref = f32[8,8]{1,0:T(8,128)S(1)} collective-permute-done((f32[8,8]{1,0:T(8,128)S(1)}, f32[8,8]{1,0:T(8,128)S(1)}, u32[]{:S(2)}, u32[]{:S(2)}) %collective-permute-start.19) | collective-permute-done | bytes 288 | tf_op jit(solution)/shard_map/ppermute | solution.py:71
  118.5 0.0 copy-done.4
  118.5 0.6 copy-done.5
  119.1 4.8 %shard_map.77 = (f32[8,8]{1,0:T(8,128)}, f32[8,128,256]{2,1,0:T(8,128)}) custom-call(f32[8,8]{1,0:T(8,128)} %copy-done.4, f32[8,8]{1,0:T(8,128)} %copy-done.5, f32[8,128,256]{2,1,0:T(8,128)} %get-tuple-element.9.w_ref), custom_call_target="tpu_custom_call" | custom-call | flops 2097152 | bytes 2097152 | tf_op jit(solution)/shard_map/pallas_call | solution.py:207
  (22 shorter events, 0.1 us)
Async XLA Ops:
  0.6 21.0 %collective-permute-start.1 = (f32[4,2,64,256]{3,2,1,0:T(8,128)}, f32[4,2,64,256]{3,2,1,0:T(8,128)S(1)}, u32[]{:S(2)}, u32[]{:S(2)}) collective-permute-start(f32[4,2,64,256]{3,2,1,0:T(8,128)} %param.4), channel_id=1, source_target_pairs={{0,1},{1,2},{2,3},{3,4},{4,5},{5,6},{6,7},{7,8},{8,9},{9,10},{10,1... | collective-permute-start | bytes 1572872 | tf_op jit(solution)/shard_map/ppermute | solution.py:30
  2.7 18.9 %collective-permute-start = (f32[4,2,64,256]{3,2,1,0:T(8,128)}, f32[4,2,64,256]{3,2,1,0:T(8,128)S(1)}, u32[]{:S(2)}, u32[]{:S(2)}) collective-permute-start(f32[4,2,64,256]{3,2,1,0:T(8,128)} %param.4), channel_id=1, source_target_pairs={{1,0},{2,1},{3,2},{4,3},{5,4},{6,5},{7,6},{8,7},{9,8},{10,9},{11,1... | collective-permute-start | bytes 1572872 | tf_op jit(solution)/shard_map/ppermute | solution.py:32
  10.4 2.7 %collective-permute-start.2 = (f32[4,2,2,256]{3,2,1,0:T(2,128)S(1)}, f32[4,2,2,256]{3,2,1,0:T(2,128)S(1)}, u32[]{:S(2)}, u32[]{:S(2)}) collective-permute-start(f32[4,2,2,256]{3,2,1,0:T(2,128)S(1)} %slice_select_fusion.1), channel_id=1, source_target_pairs={{0,64},{64,0},{1,65},{65,1},{2,66},{66,2},{3,67},{67,3},{4,68},{68... | collective-permute-start | bytes 49160 | tf_op jit(solution)/shard_map/ppermute | solution.py:22
  23.2 7.8 %collective-permute-start.5 = (f32[4,2,2,256]{3,2,1,0:T(2,128)S(1)}, f32[4,2,2,256]{3,2,1,0:T(2,128)S(1)}, u32[]{:S(2)}, u32[]{:S(2)}) collective-permute-start(f32[4,2,2,256]{3,2,1,0:T(2,128)S(1)} %slice_select_fusion), channel_id=1, source_target_pairs={{0,64},{64,0},{1,65},{65,1},{2,66},{66,2},{3,67},{67,3},{4,68},{68... | collective-permute-start | bytes 49160 | tf_op jit(solution)/shard_map/ppermute | solution.py:22
  23.5 19.9 %collective-permute-start.4 = (f32[4,2,64,256]{3,2,1,0:T(8,128)S(1)}, f32[4,2,64,256]{3,2,1,0:T(8,128)S(1)}, u32[]{:S(2)}, u32[]{:S(2)}) collective-permute-start(f32[4,2,64,256]{3,2,1,0:T(8,128)S(1)} %get-tuple-element.12), channel_id=1, source_target_pairs={{0,1},{1,2},{2,3},{3,4},{4,5},{5,6},{6,7},{7,8},{8,9},{9,10},{10,1... | collective-permute-start | bytes 1572872 | tf_op jit(solution)/shard_map/ppermute | solution.py:30
  23.5 19.8 %collective-permute-start.3 = (f32[4,2,64,256]{3,2,1,0:T(8,128)S(1)}, f32[4,2,64,256]{3,2,1,0:T(8,128)S(1)}, u32[]{:S(2)}, u32[]{:S(2)}) collective-permute-start(f32[4,2,64,256]{3,2,1,0:T(8,128)S(1)} %get-tuple-element.12), channel_id=1, source_target_pairs={{1,0},{2,1},{3,2},{4,3},{5,4},{6,5},{7,6},{8,7},{9,8},{10,9},{11,1... | collective-permute-start | bytes 1572872 | tf_op jit(solution)/shard_map/ppermute | solution.py:32
  43.8 47.3 %copy-start.1 = (f32[4,2,64,256]{3,2,1,0:T(8,128)}, f32[4,2,64,256]{3,2,1,0:T(8,128)S(1)}, u32[]{:S(2)}) copy-start(f32[4,2,64,256]{3,2,1,0:T(8,128)S(1)} %fusion.43) | copy-start | bytes 1572868
  43.9 38.1 %copy-start = (f32[8,2,64,256]{3,2,1,0:T(8,128)}, f32[8,2,64,256]{3,2,1,0:T(8,128)S(1)}, u32[]{:S(2)}) copy-start(f32[8,2,64,256]{3,2,1,0:T(8,128)S(1)} %pad_maximum_fusion) | copy-start | bytes 3145732
  54.3 1.4 %collective-permute-start.6 = (f32[8,256]{1,0:T(8,128)}, f32[8,256]{1,0:T(8,128)S(1)}, u32[]{:S(2)}, u32[]{:S(2)}) collective-permute-start(f32[8,256]{1,0:T(8,128)} %shard_map.75), channel_id=1, source_target_pairs={{0,64},{64,0},{1,65},{65,1},{2,66},{66,2},{3,67},{67,3},{4,68},{68... | collective-permute-start | bytes 24584 | tf_op jit(solution)/shard_map/ppermute | solution.py:69
  56.4 3.7 %collective-permute-start.7 = (f32[8,256]{1,0:T(8,128)S(1)}, f32[8,256]{1,0:T(8,128)S(1)}, u32[]{:S(2)}, u32[]{:S(2)}) collective-permute-start(f32[8,256]{1,0:T(8,128)S(1)} %add.140), channel_id=1, source_target_pairs={{0,1},{1,0},{2,3},{3,2},{4,5},{5,4},{6,7},{7,6},{8,9},{9,8},{10,11... | collective-permute-start | bytes 24584 | tf_op jit(solution)/shard_map/ppermute | solution.py:69
  60.1 4.9 %collective-permute-start.8 = (f32[8,256]{1,0:T(8,128)S(1)}, f32[8,256]{1,0:T(8,128)S(1)}, u32[]{:S(2)}, u32[]{:S(2)}) collective-permute-start(f32[8,256]{1,0:T(8,128)S(1)} %add.141), channel_id=1, source_target_pairs={{0,3},{1,2},{2,1},{3,0},{4,7},{5,6},{6,5},{7,4},{8,11},{9,10},{10,... | collective-permute-start | bytes 24584 | tf_op jit(solution)/shard_map/ppermute | solution.py:69
  64.9 3.7 %collective-permute-start.9 = (f32[8,256]{1,0:T(8,128)S(1)}, f32[8,256]{1,0:T(8,128)S(1)}, u32[]{:S(2)}, u32[]{:S(2)}) collective-permute-start(f32[8,256]{1,0:T(8,128)S(1)} %add.142), channel_id=1, source_target_pairs={{0,4},{1,5},{2,6},{3,7},{4,0},{5,1},{6,2},{7,3},{8,12},{9,13},{10,... | collective-permute-start | bytes 24584 | tf_op jit(solution)/shard_map/ppermute | solution.py:69
  68.6 4.9 %collective-permute-start.10 = (f32[8,256]{1,0:T(8,128)S(1)}, f32[8,256]{1,0:T(8,128)S(1)}, u32[]{:S(2)}, u32[]{:S(2)}) collective-permute-start(f32[8,256]{1,0:T(8,128)S(1)} %add.143), channel_id=1, source_target_pairs={{0,12},{1,13},{2,14},{3,15},{4,8},{5,9},{6,10},{7,11},{8,4},{9,5},... | collective-permute-start | bytes 24584 | tf_op jit(solution)/shard_map/ppermute | solution.py:69
  73.5 3.7 %collective-permute-start.11 = (f32[8,256]{1,0:T(8,128)S(1)}, f32[8,256]{1,0:T(8,128)S(1)}, u32[]{:S(2)}, u32[]{:S(2)}) collective-permute-start(f32[8,256]{1,0:T(8,128)S(1)} %add.144), channel_id=1, source_target_pairs={{0,16},{1,17},{2,18},{3,19},{4,20},{5,21},{6,22},{7,23},{8,24},{9,... | collective-permute-start | bytes 24584 | tf_op jit(solution)/shard_map/ppermute | solution.py:69
  77.1 4.9 %copy-start.2 = (f32[8,256]{1,0:T(8,128)}, f32[8,256]{1,0:T(8,128)S(1)}, u32[]{:S(2)}) copy-start(f32[8,256]{1,0:T(8,128)S(1)} %add.145.c_ref) | copy-start | bytes 24580
  77.1 4.9 %collective-permute-start.12 = (f32[8,256]{1,0:T(8,128)S(1)}, f32[8,256]{1,0:T(8,128)S(1)}, u32[]{:S(2)}, u32[]{:S(2)}) collective-permute-start(f32[8,256]{1,0:T(8,128)S(1)} %add.145.c_ref), channel_id=1, source_target_pairs={{0,48},{1,49},{2,50},{3,51},{4,52},{5,53},{6,54},{7,55},{8,56},{9,... | collective-permute-start | bytes 24584 | tf_op jit(solution)/shard_map/ppermute | solution.py:71
  82.0 0.6 copy-start.3
  91.1 1.4 %collective-permute-start.13 = (f32[8,8]{1,0:T(8,128)}, f32[8,8]{1,0:T(8,128)S(1)}, u32[]{:S(2)}, u32[]{:S(2)}) collective-permute-start(f32[8,8]{1,0:T(8,128)} %get-tuple-element.8), channel_id=1, source_target_pairs={{0,64},{64,0},{1,65},{65,1},{2,66},{66,2},{3,67},{67,3},{4,68},{68... | collective-permute-start | bytes 776 | tf_op jit(solution)/shard_map/ppermute | solution.py:69
  93.2 3.6 %collective-permute-start.14 = (f32[8,8]{1,0:T(8,128)S(1)}, f32[8,8]{1,0:T(8,128)S(1)}, u32[]{:S(2)}, u32[]{:S(2)}) collective-permute-start(f32[8,8]{1,0:T(8,128)S(1)} %add.147), channel_id=1, source_target_pairs={{0,1},{1,0},{2,3},{3,2},{4,5},{5,4},{6,7},{7,6},{8,9},{9,8},{10,11... | collective-permute-start | bytes 776 | tf_op jit(solution)/shard_map/ppermute | solution.py:69
  96.8 4.8 %collective-permute-start.15 = (f32[8,8]{1,0:T(8,128)S(1)}, f32[8,8]{1,0:T(8,128)S(1)}, u32[]{:S(2)}, u32[]{:S(2)}) collective-permute-start(f32[8,8]{1,0:T(8,128)S(1)} %add.148), channel_id=1, source_target_pairs={{0,3},{1,2},{2,1},{3,0},{4,7},{5,6},{6,5},{7,4},{8,11},{9,10},{10,... | collective-permute-start | bytes 776 | tf_op jit(solution)/shard_map/ppermute | solution.py:69
  101.6 3.6 %collective-permute-start.16 = (f32[8,8]{1,0:T(8,128)S(1)}, f32[8,8]{1,0:T(8,128)S(1)}, u32[]{:S(2)}, u32[]{:S(2)}) collective-permute-start(f32[8,8]{1,0:T(8,128)S(1)} %add.149), channel_id=1, source_target_pairs={{0,4},{1,5},{2,6},{3,7},{4,0},{5,1},{6,2},{7,3},{8,12},{9,13},{10,... | collective-permute-start | bytes 776 | tf_op jit(solution)/shard_map/ppermute | solution.py:69
  105.2 4.8 %collective-permute-start.17 = (f32[8,8]{1,0:T(8,128)S(1)}, f32[8,8]{1,0:T(8,128)S(1)}, u32[]{:S(2)}, u32[]{:S(2)}) collective-permute-start(f32[8,8]{1,0:T(8,128)S(1)} %add.150), channel_id=1, source_target_pairs={{0,12},{1,13},{2,14},{3,15},{4,8},{5,9},{6,10},{7,11},{8,4},{9,5},... | collective-permute-start | bytes 776 | tf_op jit(solution)/shard_map/ppermute | solution.py:69
  110.0 3.6 %collective-permute-start.18 = (f32[8,8]{1,0:T(8,128)S(1)}, f32[8,8]{1,0:T(8,128)S(1)}, u32[]{:S(2)}, u32[]{:S(2)}) collective-permute-start(f32[8,8]{1,0:T(8,128)S(1)} %add.151), channel_id=1, source_target_pairs={{0,16},{1,17},{2,18},{3,19},{4,20},{5,21},{6,22},{7,23},{8,24},{9,... | collective-permute-start | bytes 776 | tf_op jit(solution)/shard_map/ppermute | solution.py:69
  113.7 4.8 %copy-start.4 = (f32[8,8]{1,0:T(8,128)}, f32[8,8]{1,0:T(8,128)S(1)}, u32[]{:S(2)}) copy-start(f32[8,8]{1,0:T(8,128)S(1)} %add.152.g_ref) | copy-start | bytes 772
  113.7 4.8 %collective-permute-start.19 = (f32[8,8]{1,0:T(8,128)S(1)}, f32[8,8]{1,0:T(8,128)S(1)}, u32[]{:S(2)}, u32[]{:S(2)}) collective-permute-start(f32[8,8]{1,0:T(8,128)S(1)} %add.152.g_ref), channel_id=1, source_target_pairs={{0,48},{1,49},{2,50},{3,51},{4,52},{5,53},{6,54},{7,55},{8,56},{9,... | collective-permute-start | bytes 776 | tf_op jit(solution)/shard_map/ppermute | solution.py:71
  118.5 0.6 copy-start.5
